TPU v7x, 768 devices: a whole 4x8x12 slice. The times are simulated.
768 devices in a mesh: gx: 96 (over z, x, core), gy: 8 (over y).
Axes of the slice: x: 4, y: 8, z: 12, core: 2. Of those that a mesh axis runs over, the one named last changes fastest.
Arguments:
- queries: bfloat16 [1536, 256, 128], P('gx', 'gy'), may hold values from -6 to 6
- keys: bfloat16 [1536, 256, 128], P('gx', 'gy'), may hold values from -6 to 6
- values: bfloat16 [1536, 256, 128], P('gx', 'gy'), may hold values from -6 to 6
- out_attn: bfloat16 [1536, 256, 128], P('gx', 'gy'), may hold values from -6 to 6
- out_grad: bfloat16 [1536, 256, 128], P('gx', 'gy'), may hold values from -6 to 6
- log_norm: bfloat16 [4, 1536, 256], P(None, 'gx', 'gy'), may hold values from 3 to 4
- neighbour_blocks: int32 [96, 32, 3], P('gx', 'gy'), may hold values from 0 to 31, as said below
- stencil: float32 [5, 128], replicated, may hold values from -3 to 3
Outputs:
- query_grad: bfloat16 [1536, 256, 128], P('gx', 'gy')
- key_grad: bfloat16 [1536, 256, 128], P('gx', 'gy')
- value_grad: bfloat16 [1536, 256, 128], P('gx', 'gy')
- stencil_grad: float32 [5, 128], replicated
Inputs may be any that keep to these rules, and one draw needn't show every extreme that they name: `neighbour_blocks`: among the entries of the 4 row blocks of one tile, at most 2 name blocks of any one tile of the strip (the tile of block c is c // 4), and exactly 2 do for some tile.
All inputs are finite; a program needn't handle non-finite values.
Results may differ from a plain program's by a relative error of at most 0.0054.
Values may be sent and summed in bfloat16 or wider, within the bound.
No kernel may reach another device: no remote copies, remote signals or barrier semaphores. Data moves between devices by JAX's collectives and lax.ppermute only.
A program may use at most 32 MiB of HBM per device.

v0:
```python
import math

import jax
import jax.numpy as jnp
from jax import lax
from jax.sharding import PartitionSpec as P

BLOCK = 128
HEADS = 4


def with_halo(block, sides, width):
    for axis, dim in sides:
        count = lax.axis_size(axis)
        forward = [(i, i + 1) for i in range(count - 1)]
        forward.append((count - 1, 0))
        backward = [(target, source) for source, target in forward]
        low = lax.ppermute(
            lax.slice_in_dim(block, block.shape[dim] - width, None, axis=dim), axis, forward
        )
        high = lax.ppermute(lax.slice_in_dim(block, 0, width, axis=dim), axis, backward)
        block = jnp.concatenate([low, block, high], axis=dim)
    return block


def tile_grads(row_pack, stat_pack, key_pack):
    item_count = row_pack.shape[0]
    block_rows = row_pack.shape[2]
    features = row_pack.shape[3]
    head_width = features // HEADS
    softmax_scale = 1.0 / math.sqrt(head_width)
    row_heads = row_pack.reshape(item_count, 2, block_rows, HEADS, head_width).transpose(
        0, 1, 3, 4, 2
    )
    key_heads_all = key_pack.reshape(item_count, 2, block_rows, HEADS, head_width).transpose(
        0, 1, 3, 4, 2
    )
    query_heads = row_heads[:, 0]
    grad_heads = row_heads[:, 1]
    key_heads = key_heads_all[:, 0]
    value_heads = key_heads_all[:, 1]
    log_part = stat_pack[:, 0].astype(jnp.float32)
    delta_part = stat_pack[:, 1].astype(jnp.float32)
    scores = (
        jnp.einsum("shdq,shdk->shqk", query_heads, key_heads, preferred_element_type=jnp.float32)
        * softmax_scale
    )
    weights = jnp.exp(scores - log_part[..., None])
    weight_grad = jnp.einsum(
        "shdq,shdk->shqk", grad_heads, value_heads, preferred_element_type=jnp.float32
    )
    score_grad = weights * (weight_grad - delta_part[..., None])
    weights_low = weights.astype(jnp.bfloat16)
    score_low = score_grad.astype(jnp.bfloat16)
    value_part = jnp.einsum(
        "shqk,shdq->shdk", weights_low, grad_heads, preferred_element_type=jnp.float32
    )
    key_part = (
        jnp.einsum("shqk,shdq->shdk", score_low, query_heads, preferred_element_type=jnp.float32)
        * softmax_scale
    )
    query_part = (
        jnp.einsum("shqk,shdk->shdq", score_low, key_heads, preferred_element_type=jnp.float32)
        * softmax_scale
    )

    def points_last(part):
        return part.reshape(item_count, features, block_rows).transpose(0, 2, 1)

    return (points_last(query_part), points_last(key_part), points_last(value_part))


def per_device(queries, keys, values, out_attn, out_grad, log_norm, neighbour_blocks, stencil):
    tile_x, tile_y, features = queries.shape
    row_blocks = tile_x * tile_y // BLOCK
    head_width = features // HEADS
    listed = neighbour_blocks.shape[2]
    group_size = lax.axis_size("gy")
    pair_count = row_blocks * listed
    capacity = max(2, (pair_count + group_size - 1) // group_size)
    slot_count = group_size * capacity
    query_blocks = queries.reshape(row_blocks, BLOCK, features)
    key_blocks = keys.reshape(row_blocks, BLOCK, features)
    value_blocks = values.reshape(row_blocks, BLOCK, features)
    grad_blocks = out_grad.reshape(row_blocks, BLOCK, features)
    products = out_grad.astype(jnp.float32) * out_attn.astype(jnp.float32)
    delta = products.reshape(row_blocks, BLOCK, HEADS, head_width).sum(-1).astype(jnp.bfloat16)
    delta = delta.transpose(0, 2, 1)
    norm_blocks = log_norm.reshape(HEADS, row_blocks, BLOCK).transpose(1, 0, 2)
    stat_blocks = jnp.stack([norm_blocks, delta], 1)
    row_pack = jnp.stack([query_blocks, grad_blocks], 1)
    key_pack = jnp.stack([key_blocks, value_blocks], 1)
    diag_query, diag_key, diag_value = tile_grads(row_pack, stat_blocks, key_pack)
    columns = neighbour_blocks.reshape(pair_count)
    owners = columns // row_blocks
    inner = columns % row_blocks
    order = jnp.arange(pair_count, dtype=jnp.int32)
    before = (owners[:, None] == owners[None, :]) & (order[None, :] < order[:, None])
    rank = jnp.sum(before.astype(jnp.int32), 1)
    slot_of = owners * capacity + rank
    placed = (jnp.arange(slot_count, dtype=jnp.int32)[:, None] == slot_of[None, :]).astype(
        jnp.float32
    )
    source_rows = (
        (order // listed)[:, None] == jnp.arange(row_blocks, dtype=jnp.int32)[None, :]
    ).astype(jnp.float32)
    picker = jnp.dot(placed, source_rows, precision=lax.Precision.HIGHEST)
    picker_low = picker.astype(jnp.bfloat16)
    send_rows = jnp.dot(
        picker_low, row_pack.reshape(row_blocks, -1), preferred_element_type=jnp.float32
    )
    send_rows = send_rows.astype(jnp.bfloat16).reshape(group_size, capacity, 2, BLOCK, features)
    send_stats = jnp.dot(
        picker_low, stat_blocks.reshape(row_blocks, -1), preferred_element_type=jnp.float32
    )
    send_stats = send_stats.astype(jnp.bfloat16).reshape(group_size, capacity, 2, HEADS, BLOCK)
    send_ids = jnp.dot(placed, (inner + 1).astype(jnp.float32), precision=lax.Precision.HIGHEST)
    send_ids = send_ids.astype(jnp.bfloat16).reshape(group_size, capacity)
    rows_in = lax.all_to_all(send_rows, "gy", split_axis=0, concat_axis=0, tiled=True)
    stats_in = lax.all_to_all(send_stats, "gy", split_axis=0, concat_axis=0, tiled=True)
    ids_in = lax.all_to_all(send_ids, "gy", split_axis=0, concat_axis=0, tiled=True)
    item_count = rows_in.shape[1]
    total_items = group_size * item_count
    wanted = ids_in.astype(jnp.float32).astype(jnp.int32) - 1
    chooser = (wanted[..., None] == jnp.arange(row_blocks, dtype=jnp.int32)).astype(jnp.bfloat16)
    keys_in = jnp.dot(
        chooser.reshape(-1, row_blocks),
        key_pack.reshape(row_blocks, -1),
        preferred_element_type=jnp.float32,
    )
    keys_in = keys_in.astype(jnp.bfloat16).reshape(total_items, 2, BLOCK, features)
    query_part, key_part, value_part = tile_grads(
        rows_in.reshape(total_items, 2, BLOCK, features),
        stats_in.reshape(total_items, 2, HEADS, BLOCK),
        keys_in,
    )
    query_part = query_part.reshape(group_size, item_count, BLOCK, features)
    key_part = key_part.reshape(group_size, item_count, BLOCK, features)
    value_part = value_part.reshape(group_size, item_count, BLOCK, features)
    returned = lax.all_to_all(query_part, "gy", split_axis=0, concat_axis=0, tiled=True)
    returned, pieces, ids_in = (returned, jnp.stack([key_part, value_part], 2), ids_in)
    query_sum = diag_query + jnp.einsum(
        "sr,sbf->rbf",
        picker,
        returned.reshape(slot_count, BLOCK, features),
        precision=lax.Precision.HIGHEST,
    )
    arrived = ids_in.reshape(slot_count).astype(jnp.float32).astype(jnp.int32) - 1
    owned = (arrived[:, None] == jnp.arange(row_blocks, dtype=jnp.int32)[None, :]).astype(
        jnp.float32
    )
    key_value_sum = jnp.einsum(
        "sr,sxbf->rxbf",
        owned,
        pieces.reshape(slot_count, 2, BLOCK, features),
        precision=lax.Precision.HIGHEST,
    )
    key_total = diag_key + key_value_sum[:, 0]
    value_total = diag_value + key_value_sum[:, 1]
    rim = with_halo(out_grad, (("gx", 0), ("gy", 1)), 1)
    moved = [
        out_grad.astype(jnp.float32),
        rim[2:, 1:-1].astype(jnp.float32),
        rim[:-2, 1:-1].astype(jnp.float32),
        rim[1:-1, 2:].astype(jnp.float32),
        rim[1:-1, :-2].astype(jnp.float32),
    ]
    value_float = values.astype(jnp.float32)
    stencil_term = stencil[0] * moved[0]
    for index in range(1, 5):
        stencil_term = stencil_term + stencil[index] * moved[index]
    partial_rows = jnp.stack(
        [jnp.sum(moved[index] * value_float, axis=(0, 1)) for index in range(5)]
    )
    summed = lax.psum(partial_rows, ("gx", "gy"))
    point_count = tile_x * tile_y * lax.axis_size("gx") * group_size
    stencil_grad = summed / math.sqrt(point_count)
    query_grad = query_sum.reshape(tile_x, tile_y, features).astype(jnp.bfloat16)
    key_grad = key_total.reshape(tile_x, tile_y, features).astype(jnp.bfloat16)
    value_grad = (value_total.reshape(tile_x, tile_y, features) + stencil_term).astype(jnp.bfloat16)
    return (query_grad, key_grad, value_grad, stencil_grad)


def solution(mesh):
    placed = (
        P("gx", "gy", None),
        P("gx", "gy", None),
        P("gx", "gy", None),
        P("gx", "gy", None),
        P("gx", "gy", None),
        P(None, "gx", "gy"),
        P("gx", "gy", None),
        P(),
    )
    return jax.shard_map(
        per_device,
        mesh=mesh,
        in_specs=placed,
        out_specs=(P("gx", "gy", None), P("gx", "gy", None), P("gx", "gy", None), P()),
        check_vma=False,
    )
```

profile of v0, /device:TPU:6, one launch (start us, length us, event | category | flops | bytes accessed | tf_op | source)
XLA Modules:
  0.0 245.7 jit_solution(762154754730478568)
XLA Ops:
  0.7 0.8 copy.122
  2.6 7.1 %all-to-all-start = ((bf16[8,1,2]{2,1,0:T(2,128)(2,1)}), bf16[8,1,2]{2,1,0:T(2,128)(2,1)S(1)}, u32[]{:S(2)}, u32[]{:S(2)}) async-start(bf16[8,1,2]{2,1,0:T(2,128)(2,1)} %all_to_all.20), calls=%async_computation | async-start | bytes 8192 | tf_op jit(solution)/shard_map/all_to_all | solution.py:121
  9.7 0.7 fusion.64
  10.4 1.9 collective-permute-start
  12.3 2.5 %collective-permute-start.1 = (bf16[1,32,128]{2,1,0:T(8,128)(2,1)S(1)}, bf16[1,32,128]{2,1,0:T(8,128)(2,1)S(1)}, u32[]{:S(2)}, u32[]{:S(2)}) collective-permute-start(bf16[1,32,128]{2,1,0:T(8,128)(2,1)S(1)} %get-tuple-element.18), channel_id=1, source_target_pairs={{0,8},{8,16},{16,24},{24,32},{32,40},{40,48},{48,56},{56,64},{64,7... | collective-permute-start | bytes 24584 | tf_op jit(solution)/shard_map/ppermute | solution.py:18
  14.9 1.1 reshape.238
  16.0 0.8 reshape.211
  16.9 1.1 reshape.237
  18.3 1.1 reshape.235
  19.7 1.1 reshape.236
  22.3 3.9 %collective-permute-start.3 = (bf16[18,1,128]{2,1,0:T(2,128)(2,1)S(1)}, bf16[18,1,128]{2,1,0:T(2,128)(2,1)S(1)}, u32[]{:S(2)}, u32[]{:S(2)}) collective-permute-start(bf16[18,1,128]{2,1,0:T(2,128)(2,1)S(1)} %get-tuple-element.14), channel_id=1, source_target_pairs={{0,1},{1,2},{2,3},{3,4},{4,5},{5,6},{6,7},{7,0},{8,9},{9,10},{10,1... | collective-permute-start | bytes 13832 | tf_op jit(solution)/shard_map/ppermute | solution.py:18
  26.2 3.1 %collective-permute-start.2 = (bf16[18,1,128]{2,1,0:T(2,128)(2,1)S(1)}, bf16[18,1,128]{2,1,0:T(2,128)(2,1)S(1)}, u32[]{:S(2)}, u32[]{:S(2)}) collective-permute-start(bf16[18,1,128]{2,1,0:T(2,128)(2,1)S(1)} %get-tuple-element.15), channel_id=1, source_target_pairs={{1,0},{2,1},{3,2},{4,3},{5,4},{6,5},{7,6},{0,7},{9,8},{10,9},{11,1... | collective-permute-start | bytes 13832 | tf_op jit(solution)/shard_map/ppermute | solution.py:21
  29.4 2.3 collective-permute-done.2
  31.8 0.8 fusion.29
  33.0 0.7 reduce_sum.63
  34.8 7.0 %all-to-all-start.2 = ((bf16[8,2,2,4,128]{4,3,2,1,0:T(4,128)(2,1)}), bf16[8,2,2,4,128]{4,3,2,1,0:T(4,128)(2,1)S(1)}, u32[]{:S(2)}, u32[]{:S(2)}) async-start(bf16[8,2,2,4,128]{4,3,2,1,0:T(4,128)(2,1)} %reshape.219), calls=%async_computation.2 | async-start | bytes 65536 | tf_op jit(solution)/shard_map/all_to_all | solution.py:120
  42.2 1.2 copy.155
  43.4 6.6 %all-to-all-done.2 = bf16[8,2,2,4,128]{4,3,2,1,0:T(4,128)(2,1)S(1)} async-done(((bf16[8,2,2,4,128]{4,3,2,1,0:T(4,128)(2,1)}), bf16[8,2,2,4,128]{4,3,2,1,0:T(4,128)(2,1)S(1)}, u32[]{:S(2)}, u32[]{:S(2)}) %all-to-all-start.2) | async-done | bytes 32800 | tf_op jit(solution)/shard_map/all_to_all | solution.py:120
  50.7 3.6 %all-to-all-start.1 = ((bf16[8,2,2,128,128]{4,3,2,1,0:T(8,128)(2,1)}), bf16[8,2,2,128,128]{4,3,2,1,0:T(8,128)(2,1)S(1)}, u32[]{:S(2)}, u32[]{:S(2)}) async-start(bf16[8,2,2,128,128]{4,3,2,1,0:T(8,128)(2,1)} %bitcast.87), calls=%async_computation.1 | async-start | bytes 2097152 | tf_op jit(solution)/shard_map/all_to_all | solution.py:119
  54.5 0.8 copy.139
  55.3 0.7 pad_maximum_fusion
  56.6 0.7 add_reduce_fusion
  57.9 1.5 convolution_convert_fusion.1
  59.4 4.6 %reshape_reshape.6 = bf16[16,2,128,4,32]{4,3,2,1,0:T(4,128)(2,1)} reshape(bf16[16,32768]{1,0:T(8,128)(2,1)S(1)} %convolution_convert_fusion.1) | data formatting | bytes 2097152 | tf_op jit(solution)/shard_map/reshape;reshape | solution.py:35
  64.0 5.4 %copy.126 = bf16[16,2,128,4,32]{2,4,3,0,1:T(8,128)(2,1)S(1)} copy(bf16[16,2,128,4,32]{4,3,2,1,0:T(4,128)(2,1)} %reshape_reshape.6) | data formatting | bytes 2097152 | tf_op jit(solution)/shard_map/reshape;reshape | solution.py:35
  69.4 0.7 bitcast_convert_fusion
  70.1 1.4 fusion.13
  71.5 0.8 copy-done.3
  72.3 1.3 convolution_multiply_fusion.4
  73.6 0.8 copy.121
  74.4 0.8 copy.130
  75.8 7.3 %all-to-all-done.1 = bf16[8,2,2,128,128]{4,3,2,1,0:T(8,128)(2,1)S(1)} async-done(((bf16[8,2,2,128,128]{4,3,2,1,0:T(8,128)(2,1)}), bf16[8,2,2,128,128]{4,3,2,1,0:T(8,128)(2,1)S(1)}, u32[]{:S(2)}, u32[]{:S(2)}) %all-to-all-start.1) | async-done | bytes 1048608 | tf_op jit(solution)/shard_map/all_to_all | solution.py:119
  83.8 0.8 fusion.18
  84.6 4.3 %multiply_convert_fusion = bf16[16,4,128,128]{3,2,1,0:T(8,128)(2,1)S(1)} fusion(f32[16,4,128,128]{3,2,1,0:T(8,128)S(1)} %fusion.18, f32[16,4,128]{2,1,0:T(4,128)S(1)} %copy-done.15, f32[16,4,128]{2,1,0:T(4,128)S(1)} %copy-done.14, bf16[16,2,4,32,128]{4,3,2,0,1:T(8,128)(2,1)} %bitcast.161, bf16[16,2,4,32,128]{4,3,2,0,1:T(8,128)(2,1)S(1)} %bitcast.157), kind=kOutput, calls=%fused_computation.2 | convolution fusion | flops 72351744 | bytes 7405568 | tf_op jit(solution)/shard_map/shdq,shdk->shqk/dot_general | solution.py:49
  89.0 2.2 convolution_multiply_fusion.2
  91.2 2.3 copy.132
  93.5 4.2 %all-to-all-start.3 = ((f32[8,2,128,128]{3,1,2,0:T(2,128)}), f32[8,2,128,128]{3,1,2,0:T(2,128)}, u32[]{:S(2)}, u32[]{:S(2)}) async-start(f32[8,2,128,128]{3,1,2,0:T(2,128)} %copy.132), calls=%async_computation.3 | async-start | bytes 2097152 | tf_op jit(solution)/shard_map/all_to_all | solution.py:140
  97.7 2.0 convolution_multiply_fusion.3
  99.7 1.8 copy.135
  101.6 0.7 stack.71
  102.3 128.7 %psum.7 = f32[5,128]{1,0:T(8,128)S(1)} all-reduce(f32[5,128]{1,0:T(8,128)S(1)} %stack.71), channel_id=1, replica_groups=mesh['gx'=96,'gy'=8] {'gx','gy'}, use_global_device_ids=true, to_apply=%region_7.8 | all-reduce | flops 640 | bytes 5120 | tf_op jit(solution)/shard_map/psum | solution.py:175
  231.5 1.6 convolution_multiply_fusion.1
  233.2 1.7 copy.136
  234.9 3.1 %fusion.1 = f32[16,4,32,128]{3,2,1,0:T(8,128)S(1)} fusion(f32[16,4,128,128]{3,2,1,0:T(8,128)} %copy-done, f32[16,4,128]{2,1,0:T(4,128)} %get-tuple-element.19, bf16[16,2,4,32,128]{4,3,2,0,1:T(8,128)(2,1)S(1)} %bitcast.159), kind=kOutput, calls=%fused_computation.5 | convolution fusion | flops 70254592 | bytes 5799936 | tf_op jit(solution)/shard_map/shqk,shdq->shdk/dot_general | solution.py:55
  238.6 1.5 fusion.3
  240.1 1.1 fusion.34
  242.0 0.8 fusion.24
  242.8 1.6 copy.133
  (106 shorter events, 11.4 us)
Async XLA Ops:
  0.6 21.5 %copy-start.4 = (bf16[16,32,128]{2,1,0:T(8,128)(2,1)S(1)}, bf16[16,32,128]{2,1,0:T(8,128)(2,1)}, u32[]{:S(2)}) copy-start(bf16[16,32,128]{2,1,0:T(8,128)(2,1)} %param.12) | copy-start | bytes 393220
  0.6 28.7 %copy-start.12 = (bf16[16,32,128]{2,1,0:T(8,128)(2,1)S(1)}, bf16[16,32,128]{2,1,0:T(8,128)(2,1)}, u32[]{:S(2)}) copy-start(bf16[16,32,128]{2,1,0:T(8,128)(2,1)} %param.8) | copy-start | bytes 393220
  2.6 32.2 %all-to-all-start = ((bf16[8,1,2]{2,1,0:T(2,128)(2,1)}), bf16[8,1,2]{2,1,0:T(2,128)(2,1)S(1)}, u32[]{:S(2)}, u32[]{:S(2)}) async-start(bf16[8,1,2]{2,1,0:T(2,128)(2,1)} %all_to_all.20), calls=%async_computation | async-start | bytes 8192 | tf_op jit(solution)/shard_map/all_to_all | solution.py:121
  10.4 11.8 %collective-permute-start = (bf16[1,32,128]{2,1,0:T(8,128)(2,1)S(1)}, bf16[1,32,128]{2,1,0:T(8,128)(2,1)S(1)}, u32[]{:S(2)}, u32[]{:S(2)}) collective-permute-start(bf16[1,32,128]{2,1,0:T(8,128)(2,1)S(1)} %get-tuple-element.17), channel_id=1, source_target_pairs={{8,0},{16,8},{24,16},{32,24},{40,32},{48,40},{56,48},{64,56},{72,6... | collective-permute-start | bytes 24584 | tf_op jit(solution)/shard_map/ppermute | solution.py:21
  12.3 19.4 %copy-start.6 = (bf16[16,32,128]{2,1,0:T(8,128)(2,1)S(1)}, bf16[16,32,128]{2,1,0:T(8,128)(2,1)}, u32[]{:S(2)}) copy-start(bf16[16,32,128]{2,1,0:T(8,128)(2,1)} %param.10) | copy-start | bytes 393220
  12.3 19.4 %copy-start.17 = (bf16[16,32,128]{2,1,0:T(8,128)(2,1)S(1)}, bf16[16,32,128]{2,1,0:T(8,128)(2,1)}, u32[]{:S(2)}) copy-start(bf16[16,32,128]{2,1,0:T(8,128)(2,1)} %param.11) | copy-start | bytes 393220
  12.3 9.8 %collective-permute-start.1 = (bf16[1,32,128]{2,1,0:T(8,128)(2,1)S(1)}, bf16[1,32,128]{2,1,0:T(8,128)(2,1)S(1)}, u32[]{:S(2)}, u32[]{:S(2)}) collective-permute-start(bf16[1,32,128]{2,1,0:T(8,128)(2,1)S(1)} %get-tuple-element.18), channel_id=1, source_target_pairs={{0,8},{8,16},{16,24},{24,32},{32,40},{40,48},{48,56},{56,64},{64,7... | collective-permute-start | bytes 24584 | tf_op jit(solution)/shard_map/ppermute | solution.py:18
  21.4 11.2 %copy-start.5 = (bf16[4,2,4,32,128]{4,3,2,0,1:T(8,128)(2,1)}, bf16[4,2,4,32,128]{4,3,2,0,1:T(8,128)(2,1)S(1)}, u32[]{:S(2)}) copy-start(bf16[4,2,4,32,128]{4,3,2,0,1:T(8,128)(2,1)S(1)} %get-tuple-element.28) | copy-start | bytes 786436
  22.2 27.9 %copy-start.23 = (f32[16,4]{0,1:T(4,128)}, f32[16,4]{0,1:T(4,128)S(1)}, u32[]{:S(2)}) copy-start(f32[16,4]{0,1:T(4,128)S(1)} %fusion.39) | copy-start | bytes 772
  22.2 27.8 %copy-start.10 = (bf16[18,32,128]{2,1,0:T(8,128)(2,1)}, bf16[18,32,128]{2,1,0:T(8,128)(2,1)S(1)}, u32[]{:S(2)}) copy-start(bf16[18,32,128]{2,1,0:T(8,128)(2,1)S(1)} %constant_dynamic-update-slice_fusion) | copy-start | bytes 442372
  22.3 7.1 %collective-permute-start.3 = (bf16[18,1,128]{2,1,0:T(2,128)(2,1)S(1)}, bf16[18,1,128]{2,1,0:T(2,128)(2,1)S(1)}, u32[]{:S(2)}, u32[]{:S(2)}) collective-permute-start(bf16[18,1,128]{2,1,0:T(2,128)(2,1)S(1)} %get-tuple-element.14), channel_id=1, source_target_pairs={{0,1},{1,2},{2,3},{3,4},{4,5},{5,6},{6,7},{7,0},{8,9},{9,10},{10,1... | collective-permute-start | bytes 13832 | tf_op jit(solution)/shard_map/ppermute | solution.py:18
  26.2 5.6 %collective-permute-start.2 = (bf16[18,1,128]{2,1,0:T(2,128)(2,1)S(1)}, bf16[18,1,128]{2,1,0:T(2,128)(2,1)S(1)}, u32[]{:S(2)}, u32[]{:S(2)}) collective-permute-start(bf16[18,1,128]{2,1,0:T(2,128)(2,1)S(1)} %get-tuple-element.15), channel_id=1, source_target_pairs={{1,0},{2,1},{3,2},{4,3},{5,4},{6,5},{7,6},{0,7},{9,8},{10,9},{11,1... | collective-permute-start | bytes 13832 | tf_op jit(solution)/shard_map/ppermute | solution.py:21
  29.4 3.6 %copy-start.19 = (bf16[18,1,128]{2,1,0:T(2,128)(2,1)}, bf16[18,1,128]{2,1,0:T(2,128)(2,1)S(1)}, u32[]{:S(2)}) copy-start(bf16[18,1,128]{2,1,0:T(2,128)(2,1)S(1)} %collective-permute-done.3) | copy-start | bytes 13828
  31.8 18.3 %copy-start.21 = (bf16[18,1,128]{2,1,0:T(2,128)(2,1)}, bf16[18,1,128]{2,1,0:T(2,128)(2,1)S(1)}, u32[]{:S(2)}) copy-start(bf16[18,1,128]{2,1,0:T(2,128)(2,1)S(1)} %collective-permute-done.2) | copy-start | bytes 13828
  33.8 21.6 %copy-start.7 = (bf16[16,32,128]{2,1,0:T(8,128)(2,1)S(1)}, bf16[16,32,128]{2,1,0:T(8,128)(2,1)}, u32[]{:S(2)}) copy-start(bf16[16,32,128]{2,1,0:T(8,128)(2,1)} %param.10) | copy-start | bytes 393220
  33.8 21.5 %copy-start.13 = (bf16[16,32,128]{2,1,0:T(8,128)(2,1)S(1)}, bf16[16,32,128]{2,1,0:T(8,128)(2,1)}, u32[]{:S(2)}) copy-start(bf16[16,32,128]{2,1,0:T(8,128)(2,1)} %param.9) | copy-start | bytes 393220
  33.8 22.3 %copy-start.31 = (f32[5,128]{1,0:T(8,128)S(1)}, f32[5,128]{1,0:T(8,128)}, u32[]{:S(2)}) copy-start(f32[5,128]{1,0:T(8,128)} %param.15) | copy-start | bytes 7684
  33.9 16.2 %copy-start.18 = (bf16[4,128,4]{1,0,2:T(4,128)(2,1)}, bf16[4,128,4]{1,0,2:T(4,128)(2,1)S(1)}, u32[]{:S(2)}) copy-start(bf16[4,128,4]{1,0,2:T(4,128)(2,1)S(1)} %copy.156) | copy-start | bytes 12292
  34.8 15.3 %copy-start.25 = (bf16[8,1,2]{2,1,0:T(2,128)(2,1)}, bf16[8,1,2]{2,1,0:T(2,128)(2,1)S(1)}, u32[]{:S(2)}) copy-start(bf16[8,1,2]{2,1,0:T(2,128)(2,1)S(1)} %all-to-all-done) | copy-start | bytes 100
  34.8 15.3 %all-to-all-start.2 = ((bf16[8,2,2,4,128]{4,3,2,1,0:T(4,128)(2,1)}), bf16[8,2,2,4,128]{4,3,2,1,0:T(4,128)(2,1)S(1)}, u32[]{:S(2)}, u32[]{:S(2)}) async-start(bf16[8,2,2,4,128]{4,3,2,1,0:T(4,128)(2,1)} %reshape.219), calls=%async_computation.2 | async-start | bytes 65536 | tf_op jit(solution)/shard_map/all_to_all | solution.py:120
  50.0 0.6 copy-start.16
  50.7 32.5 %all-to-all-start.1 = ((bf16[8,2,2,128,128]{4,3,2,1,0:T(8,128)(2,1)}), bf16[8,2,2,128,128]{4,3,2,1,0:T(8,128)(2,1)S(1)}, u32[]{:S(2)}, u32[]{:S(2)}) async-start(bf16[8,2,2,128,128]{4,3,2,1,0:T(8,128)(2,1)} %bitcast.87), calls=%async_computation.1 | async-start | bytes 2097152 | tf_op jit(solution)/shard_map/all_to_all | solution.py:119
  69.4 15.2 %copy-start.1 = (bf16[16,2,128,4,32]{2,4,3,0,1:T(8,128)(2,1)}, bf16[16,2,128,4,32]{2,4,3,0,1:T(8,128)(2,1)S(1)}, u32[]{:S(2)}) copy-start(bf16[16,2,128,4,32]{2,4,3,0,1:T(8,128)(2,1)S(1)} %copy.126) | copy-start | bytes 3145732
  71.5 0.8 copy-start.3
  83.8 0.8 copy-start.14
  83.8 0.8 copy-start.15
  84.6 6.6 %copy-start = (f32[16,4,128,128]{3,2,1,0:T(8,128)}, f32[16,4,128,128]{3,2,1,0:T(8,128)S(1)}, u32[]{:S(2)}) copy-start(f32[16,4,128,128]{3,2,1,0:T(8,128)S(1)} %fusion.18) | copy-start | bytes 12582916
  84.6 4.4 %copy-start.2 = (bf16[16,2,128,4,32]{2,4,3,0,1:T(8,128)(2,1)S(1)}, bf16[16,2,128,4,32]{2,4,3,0,1:T(8,128)(2,1)}, u32[]{:S(2)}) copy-start(bf16[16,2,128,4,32]{2,4,3,0,1:T(8,128)(2,1)} %copy-done.1) | copy-start | bytes 3145732
  93.5 149.4 %all-to-all-start.3 = ((f32[8,2,128,128]{3,1,2,0:T(2,128)}), f32[8,2,128,128]{3,1,2,0:T(2,128)}, u32[]{:S(2)}, u32[]{:S(2)}) async-start(f32[8,2,128,128]{3,1,2,0:T(2,128)} %copy.132), calls=%async_computation.3 | async-start | bytes 2097152 | tf_op jit(solution)/shard_map/all_to_all | solution.py:140
  234.9 5.2 %copy-start.9 = (f32[4,128,128]{1,0,2:T(4,128)S(1)}, f32[4,128,128]{1,0,2:T(4,128)}, u32[]{:S(2)}) copy-start(f32[4,128,128]{1,0,2:T(4,128)} %copy.139) | copy-start | bytes 786436
  238.6 3.4 %copy-start.11 = (bf16[18,32,128]{2,1,0:T(8,128)(2,1)S(1)}, bf16[18,32,128]{2,1,0:T(8,128)(2,1)}, u32[]{:S(2)}) copy-start(bf16[18,32,128]{2,1,0:T(8,128)(2,1)} %copy-done.10) | copy-start | bytes 442372
  238.6 3.4 %copy-start.20 = (bf16[18,1,128]{2,1,0:T(2,128)(2,1)S(1)}, bf16[18,1,128]{2,1,0:T(2,128)(2,1)}, u32[]{:S(2)}) copy-start(bf16[18,1,128]{2,1,0:T(2,128)(2,1)} %copy-done.19) | copy-start | bytes 13828
  238.6 3.4 %copy-start.22 = (bf16[18,1,128]{2,1,0:T(2,128)(2,1)S(1)}, bf16[18,1,128]{2,1,0:T(2,128)(2,1)}, u32[]{:S(2)}) copy-start(bf16[18,1,128]{2,1,0:T(2,128)(2,1)} %copy-done.21) | copy-start | bytes 13828
  238.6 3.3 %copy-start.26 = (f32[128]{0:T(128)S(1)}, f32[128]{0:T(128)}, u32[]{:S(2)}) copy-start(f32[128]{0:T(128)} %get-tuple-element.21) | copy-start | bytes 1540
  238.6 3.3 %copy-start.27 = (f32[128]{0:T(128)S(1)}, f32[128]{0:T(128)}, u32[]{:S(2)}) copy-start(f32[128]{0:T(128)} %get-tuple-element.22) | copy-start | bytes 1540
  238.6 3.3 %copy-start.28 = (f32[128]{0:T(128)S(1)}, f32[128]{0:T(128)}, u32[]{:S(2)}) copy-start(f32[128]{0:T(128)} %get-tuple-element.23) | copy-start | bytes 1540
  238.6 3.3 %copy-start.29 = (f32[128]{0:T(128)S(1)}, f32[128]{0:T(128)}, u32[]{:S(2)}) copy-start(f32[128]{0:T(128)} %get-tuple-element.24) | copy-start | bytes 1540
  238.6 3.3 %copy-start.30 = (f32[128]{0:T(128)S(1)}, f32[128]{0:T(128)}, u32[]{:S(2)}) copy-start(f32[128]{0:T(128)} %get-tuple-element.25) | copy-start | bytes 1540
  238.6 5.8 %copy-start.8 = (f32[4,128,128]{1,0,2:T(4,128)S(1)}, f32[4,128,128]{1,0,2:T(4,128)}, u32[]{:S(2)}) copy-start(f32[4,128,128]{1,0,2:T(4,128)} %copy.121) | copy-start | bytes 786436
  240.1 4.3 %copy-start.24 = (f32[16,4]{0,1:T(4,128)S(1)}, f32[16,4]{0,1:T(4,128)}, u32[]{:S(2)}) copy-start(f32[16,4]{0,1:T(4,128)} %copy-done.23) | copy-start | bytes 772
where the time goes:
time: 249 us; the launch traced here: 246 us
  blocking collectives  129 us (52%)
  local copies, waits for them, and re-layouts  36.8 us (15%)
  starting transfers between devices  33.4 us (13%)
  matrix products  22.2 us (9%)
  waiting for transfers between devices  16.2 us (7%)
  other arithmetic  7.14 us (3%)
    psum x1, blocking collectives, per_device(): summed = lax.psum(partial_rows, ('gx', 'gy'))  129 us
    another operation x2, local copies, waits for them, and re-layouts, tile_grads(): key_pack.reshape(item_count, 2, block_rows, HEADS, head_width)  9.97 us
    all_to_all x1, waiting for transfers between devices, per_device(): lax.all_to_all(send_rows, 'gy', split_axis=0, concat_axis=0, tiled=True)  7.27 us
    all_to_all x1, starting transfers between devices, per_device(): lax.all_to_all(send_ids, 'gy', split_axis=0, concat_axis=0, tiled=True)  7.1 us
    all_to_all x1, starting transfers between devices, per_device(): lax.all_to_all(send_stats, 'gy', split_axis=0, concat_axis=0, tiled=True)  6.96 us
    all_to_all x1, waiting for transfers between devices, per_device(): lax.all_to_all(send_stats, 'gy', split_axis=0, concat_axis=0, tiled=True)  6.59 us
    ppermute x2, starting transfers between devices, with_halo(): lax.ppermute(lax.slice_in_dim(block, block.shape[dim] - width, None, axis...  6.47 us
    dot_general x2, matrix products, tile_grads(): jnp.einsum('shdq,shdk->shqk', grad_heads, value_heads, preferred_element_...  5.76 us
  transfers between devices with their start and end apart: 8, of which 3 were waited for; matrix products, arithmetic and copies ran while one was open for 20% of the time, Pallas kernels for 0%

commit v1 on v0

--- a/solution.py
+++ b/solution.py
@@ -21,6 +21,46 @@
         high = lax.ppermute(lax.slice_in_dim(block, 0, width, axis=dim), axis, backward)
         block = jnp.concatenate([low, block, high], axis=dim)
     return block
+
+
+def prime_factors(count):
+    factors = []
+    base = 2
+    while count > 1:
+        while count % base == 0:
+            factors.append(base)
+            count //= base
+        base += 1
+    return factors
+
+
+def exchange_sum(value, axis):
+    count = lax.axis_size(axis)
+    index = lax.axis_index(axis)
+    stride = 1
+    for radix in prime_factors(count):
+        digit = (index // stride) % radix
+        if radix == 2:
+            pairs = [(i, i + stride) if (i // stride) % 2 == 0 else (i, i - stride) for i in range(count)]
+            value = value + lax.ppermute(value, axis, pairs)
+        else:
+            received = [value]
+            for shift in range(1, radix):
+                pairs = []
+                for i in range(count):
+                    d = (i // stride) % radix
+                    pairs.append((i, i + (((d + shift) % radix) - d) * stride))
+                received.append(lax.ppermute(value, axis, pairs))
+            total = None
+            for position in range(radix):
+                offset = (digit - position) % radix
+                term = received[0]
+                for shift in range(1, radix):
+                    term = jnp.where(offset == shift, received[shift], term)
+                total = term if total is None else total + term
+            value = total
+        stride *= radix
+    return value
 
 
 def tile_grads(row_pack, stat_pack, key_pack):
@@ -172,7 +212,7 @@
     partial_rows = jnp.stack(
         [jnp.sum(moved[index] * value_float, axis=(0, 1)) for index in range(5)]
     )
-    summed = lax.psum(partial_rows, ("gx", "gy"))
+    summed = exchange_sum(exchange_sum(partial_rows, "gy"), "gx")
     point_count = tile_x * tile_y * lax.axis_size("gx") * group_size
     stencil_grad = summed / math.sqrt(point_count)
     query_grad = query_sum.reshape(tile_x, tile_y, features).astype(jnp.bfloat16)

time: 249 us -> 198 us (0.80)
  blocking collectives: 129 us -> 0 us
  starting transfers between devices: 33.4 us -> 81.7 us
  waiting for transfers between devices: 16.2 us -> 45 us
    psum x1 -> x0, blocking collectives: 129 us -> none  [per_device(): summed = lax.psum(partial_rows, ('gx', 'gy'))]
    ppermute x0 -> x10, starting transfers between devices: none -> 46.7 us  [the longest x8 32.6 us: exchange_sum(): value = value + lax.ppermute(value, axis, pairs)]
    ppermute x0 -> x10, waiting for transfers between devices: none -> 27.7 us  [the longest x8 27.7 us: exchange_sum(): value = value + lax.ppermute(value, axis, pairs)]
    all_to_all x1, waiting for transfers between devices: 0.01 us -> 8.41 us  [per_device(): lax.all_to_all(query_part, 'gy', split_axis=0, concat_axis=0, tiled=True)]
    all_to_all x1, waiting for transfers between devices: 7.27 us -> 0.01 us  [per_device(): lax.all_to_all(send_rows, 'gy', split_axis=0, concat_axis=0, tiled=True)]
  transfers between devices with their start and end apart: 8 -> 18, of which waited for: 3 -> 9; matrix products, arithmetic and copies ran while one was open for 20% -> 32% of each run, Pallas kernels for 0% -> 0%
where the time goes in v1:
time: 198 us; the launch traced here: 196 us
  starting transfers between devices  81.7 us (41%)
  waiting for transfers between devices  45 us (23%)
  local copies, waits for them, and re-layouts  36.4 us (18%)
  matrix products  21.9 us (11%)
  other arithmetic  9.17 us (5%)
    ppermute x8, starting transfers between devices, exchange_sum(): value = value + lax.ppermute(value, axis, pairs)  32.6 us
    ppermute x8, waiting for transfers between devices, exchange_sum(): value = value + lax.ppermute(value, axis, pairs)  27.7 us
    ppermute x2, starting transfers between devices, exchange_sum(): received.append(lax.ppermute(value, axis, pairs))  14.1 us
    another operation x2, local copies, waits for them, and re-layouts, tile_grads(): key_pack.reshape(item_count, 2, block_rows, HEADS, head_width)  9.99 us
    all_to_all x1, waiting for transfers between devices, per_device(): lax.all_to_all(query_part, 'gy', split_axis=0, concat_axis=0, tiled=True)  8.41 us
    all_to_all x1, starting transfers between devices, per_device(): lax.all_to_all(send_ids, 'gy', split_axis=0, concat_axis=0, tiled=True)  7.1 us
    all_to_all x1, starting transfers between devices, per_device(): lax.all_to_all(send_stats, 'gy', split_axis=0, concat_axis=0, tiled=True)  6.96 us
    reshape x5, local copies, waits for them, and re-layouts, points_last(): return part.reshape(item_count, features, block_rows).transpose(0, 2, 1)  6.7 us
  transfers between devices with their start and end apart: 18, of which 9 were waited for; matrix products, arithmetic and copies ran while one was open for 32% of the time, Pallas kernels for 0%

profile of v1, /device:TPU:6, one launch (start us, length us, event | category | flops | bytes accessed | tf_op | source)
XLA Modules:
  0.0 195.8 jit_solution(2120153110930997852)
XLA Ops:
  2.6 7.1 %all-to-all-start = ((bf16[8,1,2]{2,1,0:T(2,128)(2,1)}), bf16[8,1,2]{2,1,0:T(2,128)(2,1)S(1)}, u32[]{:S(2)}, u32[]{:S(2)}) async-start(bf16[8,1,2]{2,1,0:T(2,128)(2,1)} %all_to_all.20), calls=%async_computation | async-start | bytes 8192 | tf_op jit(solution)/shard_map/all_to_all | solution.py:161
  10.4 1.9 collective-permute-start
  12.3 2.5 %collective-permute-start.1 = (bf16[1,32,128]{2,1,0:T(8,128)(2,1)S(1)}, bf16[1,32,128]{2,1,0:T(8,128)(2,1)S(1)}, u32[]{:S(2)}, u32[]{:S(2)}) collective-permute-start(bf16[1,32,128]{2,1,0:T(8,128)(2,1)S(1)} %get-tuple-element.18), channel_id=1, source_target_pairs={{0,8},{8,16},{16,24},{24,32},{32,40},{40,48},{48,56},{56,64},{64,7... | collective-permute-start | bytes 24584 | tf_op jit(solution)/shard_map/ppermute | solution.py:18
  14.9 1.1 reshape.238
  16.9 1.1 reshape.237
  18.3 1.1 reshape.235
  19.7 1.1 reshape.236
  22.3 3.9 %collective-permute-start.3 = (bf16[18,1,128]{2,1,0:T(2,128)(2,1)S(1)}, bf16[18,1,128]{2,1,0:T(2,128)(2,1)S(1)}, u32[]{:S(2)}, u32[]{:S(2)}) collective-permute-start(bf16[18,1,128]{2,1,0:T(2,128)(2,1)S(1)} %get-tuple-element.14), channel_id=1, source_target_pairs={{0,1},{1,2},{2,3},{3,4},{4,5},{5,6},{6,7},{7,0},{8,9},{9,10},{10,1... | collective-permute-start | bytes 13832 | tf_op jit(solution)/shard_map/ppermute | solution.py:18
  26.2 3.1 %collective-permute-start.2 = (bf16[18,1,128]{2,1,0:T(2,128)(2,1)S(1)}, bf16[18,1,128]{2,1,0:T(2,128)(2,1)S(1)}, u32[]{:S(2)}, u32[]{:S(2)}) collective-permute-start(bf16[18,1,128]{2,1,0:T(2,128)(2,1)S(1)} %get-tuple-element.15), channel_id=1, source_target_pairs={{1,0},{2,1},{3,2},{4,3},{5,4},{6,5},{7,6},{0,7},{9,8},{10,9},{11,1... | collective-permute-start | bytes 13832 | tf_op jit(solution)/shard_map/ppermute | solution.py:21
  29.4 2.3 %collective-permute-done.2 = bf16[18,1,128]{2,1,0:T(2,128)(2,1)S(1)} collective-permute-done((bf16[18,1,128]{2,1,0:T(2,128)(2,1)S(1)}, bf16[18,1,128]{2,1,0:T(2,128)(2,1)S(1)}, u32[]{:S(2)}, u32[]{:S(2)}) %collective-permute-start.2) | collective-permute-done | bytes 4640 | tf_op jit(solution)/shard_map/ppermute | solution.py:21
  34.8 7.0 %all-to-all-start.2 = ((bf16[8,2,2,4,128]{4,3,2,1,0:T(4,128)(2,1)}), bf16[8,2,2,4,128]{4,3,2,1,0:T(4,128)(2,1)S(1)}, u32[]{:S(2)}, u32[]{:S(2)}) async-start(bf16[8,2,2,4,128]{4,3,2,1,0:T(4,128)(2,1)} %reshape.219), calls=%async_computation.2 | async-start | bytes 65536 | tf_op jit(solution)/shard_map/all_to_all | solution.py:160
  42.3 1.2 copy.155
  43.5 6.6 %all-to-all-done.2 = bf16[8,2,2,4,128]{4,3,2,1,0:T(4,128)(2,1)S(1)} async-done(((bf16[8,2,2,4,128]{4,3,2,1,0:T(4,128)(2,1)}), bf16[8,2,2,4,128]{4,3,2,1,0:T(4,128)(2,1)S(1)}, u32[]{:S(2)}, u32[]{:S(2)}) %all-to-all-start.2) | async-done | bytes 32800 | tf_op jit(solution)/shard_map/all_to_all | solution.py:160
  50.7 3.6 %all-to-all-start.1 = ((bf16[8,2,2,128,128]{4,3,2,1,0:T(8,128)(2,1)}), bf16[8,2,2,128,128]{4,3,2,1,0:T(8,128)(2,1)S(1)}, u32[]{:S(2)}, u32[]{:S(2)}) async-start(bf16[8,2,2,128,128]{4,3,2,1,0:T(8,128)(2,1)} %bitcast.87), calls=%async_computation.1 | async-start | bytes 2097152 | tf_op jit(solution)/shard_map/all_to_all | solution.py:159
  54.6 3.8 %collective-permute-start.4 = (f32[5,128]{1,0:T(8,128)S(1)}, f32[5,128]{1,0:T(8,128)S(1)}, u32[]{:S(2)}, u32[]{:S(2)}) collective-permute-start(f32[5,128]{1,0:T(8,128)S(1)} %stack.71), channel_id=1, source_target_pairs={{0,1},{1,0},{2,3},{3,2},{4,5},{5,4},{6,7},{7,6},{8,9},{9,8},{10,11... | collective-permute-start | bytes 7688 | tf_op jit(solution)/shard_map/ppermute | solution.py:45
  59.0 20.3 %collective-permute-done.4 = f32[5,128]{1,0:T(8,128)S(1)} collective-permute-done((f32[5,128]{1,0:T(8,128)S(1)}, f32[5,128]{1,0:T(8,128)S(1)}, u32[]{:S(2)}, u32[]{:S(2)}) %collective-permute-start.4) | collective-permute-done | bytes 2592 | tf_op jit(solution)/shard_map/ppermute | solution.py:45
  79.3 2.2 %collective-permute-start.5 = (f32[5,128]{1,0:T(8,128)S(1)}, f32[5,128]{1,0:T(8,128)S(1)}, u32[]{:S(2)}, u32[]{:S(2)}) collective-permute-start(f32[5,128]{1,0:T(8,128)S(1)} %add.127), channel_id=1, source_target_pairs={{0,2},{1,3},{2,0},{3,1},{4,6},{5,7},{6,4},{7,5},{8,10},{9,11},{10,... | collective-permute-start | bytes 7688 | tf_op jit(solution)/shard_map/ppermute | solution.py:45
  82.2 3.5 %collective-permute-done.5 = f32[5,128]{1,0:T(8,128)S(1)} collective-permute-done((f32[5,128]{1,0:T(8,128)S(1)}, f32[5,128]{1,0:T(8,128)S(1)}, u32[]{:S(2)}, u32[]{:S(2)}) %collective-permute-start.5) | collective-permute-done | bytes 2592 | tf_op jit(solution)/shard_map/ppermute | solution.py:45
  85.7 6.4 %collective-permute-start.6 = (f32[5,128]{1,0:T(8,128)S(1)}, f32[5,128]{1,0:T(8,128)S(1)}, u32[]{:S(2)}, u32[]{:S(2)}) collective-permute-start(f32[5,128]{1,0:T(8,128)S(1)} %add.128), channel_id=1, source_target_pairs={{0,4},{1,5},{2,6},{3,7},{4,0},{5,1},{6,2},{7,3},{8,12},{9,13},{10,... | collective-permute-start | bytes 7688 | tf_op jit(solution)/shard_map/ppermute | solution.py:45
  93.0 2.1 %collective-permute-done.6 = f32[5,128]{1,0:T(8,128)S(1)} collective-permute-done((f32[5,128]{1,0:T(8,128)S(1)}, f32[5,128]{1,0:T(8,128)S(1)}, u32[]{:S(2)}, u32[]{:S(2)}) %collective-permute-start.6) | collective-permute-done | bytes 2592 | tf_op jit(solution)/shard_map/ppermute | solution.py:45
  95.1 1.9 collective-permute-start.7
  98.9 1.9 collective-permute-start.8
  100.8 1.5 convolution_convert_fusion.1
  102.3 4.6 %reshape_reshape.6 = bf16[16,2,128,4,32]{4,3,2,1,0:T(4,128)(2,1)} reshape(bf16[16,32768]{1,0:T(8,128)(2,1)S(1)} %convolution_convert_fusion.1) | data formatting | bytes 2097152 | tf_op jit(solution)/shard_map/reshape;reshape | solution.py:75
  106.9 5.4 %copy.126 = bf16[16,2,128,4,32]{2,4,3,0,1:T(8,128)(2,1)S(1)} copy(bf16[16,2,128,4,32]{4,3,2,1,0:T(4,128)(2,1)} %reshape_reshape.6) | data formatting | bytes 2097152 | tf_op jit(solution)/shard_map/reshape;reshape | solution.py:75
  113.1 6.0 %collective-permute-start.9 = (f32[5,128]{1,0:T(8,128)S(1)}, f32[5,128]{1,0:T(8,128)S(1)}, u32[]{:S(2)}, u32[]{:S(2)}) collective-permute-start(f32[5,128]{1,0:T(8,128)S(1)} %add.131), channel_id=1, source_target_pairs={{0,32},{8,40},{16,48},{24,56},{32,0},{40,8},{48,16},{56,24},{64,96... | collective-permute-start | bytes 7688 | tf_op jit(solution)/shard_map/ppermute | solution.py:45
  119.8 0.9 collective-permute-done.9
  120.7 3.7 %collective-permute-start.10 = (f32[5,128]{1,0:T(8,128)S(1)}, f32[5,128]{1,0:T(8,128)S(1)}, u32[]{:S(2)}, u32[]{:S(2)}) collective-permute-start(f32[5,128]{1,0:T(8,128)S(1)} %add.132), channel_id=1, source_target_pairs={{0,64},{8,72},{16,80},{24,88},{32,96},{40,104},{48,112},{56,120},{... | collective-permute-start | bytes 7688 | tf_op jit(solution)/shard_map/ppermute | solution.py:45
  124.3 1.4 fusion.13
  126.2 6.7 %collective-permute-start.11 = (f32[5,128]{1,0:T(8,128)S(1)}, f32[5,128]{1,0:T(8,128)S(1)}, u32[]{:S(2)}, u32[]{:S(2)}) collective-permute-start(f32[5,128]{1,0:T(8,128)S(1)} %add.133), channel_id=1, source_target_pairs={{0,128},{8,136},{16,144},{24,152},{32,160},{40,168},{48,176},{56,1... | collective-permute-start | bytes 7688 | tf_op jit(solution)/shard_map/ppermute | solution.py:45
  132.9 1.0 convolution_multiply_fusion.3
  135.1 10.6 %collective-permute-start.13 = (f32[5,128]{1,0:T(8,128)}, f32[5,128]{1,0:T(8,128)}, u32[]{:S(2)}, u32[]{:S(2)}) collective-permute-start(f32[5,128]{1,0:T(8,128)} %add.134), channel_id=1, source_target_pairs={{0,256},{8,264},{16,272},{24,280},{32,288},{40,296},{48,304},{56,3... | collective-permute-start | bytes 7688 | tf_op jit(solution)/shard_map/ppermute | solution.py:53
  145.7 3.5 %collective-permute-start.12 = (f32[5,128]{1,0:T(8,128)}, f32[5,128]{1,0:T(8,128)}, u32[]{:S(2)}, u32[]{:S(2)}) collective-permute-start(f32[5,128]{1,0:T(8,128)} %add.134), channel_id=1, source_target_pairs={{0,512},{8,520},{16,528},{24,536},{32,544},{40,552},{48,560},{56,5... | collective-permute-start | bytes 7688 | tf_op jit(solution)/shard_map/ppermute | solution.py:53
  151.5 4.3 %multiply_convert_fusion = bf16[16,4,128,128]{3,2,1,0:T(8,128)(2,1)S(1)} fusion(f32[16,4,128,128]{3,2,1,0:T(8,128)S(1)} %fusion.18, f32[16,4,128]{2,1,0:T(4,128)S(1)} %get-tuple-element.20, f32[16,4,128]{2,1,0:T(4,128)S(1)} %get-tuple-element.19, bf16[16,2,4,32,128]{4,3,2,0,1:T(8,128)(2,1)} %bitcast.161, bf16[16,2,4,32,128]{4,3,2,0,1:T(8,128)(2,1)S(1)} %bitcast.157), kind=kOutput, calls=%fused_computation.2 | convolution fusion | flops 72351744 | bytes 7405568 | tf_op jit(solution)/shard_map/shdq,shdk->shqk/dot_general | solution.py:89
  155.8 2.2 %convolution_multiply_fusion.2 = f32[16,4,32,128]{3,2,1,0:T(8,128)} fusion(bf16[16,4,128,128]{3,2,1,0:T(8,128)(2,1)S(1)} %multiply_convert_fusion, bf16[16,2,4,32,128]{4,3,2,0,1:T(8,128)(2,1)S(1)} %bitcast.162), kind=kOutput, calls=%fused_computation.19 | convolution fusion | flops 67371008 | bytes 3670016 | tf_op jit(solution)/shard_map/shqk,shdk->shdq/dot_general | solution.py:103
  158.0 2.3 %copy.132 = f32[8,2,128,128]{3,1,2,0:T(2,128)} copy(f32[8,2,128,128]{2,3,1,0:T(8,128)} %bitcast.163) | data formatting | bytes 2097152 | tf_op jit(solution)/shard_map/reshape | solution.py:177
  160.3 5.8 %all-to-all-start.3 = ((f32[8,2,128,128]{3,1,2,0:T(2,128)}), f32[8,2,128,128]{3,1,2,0:T(2,128)}, u32[]{:S(2)}, u32[]{:S(2)}) async-start(f32[8,2,128,128]{3,1,2,0:T(2,128)} %copy.132), calls=%async_computation.3 | async-start | bytes 2097152 | tf_op jit(solution)/shard_map/all_to_all | solution.py:180
  166.1 2.1 %convolution_multiply_fusion.4 = f32[4,4,32,128]{3,2,1,0:T(8,128)} fusion(bf16[4,4,128,128]{3,2,1,0:T(8,128)(2,1)} %copy-done.3, bf16[4,2,4,32,128]{4,3,2,0,1:T(8,128)(2,1)S(1)} %copy-done.6), kind=kOutput, calls=%fused_computation.22 | convolution fusion | flops 16842752 | bytes 917504 | tf_op jit(solution)/shard_map/shqk,shdk->shdq/dot_general | solution.py:103
  168.2 1.8 copy.121
  170.1 1.8 copy.135
  171.9 1.3 add_multiply_fusion
  173.2 1.6 convolution_multiply_fusion.1
  174.8 1.7 copy.136
  176.6 3.1 %fusion.1 = f32[16,4,32,128]{3,2,1,0:T(8,128)S(1)} fusion(f32[16,4,128,128]{3,2,1,0:T(8,128)} %copy-done, f32[16,4,128]{2,1,0:T(4,128)} %copy-done.15, bf16[16,2,4,32,128]{4,3,2,0,1:T(8,128)(2,1)S(1)} %bitcast.159), kind=kOutput, calls=%fused_computation.5 | convolution fusion | flops 70254592 | bytes 5799936 | tf_op jit(solution)/shard_map/shqk,shdq->shdk/dot_general | solution.py:95
  180.3 1.5 fusion.3
  181.8 1.1 fusion.34
  184.4 8.4 %all-to-all-done.3 = f32[8,2,128,128]{3,1,2,0:T(2,128)} async-done(((f32[8,2,128,128]{3,1,2,0:T(2,128)}), f32[8,2,128,128]{3,1,2,0:T(2,128)}, u32[]{:S(2)}, u32[]{:S(2)}) %all-to-all-start.3) | async-done | bytes 1048608 | tf_op jit(solution)/shard_map/all_to_all | solution.py:180
  192.9 1.6 copy.133
  (143 shorter events, 22.4 us)
Async XLA Ops:
  0.6 21.5 %copy-start.4 = (bf16[16,32,128]{2,1,0:T(8,128)(2,1)S(1)}, bf16[16,32,128]{2,1,0:T(8,128)(2,1)}, u32[]{:S(2)}) copy-start(bf16[16,32,128]{2,1,0:T(8,128)(2,1)} %param.12) | copy-start | bytes 393220
  0.6 28.7 %copy-start.13 = (bf16[16,32,128]{2,1,0:T(8,128)(2,1)S(1)}, bf16[16,32,128]{2,1,0:T(8,128)(2,1)}, u32[]{:S(2)}) copy-start(bf16[16,32,128]{2,1,0:T(8,128)(2,1)} %param.8) | copy-start | bytes 393220
  2.6 32.2 %all-to-all-start = ((bf16[8,1,2]{2,1,0:T(2,128)(2,1)}), bf16[8,1,2]{2,1,0:T(2,128)(2,1)S(1)}, u32[]{:S(2)}, u32[]{:S(2)}) async-start(bf16[8,1,2]{2,1,0:T(2,128)(2,1)} %all_to_all.20), calls=%async_computation | async-start | bytes 8192 | tf_op jit(solution)/shard_map/all_to_all | solution.py:161
  10.4 11.8 %collective-permute-start = (bf16[1,32,128]{2,1,0:T(8,128)(2,1)S(1)}, bf16[1,32,128]{2,1,0:T(8,128)(2,1)S(1)}, u32[]{:S(2)}, u32[]{:S(2)}) collective-permute-start(bf16[1,32,128]{2,1,0:T(8,128)(2,1)S(1)} %get-tuple-element.17), channel_id=1, source_target_pairs={{8,0},{16,8},{24,16},{32,24},{40,32},{48,40},{56,48},{64,56},{72,6... | collective-permute-start | bytes 24584 | tf_op jit(solution)/shard_map/ppermute | solution.py:21
  12.3 19.4 %copy-start.7 = (bf16[16,32,128]{2,1,0:T(8,128)(2,1)S(1)}, bf16[16,32,128]{2,1,0:T(8,128)(2,1)}, u32[]{:S(2)}) copy-start(bf16[16,32,128]{2,1,0:T(8,128)(2,1)} %param.10) | copy-start | bytes 393220
  12.3 19.4 %copy-start.17 = (bf16[16,32,128]{2,1,0:T(8,128)(2,1)S(1)}, bf16[16,32,128]{2,1,0:T(8,128)(2,1)}, u32[]{:S(2)}) copy-start(bf16[16,32,128]{2,1,0:T(8,128)(2,1)} %param.11) | copy-start | bytes 393220
  12.3 9.8 %collective-permute-start.1 = (bf16[1,32,128]{2,1,0:T(8,128)(2,1)S(1)}, bf16[1,32,128]{2,1,0:T(8,128)(2,1)S(1)}, u32[]{:S(2)}, u32[]{:S(2)}) collective-permute-start(bf16[1,32,128]{2,1,0:T(8,128)(2,1)S(1)} %get-tuple-element.18), channel_id=1, source_target_pairs={{0,8},{8,16},{16,24},{24,32},{32,40},{40,48},{48,56},{56,64},{64,7... | collective-permute-start | bytes 24584 | tf_op jit(solution)/shard_map/ppermute | solution.py:18
  21.4 11.2 %copy-start.5 = (bf16[4,2,4,32,128]{4,3,2,0,1:T(8,128)(2,1)}, bf16[4,2,4,32,128]{4,3,2,0,1:T(8,128)(2,1)S(1)}, u32[]{:S(2)}) copy-start(bf16[4,2,4,32,128]{4,3,2,0,1:T(8,128)(2,1)S(1)} %get-tuple-element.28) | copy-start | bytes 786436
  22.2 27.9 %copy-start.23 = (f32[16,4]{0,1:T(4,128)}, f32[16,4]{0,1:T(4,128)S(1)}, u32[]{:S(2)}) copy-start(f32[16,4]{0,1:T(4,128)S(1)} %fusion.39) | copy-start | bytes 772
  22.2 27.8 %copy-start.11 = (bf16[18,32,128]{2,1,0:T(8,128)(2,1)}, bf16[18,32,128]{2,1,0:T(8,128)(2,1)S(1)}, u32[]{:S(2)}) copy-start(bf16[18,32,128]{2,1,0:T(8,128)(2,1)S(1)} %constant_dynamic-update-slice_fusion) | copy-start | bytes 442372
  22.3 7.1 %collective-permute-start.3 = (bf16[18,1,128]{2,1,0:T(2,128)(2,1)S(1)}, bf16[18,1,128]{2,1,0:T(2,128)(2,1)S(1)}, u32[]{:S(2)}, u32[]{:S(2)}) collective-permute-start(bf16[18,1,128]{2,1,0:T(2,128)(2,1)S(1)} %get-tuple-element.14), channel_id=1, source_target_pairs={{0,1},{1,2},{2,3},{3,4},{4,5},{5,6},{6,7},{7,0},{8,9},{9,10},{10,1... | collective-permute-start | bytes 13832 | tf_op jit(solution)/shard_map/ppermute | solution.py:18
  26.2 5.6 %collective-permute-start.2 = (bf16[18,1,128]{2,1,0:T(2,128)(2,1)S(1)}, bf16[18,1,128]{2,1,0:T(2,128)(2,1)S(1)}, u32[]{:S(2)}, u32[]{:S(2)}) collective-permute-start(bf16[18,1,128]{2,1,0:T(2,128)(2,1)S(1)} %get-tuple-element.15), channel_id=1, source_target_pairs={{1,0},{2,1},{3,2},{4,3},{5,4},{6,5},{7,6},{0,7},{9,8},{10,9},{11,1... | collective-permute-start | bytes 13832 | tf_op jit(solution)/shard_map/ppermute | solution.py:21
  29.4 20.7 %copy-start.19 = (bf16[18,1,128]{2,1,0:T(2,128)(2,1)}, bf16[18,1,128]{2,1,0:T(2,128)(2,1)S(1)}, u32[]{:S(2)}) copy-start(bf16[18,1,128]{2,1,0:T(2,128)(2,1)S(1)} %collective-permute-done.3) | copy-start | bytes 13828
  31.8 18.3 %copy-start.21 = (bf16[18,1,128]{2,1,0:T(2,128)(2,1)}, bf16[18,1,128]{2,1,0:T(2,128)(2,1)S(1)}, u32[]{:S(2)}) copy-start(bf16[18,1,128]{2,1,0:T(2,128)(2,1)S(1)} %collective-permute-done.2) | copy-start | bytes 13828
  33.7 20.8 %copy-start.31 = (f32[128]{0:T(128)S(1)}, f32[128]{0:T(128)}, u32[]{:S(2)}) copy-start(f32[128]{0:T(128)} %get-tuple-element.4) | copy-start | bytes 1540
  33.7 20.8 %copy-start.32 = (f32[128]{0:T(128)S(1)}, f32[128]{0:T(128)}, u32[]{:S(2)}) copy-start(f32[128]{0:T(128)} %get-tuple-element.5) | copy-start | bytes 1540
  33.8 20.8 %copy-start.33 = (f32[128]{0:T(128)S(1)}, f32[128]{0:T(128)}, u32[]{:S(2)}) copy-start(f32[128]{0:T(128)} %get-tuple-element.9) | copy-start | bytes 1540
  33.8 20.8 %copy-start.34 = (f32[128]{0:T(128)S(1)}, f32[128]{0:T(128)}, u32[]{:S(2)}) copy-start(f32[128]{0:T(128)} %get-tuple-element.10) | copy-start | bytes 1540
  33.8 20.8 %copy-start.35 = (f32[128]{0:T(128)S(1)}, f32[128]{0:T(128)}, u32[]{:S(2)}) copy-start(f32[128]{0:T(128)} %get-tuple-element.11) | copy-start | bytes 1540
  33.8 24.6 %copy-start.36 = (f32[5,128]{1,0:T(8,128)S(1)}, f32[5,128]{1,0:T(8,128)}, u32[]{:S(2)}) copy-start(f32[5,128]{1,0:T(8,128)} %param.15) | copy-start | bytes 7684
  33.8 47.7 %copy-start.8 = (bf16[16,32,128]{2,1,0:T(8,128)(2,1)S(1)}, bf16[16,32,128]{2,1,0:T(8,128)(2,1)}, u32[]{:S(2)}) copy-start(bf16[16,32,128]{2,1,0:T(8,128)(2,1)} %param.10) | copy-start | bytes 393220
  33.8 47.7 %copy-start.14 = (bf16[16,32,128]{2,1,0:T(8,128)(2,1)S(1)}, bf16[16,32,128]{2,1,0:T(8,128)(2,1)}, u32[]{:S(2)}) copy-start(bf16[16,32,128]{2,1,0:T(8,128)(2,1)} %param.9) | copy-start | bytes 393220
  33.9 16.2 %copy-start.18 = (bf16[4,128,4]{1,0,2:T(4,128)(2,1)}, bf16[4,128,4]{1,0,2:T(4,128)(2,1)S(1)}, u32[]{:S(2)}) copy-start(bf16[4,128,4]{1,0,2:T(4,128)(2,1)S(1)} %copy.156) | copy-start | bytes 12292
  34.8 15.3 %copy-start.25 = (bf16[8,1,2]{2,1,0:T(2,128)(2,1)}, bf16[8,1,2]{2,1,0:T(2,128)(2,1)S(1)}, u32[]{:S(2)}) copy-start(bf16[8,1,2]{2,1,0:T(2,128)(2,1)S(1)} %all-to-all-done) | copy-start | bytes 100
  34.8 15.3 %all-to-all-start.2 = ((bf16[8,2,2,4,128]{4,3,2,1,0:T(4,128)(2,1)}), bf16[8,2,2,4,128]{4,3,2,1,0:T(4,128)(2,1)S(1)}, u32[]{:S(2)}, u32[]{:S(2)}) async-start(bf16[8,2,2,4,128]{4,3,2,1,0:T(4,128)(2,1)} %reshape.219), calls=%async_computation.2 | async-start | bytes 65536 | tf_op jit(solution)/shard_map/all_to_all | solution.py:160
  50.7 99.3 %all-to-all-start.1 = ((bf16[8,2,2,128,128]{4,3,2,1,0:T(8,128)(2,1)}), bf16[8,2,2,128,128]{4,3,2,1,0:T(8,128)(2,1)S(1)}, u32[]{:S(2)}, u32[]{:S(2)}) async-start(bf16[8,2,2,128,128]{4,3,2,1,0:T(8,128)(2,1)} %bitcast.87), calls=%async_computation.1 | async-start | bytes 2097152 | tf_op jit(solution)/shard_map/all_to_all | solution.py:159
  54.6 24.7 %collective-permute-start.4 = (f32[5,128]{1,0:T(8,128)S(1)}, f32[5,128]{1,0:T(8,128)S(1)}, u32[]{:S(2)}, u32[]{:S(2)}) collective-permute-start(f32[5,128]{1,0:T(8,128)S(1)} %stack.71), channel_id=1, source_target_pairs={{0,1},{1,0},{2,3},{3,2},{4,5},{5,4},{6,7},{7,6},{8,9},{9,8},{10,11... | collective-permute-start | bytes 7688 | tf_op jit(solution)/shard_map/ppermute | solution.py:45
  79.3 6.4 %collective-permute-start.5 = (f32[5,128]{1,0:T(8,128)S(1)}, f32[5,128]{1,0:T(8,128)S(1)}, u32[]{:S(2)}, u32[]{:S(2)}) collective-permute-start(f32[5,128]{1,0:T(8,128)S(1)} %add.127), channel_id=1, source_target_pairs={{0,2},{1,3},{2,0},{3,1},{4,6},{5,7},{6,4},{7,5},{8,10},{9,11},{10,... | collective-permute-start | bytes 7688 | tf_op jit(solution)/shard_map/ppermute | solution.py:45
  85.7 9.4 %collective-permute-start.6 = (f32[5,128]{1,0:T(8,128)S(1)}, f32[5,128]{1,0:T(8,128)S(1)}, u32[]{:S(2)}, u32[]{:S(2)}) collective-permute-start(f32[5,128]{1,0:T(8,128)S(1)} %add.128), channel_id=1, source_target_pairs={{0,4},{1,5},{2,6},{3,7},{4,0},{5,1},{6,2},{7,3},{8,12},{9,13},{10,... | collective-permute-start | bytes 7688 | tf_op jit(solution)/shard_map/ppermute | solution.py:45
  95.1 3.2 %collective-permute-start.7 = (f32[5,128]{1,0:T(8,128)S(1)}, f32[5,128]{1,0:T(8,128)S(1)}, u32[]{:S(2)}, u32[]{:S(2)}) collective-permute-start(f32[5,128]{1,0:T(8,128)S(1)} %add.129), channel_id=1, source_target_pairs={{0,8},{8,0},{16,24},{24,16},{32,40},{40,32},{48,56},{56,48},{64,72... | collective-permute-start | bytes 7688 | tf_op jit(solution)/shard_map/ppermute | solution.py:45
  98.9 13.4 %collective-permute-start.8 = (f32[5,128]{1,0:T(8,128)}, f32[5,128]{1,0:T(8,128)}, u32[]{:S(2)}, u32[]{:S(2)}) collective-permute-start(f32[5,128]{1,0:T(8,128)} %add.130), channel_id=1, source_target_pairs={{0,16},{8,24},{16,0},{24,8},{32,48},{40,56},{48,32},{56,40},{64,80... | collective-permute-start | bytes 7688 | tf_op jit(solution)/shard_map/ppermute | solution.py:45
  112.3 39.2 %copy-start.1 = (bf16[16,2,128,4,32]{2,4,3,0,1:T(8,128)(2,1)}, bf16[16,2,128,4,32]{2,4,3,0,1:T(8,128)(2,1)S(1)}, u32[]{:S(2)}) copy-start(bf16[16,2,128,4,32]{2,4,3,0,1:T(8,128)(2,1)S(1)} %copy.126) | copy-start | bytes 3145732
  113.1 7.6 %collective-permute-start.9 = (f32[5,128]{1,0:T(8,128)S(1)}, f32[5,128]{1,0:T(8,128)S(1)}, u32[]{:S(2)}, u32[]{:S(2)}) collective-permute-start(f32[5,128]{1,0:T(8,128)S(1)} %add.131), channel_id=1, source_target_pairs={{0,32},{8,40},{16,48},{24,56},{32,0},{40,8},{48,16},{56,24},{64,96... | collective-permute-start | bytes 7688 | tf_op jit(solution)/shard_map/ppermute | solution.py:45
  120.7 5.5 %collective-permute-start.10 = (f32[5,128]{1,0:T(8,128)S(1)}, f32[5,128]{1,0:T(8,128)S(1)}, u32[]{:S(2)}, u32[]{:S(2)}) collective-permute-start(f32[5,128]{1,0:T(8,128)S(1)} %add.132), channel_id=1, source_target_pairs={{0,64},{8,72},{16,80},{24,88},{32,96},{40,104},{48,112},{56,120},{... | collective-permute-start | bytes 7688 | tf_op jit(solution)/shard_map/ppermute | solution.py:45
  125.8 7.2 %copy-start.3 = (bf16[4,4,128,128]{3,2,1,0:T(8,128)(2,1)}, bf16[4,4,128,128]{3,2,1,0:T(8,128)(2,1)S(1)}, u32[]{:S(2)}) copy-start(bf16[4,4,128,128]{3,2,1,0:T(8,128)(2,1)S(1)} %fusion.13) | copy-start | bytes 1572868
  126.2 8.3 %collective-permute-start.11 = (f32[5,128]{1,0:T(8,128)S(1)}, f32[5,128]{1,0:T(8,128)S(1)}, u32[]{:S(2)}, u32[]{:S(2)}) collective-permute-start(f32[5,128]{1,0:T(8,128)S(1)} %add.133), channel_id=1, source_target_pairs={{0,128},{8,136},{16,144},{24,152},{32,160},{40,168},{48,176},{56,1... | collective-permute-start | bytes 7688 | tf_op jit(solution)/shard_map/ppermute | solution.py:45
  135.1 36.8 %collective-permute-start.13 = (f32[5,128]{1,0:T(8,128)}, f32[5,128]{1,0:T(8,128)}, u32[]{:S(2)}, u32[]{:S(2)}) collective-permute-start(f32[5,128]{1,0:T(8,128)} %add.134), channel_id=1, source_target_pairs={{0,256},{8,264},{16,272},{24,280},{32,288},{40,296},{48,304},{56,3... | collective-permute-start | bytes 7688 | tf_op jit(solution)/shard_map/ppermute | solution.py:53
  145.7 26.2 %collective-permute-start.12 = (f32[5,128]{1,0:T(8,128)}, f32[5,128]{1,0:T(8,128)}, u32[]{:S(2)}, u32[]{:S(2)}) collective-permute-start(f32[5,128]{1,0:T(8,128)} %add.134), channel_id=1, source_target_pairs={{0,512},{8,520},{16,528},{24,536},{32,544},{40,552},{48,560},{56,5... | collective-permute-start | bytes 7688 | tf_op jit(solution)/shard_map/ppermute | solution.py:53
  151.5 6.6 %copy-start = (f32[16,4,128,128]{3,2,1,0:T(8,128)}, f32[16,4,128,128]{3,2,1,0:T(8,128)S(1)}, u32[]{:S(2)}) copy-start(f32[16,4,128,128]{3,2,1,0:T(8,128)S(1)} %fusion.18) | copy-start | bytes 12582916
  151.5 4.3 %copy-start.2 = (bf16[16,2,128,4,32]{2,4,3,0,1:T(8,128)(2,1)S(1)}, bf16[16,2,128,4,32]{2,4,3,0,1:T(8,128)(2,1)}, u32[]{:S(2)}) copy-start(bf16[16,2,128,4,32]{2,4,3,0,1:T(8,128)(2,1)} %copy-done.1) | copy-start | bytes 3145732
  155.8 10.3 %copy-start.6 = (bf16[4,2,4,32,128]{4,3,2,0,1:T(8,128)(2,1)S(1)}, bf16[4,2,4,32,128]{4,3,2,0,1:T(8,128)(2,1)}, u32[]{:S(2)}) copy-start(bf16[4,2,4,32,128]{4,3,2,0,1:T(8,128)(2,1)} %copy-done.5) | copy-start | bytes 786436
  160.3 32.6 %all-to-all-start.3 = ((f32[8,2,128,128]{3,1,2,0:T(2,128)}), f32[8,2,128,128]{3,1,2,0:T(2,128)}, u32[]{:S(2)}, u32[]{:S(2)}) async-start(f32[8,2,128,128]{3,1,2,0:T(2,128)} %copy.132), calls=%async_computation.3 | async-start | bytes 2097152 | tf_op jit(solution)/shard_map/all_to_all | solution.py:180
  176.5 5.2 %copy-start.9 = (f32[4,128,128]{1,0,2:T(4,128)S(1)}, f32[4,128,128]{1,0,2:T(4,128)}, u32[]{:S(2)}) copy-start(f32[4,128,128]{1,0,2:T(4,128)} %copy.139) | copy-start | bytes 786436
  180.2 3.4 %copy-start.12 = (bf16[18,32,128]{2,1,0:T(8,128)(2,1)S(1)}, bf16[18,32,128]{2,1,0:T(8,128)(2,1)}, u32[]{:S(2)}) copy-start(bf16[18,32,128]{2,1,0:T(8,128)(2,1)} %copy-done.11) | copy-start | bytes 442372
  180.2 3.4 %copy-start.20 = (bf16[18,1,128]{2,1,0:T(2,128)(2,1)S(1)}, bf16[18,1,128]{2,1,0:T(2,128)(2,1)}, u32[]{:S(2)}) copy-start(bf16[18,1,128]{2,1,0:T(2,128)(2,1)} %copy-done.19) | copy-start | bytes 13828
  180.2 3.4 %copy-start.22 = (bf16[18,1,128]{2,1,0:T(2,128)(2,1)S(1)}, bf16[18,1,128]{2,1,0:T(2,128)(2,1)}, u32[]{:S(2)}) copy-start(bf16[18,1,128]{2,1,0:T(2,128)(2,1)} %copy-done.21) | copy-start | bytes 13828
  180.3 14.2 %copy-start.10 = (f32[4,128,128]{1,0,2:T(4,128)S(1)}, f32[4,128,128]{1,0,2:T(4,128)}, u32[]{:S(2)}) copy-start(f32[4,128,128]{1,0,2:T(4,128)} %copy.121) | copy-start | bytes 786436
  181.7 12.7 %copy-start.24 = (f32[16,4]{0,1:T(4,128)S(1)}, f32[16,4]{0,1:T(4,128)}, u32[]{:S(2)}) copy-start(f32[16,4]{0,1:T(4,128)} %copy-done.23) | copy-start | bytes 772
  (7 other events, 18.8 us)

commit v2 on v1

--- a/solution.py
+++ b/solution.py
@@ -212,7 +212,8 @@
     partial_rows = jnp.stack(
         [jnp.sum(moved[index] * value_float, axis=(0, 1)) for index in range(5)]
     )
-    summed = exchange_sum(exchange_sum(partial_rows, "gy"), "gx")
+    gathered = lax.all_gather(partial_rows, ("gx", "gy"), tiled=False)
+    summed = jnp.sum(gathered, axis=0)
     point_count = tile_x * tile_y * lax.axis_size("gx") * group_size
     stencil_grad = summed / math.sqrt(point_count)
     query_grad = query_sum.reshape(tile_x, tile_y, features).astype(jnp.bfloat16)

time: 198 us -> 266 us (1.34)
  waiting for transfers between devices: 45 us -> 141 us
  starting transfers between devices: 81.7 us -> 33.7 us
  between operations: 1.57 us -> 14.7 us
    all_gather x0 -> x1, waiting for transfers between devices: none -> 117 us  [per_device(): gathered = lax.all_gather(partial_rows, ('gx', 'gy'), tiled=False)]
    ppermute x10 -> x0, starting transfers between devices: 46.7 us -> none  [the longest x8 32.6 us: exchange_sum(): value = value + lax.ppermute(value, axis, pairs)]
    ppermute x10 -> x0, waiting for transfers between devices: 27.7 us -> none  [the longest x8 27.7 us: exchange_sum(): value = value + lax.ppermute(value, axis, pairs)]
    all_to_all x1, waiting for transfers between devices: 0.01 us -> 7.9 us  [per_device(): lax.all_to_all(send_rows, 'gy', split_axis=0, concat_axis=0, tiled=True)]
    reduce_sum x0 -> x1, other arithmetic: none -> 2.7 us  [per_device(): summed = jnp.sum(gathered, axis=0)]
  transfers between devices with their start and end apart: 18 -> 9, of which waited for: 9 -> 5; matrix products, arithmetic and copies ran while one was open for 32% -> 26% of each run, Pallas kernels for 0% -> 0%
where the time goes in v2:
time: 266 us; the launch traced here: 263 us
  waiting for transfers between devices  141 us (53%)
  local copies, waits for them, and re-layouts  38 us (14%)
  starting transfers between devices  33.7 us (13%)
  matrix products  24 us (9%)
  between operations  14.7 us (6%)
  other arithmetic  11.7 us (4%)
    all_gather x1, waiting for transfers between devices, per_device(): gathered = lax.all_gather(partial_rows, ('gx', 'gy'), tiled=False)  117 us
    all_to_all x1, waiting for transfers between devices, per_device(): lax.all_to_all(query_part, 'gy', split_axis=0, concat_axis=0, tiled=True)  10.1 us
    another operation x2, local copies, waits for them, and re-layouts, tile_grads(): key_pack.reshape(item_count, 2, block_rows, HEADS, head_width)  9.96 us
    all_to_all x1, waiting for transfers between devices, per_device(): lax.all_to_all(send_rows, 'gy', split_axis=0, concat_axis=0, tiled=True)  7.9 us
    all_to_all x1, starting transfers between devices, per_device(): lax.all_to_all(send_stats, 'gy', split_axis=0, concat_axis=0, tiled=True)  7.2 us
    all_to_all x1, starting transfers between devices, per_device(): lax.all_to_all(send_ids, 'gy', split_axis=0, concat_axis=0, tiled=True)  7.1 us
    reshape x5, local copies, waits for them, and re-layouts, points_last(): return part.reshape(item_count, features, block_rows).transpose(0, 2, 1)  6.65 us
    dot_general x2, matrix products, tile_grads(): jnp.einsum('shdq,shdk->shqk', grad_heads, value_heads, preferred_element_...  6.56 us
  transfers between devices with their start and end apart: 9, of which 5 were waited for; matrix products, arithmetic and copies ran while one was open for 26% of the time, Pallas kernels for 0%

profile of v2, /device:TPU:6, one launch (start us, length us, event | category | flops | bytes accessed | tf_op | source)
XLA Modules:
  0.0 263.3 jit_solution(14048559832980250842)
XLA Ops:
  7.2 0.8 copy.122
  9.2 7.1 %all-to-all-start = ((bf16[8,1,2]{2,1,0:T(2,128)(2,1)}), bf16[8,1,2]{2,1,0:T(2,128)(2,1)S(1)}, u32[]{:S(2)}, u32[]{:S(2)}) async-start(bf16[8,1,2]{2,1,0:T(2,128)(2,1)} %all_to_all.20), calls=%async_computation | async-start | bytes 8192 | tf_op jit(solution)/shard_map/all_to_all | solution.py:161
  16.3 0.7 fusion.64
  17.0 1.9 collective-permute-start
  18.9 2.4 collective-permute-start.1
  21.6 0.8 reshape.211
  22.4 1.0 pad_maximum_fusion.1
  23.9 0.9 constant_dynamic-update-slice_fusion.1
  24.9 3.9 %collective-permute-start.3 = (bf16[18,1,128]{2,1,0:T(2,128)(2,1)S(1)}, bf16[18,1,128]{2,1,0:T(2,128)(2,1)S(1)}, u32[]{:S(2)}, u32[]{:S(2)}) collective-permute-start(bf16[18,1,128]{2,1,0:T(2,128)(2,1)S(1)} %get-tuple-element.14), channel_id=1, source_target_pairs={{0,1},{1,2},{2,3},{3,4},{4,5},{5,6},{6,7},{7,0},{8,9},{9,10},{10,1... | collective-permute-start | bytes 13832 | tf_op jit(solution)/shard_map/ppermute | solution.py:18
  28.8 3.1 %collective-permute-start.2 = (bf16[18,1,128]{2,1,0:T(2,128)(2,1)S(1)}, bf16[18,1,128]{2,1,0:T(2,128)(2,1)S(1)}, u32[]{:S(2)}, u32[]{:S(2)}) collective-permute-start(bf16[18,1,128]{2,1,0:T(2,128)(2,1)S(1)} %get-tuple-element.15), channel_id=1, source_target_pairs={{1,0},{2,1},{3,2},{4,3},{5,4},{6,5},{7,6},{0,7},{9,8},{10,9},{11,1... | collective-permute-start | bytes 13832 | tf_op jit(solution)/shard_map/ppermute | solution.py:21
  32.5 1.1 reshape.241
  33.6 1.1 reshape.242
  36.0 0.9 copy.117
  37.0 0.8 fusion.29
  38.2 0.7 reduce_sum.72
  40.5 7.2 %all-to-all-start.2 = ((bf16[8,2,2,4,128]{4,3,2,1,0:T(4,128)(2,1)}), bf16[8,2,2,4,128]{4,3,2,1,0:T(4,128)(2,1)S(1)}, u32[]{:S(2)}, u32[]{:S(2)}) async-start(bf16[8,2,2,4,128]{4,3,2,1,0:T(4,128)(2,1)} %reshape.219), calls=%async_computation.2 | async-start | bytes 65536 | tf_op jit(solution)/shard_map/all_to_all | solution.py:160
  47.7 1.0 maximum_bitcast_fusion
  48.7 1.3 copy.155
  50.0 5.7 %all-to-all-done.2 = bf16[8,2,2,4,128]{4,3,2,1,0:T(4,128)(2,1)S(1)} async-done(((bf16[8,2,2,4,128]{4,3,2,1,0:T(4,128)(2,1)}), bf16[8,2,2,4,128]{4,3,2,1,0:T(4,128)(2,1)S(1)}, u32[]{:S(2)}, u32[]{:S(2)}) %all-to-all-start.2) | async-done | bytes 32800 | tf_op jit(solution)/shard_map/all_to_all | solution.py:160
  56.3 3.6 %all-to-all-start.1 = ((bf16[8,2,2,128,128]{4,3,2,1,0:T(8,128)(2,1)}), bf16[8,2,2,128,128]{4,3,2,1,0:T(8,128)(2,1)S(1)}, u32[]{:S(2)}, u32[]{:S(2)}) async-start(bf16[8,2,2,128,128]{4,3,2,1,0:T(8,128)(2,1)} %bitcast.88), calls=%async_computation.1 | async-start | bytes 2097152 | tf_op jit(solution)/shard_map/all_to_all | solution.py:159
  60.7 0.9 copy.139
  61.5 0.7 pad_maximum_fusion
  64.1 1.5 convolution_convert_fusion.1
  65.6 4.6 %reshape_reshape.6 = bf16[16,2,128,4,32]{4,3,2,1,0:T(4,128)(2,1)} reshape(bf16[16,32768]{1,0:T(8,128)(2,1)S(1)} %convolution_convert_fusion.1) | data formatting | bytes 2097152 | tf_op jit(solution)/shard_map/reshape;reshape | solution.py:75
  70.2 5.4 %copy.126 = bf16[16,2,128,4,32]{2,4,3,0,1:T(8,128)(2,1)S(1)} copy(bf16[16,2,128,4,32]{4,3,2,1,0:T(4,128)(2,1)} %reshape_reshape.6) | data formatting | bytes 2097152 | tf_op jit(solution)/shard_map/reshape;reshape | solution.py:75
  75.6 1.3 stack.71
  77.7 2.2 fusion.13
  79.9 0.8 copy.130
  81.3 7.9 %all-to-all-done.1 = bf16[8,2,2,128,128]{4,3,2,1,0:T(8,128)(2,1)S(1)} async-done(((bf16[8,2,2,128,128]{4,3,2,1,0:T(8,128)(2,1)}), bf16[8,2,2,128,128]{4,3,2,1,0:T(8,128)(2,1)S(1)}, u32[]{:S(2)}, u32[]{:S(2)}) %all-to-all-start.1) | async-done | bytes 1048608 | tf_op jit(solution)/shard_map/all_to_all | solution.py:159
  89.9 0.8 fusion.18
  90.7 4.3 %multiply_convert_fusion = bf16[16,4,128,128]{3,2,1,0:T(8,128)(2,1)S(1)} fusion(f32[16,4,128,128]{3,2,1,0:T(8,128)S(1)} %fusion.18, f32[16,4,128]{2,1,0:T(4,128)S(1)} %copy-done.14, f32[16,4,128]{2,1,0:T(4,128)S(1)} %copy-done.13, bf16[16,2,4,32,128]{4,3,2,0,1:T(8,128)(2,1)} %bitcast.162, bf16[16,2,4,32,128]{4,3,2,0,1:T(8,128)(2,1)S(1)} %bitcast.158), kind=kOutput, calls=%fused_computation.2 | convolution fusion | flops 72351744 | bytes 7405568 | tf_op jit(solution)/shard_map/shdq,shdk->shqk/dot_general | solution.py:89
  95.0 2.3 convolution_multiply_fusion.2
  97.3 2.3 copy.132
  99.7 4.4 %all-to-all-start.3 = ((f32[8,2,128,128]{3,1,2,0:T(2,128)}), f32[8,2,128,128]{3,1,2,0:T(2,128)}, u32[]{:S(2)}, u32[]{:S(2)}) async-start(f32[8,2,128,128]{3,1,2,0:T(2,128)} %copy.132), calls=%async_computation.3 | async-start | bytes 2097152 | tf_op jit(solution)/shard_map/all_to_all | solution.py:180
  104.1 2.2 convolution_multiply_fusion.4
  106.3 1.8 copy.121
  108.1 2.0 convolution_multiply_fusion.3
  110.1 1.8 copy.135
  111.9 1.7 convolution_multiply_fusion.1
  113.5 1.7 copy.136
  115.3 3.1 %fusion.1 = f32[16,4,32,128]{3,2,1,0:T(8,128)S(1)} fusion(f32[16,4,128,128]{3,2,1,0:T(8,128)} %copy-done, f32[16,4,128]{2,1,0:T(4,128)} %get-tuple-element.19, bf16[16,2,4,32,128]{4,3,2,0,1:T(8,128)(2,1)S(1)} %bitcast.160), kind=kOutput, calls=%fused_computation.5 | convolution fusion | flops 70254592 | bytes 5799936 | tf_op jit(solution)/shard_map/shqk,shdq->shdk/dot_general | solution.py:95
  119.0 1.5 fusion.3
  120.5 1.1 fusion.34
  122.3 0.8 fusion.24
  123.2 10.1 %all-to-all-done.3 = f32[8,2,128,128]{3,1,2,0:T(2,128)} async-done(((f32[8,2,128,128]{3,1,2,0:T(2,128)}), f32[8,2,128,128]{3,1,2,0:T(2,128)}, u32[]{:S(2)}, u32[]{:S(2)}) %all-to-all-start.3) | async-done | bytes 1048608 | tf_op jit(solution)/shard_map/all_to_all | solution.py:180
  133.3 1.6 copy.133
  136.2 117.0 %all-gather.4.cloned.1.call-done = f32[768,5,128]{2,1,0:T(8,128)} async-done(((f32[1,5,128]{2,1,0:T(8,128)}), f32[768,5,128]{2,1,0:T(8,128)}) %all-gather.4.cloned.1.call-update) | async-done | bytes 1966096 | tf_op jit(solution)/shard_map/all_gather | solution.py:215
  253.1 2.7 %reduce_sum.79 = f32[5,128]{1,0:T(8,128)S(1)} reduce(f32[768,5,128]{2,1,0:T(8,128)} %all-gather.4.cloned.1.call-done, f32[]{:T(128)} %constant.42.clone.1), dimensions={0}, to_apply=%region_7.8 | reduce | flops 490880 | bytes 1968644 | tf_op jit(solution)/shard_map/reduce_sum | solution.py:216
  (107 shorter events, 14.1 us)
Async XLA Ops:
  7.2 29.8 %copy-start.3 = (bf16[16,32,128]{2,1,0:T(8,128)(2,1)S(1)}, bf16[16,32,128]{2,1,0:T(8,128)(2,1)}, u32[]{:S(2)}) copy-start(bf16[16,32,128]{2,1,0:T(8,128)(2,1)} %param.12) | copy-start | bytes 393220
  7.2 27.8 %copy-start.11 = (bf16[16,32,128]{2,1,0:T(8,128)(2,1)S(1)}, bf16[16,32,128]{2,1,0:T(8,128)(2,1)}, u32[]{:S(2)}) copy-start(bf16[16,32,128]{2,1,0:T(8,128)(2,1)} %param.9) | copy-start | bytes 393220
  7.2 28.3 %copy-start.5 = (bf16[16,32,128]{2,1,0:T(8,128)(2,1)S(1)}, bf16[16,32,128]{2,1,0:T(8,128)(2,1)}, u32[]{:S(2)}) copy-start(bf16[16,32,128]{2,1,0:T(8,128)(2,1)} %param.10) | copy-start | bytes 393220
  7.2 29.7 %copy-start.16 = (bf16[16,32,128]{2,1,0:T(8,128)(2,1)S(1)}, bf16[16,32,128]{2,1,0:T(8,128)(2,1)}, u32[]{:S(2)}) copy-start(bf16[16,32,128]{2,1,0:T(8,128)(2,1)} %param.11) | copy-start | bytes 393220
  9.2 31.3 %all-to-all-start = ((bf16[8,1,2]{2,1,0:T(2,128)(2,1)}), bf16[8,1,2]{2,1,0:T(2,128)(2,1)S(1)}, u32[]{:S(2)}, u32[]{:S(2)}) async-start(bf16[8,1,2]{2,1,0:T(2,128)(2,1)} %all_to_all.20), calls=%async_computation | async-start | bytes 8192 | tf_op jit(solution)/shard_map/all_to_all | solution.py:161
  17.0 7.8 %collective-permute-start = (bf16[1,32,128]{2,1,0:T(8,128)(2,1)S(1)}, bf16[1,32,128]{2,1,0:T(8,128)(2,1)S(1)}, u32[]{:S(2)}, u32[]{:S(2)}) collective-permute-start(bf16[1,32,128]{2,1,0:T(8,128)(2,1)S(1)} %get-tuple-element.17), channel_id=1, source_target_pairs={{8,0},{16,8},{24,16},{32,24},{40,32},{48,40},{56,48},{64,56},{72,6... | collective-permute-start | bytes 24584 | tf_op jit(solution)/shard_map/ppermute | solution.py:21
  18.9 5.0 %collective-permute-start.1 = (bf16[1,32,128]{2,1,0:T(8,128)(2,1)S(1)}, bf16[1,32,128]{2,1,0:T(8,128)(2,1)S(1)}, u32[]{:S(2)}, u32[]{:S(2)}) collective-permute-start(bf16[1,32,128]{2,1,0:T(8,128)(2,1)S(1)} %get-tuple-element.18), channel_id=1, source_target_pairs={{0,8},{8,16},{16,24},{24,32},{32,40},{40,48},{48,56},{56,64},{64,7... | collective-permute-start | bytes 24584 | tf_op jit(solution)/shard_map/ppermute | solution.py:18
  21.6 18.1 %copy-start.22 = (f32[16,4]{0,1:T(4,128)}, f32[16,4]{0,1:T(4,128)S(1)}, u32[]{:S(2)}) copy-start(f32[16,4]{0,1:T(4,128)S(1)} %fusion.39) | copy-start | bytes 772
  24.8 13.4 %copy-start.9 = (bf16[18,32,128]{2,1,0:T(8,128)(2,1)}, bf16[18,32,128]{2,1,0:T(8,128)(2,1)S(1)}, u32[]{:S(2)}) copy-start(bf16[18,32,128]{2,1,0:T(8,128)(2,1)S(1)} %constant_dynamic-update-slice_fusion) | copy-start | bytes 442372
  24.9 12.1 %collective-permute-start.3 = (bf16[18,1,128]{2,1,0:T(2,128)(2,1)S(1)}, bf16[18,1,128]{2,1,0:T(2,128)(2,1)S(1)}, u32[]{:S(2)}, u32[]{:S(2)}) collective-permute-start(bf16[18,1,128]{2,1,0:T(2,128)(2,1)S(1)} %get-tuple-element.14), channel_id=1, source_target_pairs={{0,1},{1,2},{2,3},{3,4},{4,5},{5,6},{6,7},{7,0},{8,9},{9,10},{10,1... | collective-permute-start | bytes 13832 | tf_op jit(solution)/shard_map/ppermute | solution.py:18
  28.8 8.1 %collective-permute-start.2 = (bf16[18,1,128]{2,1,0:T(2,128)(2,1)S(1)}, bf16[18,1,128]{2,1,0:T(2,128)(2,1)S(1)}, u32[]{:S(2)}, u32[]{:S(2)}) collective-permute-start(bf16[18,1,128]{2,1,0:T(2,128)(2,1)S(1)} %get-tuple-element.15), channel_id=1, source_target_pairs={{1,0},{2,1},{3,2},{4,3},{5,4},{6,5},{7,6},{0,7},{9,8},{10,9},{11,1... | collective-permute-start | bytes 13832 | tf_op jit(solution)/shard_map/ppermute | solution.py:21
  36.9 2.2 copy-start.18
  36.9 2.1 copy-start.20
  39.0 0.6 copy-start.17
  40.5 15.2 %copy-start.24 = (bf16[8,1,2]{2,1,0:T(2,128)(2,1)}, bf16[8,1,2]{2,1,0:T(2,128)(2,1)S(1)}, u32[]{:S(2)}) copy-start(bf16[8,1,2]{2,1,0:T(2,128)(2,1)S(1)} %all-to-all-done) | copy-start | bytes 100
  40.5 15.2 %all-to-all-start.2 = ((bf16[8,2,2,4,128]{4,3,2,1,0:T(4,128)(2,1)}), bf16[8,2,2,4,128]{4,3,2,1,0:T(4,128)(2,1)S(1)}, u32[]{:S(2)}, u32[]{:S(2)}) async-start(bf16[8,2,2,4,128]{4,3,2,1,0:T(4,128)(2,1)} %reshape.219), calls=%async_computation.2 | async-start | bytes 65536 | tf_op jit(solution)/shard_map/all_to_all | solution.py:160
  47.7 13.8 %copy-start.6 = (bf16[16,32,128]{2,1,0:T(8,128)(2,1)S(1)}, bf16[16,32,128]{2,1,0:T(8,128)(2,1)}, u32[]{:S(2)}) copy-start(bf16[16,32,128]{2,1,0:T(8,128)(2,1)} %param.10) | copy-start | bytes 393220
  47.7 13.8 %copy-start.12 = (bf16[16,32,128]{2,1,0:T(8,128)(2,1)S(1)}, bf16[16,32,128]{2,1,0:T(8,128)(2,1)}, u32[]{:S(2)}) copy-start(bf16[16,32,128]{2,1,0:T(8,128)(2,1)} %param.9) | copy-start | bytes 393220
  48.7 15.4 %copy-start.4 = (bf16[4,2,4,32,128]{4,3,2,0,1:T(8,128)(2,1)}, bf16[4,2,4,32,128]{4,3,2,0,1:T(8,128)(2,1)S(1)}, u32[]{:S(2)}) copy-start(bf16[4,2,4,32,128]{4,3,2,0,1:T(8,128)(2,1)S(1)} %get-tuple-element.28) | copy-start | bytes 786436
  48.7 13.6 %copy-start.30 = (f32[5,128]{1,0:T(8,128)S(1)}, f32[5,128]{1,0:T(8,128)}, u32[]{:S(2)}) copy-start(f32[5,128]{1,0:T(8,128)} %param.15) | copy-start | bytes 7684
  55.7 0.6 copy-start.15
  56.3 32.9 %all-to-all-start.1 = ((bf16[8,2,2,128,128]{4,3,2,1,0:T(8,128)(2,1)}), bf16[8,2,2,128,128]{4,3,2,1,0:T(8,128)(2,1)S(1)}, u32[]{:S(2)}, u32[]{:S(2)}) async-start(bf16[8,2,2,128,128]{4,3,2,1,0:T(8,128)(2,1)} %bitcast.88), calls=%async_computation.1 | async-start | bytes 2097152 | tf_op jit(solution)/shard_map/all_to_all | solution.py:159
  59.8 193.3 %all-gather.4.cloned.1.call-start = ((), (), s32[]{:S(2)}) async-start(), calls=%async_computation.4 | async-start | bytes 3149824 | tf_op jit(solution)/shard_map/all_gather | solution.py:215
  75.6 15.1 %copy-start.1 = (bf16[16,2,128,4,32]{2,4,3,0,1:T(8,128)(2,1)}, bf16[16,2,128,4,32]{2,4,3,0,1:T(8,128)(2,1)S(1)}, u32[]{:S(2)}) copy-start(bf16[16,2,128,4,32]{2,4,3,0,1:T(8,128)(2,1)S(1)} %copy.126) | copy-start | bytes 3145732
  89.8 0.8 copy-start.13
  89.9 0.8 copy-start.14
  90.6 6.7 %copy-start = (f32[16,4,128,128]{3,2,1,0:T(8,128)}, f32[16,4,128,128]{3,2,1,0:T(8,128)S(1)}, u32[]{:S(2)}) copy-start(f32[16,4,128,128]{3,2,1,0:T(8,128)S(1)} %fusion.18) | copy-start | bytes 12582916
  90.7 4.4 %copy-start.2 = (bf16[16,2,128,4,32]{2,4,3,0,1:T(8,128)(2,1)S(1)}, bf16[16,2,128,4,32]{2,4,3,0,1:T(8,128)(2,1)}, u32[]{:S(2)}) copy-start(bf16[16,2,128,4,32]{2,4,3,0,1:T(8,128)(2,1)} %copy-done.1) | copy-start | bytes 3145732
  99.7 33.6 %all-to-all-start.3 = ((f32[8,2,128,128]{3,1,2,0:T(2,128)}), f32[8,2,128,128]{3,1,2,0:T(2,128)}, u32[]{:S(2)}, u32[]{:S(2)}) async-start(f32[8,2,128,128]{3,1,2,0:T(2,128)} %copy.132), calls=%async_computation.3 | async-start | bytes 2097152 | tf_op jit(solution)/shard_map/all_to_all | solution.py:180
  115.3 5.2 %copy-start.7 = (f32[4,128,128]{1,0,2:T(4,128)S(1)}, f32[4,128,128]{1,0,2:T(4,128)}, u32[]{:S(2)}) copy-start(f32[4,128,128]{1,0,2:T(4,128)} %copy.139) | copy-start | bytes 786436
  118.9 3.4 %copy-start.10 = (bf16[18,32,128]{2,1,0:T(8,128)(2,1)S(1)}, bf16[18,32,128]{2,1,0:T(8,128)(2,1)}, u32[]{:S(2)}) copy-start(bf16[18,32,128]{2,1,0:T(8,128)(2,1)} %copy-done.9) | copy-start | bytes 442372
  118.9 3.4 %copy-start.19 = (bf16[18,1,128]{2,1,0:T(2,128)(2,1)S(1)}, bf16[18,1,128]{2,1,0:T(2,128)(2,1)}, u32[]{:S(2)}) copy-start(bf16[18,1,128]{2,1,0:T(2,128)(2,1)} %copy-done.18) | copy-start | bytes 13828
  118.9 3.4 %copy-start.21 = (bf16[18,1,128]{2,1,0:T(2,128)(2,1)S(1)}, bf16[18,1,128]{2,1,0:T(2,128)(2,1)}, u32[]{:S(2)}) copy-start(bf16[18,1,128]{2,1,0:T(2,128)(2,1)} %copy-done.20) | copy-start | bytes 13828
  118.9 3.4 %copy-start.25 = (f32[128]{0:T(128)S(1)}, f32[128]{0:T(128)}, u32[]{:S(2)}) copy-start(f32[128]{0:T(128)} %get-tuple-element.21) | copy-start | bytes 1540
  119.0 3.3 %copy-start.26 = (f32[128]{0:T(128)S(1)}, f32[128]{0:T(128)}, u32[]{:S(2)}) copy-start(f32[128]{0:T(128)} %get-tuple-element.22) | copy-start | bytes 1540
  119.0 3.3 %copy-start.27 = (f32[128]{0:T(128)S(1)}, f32[128]{0:T(128)}, u32[]{:S(2)}) copy-start(f32[128]{0:T(128)} %get-tuple-element.23) | copy-start | bytes 1540
  119.0 3.3 %copy-start.28 = (f32[128]{0:T(128)S(1)}, f32[128]{0:T(128)}, u32[]{:S(2)}) copy-start(f32[128]{0:T(128)} %get-tuple-element.24) | copy-start | bytes 1540
  119.0 3.3 %copy-start.29 = (f32[128]{0:T(128)S(1)}, f32[128]{0:T(128)}, u32[]{:S(2)}) copy-start(f32[128]{0:T(128)} %get-tuple-element.25) | copy-start | bytes 1540
  119.0 15.9 %copy-start.8 = (f32[4,128,128]{1,0,2:T(4,128)S(1)}, f32[4,128,128]{1,0,2:T(4,128)}, u32[]{:S(2)}) copy-start(f32[4,128,128]{1,0,2:T(4,128)} %copy.121) | copy-start | bytes 786436
  120.5 14.4 %copy-start.23 = (f32[16,4]{0,1:T(4,128)S(1)}, f32[16,4]{0,1:T(4,128)}, u32[]{:S(2)}) copy-start(f32[16,4]{0,1:T(4,128)} %copy-done.22) | copy-start | bytes 772
Sparse Core Ops, SparseCore 0:
  77.1 175.9 all-gather.3

commit v3 on v1

--- a/solution.py
+++ b/solution.py
@@ -61,6 +61,13 @@
             value = total
         stride *= radix
     return value
+
+
+def gather_sum(value, axis):
+    count = lax.axis_size(axis)
+    spread = jnp.broadcast_to(value[None], (count,) + value.shape)
+    parts = lax.all_to_all(spread, axis, split_axis=0, concat_axis=0, tiled=True)
+    return jnp.sum(parts, axis=0)
 
 
 def tile_grads(row_pack, stat_pack, key_pack):
@@ -212,7 +219,7 @@
     partial_rows = jnp.stack(
         [jnp.sum(moved[index] * value_float, axis=(0, 1)) for index in range(5)]
     )
-    summed = exchange_sum(exchange_sum(partial_rows, "gy"), "gx")
+    summed = gather_sum(gather_sum(partial_rows, "gy"), "gx")
     point_count = tile_x * tile_y * lax.axis_size("gx") * group_size
     stencil_grad = summed / math.sqrt(point_count)
     query_grad = query_sum.reshape(tile_x, tile_y, features).astype(jnp.bfloat16)

time: 198 us -> 174 us (0.88)
  starting transfers between devices: 81.7 us -> 57 us
    ppermute x10 -> x0, starting transfers between devices: 46.7 us -> none  [the longest x8 32.6 us: exchange_sum(): value = value + lax.ppermute(value, axis, pairs)]
    ppermute x10 -> x0, waiting for transfers between devices: 27.7 us -> none  [the longest x8 27.7 us: exchange_sum(): value = value + lax.ppermute(value, axis, pairs)]
    all_to_all x0 -> x2, starting transfers between devices: none -> 27.3 us  [gather_sum(): lax.all_to_all(spread, axis, split_axis=0, concat_axis=0, tiled=True)]
    all_to_all x0 -> x2, waiting for transfers between devices: none -> 17.3 us  [gather_sum(): lax.all_to_all(spread, axis, split_axis=0, concat_axis=0, tiled=True)]
    all_to_all x1, waiting for transfers between devices: 0.01 us -> 5.21 us  [per_device(): lax.all_to_all(send_rows, 'gy', split_axis=0, concat_axis=0, tiled=True)]
    all_to_all x1, waiting for transfers between devices: 8.41 us -> 13.3 us  [per_device(): lax.all_to_all(query_part, 'gy', split_axis=0, concat_axis=0, tiled=True)]
    all_to_all x1, starting transfers between devices: 6.96 us -> 3.34 us  [per_device(): lax.all_to_all(send_stats, 'gy', split_axis=0, concat_axis=0, tiled=True)]
  transfers between devices with their start and end apart: 18 -> 10, of which waited for: 9 -> 6; matrix products, arithmetic and copies ran while one was open for 32% -> 35% of each run, Pallas kernels for 0% -> 0%
where the time goes in v3:
time: 174 us; the launch traced here: 171 us
  starting transfers between devices  57 us (33%)
  waiting for transfers between devices  44.3 us (25%)
  local copies, waits for them, and re-layouts  37.6 us (22%)
  matrix products  22.3 us (13%)
  other arithmetic  8.37 us (5%)
    all_to_all x2, starting transfers between devices, gather_sum(): lax.all_to_all(spread, axis, split_axis=0, concat_axis=0, tiled=True)  27.3 us
    all_to_all x2, waiting for transfers between devices, gather_sum(): lax.all_to_all(spread, axis, split_axis=0, concat_axis=0, tiled=True)  17.3 us
    all_to_all x1, waiting for transfers between devices, per_device(): lax.all_to_all(query_part, 'gy', split_axis=0, concat_axis=0, tiled=True)  13.3 us
    another operation x2, local copies, waits for them, and re-layouts, tile_grads(): key_pack.reshape(item_count, 2, block_rows, HEADS, head_width)  9.96 us
    all_to_all x1, starting transfers between devices, per_device(): lax.all_to_all(send_ids, 'gy', split_axis=0, concat_axis=0, tiled=True)  7.1 us
    ppermute x2, starting transfers between devices, with_halo(): lax.ppermute(lax.slice_in_dim(block, block.shape[dim] - width, None, axis...  6.47 us
    all_to_all x1, waiting for transfers between devices, per_device(): lax.all_to_all(send_stats, 'gy', split_axis=0, concat_axis=0, tiled=True)  6.22 us
    dot_general x2, matrix products, tile_grads(): jnp.einsum('shdq,shdk->shqk', grad_heads, value_heads, preferred_element_...  5.76 us
  transfers between devices with their start and end apart: 10, of which 6 were waited for; matrix products, arithmetic and copies ran while one was open for 35% of the time, Pallas kernels for 0%

profile of v3, /device:TPU:6, one launch (start us, length us, event | category | flops | bytes accessed | tf_op | source)
XLA Modules:
  0.0 171.0 jit_solution(17638696829980900383)
XLA Ops:
  0.7 0.8 copy.153
  2.6 7.1 %all-to-all-start = ((bf16[8,1,2]{2,1,0:T(2,128)(2,1)}), bf16[8,1,2]{2,1,0:T(2,128)(2,1)S(1)}, u32[]{:S(2)}, u32[]{:S(2)}) async-start(bf16[8,1,2]{2,1,0:T(2,128)(2,1)} %all_to_all.28), calls=%async_computation | async-start | bytes 8192 | tf_op jit(solution)/shard_map/all_to_all | solution.py:168
  10.4 1.9 %collective-permute-start = (bf16[1,32,128]{2,1,0:T(8,128)(2,1)S(1)}, bf16[1,32,128]{2,1,0:T(8,128)(2,1)S(1)}, u32[]{:S(2)}, u32[]{:S(2)}) collective-permute-start(bf16[1,32,128]{2,1,0:T(8,128)(2,1)S(1)} %get-tuple-element.17), channel_id=1, source_target_pairs={{8,0},{16,8},{24,16},{32,24},{40,32},{48,40},{56,48},{64,56},{72,6... | collective-permute-start | bytes 24584 | tf_op jit(solution)/shard_map/ppermute | solution.py:21
  12.3 2.5 %collective-permute-start.1 = (bf16[1,32,128]{2,1,0:T(8,128)(2,1)S(1)}, bf16[1,32,128]{2,1,0:T(8,128)(2,1)S(1)}, u32[]{:S(2)}, u32[]{:S(2)}) collective-permute-start(bf16[1,32,128]{2,1,0:T(8,128)(2,1)S(1)} %get-tuple-element.18), channel_id=1, source_target_pairs={{0,8},{8,16},{16,24},{24,32},{32,40},{40,48},{48,56},{56,64},{64,7... | collective-permute-start | bytes 24584 | tf_op jit(solution)/shard_map/ppermute | solution.py:18
  14.9 1.1 reshape.240
  16.0 0.8 reshape.213
  16.9 1.1 reshape.239
  18.3 1.1 reshape.237
  19.7 1.1 reshape.238
  22.3 3.9 %collective-permute-start.3 = (bf16[18,1,128]{2,1,0:T(2,128)(2,1)S(1)}, bf16[18,1,128]{2,1,0:T(2,128)(2,1)S(1)}, u32[]{:S(2)}, u32[]{:S(2)}) collective-permute-start(bf16[18,1,128]{2,1,0:T(2,128)(2,1)S(1)} %get-tuple-element.14), channel_id=1, source_target_pairs={{0,1},{1,2},{2,3},{3,4},{4,5},{5,6},{6,7},{7,0},{8,9},{9,10},{10,1... | collective-permute-start | bytes 13832 | tf_op jit(solution)/shard_map/ppermute | solution.py:18
  26.2 3.1 %collective-permute-start.2 = (bf16[18,1,128]{2,1,0:T(2,128)(2,1)S(1)}, bf16[18,1,128]{2,1,0:T(2,128)(2,1)S(1)}, u32[]{:S(2)}, u32[]{:S(2)}) collective-permute-start(bf16[18,1,128]{2,1,0:T(2,128)(2,1)S(1)} %get-tuple-element.15), channel_id=1, source_target_pairs={{1,0},{2,1},{3,2},{4,3},{5,4},{6,5},{7,6},{0,7},{9,8},{10,9},{11,1... | collective-permute-start | bytes 13832 | tf_op jit(solution)/shard_map/ppermute | solution.py:21
  29.4 2.3 %collective-permute-done.2 = bf16[18,1,128]{2,1,0:T(2,128)(2,1)S(1)} collective-permute-done((bf16[18,1,128]{2,1,0:T(2,128)(2,1)S(1)}, bf16[18,1,128]{2,1,0:T(2,128)(2,1)S(1)}, u32[]{:S(2)}, u32[]{:S(2)}) %collective-permute-start.2) | collective-permute-done | bytes 4640 | tf_op jit(solution)/shard_map/ppermute | solution.py:21
  34.0 7.0 %all-to-all-start.4 = ((f32[8,5,128]{2,1,0:T(8,128)}), f32[8,5,128]{2,1,0:T(8,128)S(1)}, u32[]{:S(2)}, u32[]{:S(2)}) async-start(f32[8,5,128]{2,1,0:T(8,128)} %broadcast_in_dim.4), calls=%async_computation.4 | async-start | bytes 65536 | tf_op jit(solution)/shard_map/all_to_all | solution.py:69
  41.8 7.5 %all-to-all-done.4 = f32[8,5,128]{2,1,0:T(8,128)S(1)} async-done(((f32[8,5,128]{2,1,0:T(8,128)}), f32[8,5,128]{2,1,0:T(8,128)S(1)}, u32[]{:S(2)}, u32[]{:S(2)}) %all-to-all-start.4) | async-done | bytes 20512 | tf_op jit(solution)/shard_map/all_to_all | solution.py:69
  49.3 3.3 %all-to-all-start.2 = ((bf16[8,2,2,4,128]{4,3,2,1,0:T(4,128)(2,1)}), bf16[8,2,2,4,128]{4,3,2,1,0:T(4,128)(2,1)S(1)}, u32[]{:S(2)}, u32[]{:S(2)}) async-start(bf16[8,2,2,4,128]{4,3,2,1,0:T(4,128)(2,1)} %reshape.221), calls=%async_computation.2 | async-start | bytes 65536 | tf_op jit(solution)/shard_map/all_to_all | solution.py:167
  53.1 1.2 copy.190
  54.3 6.2 %all-to-all-done.2 = bf16[8,2,2,4,128]{4,3,2,1,0:T(4,128)(2,1)S(1)} async-done(((bf16[8,2,2,4,128]{4,3,2,1,0:T(4,128)(2,1)}), bf16[8,2,2,4,128]{4,3,2,1,0:T(4,128)(2,1)S(1)}, u32[]{:S(2)}, u32[]{:S(2)}) %all-to-all-start.2) | async-done | bytes 32800 | tf_op jit(solution)/shard_map/all_to_all | solution.py:167
  61.2 3.6 %all-to-all-start.1 = ((bf16[8,2,2,128,128]{4,3,2,1,0:T(8,128)(2,1)}), bf16[8,2,2,128,128]{4,3,2,1,0:T(8,128)(2,1)S(1)}, u32[]{:S(2)}, u32[]{:S(2)}) async-start(bf16[8,2,2,128,128]{4,3,2,1,0:T(8,128)(2,1)} %bitcast.87), calls=%async_computation.1 | async-start | bytes 2097152 | tf_op jit(solution)/shard_map/all_to_all | solution.py:166
  65.0 0.8 copy.170
  68.5 1.5 convolution_convert_fusion.1
  70.0 4.6 %reshape_reshape.6 = bf16[16,2,128,4,32]{4,3,2,1,0:T(4,128)(2,1)} reshape(bf16[16,32768]{1,0:T(8,128)(2,1)S(1)} %convolution_convert_fusion.1) | data formatting | bytes 2097152 | tf_op jit(solution)/shard_map/reshape;reshape | solution.py:82
  74.6 5.4 %copy.157 = bf16[16,2,128,4,32]{2,4,3,0,1:T(8,128)(2,1)S(1)} copy(bf16[16,2,128,4,32]{4,3,2,1,0:T(4,128)(2,1)} %reshape_reshape.6) | data formatting | bytes 2097152 | tf_op jit(solution)/shard_map/reshape;reshape | solution.py:82
  80.7 1.4 fusion.13
  82.1 0.8 copy-done.3
  82.9 1.3 convolution_multiply_fusion.4
  84.2 0.9 copy.152
  85.1 0.8 reduce_sum.88
  85.8 0.8 copy.161
  87.2 5.2 %all-to-all-done.1 = bf16[8,2,2,128,128]{4,3,2,1,0:T(8,128)(2,1)S(1)} async-done(((bf16[8,2,2,128,128]{4,3,2,1,0:T(8,128)(2,1)}), bf16[8,2,2,128,128]{4,3,2,1,0:T(8,128)(2,1)S(1)}, u32[]{:S(2)}, u32[]{:S(2)}) %all-to-all-start.1) | async-done | bytes 1048608 | tf_op jit(solution)/shard_map/all_to_all | solution.py:166
  92.4 0.8 broadcast_in_dim.5
  93.2 20.3 %all-to-all-start.5 = ((f32[96,5,128]{2,1,0:T(8,128)}), f32[96,5,128]{2,1,0:T(8,128)}, u32[]{:S(2)}, u32[]{:S(2)}) async-start(f32[96,5,128]{2,1,0:T(8,128)} %broadcast_in_dim.5), calls=%async_computation.5 | async-start | bytes 786432 | tf_op jit(solution)/shard_map/all_to_all | solution.py:69
  114.2 0.8 fusion.18
  115.0 4.3 %multiply_convert_fusion = bf16[16,4,128,128]{3,2,1,0:T(8,128)(2,1)S(1)} fusion(f32[16,4,128,128]{3,2,1,0:T(8,128)S(1)} %fusion.18, f32[16,4,128]{2,1,0:T(4,128)S(1)} %copy-done.15, f32[16,4,128]{2,1,0:T(4,128)S(1)} %copy-done.14, bf16[16,2,4,32,128]{4,3,2,0,1:T(8,128)(2,1)} %bitcast.161, bf16[16,2,4,32,128]{4,3,2,0,1:T(8,128)(2,1)S(1)} %bitcast.157), kind=kOutput, calls=%fused_computation.2 | convolution fusion | flops 72351744 | bytes 7405568 | tf_op jit(solution)/shard_map/shdq,shdk->shqk/dot_general | solution.py:96
  119.4 2.2 %convolution_multiply_fusion.2 = f32[16,4,32,128]{3,2,1,0:T(8,128)} fusion(bf16[16,4,128,128]{3,2,1,0:T(8,128)(2,1)S(1)} %multiply_convert_fusion, bf16[16,2,4,32,128]{4,3,2,0,1:T(8,128)(2,1)S(1)} %bitcast.162), kind=kOutput, calls=%fused_computation.19 | convolution fusion | flops 67371008 | bytes 3670016 | tf_op jit(solution)/shard_map/shqk,shdk->shdq/dot_general | solution.py:110
  121.6 2.3 %copy.163 = f32[8,2,128,128]{3,1,2,0:T(2,128)} copy(f32[8,2,128,128]{2,3,1,0:T(8,128)} %bitcast.163) | data formatting | bytes 2097152 | tf_op jit(solution)/shard_map/reshape | solution.py:184
  123.9 9.8 %all-to-all-done.5 = f32[96,5,128]{2,1,0:T(8,128)} async-done(((f32[96,5,128]{2,1,0:T(8,128)}), f32[96,5,128]{2,1,0:T(8,128)}, u32[]{:S(2)}, u32[]{:S(2)}) %all-to-all-start.5) | async-done | bytes 245792 | tf_op jit(solution)/shard_map/all_to_all | solution.py:69
  133.6 4.2 %all-to-all-start.3 = ((f32[8,2,128,128]{3,1,2,0:T(2,128)}), f32[8,2,128,128]{3,1,2,0:T(2,128)}, u32[]{:S(2)}, u32[]{:S(2)}) async-start(f32[8,2,128,128]{3,1,2,0:T(2,128)} %copy.163), calls=%async_computation.3 | async-start | bytes 2097152 | tf_op jit(solution)/shard_map/all_to_all | solution.py:187
  137.9 2.0 %convolution_multiply_fusion.3 = f32[4,4,32,128]{3,2,1,0:T(8,128)} fusion(bf16[4,4,128,128]{3,2,1,0:T(8,128)(2,1)} %copy-done.3, bf16[4,2,4,32,128]{4,3,2,0,1:T(8,128)(2,1)S(1)} %get-tuple-element.29), kind=kOutput, calls=%fused_computation.21 | convolution fusion | flops 16842752 | bytes 917504 | tf_op jit(solution)/shard_map/shqk,shdq->shdk/dot_general | solution.py:106
  139.9 1.8 %copy.166 = f32[4,128,128]{1,0,2:T(4,128)} copy(f32[4,128,128]{2,1,0:T(8,128)} %bitcast.173) | data formatting | bytes 524288 | tf_op jit(solution)/shard_map/reshape | solution.py:115
  141.7 1.1 reduce_sum.89
  143.4 1.6 convolution_multiply_fusion.1
  145.0 1.7 %copy.167 = f32[16,128,128]{1,0,2:T(8,128)S(1)} copy(f32[16,128,128]{2,1,0:T(8,128)} %bitcast.164) | data formatting | bytes 2097152 | tf_op jit(solution)/shard_map/reshape | solution.py:115
  146.8 3.1 %fusion.1 = f32[16,4,32,128]{3,2,1,0:T(8,128)S(1)} fusion(f32[16,4,128,128]{3,2,1,0:T(8,128)} %copy-done, f32[16,4,128]{2,1,0:T(4,128)} %get-tuple-element.19, bf16[16,2,4,32,128]{4,3,2,0,1:T(8,128)(2,1)S(1)} %bitcast.159), kind=kOutput, calls=%fused_computation.5 | convolution fusion | flops 70254592 | bytes 5799936 | tf_op jit(solution)/shard_map/shqk,shdq->shdk/dot_general | solution.py:102
  150.5 1.5 fusion.3
  152.1 1.1 fusion.34
  153.9 0.8 fusion.24
  154.7 13.3 %all-to-all-done.3 = f32[8,2,128,128]{3,1,2,0:T(2,128)} async-done(((f32[8,2,128,128]{3,1,2,0:T(2,128)}), f32[8,2,128,128]{3,1,2,0:T(2,128)}, u32[]{:S(2)}, u32[]{:S(2)}) %all-to-all-start.3) | async-done | bytes 1048608 | tf_op jit(solution)/shard_map/all_to_all | solution.py:187
  168.0 1.6 copy.164
  (115 shorter events, 15.9 us)
Async XLA Ops:
  0.6 21.5 %copy-start.4 = (bf16[16,32,128]{2,1,0:T(8,128)(2,1)S(1)}, bf16[16,32,128]{2,1,0:T(8,128)(2,1)}, u32[]{:S(2)}) copy-start(bf16[16,32,128]{2,1,0:T(8,128)(2,1)} %param.12) | copy-start | bytes 393220
  0.6 28.7 %copy-start.12 = (bf16[16,32,128]{2,1,0:T(8,128)(2,1)S(1)}, bf16[16,32,128]{2,1,0:T(8,128)(2,1)}, u32[]{:S(2)}) copy-start(bf16[16,32,128]{2,1,0:T(8,128)(2,1)} %param.8) | copy-start | bytes 393220
  2.6 30.8 %all-to-all-start = ((bf16[8,1,2]{2,1,0:T(2,128)(2,1)}), bf16[8,1,2]{2,1,0:T(2,128)(2,1)S(1)}, u32[]{:S(2)}, u32[]{:S(2)}) async-start(bf16[8,1,2]{2,1,0:T(2,128)(2,1)} %all_to_all.28), calls=%async_computation | async-start | bytes 8192 | tf_op jit(solution)/shard_map/all_to_all | solution.py:168
  10.4 11.8 %collective-permute-start = (bf16[1,32,128]{2,1,0:T(8,128)(2,1)S(1)}, bf16[1,32,128]{2,1,0:T(8,128)(2,1)S(1)}, u32[]{:S(2)}, u32[]{:S(2)}) collective-permute-start(bf16[1,32,128]{2,1,0:T(8,128)(2,1)S(1)} %get-tuple-element.17), channel_id=1, source_target_pairs={{8,0},{16,8},{24,16},{32,24},{40,32},{48,40},{56,48},{64,56},{72,6... | collective-permute-start | bytes 24584 | tf_op jit(solution)/shard_map/ppermute | solution.py:21
  12.3 19.4 %copy-start.6 = (bf16[16,32,128]{2,1,0:T(8,128)(2,1)S(1)}, bf16[16,32,128]{2,1,0:T(8,128)(2,1)}, u32[]{:S(2)}) copy-start(bf16[16,32,128]{2,1,0:T(8,128)(2,1)} %param.10) | copy-start | bytes 393220
  12.3 19.4 %copy-start.18 = (bf16[16,32,128]{2,1,0:T(8,128)(2,1)S(1)}, bf16[16,32,128]{2,1,0:T(8,128)(2,1)}, u32[]{:S(2)}) copy-start(bf16[16,32,128]{2,1,0:T(8,128)(2,1)} %param.11) | copy-start | bytes 393220
  12.3 9.8 %collective-permute-start.1 = (bf16[1,32,128]{2,1,0:T(8,128)(2,1)S(1)}, bf16[1,32,128]{2,1,0:T(8,128)(2,1)S(1)}, u32[]{:S(2)}, u32[]{:S(2)}) collective-permute-start(bf16[1,32,128]{2,1,0:T(8,128)(2,1)S(1)} %get-tuple-element.18), channel_id=1, source_target_pairs={{0,8},{8,16},{16,24},{24,32},{32,40},{40,48},{48,56},{56,64},{64,7... | collective-permute-start | bytes 24584 | tf_op jit(solution)/shard_map/ppermute | solution.py:18
  21.4 10.6 %copy-start.5 = (bf16[4,2,4,32,128]{4,3,2,0,1:T(8,128)(2,1)}, bf16[4,2,4,32,128]{4,3,2,0,1:T(8,128)(2,1)S(1)}, u32[]{:S(2)}) copy-start(bf16[4,2,4,32,128]{4,3,2,0,1:T(8,128)(2,1)S(1)} %get-tuple-element.28) | copy-start | bytes 786436
  22.2 38.4 %copy-start.24 = (f32[16,4]{0,1:T(4,128)}, f32[16,4]{0,1:T(4,128)S(1)}, u32[]{:S(2)}) copy-start(f32[16,4]{0,1:T(4,128)S(1)} %fusion.39) | copy-start | bytes 772
  22.2 38.3 %copy-start.10 = (bf16[18,32,128]{2,1,0:T(8,128)(2,1)}, bf16[18,32,128]{2,1,0:T(8,128)(2,1)S(1)}, u32[]{:S(2)}) copy-start(bf16[18,32,128]{2,1,0:T(8,128)(2,1)S(1)} %constant_dynamic-update-slice_fusion) | copy-start | bytes 442372
  22.3 7.1 %collective-permute-start.3 = (bf16[18,1,128]{2,1,0:T(2,128)(2,1)S(1)}, bf16[18,1,128]{2,1,0:T(2,128)(2,1)S(1)}, u32[]{:S(2)}, u32[]{:S(2)}) collective-permute-start(bf16[18,1,128]{2,1,0:T(2,128)(2,1)S(1)} %get-tuple-element.14), channel_id=1, source_target_pairs={{0,1},{1,2},{2,3},{3,4},{4,5},{5,6},{6,7},{7,0},{8,9},{9,10},{10,1... | collective-permute-start | bytes 13832 | tf_op jit(solution)/shard_map/ppermute | solution.py:18
  26.2 5.6 %collective-permute-start.2 = (bf16[18,1,128]{2,1,0:T(2,128)(2,1)S(1)}, bf16[18,1,128]{2,1,0:T(2,128)(2,1)S(1)}, u32[]{:S(2)}, u32[]{:S(2)}) collective-permute-start(bf16[18,1,128]{2,1,0:T(2,128)(2,1)S(1)} %get-tuple-element.15), channel_id=1, source_target_pairs={{1,0},{2,1},{3,2},{4,3},{5,4},{6,5},{7,6},{0,7},{9,8},{10,9},{11,1... | collective-permute-start | bytes 13832 | tf_op jit(solution)/shard_map/ppermute | solution.py:21
  29.4 3.0 %copy-start.20 = (bf16[18,1,128]{2,1,0:T(2,128)(2,1)}, bf16[18,1,128]{2,1,0:T(2,128)(2,1)S(1)}, u32[]{:S(2)}) copy-start(bf16[18,1,128]{2,1,0:T(2,128)(2,1)S(1)} %collective-permute-done.3) | copy-start | bytes 13828
  31.8 28.8 %copy-start.22 = (bf16[18,1,128]{2,1,0:T(2,128)(2,1)}, bf16[18,1,128]{2,1,0:T(2,128)(2,1)S(1)}, u32[]{:S(2)}) copy-start(bf16[18,1,128]{2,1,0:T(2,128)(2,1)S(1)} %collective-permute-done.2) | copy-start | bytes 13828
  33.2 32.7 %copy-start.7 = (bf16[16,32,128]{2,1,0:T(8,128)(2,1)S(1)}, bf16[16,32,128]{2,1,0:T(8,128)(2,1)}, u32[]{:S(2)}) copy-start(bf16[16,32,128]{2,1,0:T(8,128)(2,1)} %param.10) | copy-start | bytes 393220
  33.2 32.7 %copy-start.13 = (bf16[16,32,128]{2,1,0:T(8,128)(2,1)S(1)}, bf16[16,32,128]{2,1,0:T(8,128)(2,1)}, u32[]{:S(2)}) copy-start(bf16[16,32,128]{2,1,0:T(8,128)(2,1)} %param.9) | copy-start | bytes 393220
  33.3 27.3 %copy-start.19 = (bf16[4,128,4]{1,0,2:T(4,128)(2,1)}, bf16[4,128,4]{1,0,2:T(4,128)(2,1)S(1)}, u32[]{:S(2)}) copy-start(bf16[4,128,4]{1,0,2:T(4,128)(2,1)S(1)} %copy.191) | copy-start | bytes 12292
  33.3 33.3 %copy-start.32 = (f32[5,128]{1,0:T(8,128)S(1)}, f32[5,128]{1,0:T(8,128)}, u32[]{:S(2)}) copy-start(f32[5,128]{1,0:T(8,128)} %param.15) | copy-start | bytes 7684
  33.4 27.2 %copy-start.26 = (bf16[8,1,2]{2,1,0:T(2,128)(2,1)}, bf16[8,1,2]{2,1,0:T(2,128)(2,1)S(1)}, u32[]{:S(2)}) copy-start(bf16[8,1,2]{2,1,0:T(2,128)(2,1)S(1)} %all-to-all-done) | copy-start | bytes 100
  34.0 15.3 %all-to-all-start.4 = ((f32[8,5,128]{2,1,0:T(8,128)}), f32[8,5,128]{2,1,0:T(8,128)S(1)}, u32[]{:S(2)}, u32[]{:S(2)}) async-start(f32[8,5,128]{2,1,0:T(8,128)} %broadcast_in_dim.4), calls=%async_computation.4 | async-start | bytes 65536 | tf_op jit(solution)/shard_map/all_to_all | solution.py:69
  49.3 11.3 %copy-start.16 = (f32[8,5,128]{2,1,0:T(8,128)}, f32[8,5,128]{2,1,0:T(8,128)S(1)}, u32[]{:S(2)}) copy-start(f32[8,5,128]{2,1,0:T(8,128)S(1)} %all-to-all-done.4) | copy-start | bytes 61444
  49.3 11.3 %all-to-all-start.2 = ((bf16[8,2,2,4,128]{4,3,2,1,0:T(4,128)(2,1)}), bf16[8,2,2,4,128]{4,3,2,1,0:T(4,128)(2,1)S(1)}, u32[]{:S(2)}, u32[]{:S(2)}) async-start(bf16[8,2,2,4,128]{4,3,2,1,0:T(4,128)(2,1)} %reshape.221), calls=%async_computation.2 | async-start | bytes 65536 | tf_op jit(solution)/shard_map/all_to_all | solution.py:167
  60.6 0.6 copy-start.17
  61.2 31.3 %all-to-all-start.1 = ((bf16[8,2,2,128,128]{4,3,2,1,0:T(8,128)(2,1)}), bf16[8,2,2,128,128]{4,3,2,1,0:T(8,128)(2,1)S(1)}, u32[]{:S(2)}, u32[]{:S(2)}) async-start(bf16[8,2,2,128,128]{4,3,2,1,0:T(8,128)(2,1)} %bitcast.87), calls=%async_computation.1 | async-start | bytes 2097152 | tf_op jit(solution)/shard_map/all_to_all | solution.py:166
  80.0 35.0 %copy-start.1 = (bf16[16,2,128,4,32]{2,4,3,0,1:T(8,128)(2,1)}, bf16[16,2,128,4,32]{2,4,3,0,1:T(8,128)(2,1)S(1)}, u32[]{:S(2)}) copy-start(bf16[16,2,128,4,32]{2,4,3,0,1:T(8,128)(2,1)S(1)} %copy.157) | copy-start | bytes 3145732
  82.1 0.8 copy-start.3
  93.2 40.4 %all-to-all-start.5 = ((f32[96,5,128]{2,1,0:T(8,128)}), f32[96,5,128]{2,1,0:T(8,128)}, u32[]{:S(2)}, u32[]{:S(2)}) async-start(f32[96,5,128]{2,1,0:T(8,128)} %broadcast_in_dim.5), calls=%async_computation.5 | async-start | bytes 786432 | tf_op jit(solution)/shard_map/all_to_all | solution.py:69
  114.2 0.8 copy-start.14
  114.2 0.8 copy-start.15
  115.0 6.6 %copy-start = (f32[16,4,128,128]{3,2,1,0:T(8,128)}, f32[16,4,128,128]{3,2,1,0:T(8,128)S(1)}, u32[]{:S(2)}) copy-start(f32[16,4,128,128]{3,2,1,0:T(8,128)S(1)} %fusion.18) | copy-start | bytes 12582916
  115.0 4.4 %copy-start.2 = (bf16[16,2,128,4,32]{2,4,3,0,1:T(8,128)(2,1)S(1)}, bf16[16,2,128,4,32]{2,4,3,0,1:T(8,128)(2,1)}, u32[]{:S(2)}) copy-start(bf16[16,2,128,4,32]{2,4,3,0,1:T(8,128)(2,1)} %copy-done.1) | copy-start | bytes 3145732
  133.6 34.4 %all-to-all-start.3 = ((f32[8,2,128,128]{3,1,2,0:T(2,128)}), f32[8,2,128,128]{3,1,2,0:T(2,128)}, u32[]{:S(2)}, u32[]{:S(2)}) async-start(f32[8,2,128,128]{3,1,2,0:T(2,128)} %copy.163), calls=%async_computation.3 | async-start | bytes 2097152 | tf_op jit(solution)/shard_map/all_to_all | solution.py:187
  146.7 5.3 %copy-start.9 = (f32[4,128,128]{1,0,2:T(4,128)S(1)}, f32[4,128,128]{1,0,2:T(4,128)}, u32[]{:S(2)}) copy-start(f32[4,128,128]{1,0,2:T(4,128)} %copy.170) | copy-start | bytes 786436
  150.4 3.5 %copy-start.11 = (bf16[18,32,128]{2,1,0:T(8,128)(2,1)S(1)}, bf16[18,32,128]{2,1,0:T(8,128)(2,1)}, u32[]{:S(2)}) copy-start(bf16[18,32,128]{2,1,0:T(8,128)(2,1)} %copy-done.10) | copy-start | bytes 442372
  150.4 3.5 %copy-start.21 = (bf16[18,1,128]{2,1,0:T(2,128)(2,1)S(1)}, bf16[18,1,128]{2,1,0:T(2,128)(2,1)}, u32[]{:S(2)}) copy-start(bf16[18,1,128]{2,1,0:T(2,128)(2,1)} %copy-done.20) | copy-start | bytes 13828
  150.4 3.4 %copy-start.23 = (bf16[18,1,128]{2,1,0:T(2,128)(2,1)S(1)}, bf16[18,1,128]{2,1,0:T(2,128)(2,1)}, u32[]{:S(2)}) copy-start(bf16[18,1,128]{2,1,0:T(2,128)(2,1)} %copy-done.22) | copy-start | bytes 13828
  150.4 3.4 %copy-start.27 = (f32[128]{0:T(128)S(1)}, f32[128]{0:T(128)}, u32[]{:S(2)}) copy-start(f32[128]{0:T(128)} %get-tuple-element.21) | copy-start | bytes 1540
  150.4 3.4 %copy-start.28 = (f32[128]{0:T(128)S(1)}, f32[128]{0:T(128)}, u32[]{:S(2)}) copy-start(f32[128]{0:T(128)} %get-tuple-element.22) | copy-start | bytes 1540
  150.4 3.4 %copy-start.29 = (f32[128]{0:T(128)S(1)}, f32[128]{0:T(128)}, u32[]{:S(2)}) copy-start(f32[128]{0:T(128)} %get-tuple-element.23) | copy-start | bytes 1540
  150.4 3.4 %copy-start.30 = (f32[128]{0:T(128)S(1)}, f32[128]{0:T(128)}, u32[]{:S(2)}) copy-start(f32[128]{0:T(128)} %get-tuple-element.24) | copy-start | bytes 1540
  150.5 3.4 %copy-start.31 = (f32[128]{0:T(128)S(1)}, f32[128]{0:T(128)}, u32[]{:S(2)}) copy-start(f32[128]{0:T(128)} %get-tuple-element.25) | copy-start | bytes 1540
  150.5 19.2 %copy-start.8 = (f32[4,128,128]{1,0,2:T(4,128)S(1)}, f32[4,128,128]{1,0,2:T(4,128)}, u32[]{:S(2)}) copy-start(f32[4,128,128]{1,0,2:T(4,128)} %copy.152) | copy-start | bytes 786436
  152.0 17.6 %copy-start.25 = (f32[16,4]{0,1:T(4,128)S(1)}, f32[16,4]{0,1:T(4,128)}, u32[]{:S(2)}) copy-start(f32[16,4]{0,1:T(4,128)} %copy-done.24) | copy-start | bytes 772

commit v4 on v3

--- a/solution.py
+++ b/solution.py
@@ -138,72 +138,6 @@
     row_pack = jnp.stack([query_blocks, grad_blocks], 1)
     key_pack = jnp.stack([key_blocks, value_blocks], 1)
     diag_query, diag_key, diag_value = tile_grads(row_pack, stat_blocks, key_pack)
-    columns = neighbour_blocks.reshape(pair_count)
-    owners = columns // row_blocks
-    inner = columns % row_blocks
-    order = jnp.arange(pair_count, dtype=jnp.int32)
-    before = (owners[:, None] == owners[None, :]) & (order[None, :] < order[:, None])
-    rank = jnp.sum(before.astype(jnp.int32), 1)
-    slot_of = owners * capacity + rank
-    placed = (jnp.arange(slot_count, dtype=jnp.int32)[:, None] == slot_of[None, :]).astype(
-        jnp.float32
-    )
-    source_rows = (
-        (order // listed)[:, None] == jnp.arange(row_blocks, dtype=jnp.int32)[None, :]
-    ).astype(jnp.float32)
-    picker = jnp.dot(placed, source_rows, precision=lax.Precision.HIGHEST)
-    picker_low = picker.astype(jnp.bfloat16)
-    send_rows = jnp.dot(
-        picker_low, row_pack.reshape(row_blocks, -1), preferred_element_type=jnp.float32
-    )
-    send_rows = send_rows.astype(jnp.bfloat16).reshape(group_size, capacity, 2, BLOCK, features)
-    send_stats = jnp.dot(
-        picker_low, stat_blocks.reshape(row_blocks, -1), preferred_element_type=jnp.float32
-    )
-    send_stats = send_stats.astype(jnp.bfloat16).reshape(group_size, capacity, 2, HEADS, BLOCK)
-    send_ids = jnp.dot(placed, (inner + 1).astype(jnp.float32), precision=lax.Precision.HIGHEST)
-    send_ids = send_ids.astype(jnp.bfloat16).reshape(group_size, capacity)
-    rows_in = lax.all_to_all(send_rows, "gy", split_axis=0, concat_axis=0, tiled=True)
-    stats_in = lax.all_to_all(send_stats, "gy", split_axis=0, concat_axis=0, tiled=True)
-    ids_in = lax.all_to_all(send_ids, "gy", split_axis=0, concat_axis=0, tiled=True)
-    item_count = rows_in.shape[1]
-    total_items = group_size * item_count
-    wanted = ids_in.astype(jnp.float32).astype(jnp.int32) - 1
-    chooser = (wanted[..., None] == jnp.arange(row_blocks, dtype=jnp.int32)).astype(jnp.bfloat16)
-    keys_in = jnp.dot(
-        chooser.reshape(-1, row_blocks),
-        key_pack.reshape(row_blocks, -1),
-        preferred_element_type=jnp.float32,
-    )
-    keys_in = keys_in.astype(jnp.bfloat16).reshape(total_items, 2, BLOCK, features)
-    query_part, key_part, value_part = tile_grads(
-        rows_in.reshape(total_items, 2, BLOCK, features),
-        stats_in.reshape(total_items, 2, HEADS, BLOCK),
-        keys_in,
-    )
-    query_part = query_part.reshape(group_size, item_count, BLOCK, features)
-    key_part = key_part.reshape(group_size, item_count, BLOCK, features)
-    value_part = value_part.reshape(group_size, item_count, BLOCK, features)
-    returned = lax.all_to_all(query_part, "gy", split_axis=0, concat_axis=0, tiled=True)
-    returned, pieces, ids_in = (returned, jnp.stack([key_part, value_part], 2), ids_in)
-    query_sum = diag_query + jnp.einsum(
-        "sr,sbf->rbf",
-        picker,
-        returned.reshape(slot_count, BLOCK, features),
-        precision=lax.Precision.HIGHEST,
-    )
-    arrived = ids_in.reshape(slot_count).astype(jnp.float32).astype(jnp.int32) - 1
-    owned = (arrived[:, None] == jnp.arange(row_blocks, dtype=jnp.int32)[None, :]).astype(
-        jnp.float32
-    )
-    key_value_sum = jnp.einsum(
-        "sr,sxbf->rxbf",
-        owned,
-        pieces.reshape(slot_count, 2, BLOCK, features),
-        precision=lax.Precision.HIGHEST,
-    )
-    key_total = diag_key + key_value_sum[:, 0]
-    value_total = diag_value + key_value_sum[:, 1]
     rim = with_halo(out_grad, (("gx", 0), ("gy", 1)), 1)
     moved = [
         out_grad.astype(jnp.float32),
@@ -219,8 +153,94 @@
     partial_rows = jnp.stack(
         [jnp.sum(moved[index] * value_float, axis=(0, 1)) for index in range(5)]
     )
-    summed = gather_sum(gather_sum(partial_rows, "gy"), "gx")
+    column_sum = gather_sum(partial_rows, "gx")
     point_count = tile_x * tile_y * lax.axis_size("gx") * group_size
+    columns = neighbour_blocks.reshape(pair_count)
+    owners = columns // row_blocks
+    inner = columns % row_blocks
+    order = jnp.arange(pair_count, dtype=jnp.int32)
+    before = (owners[:, None] == owners[None, :]) & (order[None, :] < order[:, None])
+    rank = jnp.sum(before.astype(jnp.int32), 1)
+    slot_of = owners * capacity + rank
+    placed = (jnp.arange(slot_count, dtype=jnp.int32)[:, None] == slot_of[None, :]).astype(
+        jnp.float32
+    )
+    source_rows = (
+        (order // listed)[:, None] == jnp.arange(row_blocks, dtype=jnp.int32)[None, :]
+    ).astype(jnp.float32)
+    picker = jnp.dot(placed, source_rows, precision=lax.Precision.HIGHEST)
+    picker_low = picker.astype(jnp.bfloat16)
+    send_rows = jnp.dot(
+        picker_low, row_pack.reshape(row_blocks, -1), preferred_element_type=jnp.float32
+    )
+    send_rows = send_rows.astype(jnp.bfloat16).reshape(group_size, capacity, 2, BLOCK, features)
+    send_stats = jnp.dot(
+        picker_low, stat_blocks.reshape(row_blocks, -1), preferred_element_type=jnp.float32
+    )
+    send_stats = send_stats.astype(jnp.bfloat16).reshape(group_size, capacity, 2, HEADS, BLOCK)
+    send_ids = jnp.dot(placed, (inner + 1).astype(jnp.float32), precision=lax.Precision.HIGHEST)
+    send_ids = send_ids.astype(jnp.bfloat16).reshape(group_size, capacity)
+    stat_rows = send_stats.reshape(group_size, capacity, 2 * HEADS, BLOCK)
+    id_rows = jnp.broadcast_to(send_ids[:, :, None, None], (group_size, capacity, 8, features))
+    row_count = 2 * BLOCK
+    send_pack = jnp.concatenate(
+        [send_rows.reshape(group_size, capacity, row_count, features), stat_rows, id_rows], 2
+    )
+    pack_in = lax.all_to_all(send_pack, "gy", split_axis=0, concat_axis=0, tiled=True)
+    rows_in = pack_in[:, :, :row_count].reshape(group_size, capacity, 2, BLOCK, features)
+    stats_in = pack_in[:, :, row_count : row_count + 2 * HEADS].reshape(
+        group_size, capacity, 2, HEADS, BLOCK
+    )
+    ids_in = pack_in[:, :, row_count + 2 * HEADS, 0]
+    item_count = rows_in.shape[1]
+    total_items = group_size * item_count
+    wanted = ids_in.astype(jnp.float32).astype(jnp.int32) - 1
+    chooser = (wanted[..., None] == jnp.arange(row_blocks, dtype=jnp.int32)).astype(jnp.bfloat16)
+    keys_in = jnp.dot(
+        chooser.reshape(-1, row_blocks),
+        key_pack.reshape(row_blocks, -1),
+        preferred_element_type=jnp.float32,
+    )
+    keys_in = keys_in.astype(jnp.bfloat16).reshape(total_items, 2, BLOCK, features)
+    query_part, key_part, value_part = tile_grads(
+        rows_in.reshape(total_items, 2, BLOCK, features),
+        stats_in.reshape(total_items, 2, HEADS, BLOCK),
+        keys_in,
+    )
+    query_part = query_part.reshape(group_size, item_count, BLOCK, features)
+    key_part = key_part.reshape(group_size, item_count, BLOCK, features)
+    value_part = value_part.reshape(group_size, item_count, BLOCK, features)
+    stencil_count = partial_rows.shape[0]
+    stencil_pad = jnp.pad(column_sum, ((0, 8 - stencil_count), (0, 0)))
+    return_pack = jnp.concatenate(
+        [
+            query_part.reshape(group_size, item_count * BLOCK, features),
+            jnp.broadcast_to(stencil_pad[None], (group_size, 8, features)),
+        ],
+        1,
+    )
+    return_in = lax.all_to_all(return_pack, "gy", split_axis=0, concat_axis=0, tiled=True)
+    returned = return_in[:, : item_count * BLOCK]
+    summed = jnp.sum(return_in[:, item_count * BLOCK : item_count * BLOCK + stencil_count], 0)
+    returned, pieces, ids_in = (returned, jnp.stack([key_part, value_part], 2), ids_in)
+    query_sum = diag_query + jnp.einsum(
+        "sr,sbf->rbf",
+        picker,
+        returned.reshape(slot_count, BLOCK, features),
+        precision=lax.Precision.HIGHEST,
+    )
+    arrived = ids_in.reshape(slot_count).astype(jnp.float32).astype(jnp.int32) - 1
+    owned = (arrived[:, None] == jnp.arange(row_blocks, dtype=jnp.int32)[None, :]).astype(
+        jnp.float32
+    )
+    key_value_sum = jnp.einsum(
+        "sr,sxbf->rxbf",
+        owned,
+        pieces.reshape(slot_count, 2, BLOCK, features),
+        precision=lax.Precision.HIGHEST,
+    )
+    key_total = diag_key + key_value_sum[:, 0]
+    value_total = diag_value + key_value_sum[:, 1]
     stencil_grad = summed / math.sqrt(point_count)
     query_grad = query_sum.reshape(tile_x, tile_y, features).astype(jnp.bfloat16)
     key_grad = key_total.reshape(tile_x, tile_y, features).astype(jnp.bfloat16)

time: 174 us -> 167 us (0.960)
  starting transfers between devices: 57 us -> 43.2 us
  waiting for transfers between devices: 44.3 us -> 52 us
  other arithmetic: 8.37 us -> 11.3 us
  local copies, waits for them, and re-layouts: 37.6 us -> 34.8 us
    all_to_all x4 -> x2, starting transfers between devices: 18.2 us -> 8.54 us  [the longest x1 4.46 us: per_device(): lax.all_to_all(return_pack, 'gy', split_axis=0, concat_axis=0, tiled=True)]
    ppermute x2, waiting for transfers between devices: 0.01 us -> 6.45 us  [with_halo(): lax.ppermute(lax.slice_in_dim(block, block.shape[dim] - width, None, axis...]
    reshape x5 -> x6, local copies, waits for them, and re-layouts: 5.75 us -> 10.1 us  [points_last(): return part.reshape(item_count, features, block_rows).transpose(0, 2, 1)]
    all_to_all x4 -> x2, waiting for transfers between devices: 24.7 us -> 29 us  [the longest x1 18.6 us: per_device(): lax.all_to_all(send_pack, 'gy', split_axis=0, concat_axis=0, tiled=True)]
    all_to_all x2 -> x1, starting transfers between devices: 27.3 us -> 23 us  [gather_sum(): lax.all_to_all(spread, axis, split_axis=0, concat_axis=0, tiled=True)]
    all_to_all x4 -> x0, local copies, waits for them, and re-layouts: 3.72 us -> none  [the longest x1 1.58 us: per_device(): lax.all_to_all(query_part, 'gy', split_axis=0, concat_axis=0, tiled=True)]
    concatenate x0 -> x2, other arithmetic: none -> 3.4 us  [the longest x1 2.31 us: per_device(): jnp.concatenate([query_part.reshape(group_size, item_count * BLOCK, featu...]
    reshape x2 -> x0, local copies, waits for them, and re-layouts: 2.89 us -> none  [the longest x1 2.26 us: per_device(): query_part = query_part.reshape(group_size, item_count, BLOCK, features)]
  transfers between devices with their start and end apart: 10 -> 7, of which waited for: 6 -> 5; matrix products, arithmetic and copies ran while one was open for 35% -> 22% of each run, Pallas kernels for 0% -> 0%
where the time goes in v4:
time: 167 us; the launch traced here: 165 us
  waiting for transfers between devices  52 us (31%)
  starting transfers between devices  43.2 us (26%)
  local copies, waits for them, and re-layouts  34.8 us (21%)
  matrix products  22.7 us (14%)
  other arithmetic  11.3 us (7%)
    all_to_all x1, starting transfers between devices, gather_sum(): lax.all_to_all(spread, axis, split_axis=0, concat_axis=0, tiled=True)  23 us
    all_to_all x1, waiting for transfers between devices, per_device(): lax.all_to_all(send_pack, 'gy', split_axis=0, concat_axis=0, tiled=True)  18.6 us
    all_to_all x1, waiting for transfers between devices, gather_sum(): lax.all_to_all(spread, axis, split_axis=0, concat_axis=0, tiled=True)  16.5 us
    all_to_all x1, waiting for transfers between devices, per_device(): lax.all_to_all(return_pack, 'gy', split_axis=0, concat_axis=0, tiled=True)  10.4 us
    reshape x6, local copies, waits for them, and re-layouts, points_last(): return part.reshape(item_count, features, block_rows).transpose(0, 2, 1)  10.1 us
    another operation x2, local copies, waits for them, and re-layouts, tile_grads(): key_pack.reshape(item_count, 2, block_rows, HEADS, head_width)  9.98 us
    ppermute x2, starting transfers between devices, with_halo(): lax.ppermute(lax.slice_in_dim(block, 0, width, axis=dim), axis, backward)  7.54 us
    ppermute x2, waiting for transfers between devices, with_halo(): lax.ppermute(lax.slice_in_dim(block, block.shape[dim] - width, None, axis...  6.45 us
  transfers between devices with their start and end apart: 7, of which 5 were waited for; matrix products, arithmetic and copies ran while one was open for 22% of the time, Pallas kernels for 0%

profile of v4, /device:TPU:6, one launch (start us, length us, event | category | flops | bytes accessed | tf_op | source)
XLA Modules:
  0.0 165.1 jit_solution(12701454412253849002)
XLA Ops:
  0.7 0.8 fusion.69
  1.4 2.2 %collective-permute-start = (bf16[1,32,128]{2,1,0:T(8,128)(2,1)S(1)}, bf16[1,32,128]{2,1,0:T(8,128)(2,1)S(1)}, u32[]{:S(2)}, u32[]{:S(2)}) collective-permute-start(bf16[1,32,128]{2,1,0:T(8,128)(2,1)S(1)} %get-tuple-element.17), channel_id=1, source_target_pairs={{8,0},{16,8},{24,16},{32,24},{40,32},{48,40},{56,48},{64,56},{72,6... | collective-permute-start | bytes 24584 | tf_op jit(solution)/shard_map/ppermute | solution.py:21
  3.6 2.2 %collective-permute-start.1 = (bf16[1,32,128]{2,1,0:T(8,128)(2,1)S(1)}, bf16[1,32,128]{2,1,0:T(8,128)(2,1)S(1)}, u32[]{:S(2)}, u32[]{:S(2)}) collective-permute-start(bf16[1,32,128]{2,1,0:T(8,128)(2,1)S(1)} %get-tuple-element.18), channel_id=1, source_target_pairs={{0,8},{8,16},{16,24},{24,32},{32,40},{40,48},{48,56},{56,64},{64,7... | collective-permute-start | bytes 24584 | tf_op jit(solution)/shard_map/ppermute | solution.py:18
  5.8 0.8 copy.122
  6.8 1.7 %collective-permute-done.1 = bf16[1,32,128]{2,1,0:T(8,128)(2,1)S(1)} collective-permute-done((bf16[1,32,128]{2,1,0:T(8,128)(2,1)S(1)}, bf16[1,32,128]{2,1,0:T(8,128)(2,1)S(1)}, u32[]{:S(2)}, u32[]{:S(2)}) %collective-permute-start.1) | collective-permute-done | bytes 8224 | tf_op jit(solution)/shard_map/ppermute | solution.py:18
  8.6 0.9 constant_dynamic-update-slice_fusion.1
  9.5 5.4 %collective-permute-start.2 = (bf16[18,1,128]{2,1,0:T(2,128)(2,1)S(1)}, bf16[18,1,128]{2,1,0:T(2,128)(2,1)S(1)}, u32[]{:S(2)}, u32[]{:S(2)}) collective-permute-start(bf16[18,1,128]{2,1,0:T(2,128)(2,1)S(1)} %get-tuple-element.14), channel_id=1, source_target_pairs={{1,0},{2,1},{3,2},{4,3},{5,4},{6,5},{7,6},{0,7},{9,8},{10,9},{11,1... | collective-permute-start | bytes 13832 | tf_op jit(solution)/shard_map/ppermute | solution.py:21
  14.9 1.9 %collective-permute-start.3 = (bf16[18,1,128]{2,1,0:T(2,128)(2,1)S(1)}, bf16[18,1,128]{2,1,0:T(2,128)(2,1)S(1)}, u32[]{:S(2)}, u32[]{:S(2)}) collective-permute-start(bf16[18,1,128]{2,1,0:T(2,128)(2,1)S(1)} %get-tuple-element.15), channel_id=1, source_target_pairs={{0,1},{1,2},{2,3},{3,4},{4,5},{5,6},{6,7},{7,0},{8,9},{9,10},{10,1... | collective-permute-start | bytes 13832 | tf_op jit(solution)/shard_map/ppermute | solution.py:18
  17.0 4.7 %collective-permute-done.3 = bf16[18,1,128]{2,1,0:T(2,128)(2,1)S(1)} collective-permute-done((bf16[18,1,128]{2,1,0:T(2,128)(2,1)S(1)}, bf16[18,1,128]{2,1,0:T(2,128)(2,1)S(1)}, u32[]{:S(2)}, u32[]{:S(2)}) %collective-permute-start.3) | collective-permute-done | bytes 4640 | tf_op jit(solution)/shard_map/ppermute | solution.py:18
  21.7 1.4 fusion.31
  23.1 0.8 broadcast_in_dim.10
  23.9 23.0 %all-to-all-start.1 = ((f32[96,5,128]{2,1,0:T(8,128)}), f32[96,5,128]{2,1,0:T(8,128)S(1)}, u32[]{:S(2)}, u32[]{:S(2)}) async-start(f32[96,5,128]{2,1,0:T(8,128)} %broadcast_in_dim.10), calls=%async_computation.1 | async-start | bytes 786432 | tf_op jit(solution)/shard_map/all_to_all | solution.py:69
  48.6 0.7 reduce_sum.81
  49.8 1.1 pad_maximum_fusion
  50.9 16.5 %all-to-all-done.1 = f32[96,5,128]{2,1,0:T(8,128)S(1)} async-done(((f32[96,5,128]{2,1,0:T(8,128)}), f32[96,5,128]{2,1,0:T(8,128)S(1)}, u32[]{:S(2)}, u32[]{:S(2)}) %all-to-all-start.1) | async-done | bytes 245792 | tf_op jit(solution)/shard_map/all_to_all | solution.py:69
  67.4 4.1 %all-to-all-start = ((bf16[8,2,272,128]{3,2,1,0:T(8,128)(2,1)}), bf16[8,2,272,128]{3,2,1,0:T(8,128)(2,1)S(1)}, u32[]{:S(2)}, u32[]{:S(2)}) async-start(bf16[8,2,272,128]{3,2,1,0:T(8,128)(2,1)} %pad_maximum_fusion), calls=%async_computation | async-start | bytes 2228224 | tf_op jit(solution)/shard_map/all_to_all | solution.py:189
  72.2 0.9 copy.116
  73.1 1.1 reshape.216
  74.3 0.9 copy.112
  75.2 0.9 copy.113
  76.3 1.1 maximum_bitcast_fusion
  78.0 1.0 fusion.18
  78.9 1.8 %copy.138 = f32[4,128,128]{1,0,2:T(4,128)} copy(f32[4,128,128]{2,1,0:T(8,128)} %bitcast.184) | data formatting | bytes 524288 | tf_op jit(solution)/shard_map/reshape | solution.py:115
  80.7 1.6 pad_maximum_fusion.3
  82.9 1.3 fusion.13
  84.3 18.6 %all-to-all-done = bf16[8,2,272,128]{3,2,1,0:T(8,128)(2,1)S(1)} async-done(((bf16[8,2,272,128]{3,2,1,0:T(8,128)(2,1)}), bf16[8,2,272,128]{3,2,1,0:T(8,128)(2,1)S(1)}, u32[]{:S(2)}, u32[]{:S(2)}) %all-to-all-start) | async-done | bytes 1114144 | tf_op jit(solution)/shard_map/all_to_all | solution.py:189
  105.8 4.6 %reshape_reshape.17 = bf16[16,2,128,4,32]{4,3,2,1,0:T(4,128)(2,1)} reshape(bf16[16,32768]{1,0:T(8,128)(2,1)S(1)} %convolution_convert_fusion) | data formatting | bytes 2097152 | tf_op jit(solution)/shard_map/reshape;reshape | solution.py:82
  110.4 5.4 %copy.127 = bf16[16,2,128,4,32]{2,4,3,0,1:T(8,128)(2,1)S(1)} copy(bf16[16,2,128,4,32]{4,3,2,1,0:T(4,128)(2,1)} %reshape_reshape.17) | data formatting | bytes 2097152 | tf_op jit(solution)/shard_map/reshape;reshape | solution.py:82
  115.8 0.8 fusion.20
  116.8 4.2 %multiply_convert_fusion = bf16[16,4,128,128]{3,2,1,0:T(8,128)(2,1)S(1)} fusion(f32[16,4,128,128]{3,2,1,0:T(8,128)S(1)} %fusion.20, f32[16,4,128]{2,1,0:T(4,128)S(1)} %get-tuple-element.20, f32[16,4,128]{2,1,0:T(4,128)S(1)} %get-tuple-element.19, bf16[16,2,4,32,128]{4,3,2,0,1:T(8,128)(2,1)} %bitcast.167, bf16[16,2,4,32,128]{4,3,2,0,1:T(8,128)(2,1)S(1)} %bitcast.163), kind=kOutput, calls=%fused_computation.2 | convolution fusion | flops 72351744 | bytes 7405568 | tf_op jit(solution)/shard_map/shdq,shdk->shqk/dot_general | solution.py:96
  121.0 2.2 %convolution_multiply_fusion.2 = f32[16,4,32,128]{3,2,1,0:T(8,128)} fusion(bf16[16,4,128,128]{3,2,1,0:T(8,128)(2,1)S(1)} %multiply_convert_fusion, bf16[16,2,4,32,128]{4,3,2,0,1:T(8,128)(2,1)S(1)} %bitcast.168), kind=kOutput, calls=%fused_computation.19 | convolution fusion | flops 67371008 | bytes 3670016 | tf_op jit(solution)/shard_map/shqk,shdk->shdq/dot_general | solution.py:110
  123.2 2.5 %copy.130 = f32[16,128,128]{1,2,0:T(8,128)} copy(f32[16,128,128]{2,1,0:T(8,128)} %bitcast.169) | data formatting | bytes 2097152 | tf_op jit(solution)/shard_map/reshape | solution.py:115
  125.8 2.3 %pad_maximum_fusion.1 = f32[8,264,128]{2,1,0:T(8,128)} fusion(f32[8,8,128]{2,1,0:T(8,128)S(1)} %broadcast_in_dim.11, f32[8,256,128]{2,1,0:T(8,128)} %bitcast.173), kind=kLoop, calls=%fused_computation.30 | loop fusion | flops 270336 | bytes 2162688 | tf_op jit(solution)/shard_map/concatenate | solution.py:215
  128.1 4.5 %all-to-all-start.2 = ((f32[8,264,128]{2,1,0:T(8,128)}), f32[8,264,128]{2,1,0:T(8,128)}, u32[]{:S(2)}, u32[]{:S(2)}) async-start(f32[8,264,128]{2,1,0:T(8,128)} %pad_maximum_fusion.1), calls=%async_computation.2 | async-start | bytes 2162688 | tf_op jit(solution)/shard_map/all_to_all | solution.py:222
  132.6 2.2 %convolution_multiply_fusion.4 = f32[4,4,32,128]{3,2,1,0:T(8,128)} fusion(bf16[4,4,128,128]{3,2,1,0:T(8,128)(2,1)} %fusion.13, bf16[4,2,4,32,128]{4,3,2,0,1:T(8,128)(2,1)} %copy-done.5), kind=kOutput, calls=%fused_computation.22 | convolution fusion | flops 16842752 | bytes 917504 | tf_op jit(solution)/shard_map/shqk,shdk->shdq/dot_general | solution.py:110
  134.8 1.8 %copy.121 = f32[4,128,128]{1,0,2:T(4,128)} copy(f32[4,128,128]{2,1,0:T(8,128)} %bitcast.182) | data formatting | bytes 524288 | tf_op jit(solution)/shard_map/reshape | solution.py:115
  136.6 2.1 %convolution_multiply_fusion.3 = f32[4,4,32,128]{3,2,1,0:T(8,128)} fusion(bf16[4,4,128,128]{3,2,1,0:T(8,128)(2,1)} %fusion.13, bf16[4,2,4,32,128]{4,3,2,0,1:T(8,128)(2,1)} %copy-done.4), kind=kOutput, calls=%fused_computation.21 | convolution fusion | flops 16842752 | bytes 917504 | tf_op jit(solution)/shard_map/shqk,shdq->shdk/dot_general | solution.py:106
  138.6 1.8 %copy.134 = f32[4,128,128]{1,0,2:T(4,128)} copy(f32[4,128,128]{2,1,0:T(8,128)} %bitcast.181) | data formatting | bytes 524288 | tf_op jit(solution)/shard_map/reshape | solution.py:115
  140.4 1.7 %convolution_multiply_fusion.1 = f32[16,4,32,128]{3,2,1,0:T(8,128)} fusion(bf16[16,4,128,128]{3,2,1,0:T(8,128)(2,1)S(1)} %multiply_convert_fusion, bf16[16,2,4,32,128]{4,3,2,0,1:T(8,128)(2,1)S(1)} %bitcast.164), kind=kOutput, calls=%fused_computation.18 | convolution fusion | flops 67371008 | bytes 3670016 | tf_op jit(solution)/shard_map/shqk,shdq->shdk/dot_general | solution.py:106
  142.1 1.7 %copy.135 = f32[16,128,128]{1,0,2:T(8,128)S(1)} copy(f32[16,128,128]{2,1,0:T(8,128)} %bitcast.170) | data formatting | bytes 2097152 | tf_op jit(solution)/shard_map/reshape | solution.py:115
  143.8 3.1 %fusion.1 = f32[16,4,32,128]{3,2,1,0:T(8,128)S(1)} fusion(f32[16,4,128,128]{3,2,1,0:T(8,128)} %copy-done, f32[16,4,128]{2,1,0:T(4,128)S(1)} %get-tuple-element.19, bf16[16,2,4,32,128]{4,3,2,0,1:T(8,128)(2,1)S(1)} %bitcast.165), kind=kOutput, calls=%fused_computation.5 | convolution fusion | flops 70254592 | bytes 5799936 | tf_op jit(solution)/shard_map/shqk,shdq->shdk/dot_general | solution.py:102
  147.4 0.8 fusion.3
  148.6 0.7 copy.137
  149.3 0.8 fusion.26
  150.1 10.4 %all-to-all-done.2 = f32[8,264,128]{2,1,0:T(8,128)} async-done(((f32[8,264,128]{2,1,0:T(8,128)}), f32[8,264,128]{2,1,0:T(8,128)}, u32[]{:S(2)}, u32[]{:S(2)}) %all-to-all-start.2) | async-done | bytes 1081376 | tf_op jit(solution)/shard_map/all_to_all | solution.py:222
  160.6 1.3 slice.139
  161.9 1.2 fusion.14
  163.7 0.8 slice_reduce_fusion
  (86 shorter events, 9.8 us)
Async XLA Ops:
  0.6 46.3 %copy-start.3 = (bf16[16,32,128]{2,1,0:T(8,128)(2,1)S(1)}, bf16[16,32,128]{2,1,0:T(8,128)(2,1)}, u32[]{:S(2)}) copy-start(bf16[16,32,128]{2,1,0:T(8,128)(2,1)} %param.12) | copy-start | bytes 393220
  0.6 46.3 %copy-start.11 = (bf16[16,32,128]{2,1,0:T(8,128)(2,1)S(1)}, bf16[16,32,128]{2,1,0:T(8,128)(2,1)}, u32[]{:S(2)}) copy-start(bf16[16,32,128]{2,1,0:T(8,128)(2,1)} %param.8) | copy-start | bytes 393220
  0.7 46.4 %copy-start.13 = (bf16[4,16,32]{2,1,0:T(8,128)(2,1)S(1)}, bf16[4,16,32]{2,1,0:T(8,128)(2,1)}, u32[]{:S(2)}) copy-start(bf16[4,16,32]{2,1,0:T(8,128)(2,1)} %param.13) | copy-start | bytes 12292
  1.4 8.1 %collective-permute-start = (bf16[1,32,128]{2,1,0:T(8,128)(2,1)S(1)}, bf16[1,32,128]{2,1,0:T(8,128)(2,1)S(1)}, u32[]{:S(2)}, u32[]{:S(2)}) collective-permute-start(bf16[1,32,128]{2,1,0:T(8,128)(2,1)S(1)} %get-tuple-element.17), channel_id=1, source_target_pairs={{8,0},{16,8},{24,16},{32,24},{40,32},{48,40},{56,48},{64,56},{72,6... | collective-permute-start | bytes 24584 | tf_op jit(solution)/shard_map/ppermute | solution.py:21
  3.6 5.0 %collective-permute-start.1 = (bf16[1,32,128]{2,1,0:T(8,128)(2,1)S(1)}, bf16[1,32,128]{2,1,0:T(8,128)(2,1)S(1)}, u32[]{:S(2)}, u32[]{:S(2)}) collective-permute-start(bf16[1,32,128]{2,1,0:T(8,128)(2,1)S(1)} %get-tuple-element.18), channel_id=1, source_target_pairs={{0,8},{8,16},{16,24},{24,32},{32,40},{40,48},{48,56},{56,64},{64,7... | collective-permute-start | bytes 24584 | tf_op jit(solution)/shard_map/ppermute | solution.py:18
  9.5 7.4 %collective-permute-start.2 = (bf16[18,1,128]{2,1,0:T(2,128)(2,1)S(1)}, bf16[18,1,128]{2,1,0:T(2,128)(2,1)S(1)}, u32[]{:S(2)}, u32[]{:S(2)}) collective-permute-start(bf16[18,1,128]{2,1,0:T(2,128)(2,1)S(1)} %get-tuple-element.14), channel_id=1, source_target_pairs={{1,0},{2,1},{3,2},{4,3},{5,4},{6,5},{7,6},{0,7},{9,8},{10,9},{11,1... | collective-permute-start | bytes 13832 | tf_op jit(solution)/shard_map/ppermute | solution.py:21
  14.9 6.8 %collective-permute-start.3 = (bf16[18,1,128]{2,1,0:T(2,128)(2,1)S(1)}, bf16[18,1,128]{2,1,0:T(2,128)(2,1)S(1)}, u32[]{:S(2)}, u32[]{:S(2)}) collective-permute-start(bf16[18,1,128]{2,1,0:T(2,128)(2,1)S(1)} %get-tuple-element.15), channel_id=1, source_target_pairs={{0,1},{1,2},{2,3},{3,4},{4,5},{5,6},{6,7},{7,0},{8,9},{9,10},{10,1... | collective-permute-start | bytes 13832 | tf_op jit(solution)/shard_map/ppermute | solution.py:18
  23.9 43.5 %all-to-all-start.1 = ((f32[96,5,128]{2,1,0:T(8,128)}), f32[96,5,128]{2,1,0:T(8,128)S(1)}, u32[]{:S(2)}, u32[]{:S(2)}) async-start(f32[96,5,128]{2,1,0:T(8,128)} %broadcast_in_dim.10), calls=%async_computation.1 | async-start | bytes 786432 | tf_op jit(solution)/shard_map/all_to_all | solution.py:69
  49.7 21.7 %copy-start.12 = (bf16[16,32,128]{2,1,0:T(8,128)(2,1)S(1)}, bf16[16,32,128]{2,1,0:T(8,128)(2,1)}, u32[]{:S(2)}) copy-start(bf16[16,32,128]{2,1,0:T(8,128)(2,1)} %param.8) | copy-start | bytes 393220
  49.7 22.0 %copy-start.6 = (bf16[16,32,128]{2,1,0:T(8,128)(2,1)S(1)}, bf16[16,32,128]{2,1,0:T(8,128)(2,1)}, u32[]{:S(2)}) copy-start(bf16[16,32,128]{2,1,0:T(8,128)(2,1)} %param.10) | copy-start | bytes 393220
  67.4 35.5 %all-to-all-start = ((bf16[8,2,272,128]{3,2,1,0:T(8,128)(2,1)}), bf16[8,2,272,128]{3,2,1,0:T(8,128)(2,1)S(1)}, u32[]{:S(2)}, u32[]{:S(2)}) async-start(bf16[8,2,272,128]{3,2,1,0:T(8,128)(2,1)} %pad_maximum_fusion), calls=%async_computation | async-start | bytes 2228224 | tf_op jit(solution)/shard_map/all_to_all | solution.py:189
  77.4 6.8 %copy-start.4 = (bf16[4,2,4,32,128]{4,3,2,0,1:T(8,128)(2,1)}, bf16[4,2,4,32,128]{4,3,2,0,1:T(8,128)(2,1)S(1)}, u32[]{:S(2)}) copy-start(bf16[4,2,4,32,128]{4,3,2,0,1:T(8,128)(2,1)S(1)} %get-tuple-element.29) | copy-start | bytes 786436
  77.4 6.8 %copy-start.5 = (bf16[4,2,4,32,128]{4,3,2,0,1:T(8,128)(2,1)}, bf16[4,2,4,32,128]{4,3,2,0,1:T(8,128)(2,1)S(1)}, u32[]{:S(2)}) copy-start(bf16[4,2,4,32,128]{4,3,2,0,1:T(8,128)(2,1)S(1)} %get-tuple-element.28) | copy-start | bytes 786436
  77.4 4.9 %copy-start.17 = (f32[5,128]{1,0:T(8,128)S(1)}, f32[5,128]{1,0:T(8,128)}, u32[]{:S(2)}) copy-start(f32[5,128]{1,0:T(8,128)} %param.15) | copy-start | bytes 7684
  104.3 1.0 copy-start.7
  115.8 1.0 copy-start.1
  116.7 4.3 %copy-start = (f32[16,4,128,128]{3,2,1,0:T(8,128)}, f32[16,4,128,128]{3,2,1,0:T(8,128)S(1)}, u32[]{:S(2)}) copy-start(f32[16,4,128,128]{3,2,1,0:T(8,128)S(1)} %fusion.20) | copy-start | bytes 12582916
  116.8 4.3 %copy-start.2 = (bf16[16,2,128,4,32]{2,4,3,0,1:T(8,128)(2,1)S(1)}, bf16[16,2,128,4,32]{2,4,3,0,1:T(8,128)(2,1)}, u32[]{:S(2)}) copy-start(bf16[16,2,128,4,32]{2,4,3,0,1:T(8,128)(2,1)} %copy-done.1) | copy-start | bytes 3145732
  128.1 32.5 %all-to-all-start.2 = ((f32[8,264,128]{2,1,0:T(8,128)}), f32[8,264,128]{2,1,0:T(8,128)}, u32[]{:S(2)}, u32[]{:S(2)}) async-start(f32[8,264,128]{2,1,0:T(8,128)} %pad_maximum_fusion.1), calls=%async_computation.2 | async-start | bytes 2162688 | tf_op jit(solution)/shard_map/all_to_all | solution.py:222
  147.4 1.0 copy-start.8
  147.4 1.0 copy-start.10
  147.4 1.9 %copy-start.14 = (f32[128]{0:T(128)S(1)}, f32[128]{0:T(128)}, u32[]{:S(2)}) copy-start(f32[128]{0:T(128)} %get-tuple-element.23) | copy-start | bytes 1540
  147.4 1.9 %copy-start.15 = (f32[128]{0:T(128)S(1)}, f32[128]{0:T(128)}, u32[]{:S(2)}) copy-start(f32[128]{0:T(128)} %get-tuple-element.24) | copy-start | bytes 1540
  147.4 1.8 %copy-start.16 = (f32[128]{0:T(128)S(1)}, f32[128]{0:T(128)}, u32[]{:S(2)}) copy-start(f32[128]{0:T(128)} %get-tuple-element.25) | copy-start | bytes 1540
  148.6 13.3 %copy-start.9 = (f32[4,128,128]{1,0,2:T(4,128)S(1)}, f32[4,128,128]{1,0,2:T(4,128)}, u32[]{:S(2)}) copy-start(f32[4,128,128]{1,0,2:T(4,128)} %copy.121) | copy-start | bytes 786436

commit v5 on v4

--- a/solution.py
+++ b/solution.py
@@ -137,23 +137,6 @@
     stat_blocks = jnp.stack([norm_blocks, delta], 1)
     row_pack = jnp.stack([query_blocks, grad_blocks], 1)
     key_pack = jnp.stack([key_blocks, value_blocks], 1)
-    diag_query, diag_key, diag_value = tile_grads(row_pack, stat_blocks, key_pack)
-    rim = with_halo(out_grad, (("gx", 0), ("gy", 1)), 1)
-    moved = [
-        out_grad.astype(jnp.float32),
-        rim[2:, 1:-1].astype(jnp.float32),
-        rim[:-2, 1:-1].astype(jnp.float32),
-        rim[1:-1, 2:].astype(jnp.float32),
-        rim[1:-1, :-2].astype(jnp.float32),
-    ]
-    value_float = values.astype(jnp.float32)
-    stencil_term = stencil[0] * moved[0]
-    for index in range(1, 5):
-        stencil_term = stencil_term + stencil[index] * moved[index]
-    partial_rows = jnp.stack(
-        [jnp.sum(moved[index] * value_float, axis=(0, 1)) for index in range(5)]
-    )
-    column_sum = gather_sum(partial_rows, "gx")
     point_count = tile_x * tile_y * lax.axis_size("gx") * group_size
     columns = neighbour_blocks.reshape(pair_count)
     owners = columns // row_blocks
@@ -186,7 +169,53 @@
     send_pack = jnp.concatenate(
         [send_rows.reshape(group_size, capacity, row_count, features), stat_rows, id_rows], 2
     )
+    slot_rows = send_pack.shape[2]
+    edges = jnp.concatenate([out_grad[:, 0], out_grad[:, tile_y - 1]], 0)
+    send_pack = jnp.concatenate(
+        [
+            send_pack.reshape(group_size, capacity * slot_rows, features),
+            jnp.broadcast_to(edges[None], (group_size,) + edges.shape),
+        ],
+        1,
+    )
+    send_pack, diag_rows, diag_stats, diag_keys = lax.optimization_barrier(
+        (send_pack, row_pack, stat_blocks, key_pack)
+    )
     pack_in = lax.all_to_all(send_pack, "gy", split_axis=0, concat_axis=0, tiled=True)
+    diag_query, diag_key, diag_value = tile_grads(diag_rows, diag_stats, diag_keys)
+    pack_in, diag_query, diag_key, diag_value = lax.optimization_barrier(
+        (pack_in, diag_query, diag_key, diag_value)
+    )
+    column = lax.axis_index("gy")
+    edge_in = pack_in[:, capacity * slot_rows :]
+    before_col = lax.dynamic_index_in_dim(edge_in, (column + group_size - 1) % group_size, 0, False)
+    after_col = lax.dynamic_index_in_dim(edge_in, (column + 1) % group_size, 0, False)
+    before_col = before_col[tile_x:]
+    after_col = after_col[:tile_x]
+    grad_x, values_x = lax.optimization_barrier((out_grad, values))
+    count_x = lax.axis_size("gx")
+    ahead = [(i, (i + 1) % count_x) for i in range(count_x)]
+    behind = [((i + 1) % count_x, i) for i in range(count_x)]
+    from_before = lax.ppermute(grad_x[tile_x - 1 :], "gx", ahead)
+    from_after = lax.ppermute(grad_x[:1], "gx", behind)
+    moved = [
+        grad_x.astype(jnp.float32),
+        jnp.concatenate([grad_x[1:], from_after], 0).astype(jnp.float32),
+        jnp.concatenate([from_before, grad_x[:-1]], 0).astype(jnp.float32),
+        jnp.concatenate([grad_x[:, 1:], after_col[:, None]], 1).astype(jnp.float32),
+        jnp.concatenate([before_col[:, None], grad_x[:, :-1]], 1).astype(jnp.float32),
+    ]
+    value_float = values_x.astype(jnp.float32)
+    stencil_term = stencil[0] * moved[0]
+    for index in range(1, 5):
+        stencil_term = stencil_term + stencil[index] * moved[index]
+    partial_rows = jnp.stack(
+        [jnp.sum(moved[index] * value_float, axis=(0, 1)) for index in range(5)]
+    )
+    point_count = tile_x * tile_y * count_x * group_size
+    pack_in = pack_in[:, : capacity * slot_rows].reshape(group_size, capacity, slot_rows, features)
+    partial_rows, pack_in = lax.optimization_barrier((partial_rows, pack_in))
+    column_sum = gather_sum(partial_rows, "gx")
     rows_in = pack_in[:, :, :row_count].reshape(group_size, capacity, 2, BLOCK, features)
     stats_in = pack_in[:, :, row_count : row_count + 2 * HEADS].reshape(
         group_size, capacity, 2, HEADS, BLOCK

time: 167 us -> 138 us (0.83)
  waiting for transfers between devices: 52 us -> 33 us
  starting transfers between devices: 43.2 us -> 36.3 us
  local copies, waits for them, and re-layouts: 34.8 us -> 32.2 us
    all_to_all x1, waiting for transfers between devices: 16.5 us -> 0.01 us  [gather_sum(): lax.all_to_all(spread, axis, split_axis=0, concat_axis=0, tiled=True)]
    all_to_all x1, waiting for transfers between devices: 10.4 us -> 18.3 us  [per_device(): lax.all_to_all(return_pack, 'gy', split_axis=0, concat_axis=0, tiled=True)]
    ppermute x4 -> x2, waiting for transfers between devices: 6.46 us -> 0.01 us  [the longest x1 0.01 us: per_device(): from_after = lax.ppermute(grad_x[:1], 'gx', behind)]
    ppermute x4 -> x2, starting transfers between devices: 11.6 us -> 5.55 us  [the longest x1 3.64 us: per_device(): from_after = lax.ppermute(grad_x[:1], 'gx', behind)]
    another operation x8 -> x0, local copies, waits for them, and re-layouts: 4.76 us -> none  [the longest x4 3.16 us: per_device(): key_pack = jnp.stack([key_blocks, value_blocks], 1)]
    all_to_all x1, waiting for transfers between devices: 18.6 us -> 14.7 us  [per_device(): lax.all_to_all(send_pack, 'gy', split_axis=0, concat_axis=0, tiled=True)]
    all_to_all x1, starting transfers between devices: 23 us -> 19.3 us  [gather_sum(): lax.all_to_all(spread, axis, split_axis=0, concat_axis=0, tiled=True)]
    all_to_all x1, starting transfers between devices: 4.08 us -> 7.1 us  [per_device(): lax.all_to_all(send_pack, 'gy', split_axis=0, concat_axis=0, tiled=True)]
  transfers between devices with their start and end apart: 7 -> 5, of which waited for: 5 -> 2; matrix products, arithmetic and copies ran while one was open for 22% -> 32% of each run, Pallas kernels for 0% -> 0%
where the time goes in v5:
time: 138 us; the launch traced here: 137 us
  starting transfers between devices  36.3 us (26%)
  waiting for transfers between devices  33 us (24%)
  local copies, waits for them, and re-layouts  32.2 us (23%)
  matrix products  22.1 us (16%)
  other arithmetic  11.6 us (8%)
  between operations  1.41 us (1%)
    all_to_all x1, starting transfers between devices, gather_sum(): lax.all_to_all(spread, axis, split_axis=0, concat_axis=0, tiled=True)  19.3 us
    all_to_all x1, waiting for transfers between devices, per_device(): lax.all_to_all(return_pack, 'gy', split_axis=0, concat_axis=0, tiled=True)  18.3 us
    all_to_all x1, waiting for transfers between devices, per_device(): lax.all_to_all(send_pack, 'gy', split_axis=0, concat_axis=0, tiled=True)  14.7 us
    another operation x2, local copies, waits for them, and re-layouts, tile_grads(): key_pack.reshape(item_count, 2, block_rows, HEADS, head_width)  9.97 us
    reshape x6, local copies, waits for them, and re-layouts, points_last(): return part.reshape(item_count, features, block_rows).transpose(0, 2, 1)  9.24 us
    all_to_all x1, starting transfers between devices, per_device(): lax.all_to_all(send_pack, 'gy', split_axis=0, concat_axis=0, tiled=True)  7.1 us
    dot_general x2, matrix products, tile_grads(): jnp.einsum('shdq,shdk->shqk', grad_heads, value_heads, preferred_element_...  5.66 us
    all_to_all x1, starting transfers between devices, per_device(): lax.all_to_all(return_pack, 'gy', split_axis=0, concat_axis=0, tiled=True)  4.26 us
  transfers between devices with their start and end apart: 5, of which 2 were waited for; matrix products, arithmetic and copies ran while one was open for 32% of the time, Pallas kernels for 0%

profile of v5, /device:TPU:6, one launch (start us, length us, event | category | flops | bytes accessed | tf_op | source)
XLA Modules:
  0.0 136.6 jit_solution(47854845054640252)
XLA Ops:
  0.7 0.8 copy.107
  2.3 0.8 reshape.217
  3.1 0.8 fusion.67
  3.9 1.0 convert_multiply_fusion.10
  5.3 0.7 reduce_sum.82
  7.4 1.1 pad_maximum_fusion
  8.5 7.1 %all-to-all-start = ((bf16[8,576,128]{2,1,0:T(8,128)(2,1)}), bf16[8,576,128]{2,1,0:T(8,128)(2,1)S(1)}, u32[]{:S(2)}, u32[]{:S(2)}) async-start(bf16[8,576,128]{2,1,0:T(8,128)(2,1)} %pad_maximum_fusion), calls=%async_computation | async-start | bytes 2359296 | tf_op jit(solution)/shard_map/all_to_all | solution.py:184
  15.7 0.6 fusion.65
  16.3 1.9 %collective-permute-start.1 = (bf16[1,32,128]{2,1,0:T(8,128)(2,1)}, bf16[1,32,128]{2,1,0:T(8,128)(2,1)}, u32[]{:S(2)}, u32[]{:S(2)}) collective-permute-start(bf16[1,32,128]{2,1,0:T(8,128)(2,1)} %get-tuple-element.37), channel_id=1, source_target_pairs={{0,8},{8,16},{16,24},{24,32},{32,40},{40,48},{48,56},{56,64},{64,7... | collective-permute-start | bytes 24584 | tf_op jit(solution)/shard_map/ppermute | solution.py:199
  18.2 3.6 %collective-permute-start = (bf16[1,32,128]{2,1,0:T(8,128)(2,1)}, bf16[1,32,128]{2,1,0:T(8,128)(2,1)}, u32[]{:S(2)}, u32[]{:S(2)}) collective-permute-start(bf16[1,32,128]{2,1,0:T(8,128)(2,1)} %get-tuple-element.38), channel_id=1, source_target_pairs={{8,0},{16,8},{24,16},{32,24},{40,32},{48,40},{56,48},{64,56},{72,6... | collective-permute-start | bytes 24584 | tf_op jit(solution)/shard_map/ppermute | solution.py:200
  22.3 0.5 copy-done.4
  23.3 1.4 %fusion.13 = bf16[4,4,128,128]{3,2,1,0:T(8,128)(2,1)S(1)} fusion(f32[4,4,128,128]{3,2,1,0:T(8,128)S(1)} %fusion.11, f32[4,4,128]{2,1,0:T(4,128)S(1)} %copy.118, bf16[4,2,4,32,128]{4,3,2,0,1:T(8,128)(2,1)} %bitcast.202, bf16[4,2,4,32,128]{4,3,2,0,1:T(8,128)(2,1)S(1)} %bitcast.196), kind=kOutput, calls=%fused_computation.20 | convolution fusion | flops 17563648 | bytes 1843200 | tf_op jit(solution)/shard_map/shdq,shdk->shqk/dot_general | solution.py:96
  24.7 2.0 %convolution_multiply_fusion.4 = f32[4,4,32,128]{3,2,1,0:T(8,128)} fusion(bf16[4,4,128,128]{3,2,1,0:T(8,128)(2,1)S(1)} %fusion.13, bf16[4,2,4,32,128]{4,3,2,0,1:T(8,128)(2,1)} %bitcast.203), kind=kOutput, calls=%fused_computation.23 | convolution fusion | flops 16842752 | bytes 917504 | tf_op jit(solution)/shard_map/shqk,shdk->shdq/dot_general | solution.py:110
  26.8 1.8 %copy.119 = f32[4,128,128]{1,0,2:T(4,128)} copy(f32[4,128,128]{2,1,0:T(8,128)} %bitcast.204) | data formatting | bytes 524288 | tf_op jit(solution)/shard_map/reshape | solution.py:115
  28.5 1.0 convolution_multiply_fusion.3
  29.5 1.8 %copy.120 = f32[4,128,128]{1,0,2:T(4,128)} copy(f32[4,128,128]{2,1,0:T(8,128)} %bitcast.205) | data formatting | bytes 524288 | tf_op jit(solution)/shard_map/reshape | solution.py:115
  31.5 0.9 copy.121
  32.6 14.7 %all-to-all-done = bf16[8,576,128]{2,1,0:T(8,128)(2,1)S(1)} async-done(((bf16[8,576,128]{2,1,0:T(8,128)(2,1)}), bf16[8,576,128]{2,1,0:T(8,128)(2,1)S(1)}, u32[]{:S(2)}, u32[]{:S(2)}) %all-to-all-start) | async-done | bytes 1179680 | tf_op jit(solution)/shard_map/all_to_all | solution.py:184
  47.4 0.9 fusion.31
  48.3 0.6 stack.50
  49.3 0.6 slice.132
  50.0 0.7 sub.56
  52.3 0.6 fusion.40
  52.9 0.8 broadcast_in_dim.19
  53.7 19.3 %all-to-all-start.1 = ((f32[96,5,128]{2,1,0:T(8,128)}), f32[96,5,128]{2,1,0:T(8,128)}, u32[]{:S(2)}, u32[]{:S(2)}) async-start(f32[96,5,128]{2,1,0:T(8,128)} %broadcast_in_dim.19), calls=%async_computation.1 | async-start | bytes 786432 | tf_op jit(solution)/shard_map/all_to_all | solution.py:69
  73.1 1.2 convolution_convert_fusion
  74.3 4.6 %reshape_reshape.17 = bf16[16,2,128,4,32]{4,3,2,1,0:T(4,128)(2,1)} reshape(bf16[16,32768]{1,0:T(8,128)(2,1)S(1)} %convolution_convert_fusion) | data formatting | bytes 2097152 | tf_op jit(solution)/shard_map/reshape;reshape | solution.py:82
  78.9 5.4 %copy.124 = bf16[16,2,128,4,32]{2,4,3,0,1:T(8,128)(2,1)S(1)} copy(bf16[16,2,128,4,32]{4,3,2,1,0:T(4,128)(2,1)} %reshape_reshape.17) | data formatting | bytes 2097152 | tf_op jit(solution)/shard_map/reshape;reshape | solution.py:82
  84.3 0.8 fusion.20
  85.3 4.2 %multiply_convert_fusion = bf16[16,4,128,128]{3,2,1,0:T(8,128)(2,1)S(1)} fusion(f32[16,4,128,128]{3,2,1,0:T(8,128)S(1)} %fusion.20, f32[16,4,128]{2,1,0:T(4,128)S(1)} %copy-done.18, f32[16,4,128]{2,1,0:T(4,128)S(1)} %copy-done.17, bf16[16,2,4,32,128]{4,3,2,0,1:T(8,128)(2,1)} %bitcast.181, bf16[16,2,4,32,128]{4,3,2,0,1:T(8,128)(2,1)S(1)} %bitcast.176), kind=kOutput, calls=%fused_computation.2 | convolution fusion | flops 72351744 | bytes 7405568 | tf_op jit(solution)/shard_map/shdq,shdk->shqk/dot_general | solution.py:96
  89.5 2.2 %convolution_multiply_fusion.2 = f32[16,4,32,128]{3,2,1,0:T(8,128)} fusion(bf16[16,4,128,128]{3,2,1,0:T(8,128)(2,1)S(1)} %multiply_convert_fusion, bf16[16,2,4,32,128]{4,3,2,0,1:T(8,128)(2,1)S(1)} %bitcast.182), kind=kOutput, calls=%fused_computation.19 | convolution fusion | flops 67371008 | bytes 3670016 | tf_op jit(solution)/shard_map/shqk,shdk->shdq/dot_general | solution.py:110
  91.7 2.5 %copy.127 = f32[16,128,128]{1,2,0:T(8,128)} copy(f32[16,128,128]{2,1,0:T(8,128)} %bitcast.187) | data formatting | bytes 2097152 | tf_op jit(solution)/shard_map/reshape | solution.py:115
  94.3 1.1 reduce_sum.88
  95.4 2.3 %pad_maximum_fusion.2 = f32[8,264,128]{2,1,0:T(8,128)} fusion(f32[8,8,128]{2,1,0:T(8,128)S(1)} %broadcast_in_dim.20, f32[8,256,128]{2,1,0:T(8,128)} %bitcast.190), kind=kLoop, calls=%fused_computation.31 | loop fusion | flops 270336 | bytes 2162688 | tf_op jit(solution)/shard_map/concatenate | solution.py:244
  97.7 4.3 %all-to-all-start.2 = ((f32[8,264,128]{2,1,0:T(8,128)}), f32[8,264,128]{2,1,0:T(8,128)}, u32[]{:S(2)}, u32[]{:S(2)}) async-start(f32[8,264,128]{2,1,0:T(8,128)} %pad_maximum_fusion.2), calls=%async_computation.2 | async-start | bytes 2162688 | tf_op jit(solution)/shard_map/all_to_all | solution.py:251
  102.0 0.6 slice_bitcast_fusion.30
  102.6 1.6 %convolution_multiply_fusion.1 = f32[16,4,32,128]{3,2,1,0:T(8,128)} fusion(bf16[16,4,128,128]{3,2,1,0:T(8,128)(2,1)S(1)} %multiply_convert_fusion, bf16[16,2,4,32,128]{4,3,2,0,1:T(8,128)(2,1)S(1)} %bitcast.177), kind=kOutput, calls=%fused_computation.18 | convolution fusion | flops 67371008 | bytes 3670016 | tf_op jit(solution)/shard_map/shqk,shdq->shdk/dot_general | solution.py:106
  104.2 1.7 %copy.131 = f32[16,128,128]{1,0,2:T(8,128)S(1)} copy(f32[16,128,128]{2,1,0:T(8,128)} %bitcast.188) | data formatting | bytes 2097152 | tf_op jit(solution)/shard_map/reshape | solution.py:115
  105.9 3.1 %fusion.1 = f32[16,4,32,128]{3,2,1,0:T(8,128)S(1)} fusion(f32[16,4,128,128]{3,2,1,0:T(8,128)} %copy-done, f32[16,4,128]{2,1,0:T(4,128)S(1)} %copy-done.17, bf16[16,2,4,32,128]{4,3,2,0,1:T(8,128)(2,1)S(1)} %bitcast.178), kind=kOutput, calls=%fused_computation.5 | convolution fusion | flops 70254592 | bytes 5799936 | tf_op jit(solution)/shard_map/shqk,shdq->shdk/dot_general | solution.py:102
  109.6 1.6 %fusion.3 = f32[4,2,128,128]{3,0,2,1:T(4,128)S(1)} fusion(f32[16,1,128,128]{3,0,2,1:T(8,128)S(1)} %bitcast.192, f32[16,1,128,128]{3,0,2,1:T(8,128)S(1)} %bitcast.191, s32[16]{0:T(128)} %sub.56), kind=kOutput, calls=%fused_computation.6 | convolution fusion | flops 25690176 | bytes 2621504 | tf_op jit(solution)/shard_map/sr,sxbf->rxbf/dot_general | solution.py:265
  111.4 0.7 copy.133
  112.2 1.6 %fusion.26 = bf16[16,32,128]{2,1,0:T(8,128)(2,1)} fusion(f32[16,32,128]{2,1,0:T(8,128)S(1)} %bitcast.209, bf16[16,32,128]{2,1,0:T(8,128)(2,1)S(1)} %copy-done.1, f32[128]{0:T(128)S(1)} %copy-done.28, f32[128]{0:T(128)S(1)} %copy-done.29, f32[128]{0:T(128)S(1)} %copy-done.26, f32[128]{0:T(128)S(1)} %copy-done.27, f32[128]{0:T(128)S(1)} %copy-done.25, ...), kind=kLoop, calls=%fused_computation.56 | loop fusion | flops 1835008 | bytes 1051136 | tf_op jit(solution)/shard_map/convert_element_type | solution.py:276
  113.7 18.3 %all-to-all-done.2 = f32[8,264,128]{2,1,0:T(8,128)} async-done(((f32[8,264,128]{2,1,0:T(8,128)}), f32[8,264,128]{2,1,0:T(8,128)}, u32[]{:S(2)}, u32[]{:S(2)}) %all-to-all-start.2) | async-done | bytes 1081376 | tf_op jit(solution)/shard_map/all_to_all | solution.py:251
  132.1 1.3 slice.156
  133.4 1.2 fusion.14
  134.6 0.7 copy.130
  135.3 0.8 slice_reduce_fusion
  136.0 0.6 broadcast_multiply_fusion
  (108 shorter events, 6.8 us)
Async XLA Ops:
  0.6 5.8 %copy-start.1 = (bf16[16,32,128]{2,1,0:T(8,128)(2,1)S(1)}, bf16[16,32,128]{2,1,0:T(8,128)(2,1)}, u32[]{:S(2)}) copy-start(bf16[16,32,128]{2,1,0:T(8,128)(2,1)} %param.12) | copy-start | bytes 393220
  0.6 5.8 %copy-start.16 = (bf16[16,32,128]{2,1,0:T(8,128)(2,1)S(1)}, bf16[16,32,128]{2,1,0:T(8,128)(2,1)}, u32[]{:S(2)}) copy-start(bf16[16,32,128]{2,1,0:T(8,128)(2,1)} %param.10) | copy-start | bytes 393220
  0.7 5.8 %copy-start.21 = (bf16[16,32,128]{2,1,0:T(8,128)(2,1)S(1)}, bf16[16,32,128]{2,1,0:T(8,128)(2,1)}, u32[]{:S(2)}) copy-start(bf16[16,32,128]{2,1,0:T(8,128)(2,1)} %param.9) | copy-start | bytes 393220
  0.7 5.8 %copy-start.20 = (bf16[16,32,128]{2,1,0:T(8,128)(2,1)S(1)}, bf16[16,32,128]{2,1,0:T(8,128)(2,1)}, u32[]{:S(2)}) copy-start(bf16[16,32,128]{2,1,0:T(8,128)(2,1)} %param.8) | copy-start | bytes 393220
  2.2 4.3 %copy-start.22 = (f32[16,4]{0,1:T(4,128)}, f32[16,4]{0,1:T(4,128)S(1)}, u32[]{:S(2)}) copy-start(f32[16,4]{0,1:T(4,128)S(1)} %fusion.41) | copy-start | bytes 772
  8.5 38.7 %all-to-all-start = ((bf16[8,576,128]{2,1,0:T(8,128)(2,1)}), bf16[8,576,128]{2,1,0:T(8,128)(2,1)S(1)}, u32[]{:S(2)}, u32[]{:S(2)}) async-start(bf16[8,576,128]{2,1,0:T(8,128)(2,1)} %pad_maximum_fusion), calls=%async_computation | async-start | bytes 2359296 | tf_op jit(solution)/shard_map/all_to_all | solution.py:184
  16.3 31.1 %collective-permute-start.1 = (bf16[1,32,128]{2,1,0:T(8,128)(2,1)}, bf16[1,32,128]{2,1,0:T(8,128)(2,1)}, u32[]{:S(2)}, u32[]{:S(2)}) collective-permute-start(bf16[1,32,128]{2,1,0:T(8,128)(2,1)} %get-tuple-element.37), channel_id=1, source_target_pairs={{0,8},{8,16},{16,24},{24,32},{32,40},{40,48},{48,56},{56,64},{64,7... | collective-permute-start | bytes 24584 | tf_op jit(solution)/shard_map/ppermute | solution.py:199
  18.2 29.2 %collective-permute-start = (bf16[1,32,128]{2,1,0:T(8,128)(2,1)}, bf16[1,32,128]{2,1,0:T(8,128)(2,1)}, u32[]{:S(2)}, u32[]{:S(2)}) collective-permute-start(bf16[1,32,128]{2,1,0:T(8,128)(2,1)} %get-tuple-element.38), channel_id=1, source_target_pairs={{8,0},{16,8},{24,16},{32,24},{40,32},{48,40},{56,48},{64,56},{72,6... | collective-permute-start | bytes 24584 | tf_op jit(solution)/shard_map/ppermute | solution.py:200
  22.1 0.7 copy-start.4
  32.5 17.5 %copy-start.9 = (bf16[15,32,128]{2,1,0:T(8,128)(2,1)}, bf16[15,32,128]{2,1,0:T(8,128)(2,1)S(1)}, u32[]{:S(2)}) copy-start(bf16[15,32,128]{2,1,0:T(8,128)(2,1)S(1)} %get-tuple-element.39) | copy-start | bytes 368644
  32.5 17.5 %copy-start.11 = (bf16[15,32,128]{2,1,0:T(8,128)(2,1)}, bf16[15,32,128]{2,1,0:T(8,128)(2,1)S(1)}, u32[]{:S(2)}) copy-start(bf16[15,32,128]{2,1,0:T(8,128)(2,1)S(1)} %get-tuple-element.40) | copy-start | bytes 368644
  32.5 17.5 %copy-start.5 = (bf16[16,31,128]{2,1,0:T(8,128)(2,1)}, bf16[16,31,128]{2,1,0:T(8,128)(2,1)S(1)}, u32[]{:S(2)}) copy-start(bf16[16,31,128]{2,1,0:T(8,128)(2,1)S(1)} %get-tuple-element.35) | copy-start | bytes 380932
  32.5 17.5 %copy-start.7 = (bf16[16,31,128]{2,1,0:T(8,128)(2,1)}, bf16[16,31,128]{2,1,0:T(8,128)(2,1)S(1)}, u32[]{:S(2)}) copy-start(bf16[16,31,128]{2,1,0:T(8,128)(2,1)S(1)} %get-tuple-element.36) | copy-start | bytes 380932
  51.5 0.8 copy-start.19
  51.6 1.4 %copy-start.24 = (f32[5,128]{1,0:T(8,128)S(1)}, f32[5,128]{1,0:T(8,128)}, u32[]{:S(2)}) copy-start(f32[5,128]{1,0:T(8,128)} %stack.50) | copy-start | bytes 7684
  53.7 40.6 %all-to-all-start.1 = ((f32[96,5,128]{2,1,0:T(8,128)}), f32[96,5,128]{2,1,0:T(8,128)}, u32[]{:S(2)}, u32[]{:S(2)}) async-start(f32[96,5,128]{2,1,0:T(8,128)} %broadcast_in_dim.19), calls=%async_computation.1 | async-start | bytes 786432 | tf_op jit(solution)/shard_map/all_to_all | solution.py:69
  84.3 1.0 copy-start.2
  84.3 1.0 copy-start.17
  84.3 1.0 copy-start.18
  85.2 4.3 %copy-start = (f32[16,4,128,128]{3,2,1,0:T(8,128)}, f32[16,4,128,128]{3,2,1,0:T(8,128)S(1)}, u32[]{:S(2)}) copy-start(f32[16,4,128,128]{3,2,1,0:T(8,128)S(1)} %fusion.20) | copy-start | bytes 12582916
  85.2 4.3 %copy-start.3 = (bf16[16,2,128,4,32]{2,4,3,0,1:T(8,128)(2,1)S(1)}, bf16[16,2,128,4,32]{2,4,3,0,1:T(8,128)(2,1)}, u32[]{:S(2)}) copy-start(bf16[16,2,128,4,32]{2,4,3,0,1:T(8,128)(2,1)} %copy-done.2) | copy-start | bytes 3145732
  95.4 6.6 %copy-start.30 = (f32[5,128]{1,0:T(8,128)S(1)}, f32[5,128]{1,0:T(8,128)}, u32[]{:S(2)}) copy-start(f32[5,128]{1,0:T(8,128)} %param.15) | copy-start | bytes 7684
  97.7 34.3 %all-to-all-start.2 = ((f32[8,264,128]{2,1,0:T(8,128)}), f32[8,264,128]{2,1,0:T(8,128)}, u32[]{:S(2)}, u32[]{:S(2)}) async-start(f32[8,264,128]{2,1,0:T(8,128)} %pad_maximum_fusion.2), calls=%async_computation.2 | async-start | bytes 2162688 | tf_op jit(solution)/shard_map/all_to_all | solution.py:251
  109.0 2.2 %copy-start.14 = (f32[4,128,128]{1,0,2:T(4,128)S(1)}, f32[4,128,128]{1,0,2:T(4,128)}, u32[]{:S(2)}) copy-start(f32[4,128,128]{1,0,2:T(4,128)} %copy.120) | copy-start | bytes 786436
  109.5 1.7 %copy-start.15 = (f32[4,128,128]{1,0,2:T(4,128)S(1)}, f32[4,128,128]{1,0,2:T(4,128)}, u32[]{:S(2)}) copy-start(f32[4,128,128]{1,0,2:T(4,128)} %copy.121) | copy-start | bytes 786436
  109.5 2.6 %copy-start.6 = (bf16[16,31,128]{2,1,0:T(8,128)(2,1)S(1)}, bf16[16,31,128]{2,1,0:T(8,128)(2,1)}, u32[]{:S(2)}) copy-start(bf16[16,31,128]{2,1,0:T(8,128)(2,1)} %copy-done.5) | copy-start | bytes 380932
  109.5 2.6 %copy-start.8 = (bf16[16,31,128]{2,1,0:T(8,128)(2,1)S(1)}, bf16[16,31,128]{2,1,0:T(8,128)(2,1)}, u32[]{:S(2)}) copy-start(bf16[16,31,128]{2,1,0:T(8,128)(2,1)} %copy-done.7) | copy-start | bytes 380932
  109.6 2.5 %copy-start.10 = (bf16[15,32,128]{2,1,0:T(8,128)(2,1)S(1)}, bf16[15,32,128]{2,1,0:T(8,128)(2,1)}, u32[]{:S(2)}) copy-start(bf16[15,32,128]{2,1,0:T(8,128)(2,1)} %copy-done.9) | copy-start | bytes 368644
  109.6 2.5 %copy-start.12 = (bf16[15,32,128]{2,1,0:T(8,128)(2,1)S(1)}, bf16[15,32,128]{2,1,0:T(8,128)(2,1)}, u32[]{:S(2)}) copy-start(bf16[15,32,128]{2,1,0:T(8,128)(2,1)} %copy-done.11) | copy-start | bytes 368644
  109.6 2.5 %copy-start.25 = (f32[128]{0:T(128)S(1)}, f32[128]{0:T(128)}, u32[]{:S(2)}) copy-start(f32[128]{0:T(128)} %get-tuple-element.49) | copy-start | bytes 1540
  109.6 2.5 %copy-start.26 = (f32[128]{0:T(128)S(1)}, f32[128]{0:T(128)}, u32[]{:S(2)}) copy-start(f32[128]{0:T(128)} %get-tuple-element.50) | copy-start | bytes 1540
  109.6 2.5 %copy-start.27 = (f32[128]{0:T(128)S(1)}, f32[128]{0:T(128)}, u32[]{:S(2)}) copy-start(f32[128]{0:T(128)} %get-tuple-element.51) | copy-start | bytes 1540
  109.6 2.5 %copy-start.28 = (f32[128]{0:T(128)S(1)}, f32[128]{0:T(128)}, u32[]{:S(2)}) copy-start(f32[128]{0:T(128)} %get-tuple-element.52) | copy-start | bytes 1540
  109.6 2.5 %copy-start.29 = (f32[128]{0:T(128)S(1)}, f32[128]{0:T(128)}, u32[]{:S(2)}) copy-start(f32[128]{0:T(128)} %get-tuple-element.53) | copy-start | bytes 1540
  111.4 22.0 %copy-start.13 = (f32[4,128,128]{1,0,2:T(4,128)S(1)}, f32[4,128,128]{1,0,2:T(4,128)}, u32[]{:S(2)}) copy-start(f32[4,128,128]{1,0,2:T(4,128)} %copy.119) | copy-start | bytes 786436
  111.4 22.0 %copy-start.23 = (f32[16,4]{0,1:T(4,128)S(1)}, f32[16,4]{0,1:T(4,128)}, u32[]{:S(2)}) copy-start(f32[16,4]{0,1:T(4,128)} %copy-done.22) | copy-start | bytes 772

commit v6 on v5

--- a/solution.py
+++ b/solution.py
@@ -240,17 +240,25 @@
     key_part = key_part.reshape(group_size, item_count, BLOCK, features)
     value_part = value_part.reshape(group_size, item_count, BLOCK, features)
     stencil_count = partial_rows.shape[0]
-    stencil_pad = jnp.pad(column_sum, ((0, 8 - stencil_count), (0, 0)))
+    stencil_hi = column_sum.astype(jnp.bfloat16)
+    stencil_rest = column_sum - stencil_hi.astype(jnp.float32)
+    stencil_mid = stencil_rest.astype(jnp.bfloat16)
+    stencil_lo = (stencil_rest - stencil_mid.astype(jnp.float32)).astype(jnp.bfloat16)
+    stencil_terms = jnp.concatenate([stencil_hi, stencil_mid, stencil_lo], 0)
+    term_rows = 3 * stencil_count
+    stencil_pad = jnp.pad(stencil_terms, ((0, 16 - term_rows), (0, 0)))
     return_pack = jnp.concatenate(
         [
-            query_part.reshape(group_size, item_count * BLOCK, features),
-            jnp.broadcast_to(stencil_pad[None], (group_size, 8, features)),
+            query_part.reshape(group_size, item_count * BLOCK, features).astype(jnp.bfloat16),
+            jnp.broadcast_to(stencil_pad[None], (group_size, 16, features)),
         ],
         1,
     )
     return_in = lax.all_to_all(return_pack, "gy", split_axis=0, concat_axis=0, tiled=True)
-    returned = return_in[:, : item_count * BLOCK]
-    summed = jnp.sum(return_in[:, item_count * BLOCK : item_count * BLOCK + stencil_count], 0)
+    returned = return_in[:, : item_count * BLOCK].astype(jnp.float32)
+    terms_in = return_in[:, item_count * BLOCK : item_count * BLOCK + term_rows].astype(jnp.float32)
+    terms_in = terms_in.reshape(group_size, 3, stencil_count, features)
+    summed = jnp.sum(terms_in[:, 0] + terms_in[:, 1] + terms_in[:, 2], 0)
     returned, pieces, ids_in = (returned, jnp.stack([key_part, value_part], 2), ids_in)
     query_sum = diag_query + jnp.einsum(
         "sr,sbf->rbf",

time: 138 us -> 128 us (0.928)
  matrix products: 22.1 us -> 19.1 us
  local copies, waits for them, and re-layouts: 32.2 us -> 29.9 us
  waiting for transfers between devices: 33 us -> 31.2 us
  other arithmetic: 11.6 us -> 9.83 us
  starting transfers between devices: 36.3 us -> 34.9 us
    all_to_all x1, waiting for transfers between devices: 18.3 us -> 11.9 us  [per_device(): lax.all_to_all(return_pack, 'gy', split_axis=0, concat_axis=0, tiled=True)]
    all_to_all x1, waiting for transfers between devices: 14.7 us -> 19.3 us  [per_device(): lax.all_to_all(send_pack, 'gy', split_axis=0, concat_axis=0, tiled=True)]
    convert_element_type x0 -> x1, local copies, waits for them, and re-layouts: none -> 2.06 us  [per_device(): query_part.reshape(group_size, item_count * BLOCK, features)]
    ppermute x1, starting transfers between devices: 3.64 us -> 1.91 us  [per_device(): from_after = lax.ppermute(grad_x[:1], 'gx', behind)]
    reshape x6 -> x5, local copies, waits for them, and re-layouts: 9.24 us -> 7.95 us  [points_last(): return part.reshape(item_count, features, block_rows).transpose(0, 2, 1)]
  transfers between devices with their start and end apart: 5 -> 5, of which waited for: 2 -> 2; matrix products, arithmetic and copies ran while one was open for 32% -> 34% of each run, Pallas kernels for 0% -> 0%
where the time goes in v6:
time: 128 us; the launch traced here: 126 us
  starting transfers between devices  34.9 us (27%)
  waiting for transfers between devices  31.2 us (24%)
  local copies, waits for them, and re-layouts  29.9 us (23%)
  matrix products  19.1 us (15%)
  other arithmetic  9.83 us (8%)
  between operations  1.44 us (1%)
    all_to_all x1, waiting for transfers between devices, per_device(): lax.all_to_all(send_pack, 'gy', split_axis=0, concat_axis=0, tiled=True)  19.3 us
    all_to_all x1, starting transfers between devices, gather_sum(): lax.all_to_all(spread, axis, split_axis=0, concat_axis=0, tiled=True)  19.3 us
    all_to_all x1, waiting for transfers between devices, per_device(): lax.all_to_all(return_pack, 'gy', split_axis=0, concat_axis=0, tiled=True)  11.9 us
    another operation x2, local copies, waits for them, and re-layouts, tile_grads(): key_pack.reshape(item_count, 2, block_rows, HEADS, head_width)  9.97 us
    reshape x5, local copies, waits for them, and re-layouts, points_last(): return part.reshape(item_count, features, block_rows).transpose(0, 2, 1)  7.95 us
    all_to_all x1, starting transfers between devices, per_device(): lax.all_to_all(send_pack, 'gy', split_axis=0, concat_axis=0, tiled=True)  7.1 us
    dot_general x2, matrix products, tile_grads(): jnp.einsum('shdq,shdk->shqk', grad_heads, value_heads, preferred_element_...  4.76 us
    all_to_all x1, starting transfers between devices, per_device(): lax.all_to_all(return_pack, 'gy', split_axis=0, concat_axis=0, tiled=True)  4.19 us
  transfers between devices with their start and end apart: 5, of which 2 were waited for; matrix products, arithmetic and copies ran while one was open for 34% of the time, Pallas kernels for 0%

profile of v6, /device:TPU:6, one launch (start us, length us, event | category | flops | bytes accessed | tf_op | source)
XLA Modules:
  0.0 126.4 jit_solution(4207354645768309254)
XLA Ops:
  0.7 0.9 fusion.75
  1.6 0.8 copy.169
  2.8 1.0 convert_multiply_fusion.10
  3.9 0.4 reshape.252
  4.3 0.7 reduce_sum.82
  5.8 0.5 fusion.9
  6.8 1.1 pad_maximum_fusion
  7.9 7.1 %all-to-all-start = ((bf16[8,576,128]{2,1,0:T(8,128)(2,1)}), bf16[8,576,128]{2,1,0:T(8,128)(2,1)S(1)}, u32[]{:S(2)}, u32[]{:S(2)}) async-start(bf16[8,576,128]{2,1,0:T(8,128)(2,1)} %pad_maximum_fusion), calls=%async_computation | async-start | bytes 2359296 | tf_op jit(solution)/shard_map/all_to_all | solution.py:184
  15.0 0.6 fusion.73
  15.6 1.9 %collective-permute-start = (bf16[1,32,128]{2,1,0:T(8,128)(2,1)}, bf16[1,32,128]{2,1,0:T(8,128)(2,1)}, u32[]{:S(2)}, u32[]{:S(2)}) collective-permute-start(bf16[1,32,128]{2,1,0:T(8,128)(2,1)} %get-tuple-element.38), channel_id=1, source_target_pairs={{8,0},{16,8},{24,16},{32,24},{40,32},{48,40},{56,48},{64,56},{72,6... | collective-permute-start | bytes 24584 | tf_op jit(solution)/shard_map/ppermute | solution.py:200
  17.5 2.4 %collective-permute-start.1 = (bf16[1,32,128]{2,1,0:T(8,128)(2,1)}, bf16[1,32,128]{2,1,0:T(8,128)(2,1)}, u32[]{:S(2)}, u32[]{:S(2)}) collective-permute-start(bf16[1,32,128]{2,1,0:T(8,128)(2,1)} %get-tuple-element.37), channel_id=1, source_target_pairs={{0,8},{8,16},{16,24},{24,32},{32,40},{40,48},{48,56},{56,64},{64,7... | collective-permute-start | bytes 24584 | tf_op jit(solution)/shard_map/ppermute | solution.py:199
  20.4 0.5 fusion.11
  20.9 0.5 fusion.13
  21.4 1.1 convolution_multiply_fusion.4
  22.5 1.8 %copy.181 = f32[4,128,128]{1,0,2:T(4,128)} copy(f32[4,128,128]{2,1,0:T(8,128)} %bitcast.207) | data formatting | bytes 524288 | tf_op jit(solution)/shard_map/reshape | solution.py:115
  24.6 0.8 copy.182
  25.7 0.8 copy.183
  26.5 0.6 slice_bitcast_fusion.30
  27.2 19.3 %all-to-all-done = bf16[8,576,128]{2,1,0:T(8,128)(2,1)S(1)} async-done(((bf16[8,576,128]{2,1,0:T(8,128)(2,1)}), bf16[8,576,128]{2,1,0:T(8,128)(2,1)S(1)}, u32[]{:S(2)}, u32[]{:S(2)}) %all-to-all-start) | async-done | bytes 1179680 | tf_op jit(solution)/shard_map/all_to_all | solution.py:184
  46.7 0.9 fusion.32
  47.7 0.4 add_reduce_fusion
  48.2 0.8 broadcast_in_dim.19
  49.0 19.3 %all-to-all-start.1 = ((f32[96,5,128]{2,1,0:T(8,128)}), f32[96,5,128]{2,1,0:T(8,128)}, u32[]{:S(2)}, u32[]{:S(2)}) async-start(f32[96,5,128]{2,1,0:T(8,128)} %broadcast_in_dim.19), calls=%async_computation.1 | async-start | bytes 786432 | tf_op jit(solution)/shard_map/all_to_all | solution.py:69
  68.4 1.5 %convolution_convert_fusion = bf16[16,32768]{1,0:T(8,128)(2,1)S(1)} fusion(bf16[1,4,256,128]{3,2,1,0:T(8,128)(2,1)} %bitcast.198, s32[16]{0:T(128)S(1)} %sub.62), kind=kOutput, calls=%fused_computation | convolution fusion | flops 4718656 | bytes 1310784 | tf_op jit(solution)/shard_map/dot_general | solution.py:228
  69.9 4.6 %reshape_reshape.15 = bf16[16,2,128,4,32]{4,3,2,1,0:T(4,128)(2,1)} reshape(bf16[16,32768]{1,0:T(8,128)(2,1)S(1)} %convolution_convert_fusion) | data formatting | bytes 2097152 | tf_op jit(solution)/shard_map/reshape;reshape | solution.py:82
  74.5 5.4 %copy.186 = bf16[16,2,128,4,32]{2,4,3,0,1:T(8,128)(2,1)S(1)} copy(bf16[16,2,128,4,32]{4,3,2,1,0:T(4,128)(2,1)} %reshape_reshape.15) | data formatting | bytes 2097152 | tf_op jit(solution)/shard_map/reshape;reshape | solution.py:82
  79.9 0.5 copy.187
  80.4 0.3 reshape_reshape_reshape.3
  81.0 0.8 fusion.21
  81.8 4.2 %multiply_convert_fusion = bf16[16,4,128,128]{3,2,1,0:T(8,128)(2,1)S(1)} fusion(f32[16,4,128,128]{3,2,1,0:T(8,128)S(1)} %fusion.21, f32[16,4,128]{2,1,0:T(4,128)S(1)} %get-tuple-element.46, f32[16,4,128]{2,1,0:T(4,128)S(1)} %get-tuple-element.45, bf16[16,2,4,32,128]{4,3,2,0,1:T(8,128)(2,1)} %bitcast.183, bf16[16,2,4,32,128]{4,3,2,0,1:T(8,128)(2,1)S(1)} %bitcast.178), kind=kOutput, calls=%fused_computation.2 | convolution fusion | flops 72351744 | bytes 7405568 | tf_op jit(solution)/shard_map/shdq,shdk->shqk/dot_general | solution.py:96
  86.0 2.0 %fusion.14 = bf16[16,4,32,128]{3,2,1,0:T(8,128)(2,1)} fusion(bf16[16,4,128,128]{3,2,1,0:T(8,128)(2,1)S(1)} %multiply_convert_fusion, bf16[16,2,4,32,128]{4,3,2,0,1:T(8,128)(2,1)S(1)} %bitcast.184), kind=kOutput, calls=%fused_computation.21 | convolution fusion | flops 67633152 | bytes 3145728 | tf_op jit(solution)/shard_map/shqk,shdk->shdq/dot_general | solution.py:110
  88.1 2.1 %copy.189 = bf16[16,128,128]{1,2,0:T(8,128)(2,1)} copy(bf16[16,128,128]{2,1,0:T(8,128)(2,1)} %bitcast.202) | data formatting | bytes 1048576 | tf_op jit(solution)/shard_map/convert_element_type | solution.py:252
  90.1 3.8 %fusion.1 = f32[16,4,32,128]{3,2,1,0:T(8,128)} fusion(f32[16,4,128,128]{3,2,1,0:T(8,128)} %copy-done, f32[16,4,128]{2,1,0:T(4,128)S(1)} %get-tuple-element.45, bf16[16,2,4,32,128]{4,3,2,0,1:T(8,128)(2,1)S(1)} %bitcast.179), kind=kOutput, calls=%fused_computation.5 | convolution fusion | flops 70254592 | bytes 5799936 | tf_op jit(solution)/shard_map/shqk,shdq->shdk/dot_general | solution.py:102
  94.0 2.6 %copy.194 = f32[16,128,128]{1,0,2:T(8,128)} copy(f32[16,128,128]{2,1,0:T(8,128)} %bitcast.193) | data formatting | bytes 2097152 | tf_op jit(solution)/shard_map/reshape | solution.py:115
  96.6 1.1 reduce_sum.88
  97.7 1.9 %pad_maximum_fusion.2 = bf16[8,272,128]{2,1,0:T(8,128)(2,1)} fusion(bf16[8,16,128]{2,1,0:T(8,128)(2,1)S(1)} %broadcast_in_dim.20, bf16[8,256,128]{2,1,0:T(8,128)(2,1)} %bitcast.201), kind=kLoop, calls=%fused_computation.33 | loop fusion | flops 1114112 | bytes 1114112 | tf_op jit(solution)/shard_map/concatenate | solution.py:250
  99.6 4.2 %all-to-all-start.2 = ((bf16[8,272,128]{2,1,0:T(8,128)(2,1)}), bf16[8,272,128]{2,1,0:T(8,128)(2,1)}, u32[]{:S(2)}, u32[]{:S(2)}) async-start(bf16[8,272,128]{2,1,0:T(8,128)(2,1)} %pad_maximum_fusion.2), calls=%async_computation.2 | async-start | bytes 1114112 | tf_op jit(solution)/shard_map/all_to_all | solution.py:257
  103.8 1.6 %convolution_multiply_fusion.1 = f32[16,4,32,128]{3,2,1,0:T(8,128)} fusion(bf16[16,4,128,128]{3,2,1,0:T(8,128)(2,1)S(1)} %multiply_convert_fusion, bf16[16,2,4,32,128]{4,3,2,0,1:T(8,128)(2,1)S(1)} %bitcast.180), kind=kOutput, calls=%fused_computation.18 | convolution fusion | flops 67371008 | bytes 3670016 | tf_op jit(solution)/shard_map/shqk,shdq->shdk/dot_general | solution.py:106
  105.5 1.8 %copy.193 = f32[16,128,128]{1,0,2:T(8,128)S(1)} copy(f32[16,128,128]{2,1,0:T(8,128)} %bitcast.189) | data formatting | bytes 2097152 | tf_op jit(solution)/shard_map/reshape | solution.py:115
  107.4 0.8 fusion.3
  108.4 0.7 copy.195
  109.2 1.6 %fusion.27 = bf16[16,32,128]{2,1,0:T(8,128)(2,1)} fusion(f32[16,32,128]{2,1,0:T(8,128)S(1)} %bitcast.211, bf16[16,32,128]{2,1,0:T(8,128)(2,1)S(1)} %copy-done.1, f32[128]{0:T(128)S(1)} %copy-done.26, f32[128]{0:T(128)S(1)} %copy-done.27, f32[128]{0:T(128)S(1)} %copy-done.24, f32[128]{0:T(128)S(1)} %copy-done.25, f32[128]{0:T(128)S(1)} %copy-done.23, ...), kind=kLoop, calls=%fused_computation.57 | loop fusion | flops 1835008 | bytes 1051136 | tf_op jit(solution)/shard_map/convert_element_type | solution.py:284
  110.8 11.9 %all-to-all-done.2 = bf16[8,272,128]{2,1,0:T(8,128)(2,1)} async-done(((bf16[8,272,128]{2,1,0:T(8,128)(2,1)}), bf16[8,272,128]{2,1,0:T(8,128)(2,1)}, u32[]{:S(2)}, u32[]{:S(2)}) %all-to-all-start.2) | async-done | bytes 557088 | tf_op jit(solution)/shard_map/all_to_all | solution.py:257
  122.6 1.1 slice.168
  123.7 0.6 fusion.15
  124.3 0.7 copy.192
  125.0 0.8 slice.171
  125.8 0.6 broadcast_multiply_fusion
  (108 shorter events, 3.5 us)
Async XLA Ops:
  0.6 5.1 %copy-start.1 = (bf16[16,32,128]{2,1,0:T(8,128)(2,1)S(1)}, bf16[16,32,128]{2,1,0:T(8,128)(2,1)}, u32[]{:S(2)}) copy-start(bf16[16,32,128]{2,1,0:T(8,128)(2,1)} %param.12) | copy-start | bytes 393220
  0.6 4.5 %copy-start.22 = (bf16[4,16,32]{2,1,0:T(8,128)(2,1)S(1)}, bf16[4,16,32]{2,1,0:T(8,128)(2,1)}, u32[]{:S(2)}) copy-start(bf16[4,16,32]{2,1,0:T(8,128)(2,1)} %param.13) | copy-start | bytes 12292
  0.7 5.1 %copy-start.18 = (bf16[16,32,128]{2,1,0:T(8,128)(2,1)S(1)}, bf16[16,32,128]{2,1,0:T(8,128)(2,1)}, u32[]{:S(2)}) copy-start(bf16[16,32,128]{2,1,0:T(8,128)(2,1)} %param.8) | copy-start | bytes 393220
  0.7 5.1 %copy-start.17 = (bf16[16,32,128]{2,1,0:T(8,128)(2,1)S(1)}, bf16[16,32,128]{2,1,0:T(8,128)(2,1)}, u32[]{:S(2)}) copy-start(bf16[16,32,128]{2,1,0:T(8,128)(2,1)} %param.10) | copy-start | bytes 393220
  0.7 5.1 %copy-start.19 = (bf16[16,32,128]{2,1,0:T(8,128)(2,1)S(1)}, bf16[16,32,128]{2,1,0:T(8,128)(2,1)}, u32[]{:S(2)}) copy-start(bf16[16,32,128]{2,1,0:T(8,128)(2,1)} %param.9) | copy-start | bytes 393220
  5.5 1.1 copy-start.20
  5.8 14.2 %copy-start.5 = (bf16[4,2,128,128]{3,2,1,0:T(8,128)(2,1)}, bf16[4,2,128,128]{3,2,1,0:T(8,128)(2,1)S(1)}, u32[]{:S(2)}) copy-start(bf16[4,2,128,128]{3,2,1,0:T(8,128)(2,1)S(1)} %get-tuple-element.17) | copy-start | bytes 786436
  7.9 38.7 %all-to-all-start = ((bf16[8,576,128]{2,1,0:T(8,128)(2,1)}), bf16[8,576,128]{2,1,0:T(8,128)(2,1)S(1)}, u32[]{:S(2)}, u32[]{:S(2)}) async-start(bf16[8,576,128]{2,1,0:T(8,128)(2,1)} %pad_maximum_fusion), calls=%async_computation | async-start | bytes 2359296 | tf_op jit(solution)/shard_map/all_to_all | solution.py:184
  15.6 31.1 %collective-permute-start = (bf16[1,32,128]{2,1,0:T(8,128)(2,1)}, bf16[1,32,128]{2,1,0:T(8,128)(2,1)}, u32[]{:S(2)}, u32[]{:S(2)}) collective-permute-start(bf16[1,32,128]{2,1,0:T(8,128)(2,1)} %get-tuple-element.38), channel_id=1, source_target_pairs={{8,0},{16,8},{24,16},{32,24},{40,32},{48,40},{56,48},{64,56},{72,6... | collective-permute-start | bytes 24584 | tf_op jit(solution)/shard_map/ppermute | solution.py:200
  17.5 29.2 %collective-permute-start.1 = (bf16[1,32,128]{2,1,0:T(8,128)(2,1)}, bf16[1,32,128]{2,1,0:T(8,128)(2,1)}, u32[]{:S(2)}, u32[]{:S(2)}) collective-permute-start(bf16[1,32,128]{2,1,0:T(8,128)(2,1)} %get-tuple-element.37), channel_id=1, source_target_pairs={{0,8},{8,16},{16,24},{24,32},{32,40},{40,48},{48,56},{56,64},{64,7... | collective-permute-start | bytes 24584 | tf_op jit(solution)/shard_map/ppermute | solution.py:199
  22.5 4.0 %copy-start.28 = (f32[5,128]{1,0:T(8,128)S(1)}, f32[5,128]{1,0:T(8,128)}, u32[]{:S(2)}) copy-start(f32[5,128]{1,0:T(8,128)} %param.15) | copy-start | bytes 7684
  27.1 20.5 %copy-start.10 = (bf16[15,32,128]{2,1,0:T(8,128)(2,1)}, bf16[15,32,128]{2,1,0:T(8,128)(2,1)S(1)}, u32[]{:S(2)}) copy-start(bf16[15,32,128]{2,1,0:T(8,128)(2,1)S(1)} %get-tuple-element.39) | copy-start | bytes 368644
  27.1 20.5 %copy-start.12 = (bf16[15,32,128]{2,1,0:T(8,128)(2,1)}, bf16[15,32,128]{2,1,0:T(8,128)(2,1)S(1)}, u32[]{:S(2)}) copy-start(bf16[15,32,128]{2,1,0:T(8,128)(2,1)S(1)} %get-tuple-element.40) | copy-start | bytes 368644
  27.2 20.5 %copy-start.6 = (bf16[16,31,128]{2,1,0:T(8,128)(2,1)}, bf16[16,31,128]{2,1,0:T(8,128)(2,1)S(1)}, u32[]{:S(2)}) copy-start(bf16[16,31,128]{2,1,0:T(8,128)(2,1)S(1)} %get-tuple-element.35) | copy-start | bytes 380932
  27.2 20.5 %copy-start.8 = (bf16[16,31,128]{2,1,0:T(8,128)(2,1)}, bf16[16,31,128]{2,1,0:T(8,128)(2,1)S(1)}, u32[]{:S(2)}) copy-start(bf16[16,31,128]{2,1,0:T(8,128)(2,1)S(1)} %get-tuple-element.36) | copy-start | bytes 380932
  49.0 47.6 %all-to-all-start.1 = ((f32[96,5,128]{2,1,0:T(8,128)}), f32[96,5,128]{2,1,0:T(8,128)}, u32[]{:S(2)}, u32[]{:S(2)}) async-start(f32[96,5,128]{2,1,0:T(8,128)} %broadcast_in_dim.19), calls=%async_computation.1 | async-start | bytes 786432 | tf_op jit(solution)/shard_map/all_to_all | solution.py:69
  79.9 1.1 copy-start.2
  81.8 4.3 %copy-start = (f32[16,4,128,128]{3,2,1,0:T(8,128)}, f32[16,4,128,128]{3,2,1,0:T(8,128)S(1)}, u32[]{:S(2)}) copy-start(f32[16,4,128,128]{3,2,1,0:T(8,128)S(1)} %fusion.21) | copy-start | bytes 12582916
  81.8 4.3 %copy-start.3 = (bf16[16,2,128,4,32]{2,4,3,0,1:T(8,128)(2,1)S(1)}, bf16[16,2,128,4,32]{2,4,3,0,1:T(8,128)(2,1)}, u32[]{:S(2)}) copy-start(bf16[16,2,128,4,32]{2,4,3,0,1:T(8,128)(2,1)} %copy-done.2) | copy-start | bytes 3145732
  99.6 23.0 %all-to-all-start.2 = ((bf16[8,272,128]{2,1,0:T(8,128)(2,1)}), bf16[8,272,128]{2,1,0:T(8,128)(2,1)}, u32[]{:S(2)}, u32[]{:S(2)}) async-start(bf16[8,272,128]{2,1,0:T(8,128)(2,1)} %pad_maximum_fusion.2), calls=%async_computation.2 | async-start | bytes 1114112 | tf_op jit(solution)/shard_map/all_to_all | solution.py:257
  105.5 1.9 %copy-start.4 = (f32[16,128,128]{1,0,2:T(8,128)S(1)}, f32[16,128,128]{1,0,2:T(8,128)}, u32[]{:S(2)}) copy-start(f32[16,128,128]{1,0,2:T(8,128)} %copy.194) | copy-start | bytes 3145732
  105.5 2.8 %copy-start.15 = (f32[4,128,128]{1,0,2:T(4,128)S(1)}, f32[4,128,128]{1,0,2:T(4,128)}, u32[]{:S(2)}) copy-start(f32[4,128,128]{1,0,2:T(4,128)} %copy.182) | copy-start | bytes 786436
  105.5 2.8 %copy-start.16 = (f32[4,128,128]{1,0,2:T(4,128)S(1)}, f32[4,128,128]{1,0,2:T(4,128)}, u32[]{:S(2)}) copy-start(f32[4,128,128]{1,0,2:T(4,128)} %copy.183) | copy-start | bytes 786436
  107.3 1.8 %copy-start.7 = (bf16[16,31,128]{2,1,0:T(8,128)(2,1)S(1)}, bf16[16,31,128]{2,1,0:T(8,128)(2,1)}, u32[]{:S(2)}) copy-start(bf16[16,31,128]{2,1,0:T(8,128)(2,1)} %copy-done.6) | copy-start | bytes 380932
  107.3 1.8 %copy-start.9 = (bf16[16,31,128]{2,1,0:T(8,128)(2,1)S(1)}, bf16[16,31,128]{2,1,0:T(8,128)(2,1)}, u32[]{:S(2)}) copy-start(bf16[16,31,128]{2,1,0:T(8,128)(2,1)} %copy-done.8) | copy-start | bytes 380932
  107.4 1.8 %copy-start.11 = (bf16[15,32,128]{2,1,0:T(8,128)(2,1)S(1)}, bf16[15,32,128]{2,1,0:T(8,128)(2,1)}, u32[]{:S(2)}) copy-start(bf16[15,32,128]{2,1,0:T(8,128)(2,1)} %copy-done.10) | copy-start | bytes 368644
  107.4 1.8 %copy-start.13 = (bf16[15,32,128]{2,1,0:T(8,128)(2,1)S(1)}, bf16[15,32,128]{2,1,0:T(8,128)(2,1)}, u32[]{:S(2)}) copy-start(bf16[15,32,128]{2,1,0:T(8,128)(2,1)} %copy-done.12) | copy-start | bytes 368644
  107.4 1.8 %copy-start.23 = (f32[128]{0:T(128)S(1)}, f32[128]{0:T(128)}, u32[]{:S(2)}) copy-start(f32[128]{0:T(128)} %get-tuple-element.49) | copy-start | bytes 1540
  107.4 1.8 %copy-start.24 = (f32[128]{0:T(128)S(1)}, f32[128]{0:T(128)}, u32[]{:S(2)}) copy-start(f32[128]{0:T(128)} %get-tuple-element.50) | copy-start | bytes 1540
  107.4 1.8 %copy-start.25 = (f32[128]{0:T(128)S(1)}, f32[128]{0:T(128)}, u32[]{:S(2)}) copy-start(f32[128]{0:T(128)} %get-tuple-element.51) | copy-start | bytes 1540
  107.4 1.8 %copy-start.26 = (f32[128]{0:T(128)S(1)}, f32[128]{0:T(128)}, u32[]{:S(2)}) copy-start(f32[128]{0:T(128)} %get-tuple-element.52) | copy-start | bytes 1540
  107.4 1.8 %copy-start.27 = (f32[128]{0:T(128)S(1)}, f32[128]{0:T(128)}, u32[]{:S(2)}) copy-start(f32[128]{0:T(128)} %get-tuple-element.53) | copy-start | bytes 1540
  108.2 15.5 %copy-start.14 = (f32[4,128,128]{1,0,2:T(4,128)S(1)}, f32[4,128,128]{1,0,2:T(4,128)}, u32[]{:S(2)}) copy-start(f32[4,128,128]{1,0,2:T(4,128)} %copy.181) | copy-start | bytes 786436
  108.3 15.5 %copy-start.21 = (f32[16,4]{0,1:T(4,128)S(1)}, f32[16,4]{0,1:T(4,128)}, u32[]{:S(2)}) copy-start(f32[16,4]{0,1:T(4,128)} %copy-done.20) | copy-start | bytes 772

commit v7 on v6

--- a/solution.py
+++ b/solution.py
@@ -71,50 +71,47 @@
 
 
 def tile_grads(row_pack, stat_pack, key_pack):
-    item_count = row_pack.shape[0]
-    block_rows = row_pack.shape[2]
     features = row_pack.shape[3]
     head_width = features // HEADS
     softmax_scale = 1.0 / math.sqrt(head_width)
-    row_heads = row_pack.reshape(item_count, 2, block_rows, HEADS, head_width).transpose(
-        0, 1, 3, 4, 2
-    )
-    key_heads_all = key_pack.reshape(item_count, 2, block_rows, HEADS, head_width).transpose(
-        0, 1, 3, 4, 2
-    )
-    query_heads = row_heads[:, 0]
-    grad_heads = row_heads[:, 1]
-    key_heads = key_heads_all[:, 0]
-    value_heads = key_heads_all[:, 1]
+    head_of = jnp.arange(features, dtype=jnp.int32) // head_width
+    mask = (head_of[None, :] == jnp.arange(HEADS, dtype=jnp.int32)[:, None]).astype(row_pack.dtype)
+
+    def spread(part):
+        return part[:, None] * mask[None, :, None, :]
+
+    query_rows = row_pack[:, 0]
+    grad_rows = row_pack[:, 1]
+    key_rows = key_pack[:, 0]
+    value_rows = key_pack[:, 1]
+    query_heads = spread(query_rows)
+    grad_heads = spread(grad_rows)
+    key_heads = spread(key_rows)
     log_part = stat_pack[:, 0].astype(jnp.float32)
     delta_part = stat_pack[:, 1].astype(jnp.float32)
     scores = (
-        jnp.einsum("shdq,shdk->shqk", query_heads, key_heads, preferred_element_type=jnp.float32)
+        jnp.einsum("shqf,skf->shqk", query_heads, key_rows, preferred_element_type=jnp.float32)
         * softmax_scale
     )
     weights = jnp.exp(scores - log_part[..., None])
     weight_grad = jnp.einsum(
-        "shdq,shdk->shqk", grad_heads, value_heads, preferred_element_type=jnp.float32
+        "shqf,skf->shqk", grad_heads, value_rows, preferred_element_type=jnp.float32
     )
     score_grad = weights * (weight_grad - delta_part[..., None])
     weights_low = weights.astype(jnp.bfloat16)
     score_low = score_grad.astype(jnp.bfloat16)
     value_part = jnp.einsum(
-        "shqk,shdq->shdk", weights_low, grad_heads, preferred_element_type=jnp.float32
+        "shqk,shqf->skf", weights_low, grad_heads, preferred_element_type=jnp.float32
     )
     key_part = (
-        jnp.einsum("shqk,shdq->shdk", score_low, query_heads, preferred_element_type=jnp.float32)
+        jnp.einsum("shqk,shqf->skf", score_low, query_heads, preferred_element_type=jnp.float32)
         * softmax_scale
     )
     query_part = (
-        jnp.einsum("shqk,shdk->shdq", score_low, key_heads, preferred_element_type=jnp.float32)
+        jnp.einsum("shqk,shkf->sqf", score_low, key_heads, preferred_element_type=jnp.float32)
         * softmax_scale
     )
-
-    def points_last(part):
-        return part.reshape(item_count, features, block_rows).transpose(0, 2, 1)
-
-    return (points_last(query_part), points_last(key_part), points_last(value_part))
+    return (query_part, key_part, value_part)
 
 
 def per_device(queries, keys, values, out_attn, out_grad, log_norm, neighbour_blocks, stencil):

time: 128 us -> 116 us (0.906)
  local copies, waits for them, and re-layouts: 29.9 us -> 6.39 us
  waiting for transfers between devices: 31.2 us -> 46 us
    all_to_all x1, waiting for transfers between devices: 0.01 us -> 10.1 us  [gather_sum(): lax.all_to_all(spread, axis, split_axis=0, concat_axis=0, tiled=True)]
    another operation x4 -> x1, local copies, waits for them, and re-layouts: 10.5 us -> 0.74 us  [per_device(): key_pack = jnp.stack([key_blocks, value_blocks], 1)]
    reshape x5 -> x0, local copies, waits for them, and re-layouts: 7.95 us -> none  [points_last(): return part.reshape(item_count, features, block_rows).transpose(0, 2, 1)]
    convert_element_type x3 -> x0, local copies, waits for them, and re-layouts: 3.41 us -> none  [the longest x1 2.06 us: per_device(): query_part.reshape(group_size, item_count * BLOCK, features)]
    all_to_all x1, waiting for transfers between devices: 11.9 us -> 15.1 us  [per_device(): lax.all_to_all(return_pack, 'gy', split_axis=0, concat_axis=0, tiled=True)]
    dot_general x10, matrix products: 15.1 us -> 12.1 us  [the longest x2 2.95 us: tile_grads(): jnp.einsum('shqf,skf->shqk', grad_heads, value_rows, preferred_element_ty...]
    dot_general x1, matrix products: 0.8 us -> 2.63 us  [per_device(): jnp.einsum('sr,sxbf->rxbf', owned, pieces.reshape(slot_count, 2, BLOCK, f...]
    all_to_all x1, waiting for transfers between devices: 19.3 us -> 20.9 us  [per_device(): lax.all_to_all(send_pack, 'gy', split_axis=0, concat_axis=0, tiled=True)]
  transfers between devices with their start and end apart: 5 -> 5, of which waited for: 2 -> 3; matrix products, arithmetic and copies ran while one was open for 34% -> 18% of each run, Pallas kernels for 0% -> 0%
where the time goes in v7:
time: 116 us; the launch traced here: 115 us
  waiting for transfers between devices  46 us (40%)
  starting transfers between devices  34.1 us (29%)
  matrix products  17.9 us (15%)
  other arithmetic  8.9 us (8%)
  local copies, waits for them, and re-layouts  6.39 us (6%)
  between operations  1.39 us (1%)
    all_to_all x1, waiting for transfers between devices, per_device(): lax.all_to_all(send_pack, 'gy', split_axis=0, concat_axis=0, tiled=True)  20.9 us
    all_to_all x1, starting transfers between devices, gather_sum(): lax.all_to_all(spread, axis, split_axis=0, concat_axis=0, tiled=True)  19 us
    all_to_all x1, waiting for transfers between devices, per_device(): lax.all_to_all(return_pack, 'gy', split_axis=0, concat_axis=0, tiled=True)  15.1 us
    all_to_all x1, waiting for transfers between devices, gather_sum(): lax.all_to_all(spread, axis, split_axis=0, concat_axis=0, tiled=True)  10.1 us
    all_to_all x1, starting transfers between devices, per_device(): lax.all_to_all(send_pack, 'gy', split_axis=0, concat_axis=0, tiled=True)  7.12 us
    all_to_all x1, starting transfers between devices, per_device(): lax.all_to_all(return_pack, 'gy', split_axis=0, concat_axis=0, tiled=True)  3.54 us
    dot_general x2, matrix products, tile_grads(): jnp.einsum('shqf,skf->shqk', grad_heads, value_rows, preferred_element_ty...  2.95 us
    dot_general x2, matrix products, tile_grads(): jnp.einsum('shqk,shqf->skf', weights_low, grad_heads, preferred_element_t...  2.8 us
  transfers between devices with their start and end apart: 5, of which 3 were waited for; matrix products, arithmetic and copies ran while one was open for 18% of the time, Pallas kernels for 0%

profile of v7, /device:TPU:6, one launch (start us, length us, event | category | flops | bytes accessed | tf_op | source)
XLA Modules:
  0.0 114.7 jit_solution(1325009352860090351)
XLA Ops:
  0.7 0.8 fusion.140
  1.5 0.8 copy.170
  2.4 0.2 convert_reduce_fusion
  2.6 0.1 fusion.50
  2.8 1.0 convert_multiply_fusion.10
  3.8 0.4 reshape.270
  4.2 0.7 reduce_sum.82
  5.0 0.1 copy.224
  5.2 0.3 fusion.110
  5.5 0.2 fusion.49
  5.7 0.5 fusion.29
  6.2 0.2 copy.220
  6.7 1.1 pad_maximum_fusion.1
  7.9 7.1 %all-to-all-start = ((bf16[8,576,128]{2,1,0:T(8,128)(2,1)}), bf16[8,576,128]{2,1,0:T(8,128)(2,1)S(1)}, u32[]{:S(2)}, u32[]{:S(2)}) async-start(bf16[8,576,128]{2,1,0:T(8,128)(2,1)} %pad_maximum_fusion.1), calls=%async_computation | async-start | bytes 2359296 | tf_op jit(solution)/shard_map/all_to_all | solution.py:181
  15.0 0.6 fusion.138
  15.6 2.0 %collective-permute-start = (bf16[1,32,128]{2,1,0:T(8,128)(2,1)}, bf16[1,32,128]{2,1,0:T(8,128)(2,1)S(1)}, u32[]{:S(2)}, u32[]{:S(2)}) collective-permute-start(bf16[1,32,128]{2,1,0:T(8,128)(2,1)} %get-tuple-element.42), channel_id=1, source_target_pairs={{8,0},{16,8},{24,16},{32,24},{40,32},{48,40},{56,48},{64,56},{72,6... | collective-permute-start | bytes 24584 | tf_op jit(solution)/shard_map/ppermute | solution.py:197
  17.6 2.4 %collective-permute-start.1 = (bf16[1,32,128]{2,1,0:T(8,128)(2,1)}, bf16[1,32,128]{2,1,0:T(8,128)(2,1)S(1)}, u32[]{:S(2)}, u32[]{:S(2)}) collective-permute-start(bf16[1,32,128]{2,1,0:T(8,128)(2,1)} %get-tuple-element.41), channel_id=1, source_target_pairs={{0,8},{8,16},{16,24},{24,32},{32,40},{40,48},{48,56},{56,64},{64,7... | collective-permute-start | bytes 24584 | tf_op jit(solution)/shard_map/ppermute | solution.py:196
  20.1 0.7 copy.182
  20.9 0.4 fusion.33
  21.3 0.3 convolution_bitcast_fusion
  21.7 0.6 slice_bitcast_fusion.14
  22.4 0.4 fusion.46
  22.7 2.0 %fusion.48 = f32[4,128,128]{2,1,0:T(8,128)} fusion(bf16[4,4,128,128]{3,2,1,0:T(8,128)(2,1)S(1)} %fusion.46, bf16[4,128]{1,0:T(4,128)(2,1)S(1)} %fusion.121, bf16[4,128,128]{2,1,0:T(8,128)(2,1)} %copy-done.6), kind=kOutput, calls=%fused_computation.40 | convolution fusion | flops 67436544 | bytes 918528 | tf_op jit(solution)/shard_map/shqk,shqf->skf/dot_general | solution.py:107
  24.7 1.0 fusion.47
  25.7 20.9 %all-to-all-done = bf16[8,576,128]{2,1,0:T(8,128)(2,1)S(1)} async-done(((bf16[8,576,128]{2,1,0:T(8,128)(2,1)}), bf16[8,576,128]{2,1,0:T(8,128)(2,1)S(1)}, u32[]{:S(2)}, u32[]{:S(2)}) %all-to-all-start) | async-done | bytes 1179680 | tf_op jit(solution)/shard_map/all_to_all | solution.py:181
  46.7 0.2 fusion.81
  47.1 0.4 add_reduce_fusion
  47.5 0.8 broadcast_in_dim.19
  48.3 19.0 %all-to-all-start.1 = ((f32[96,5,128]{2,1,0:T(8,128)}), f32[96,5,128]{2,1,0:T(8,128)S(1)}, u32[]{:S(2)}, u32[]{:S(2)}) async-start(f32[96,5,128]{2,1,0:T(8,128)} %broadcast_in_dim.19), calls=%async_computation.1 | async-start | bytes 786432 | tf_op jit(solution)/shard_map/all_to_all | solution.py:69
  67.5 1.5 %fusion.30 = bf16[2,8,256,128]{3,1,2,0:T(8,128)(2,1)S(1)} fusion(bf16[1,4,256,128]{3,2,1,0:T(8,128)(2,1)} %bitcast.201, s32[16]{0:T(128)S(1)} %sub.81), kind=kOutput, calls=%fused_computation.24 | convolution fusion | flops 4718656 | bytes 1310784 | tf_op jit(solution)/shard_map/dot_general | solution.py:225
  69.0 0.2 copy.223
  69.2 0.7 fusion.7
  69.9 2.5 %fusion.24 = f32[16,1,128,128]{3,2,0,1:T(8,128)S(1)} fusion(f32[16,4,128,128]{3,2,1,0:T(8,128)S(1)} %fusion.7, f32[16,4,128]{2,1,0:T(4,128)S(1)} %get-tuple-element.49, bf16[16,128,128]{2,1,0:T(8,128)(2,1)S(1)} %get-tuple-element.33, bf16[4,128]{1,0:T(4,128)(2,1)S(1)} %fusion.121), kind=kOutput, calls=%fused_computation.22 | convolution fusion | flops 272629760 | bytes 5800960 | tf_op jit(solution)/shard_map/shqk,shqf->skf/dot_general | solution.py:103
  72.4 2.6 %multiply_convert_fusion = bf16[16,4,128,128]{3,2,1,0:T(8,128)(2,1)S(1)} fusion(f32[16,4,128,128]{3,2,1,0:T(8,128)S(1)} %fusion.7, f32[16,4,128]{2,1,0:T(4,128)S(1)} %get-tuple-element.50, f32[16,4,128]{2,1,0:T(4,128)S(1)} %get-tuple-element.49, bf16[16,128,128]{2,1,0:T(8,128)(2,1)S(1)} %get-tuple-element.33, bf16[4,128]{1,0:T(4,128)(2,1)S(1)} %fusion.121, ...), kind=kOutput, calls=%fused_computation.2 | convolution fusion | flops 274726912 | bytes 7406592 | tf_op jit(solution)/shard_map/shqf,skf->shqk/dot_general | solution.py:97
  75.0 0.8 fusion.37
  75.8 0.2 pad_maximum_fusion
  76.0 1.5 %fusion.43 = bf16[16,128,128]{2,1,0:T(8,128)(2,1)} fusion(bf16[16,4,128,128]{3,2,1,0:T(8,128)(2,1)S(1)} %multiply_convert_fusion, bf16[16,128,128]{2,1,0:T(8,128)(2,1)S(1)} %slice_bitcast_fusion.4, bf16[4,128]{1,0:T(4,128)(2,1)S(1)} %fusion.121), kind=kOutput, calls=%fused_computation.33 | convolution fusion | flops 270008320 | bytes 3146752 | tf_op jit(solution)/shard_map/shqk,shkf->sqf/dot_general | solution.py:111
  77.5 10.1 %all-to-all-done.1 = f32[96,5,128]{2,1,0:T(8,128)S(1)} async-done(((f32[96,5,128]{2,1,0:T(8,128)}), f32[96,5,128]{2,1,0:T(8,128)S(1)}, u32[]{:S(2)}, u32[]{:S(2)}) %all-to-all-start.1) | async-done | bytes 245792 | tf_op jit(solution)/shard_map/all_to_all | solution.py:69
  87.6 0.1 reduce_sum.88
  87.7 1.9 %pad_maximum_fusion.3 = bf16[8,272,128]{2,1,0:T(8,128)(2,1)} fusion(bf16[8,16,128]{2,1,0:T(8,128)(2,1)S(1)} %broadcast_in_dim.20, bf16[8,256,128]{2,1,0:T(8,128)(2,1)} %bitcast.203), kind=kLoop, calls=%fused_computation.60 | loop fusion | flops 1114112 | bytes 1114112 | tf_op jit(solution)/shard_map/concatenate | solution.py:247
  89.6 3.5 %all-to-all-start.2 = ((bf16[8,272,128]{2,1,0:T(8,128)(2,1)}), bf16[8,272,128]{2,1,0:T(8,128)(2,1)S(1)}, u32[]{:S(2)}, u32[]{:S(2)}) async-start(bf16[8,272,128]{2,1,0:T(8,128)(2,1)} %pad_maximum_fusion.3), calls=%async_computation.2 | async-start | bytes 1114112 | tf_op jit(solution)/shard_map/all_to_all | solution.py:254
  93.3 2.6 %fusion.10 = f32[4,2,128,128]{3,0,2,1:T(4,128)S(1)} fusion(f32[16,2,128,128]{3,2,0,1:T(8,128)S(1)} %pad_maximum_fusion, s32[16]{0:T(128)} %copy-done.18), kind=kOutput, calls=%fused_computation.14 | convolution fusion | flops 25165888 | bytes 2621504 | tf_op jit(solution)/shard_map/sr,sxbf->rxbf/dot_general | solution.py:270
  96.1 0.8 fusion.76
  97.0 0.7 fusion.88
  97.6 15.1 %all-to-all-done.2 = bf16[8,272,128]{2,1,0:T(8,128)(2,1)S(1)} async-done(((bf16[8,272,128]{2,1,0:T(8,128)(2,1)}), bf16[8,272,128]{2,1,0:T(8,128)(2,1)S(1)}, u32[]{:S(2)}, u32[]{:S(2)}) %all-to-all-start.2) | async-done | bytes 557088 | tf_op jit(solution)/shard_map/all_to_all | solution.py:254
  112.8 0.5 fusion.66
  113.4 0.6 broadcast_multiply_fusion
  114.0 0.7 fusion.89
  (97 shorter events, 1.4 us)
Async XLA Ops:
  0.6 5.0 %copy-start = (bf16[16,32,128]{2,1,0:T(8,128)(2,1)S(1)}, bf16[16,32,128]{2,1,0:T(8,128)(2,1)}, u32[]{:S(2)}) copy-start(bf16[16,32,128]{2,1,0:T(8,128)(2,1)} %param.12) | copy-start | bytes 393220
  0.6 4.4 %copy-start.17 = (bf16[4,16,32]{2,1,0:T(8,128)(2,1)S(1)}, bf16[4,16,32]{2,1,0:T(8,128)(2,1)}, u32[]{:S(2)}) copy-start(bf16[4,16,32]{2,1,0:T(8,128)(2,1)} %param.13) | copy-start | bytes 12292
  0.7 5.0 %copy-start.4 = (bf16[16,32,128]{2,1,0:T(8,128)(2,1)S(1)}, bf16[16,32,128]{2,1,0:T(8,128)(2,1)}, u32[]{:S(2)}) copy-start(bf16[16,32,128]{2,1,0:T(8,128)(2,1)} %param.8) | copy-start | bytes 393220
  5.4 1.1 copy-start.15
  6.6 1.3 %copy-start.1 = (bf16[16,32,128]{2,1,0:T(8,128)(2,1)S(1)}, bf16[16,32,128]{2,1,0:T(8,128)(2,1)}, u32[]{:S(2)}) copy-start(bf16[16,32,128]{2,1,0:T(8,128)(2,1)} %param.10) | copy-start | bytes 393220
  6.6 1.3 %copy-start.5 = (bf16[16,32,128]{2,1,0:T(8,128)(2,1)S(1)}, bf16[16,32,128]{2,1,0:T(8,128)(2,1)}, u32[]{:S(2)}) copy-start(bf16[16,32,128]{2,1,0:T(8,128)(2,1)} %param.9) | copy-start | bytes 393220
  7.9 38.7 %all-to-all-start = ((bf16[8,576,128]{2,1,0:T(8,128)(2,1)}), bf16[8,576,128]{2,1,0:T(8,128)(2,1)S(1)}, u32[]{:S(2)}, u32[]{:S(2)}) async-start(bf16[8,576,128]{2,1,0:T(8,128)(2,1)} %pad_maximum_fusion.1), calls=%async_computation | async-start | bytes 2359296 | tf_op jit(solution)/shard_map/all_to_all | solution.py:181
  15.6 6.1 %copy-start.24 = (f32[5,128]{1,0:T(8,128)S(1)}, f32[5,128]{1,0:T(8,128)}, u32[]{:S(2)}) copy-start(f32[5,128]{1,0:T(8,128)} %param.15) | copy-start | bytes 7684
  15.6 31.1 %collective-permute-start = (bf16[1,32,128]{2,1,0:T(8,128)(2,1)}, bf16[1,32,128]{2,1,0:T(8,128)(2,1)S(1)}, u32[]{:S(2)}, u32[]{:S(2)}) collective-permute-start(bf16[1,32,128]{2,1,0:T(8,128)(2,1)} %get-tuple-element.42), channel_id=1, source_target_pairs={{8,0},{16,8},{24,16},{32,24},{40,32},{48,40},{56,48},{64,56},{72,6... | collective-permute-start | bytes 24584 | tf_op jit(solution)/shard_map/ppermute | solution.py:197
  17.6 29.1 %collective-permute-start.1 = (bf16[1,32,128]{2,1,0:T(8,128)(2,1)}, bf16[1,32,128]{2,1,0:T(8,128)(2,1)S(1)}, u32[]{:S(2)}, u32[]{:S(2)}) collective-permute-start(bf16[1,32,128]{2,1,0:T(8,128)(2,1)} %get-tuple-element.41), channel_id=1, source_target_pairs={{0,8},{8,16},{16,24},{24,32},{32,40},{40,48},{48,56},{56,64},{64,7... | collective-permute-start | bytes 24584 | tf_op jit(solution)/shard_map/ppermute | solution.py:196
  20.9 1.4 %copy-start.6 = (bf16[4,128,128]{2,1,0:T(8,128)(2,1)}, bf16[4,128,128]{2,1,0:T(8,128)(2,1)S(1)}, u32[]{:S(2)}) copy-start(bf16[4,128,128]{2,1,0:T(8,128)(2,1)S(1)} %get-tuple-element.38) | copy-start | bytes 393220
  46.7 1.6 %copy-start.7 = (bf16[16,1,128]{2,1,0:T(2,128)(2,1)}, bf16[16,1,128]{2,1,0:T(2,128)(2,1)S(1)}, u32[]{:S(2)}) copy-start(bf16[16,1,128]{2,1,0:T(2,128)(2,1)S(1)} %copy.181) | copy-start | bytes 12292
  46.7 1.6 %copy-start.9 = (bf16[16,1,128]{2,1,0:T(2,128)(2,1)}, bf16[16,1,128]{2,1,0:T(2,128)(2,1)S(1)}, u32[]{:S(2)}) copy-start(bf16[16,1,128]{2,1,0:T(2,128)(2,1)S(1)} %copy.180) | copy-start | bytes 12292
  46.7 1.5 %copy-start.11 = (bf16[1,32,128]{2,1,0:T(8,128)(2,1)}, bf16[1,32,128]{2,1,0:T(8,128)(2,1)S(1)}, u32[]{:S(2)}) copy-start(bf16[1,32,128]{2,1,0:T(8,128)(2,1)S(1)} %collective-permute-done) | copy-start | bytes 24580
  46.7 1.5 %copy-start.13 = (bf16[1,32,128]{2,1,0:T(8,128)(2,1)}, bf16[1,32,128]{2,1,0:T(8,128)(2,1)S(1)}, u32[]{:S(2)}) copy-start(bf16[1,32,128]{2,1,0:T(8,128)(2,1)S(1)} %collective-permute-done.1) | copy-start | bytes 24580
  48.3 39.4 %all-to-all-start.1 = ((f32[96,5,128]{2,1,0:T(8,128)}), f32[96,5,128]{2,1,0:T(8,128)S(1)}, u32[]{:S(2)}, u32[]{:S(2)}) async-start(f32[96,5,128]{2,1,0:T(8,128)} %broadcast_in_dim.19), calls=%async_computation.1 | async-start | bytes 786432 | tf_op jit(solution)/shard_map/all_to_all | solution.py:69
  67.5 4.9 %copy-start.18 = (s32[16]{0:T(128)}, s32[16]{0:T(128)S(1)}, u32[]{:S(2)}) copy-start(s32[16]{0:T(128)S(1)} %sub.81) | copy-start | bytes 196
  89.6 23.1 %all-to-all-start.2 = ((bf16[8,272,128]{2,1,0:T(8,128)(2,1)}), bf16[8,272,128]{2,1,0:T(8,128)(2,1)S(1)}, u32[]{:S(2)}, u32[]{:S(2)}) async-start(bf16[8,272,128]{2,1,0:T(8,128)(2,1)} %pad_maximum_fusion.3), calls=%async_computation.2 | async-start | bytes 1114112 | tf_op jit(solution)/shard_map/all_to_all | solution.py:254
  93.2 2.8 %copy-start.8 = (bf16[16,1,128]{2,1,0:T(2,128)(2,1)S(1)}, bf16[16,1,128]{2,1,0:T(2,128)(2,1)}, u32[]{:S(2)}) copy-start(bf16[16,1,128]{2,1,0:T(2,128)(2,1)} %copy-done.7) | copy-start | bytes 12292
  93.2 2.8 %copy-start.10 = (bf16[16,1,128]{2,1,0:T(2,128)(2,1)S(1)}, bf16[16,1,128]{2,1,0:T(2,128)(2,1)}, u32[]{:S(2)}) copy-start(bf16[16,1,128]{2,1,0:T(2,128)(2,1)} %copy-done.9) | copy-start | bytes 12292
  93.2 2.8 %copy-start.12 = (bf16[1,32,128]{2,1,0:T(8,128)(2,1)S(1)}, bf16[1,32,128]{2,1,0:T(8,128)(2,1)}, u32[]{:S(2)}) copy-start(bf16[1,32,128]{2,1,0:T(8,128)(2,1)} %copy-done.11) | copy-start | bytes 24580
  93.2 2.8 %copy-start.14 = (bf16[1,32,128]{2,1,0:T(8,128)(2,1)S(1)}, bf16[1,32,128]{2,1,0:T(8,128)(2,1)}, u32[]{:S(2)}) copy-start(bf16[1,32,128]{2,1,0:T(8,128)(2,1)} %copy-done.13) | copy-start | bytes 24580
  93.2 2.8 %copy-start.19 = (f32[128]{0:T(128)S(1)}, f32[128]{0:T(128)}, u32[]{:S(2)}) copy-start(f32[128]{0:T(128)} %get-tuple-element.53) | copy-start | bytes 1540
  93.2 2.8 %copy-start.20 = (f32[128]{0:T(128)S(1)}, f32[128]{0:T(128)}, u32[]{:S(2)}) copy-start(f32[128]{0:T(128)} %get-tuple-element.54) | copy-start | bytes 1540
  93.2 2.8 %copy-start.21 = (f32[128]{0:T(128)S(1)}, f32[128]{0:T(128)}, u32[]{:S(2)}) copy-start(f32[128]{0:T(128)} %get-tuple-element.55) | copy-start | bytes 1540
  93.3 2.8 %copy-start.22 = (f32[128]{0:T(128)S(1)}, f32[128]{0:T(128)}, u32[]{:S(2)}) copy-start(f32[128]{0:T(128)} %get-tuple-element.56) | copy-start | bytes 1540
  93.3 2.8 %copy-start.23 = (f32[128]{0:T(128)S(1)}, f32[128]{0:T(128)}, u32[]{:S(2)}) copy-start(f32[128]{0:T(128)} %get-tuple-element.57) | copy-start | bytes 1540
  95.9 1.1 copy-start.3
  95.9 16.9 %copy-start.16 = (f32[16,4]{0,1:T(4,128)S(1)}, f32[16,4]{0,1:T(4,128)}, u32[]{:S(2)}) copy-start(f32[16,4]{0,1:T(4,128)} %copy-done.15) | copy-start | bytes 772
  96.0 18.0 %copy-start.2 = (f32[4,128,128]{2,1,0:T(8,128)S(1)}, f32[4,128,128]{2,1,0:T(8,128)}, u32[]{:S(2)}) copy-start(f32[4,128,128]{2,1,0:T(8,128)} %fusion.47) | copy-start | bytes 786436

commit v8 on v7

--- a/solution.py
+++ b/solution.py
@@ -7,20 +7,9 @@
 
 BLOCK = 128
 HEADS = 4
-
-
-def with_halo(block, sides, width):
-    for axis, dim in sides:
-        count = lax.axis_size(axis)
-        forward = [(i, i + 1) for i in range(count - 1)]
-        forward.append((count - 1, 0))
-        backward = [(target, source) for source, target in forward]
-        low = lax.ppermute(
-            lax.slice_in_dim(block, block.shape[dim] - width, None, axis=dim), axis, forward
-        )
-        high = lax.ppermute(lax.slice_in_dim(block, 0, width, axis=dim), axis, backward)
-        block = jnp.concatenate([low, block, high], axis=dim)
-    return block
+OUTER = "gx_outer"
+INNER = "gx_inner"
+PLANE = 8
 
 
 def prime_factors(count):
@@ -134,7 +123,7 @@
     stat_blocks = jnp.stack([norm_blocks, delta], 1)
     row_pack = jnp.stack([query_blocks, grad_blocks], 1)
     key_pack = jnp.stack([key_blocks, value_blocks], 1)
-    point_count = tile_x * tile_y * lax.axis_size("gx") * group_size
+    point_count = tile_x * tile_y * (lax.axis_size(OUTER) * lax.axis_size(INNER)) * group_size
     columns = neighbour_blocks.reshape(pair_count)
     owners = columns // row_blocks
     inner = columns % row_blocks
@@ -190,11 +179,11 @@
     before_col = before_col[tile_x:]
     after_col = after_col[:tile_x]
     grad_x, values_x = lax.optimization_barrier((out_grad, values))
-    count_x = lax.axis_size("gx")
+    count_x = (lax.axis_size(OUTER) * lax.axis_size(INNER))
     ahead = [(i, (i + 1) % count_x) for i in range(count_x)]
     behind = [((i + 1) % count_x, i) for i in range(count_x)]
-    from_before = lax.ppermute(grad_x[tile_x - 1 :], "gx", ahead)
-    from_after = lax.ppermute(grad_x[:1], "gx", behind)
+    from_before = lax.ppermute(grad_x[tile_x - 1 :], (OUTER, INNER), ahead)
+    from_after = lax.ppermute(grad_x[:1], (OUTER, INNER), behind)
     moved = [
         grad_x.astype(jnp.float32),
         jnp.concatenate([grad_x[1:], from_after], 0).astype(jnp.float32),
@@ -212,7 +201,7 @@
     point_count = tile_x * tile_y * count_x * group_size
     pack_in = pack_in[:, : capacity * slot_rows].reshape(group_size, capacity, slot_rows, features)
     partial_rows, pack_in = lax.optimization_barrier((partial_rows, pack_in))
-    column_sum = gather_sum(partial_rows, "gx")
+    column_sum = gather_sum(gather_sum(partial_rows, INNER), OUTER)
     rows_in = pack_in[:, :, :row_count].reshape(group_size, capacity, 2, BLOCK, features)
     stats_in = pack_in[:, :, row_count : row_count + 2 * HEADS].reshape(
         group_size, capacity, 2, HEADS, BLOCK
@@ -283,20 +272,26 @@
 
 
 def solution(mesh):
+    rows = mesh.shape["gx"]
+    inner = PLANE if rows % PLANE == 0 else 1
+    fine = jax.sharding.Mesh(
+        mesh.devices.reshape(rows // inner, inner, mesh.shape["gy"]), (OUTER, INNER, "gy")
+    )
+    split = (OUTER, INNER)
     placed = (
-        P("gx", "gy", None),
-        P("gx", "gy", None),
-        P("gx", "gy", None),
-        P("gx", "gy", None),
-        P("gx", "gy", None),
-        P(None, "gx", "gy"),
-        P("gx", "gy", None),
+        P(split, "gy", None),
+        P(split, "gy", None),
+        P(split, "gy", None),
+        P(split, "gy", None),
+        P(split, "gy", None),
+        P(None, split, "gy"),
+        P(split, "gy", None),
         P(),
     )
     return jax.shard_map(
         per_device,
-        mesh=mesh,
+        mesh=fine,
         in_specs=placed,
-        out_specs=(P("gx", "gy", None), P("gx", "gy", None), P("gx", "gy", None), P()),
+        out_specs=(P(split, "gy", None), P(split, "gy", None), P(split, "gy", None), P()),
         check_vma=False,
     )

time: 116 us -> 118 us (1.017)
  other arithmetic: 8.9 us -> 11.7 us
  waiting for transfers between devices: 46 us -> 44.3 us
    all_to_all x1, waiting for transfers between devices: 15.1 us -> 12.6 us  [per_device(): lax.all_to_all(return_pack, 'gy', split_axis=0, concat_axis=0, tiled=True)]
    all_to_all x1, waiting for transfers between devices: 20.9 us -> 22.5 us  [per_device(): lax.all_to_all(send_pack, 'gy', split_axis=0, concat_axis=0, tiled=True)]
    another operation x1, other arithmetic: 0.19 us -> 1.68 us  [per_device(): jnp.stack([key_part, value_part], 2)]
    reduce_sum x1 -> x2, other arithmetic: 0.11 us -> 1.59 us  [gather_sum(): return jnp.sum(parts, axis=0)]
    dot_general x2, matrix products: 2.8 us -> 4.01 us  [tile_grads(): jnp.einsum('shqk,shqf->skf', weights_low, grad_heads, preferred_element_t...]
    all_to_all x1 -> x2, starting transfers between devices: 19 us -> 19.9 us  [gather_sum(): lax.all_to_all(spread, axis, split_axis=0, concat_axis=0, tiled=True)]
    all_to_all x1 -> x2, waiting for transfers between devices: 10.1 us -> 9.24 us  [gather_sum(): lax.all_to_all(spread, axis, split_axis=0, concat_axis=0, tiled=True)]
  transfers between devices with their start and end apart: 5 -> 6, of which waited for: 3 -> 3; matrix products, arithmetic and copies ran while one was open for 18% -> 19% of each run, Pallas kernels for 0% -> 0%
where the time goes in v8:
time: 118 us; the launch traced here: 117 us
  waiting for transfers between devices  44.3 us (38%)
  starting transfers between devices  35.2 us (30%)
  matrix products  17.4 us (15%)
  other arithmetic  11.7 us (10%)
  local copies, waits for them, and re-layouts  7.24 us (6%)
  between operations  1.43 us (1%)
    all_to_all x1, waiting for transfers between devices, per_device(): lax.all_to_all(send_pack, 'gy', split_axis=0, concat_axis=0, tiled=True)  22.5 us
    all_to_all x2, starting transfers between devices, gather_sum(): lax.all_to_all(spread, axis, split_axis=0, concat_axis=0, tiled=True)  19.9 us
    all_to_all x1, waiting for transfers between devices, per_device(): lax.all_to_all(return_pack, 'gy', split_axis=0, concat_axis=0, tiled=True)  12.6 us
    all_to_all x2, waiting for transfers between devices, gather_sum(): lax.all_to_all(spread, axis, split_axis=0, concat_axis=0, tiled=True)  9.24 us
    all_to_all x1, starting transfers between devices, per_device(): lax.all_to_all(send_pack, 'gy', split_axis=0, concat_axis=0, tiled=True)  7.12 us
    dot_general x2, matrix products, tile_grads(): jnp.einsum('shqk,shqf->skf', weights_low, grad_heads, preferred_element_t...  4.01 us
    all_to_all x1, starting transfers between devices, per_device(): lax.all_to_all(return_pack, 'gy', split_axis=0, concat_axis=0, tiled=True)  3.72 us
    dot_general x2, matrix products, tile_grads(): jnp.einsum('shqf,skf->shqk', grad_heads, value_rows, preferred_element_ty...  2.93 us
  transfers between devices with their start and end apart: 6, of which 3 were waited for; matrix products, arithmetic and copies ran while one was open for 19% of the time, Pallas kernels for 0%

profile of v8, /device:TPU:6, one launch (start us, length us, event | category | flops | bytes accessed | tf_op | source)
XLA Modules:
  0.0 117.3 jit_solution(7694588517143257411)
XLA Ops:
  0.7 0.8 fusion.140
  1.5 0.8 copy.173
  2.8 1.0 convert_multiply_fusion.10
  3.8 0.4 reshape.271
  4.2 0.7 reduce_sum.91
  5.2 0.3 fusion.110
  5.5 0.2 fusion.49
  5.7 0.5 fusion.29
  6.7 1.1 pad_maximum_fusion.1
  7.9 7.1 %all-to-all-start = ((bf16[8,576,128]{2,1,0:T(8,128)(2,1)}), bf16[8,576,128]{2,1,0:T(8,128)(2,1)S(1)}, u32[]{:S(2)}, u32[]{:S(2)}) async-start(bf16[8,576,128]{2,1,0:T(8,128)(2,1)} %pad_maximum_fusion.1), calls=%async_computation | async-start | bytes 2359296 | tf_op jit(solution)/shard_map/all_to_all | solution.py:170
  15.0 0.6 fusion.138
  15.6 2.0 %collective-permute-start = (bf16[1,32,128]{2,1,0:T(8,128)(2,1)}, bf16[1,32,128]{2,1,0:T(8,128)(2,1)S(1)}, u32[]{:S(2)}, u32[]{:S(2)}) collective-permute-start(bf16[1,32,128]{2,1,0:T(8,128)(2,1)} %get-tuple-element.42), channel_id=1, source_target_pairs={{8,0},{16,8},{24,16},{32,24},{40,32},{48,40},{56,48},{64,56},{72,6... | collective-permute-start | bytes 24584 | tf_op jit(solution)/shard_map/ppermute | solution.py:186
  17.6 2.4 %collective-permute-start.1 = (bf16[1,32,128]{2,1,0:T(8,128)(2,1)}, bf16[1,32,128]{2,1,0:T(8,128)(2,1)S(1)}, u32[]{:S(2)}, u32[]{:S(2)}) collective-permute-start(bf16[1,32,128]{2,1,0:T(8,128)(2,1)} %get-tuple-element.41), channel_id=1, source_target_pairs={{0,8},{8,16},{16,24},{24,32},{32,40},{40,48},{48,56},{56,64},{64,7... | collective-permute-start | bytes 24584 | tf_op jit(solution)/shard_map/ppermute | solution.py:185
  20.2 0.4 fusion.33
  20.6 0.3 convolution_bitcast_fusion
  21.0 0.6 slice_bitcast_fusion.14
  21.7 0.4 fusion.46
  22.0 1.0 fusion.48
  23.1 1.0 fusion.47
  24.1 22.5 %all-to-all-done = bf16[8,576,128]{2,1,0:T(8,128)(2,1)S(1)} async-done(((bf16[8,576,128]{2,1,0:T(8,128)(2,1)}), bf16[8,576,128]{2,1,0:T(8,128)(2,1)S(1)}, u32[]{:S(2)}, u32[]{:S(2)}) %all-to-all-start) | async-done | bytes 1179680 | tf_op jit(solution)/shard_map/all_to_all | solution.py:170
  46.7 1.1 fusion.81
  48.0 0.4 add_reduce_fusion
  48.4 0.6 broadcast_in_dim.21
  49.0 4.8 %all-to-all-start.1 = ((f32[8,5,128]{2,1,0:T(8,128)}), f32[8,5,128]{2,1,0:T(8,128)}, u32[]{:S(2)}, u32[]{:S(2)}) async-start(f32[8,5,128]{2,1,0:T(8,128)} %broadcast_in_dim.21), calls=%async_computation.1 | async-start | bytes 65536 | tf_op jit(solution)/shard_map/all_to_all | solution.py:58
  53.8 0.9 slice_bitcast_fusion.2
  54.8 0.5 fusion.30
  55.3 0.2 copy.228
  55.6 0.7 fusion.7
  56.3 0.3 copy-done.1
  56.6 3.7 %fusion.24 = f32[16,1,128,128]{3,2,0,1:T(8,128)} fusion(f32[16,4,128,128]{3,2,1,0:T(8,128)S(1)} %fusion.7, f32[16,4,128]{2,1,0:T(4,128)S(1)} %get-tuple-element.49, bf16[16,128,128]{2,1,0:T(8,128)(2,1)S(1)} %copy-done.1, bf16[4,128]{1,0:T(4,128)(2,1)S(1)} %copy-done.19), kind=kOutput, calls=%fused_computation.22 | convolution fusion | flops 272629760 | bytes 5800960 | tf_op jit(solution)/shard_map/shqk,shqf->skf/dot_general | solution.py:92
  60.3 2.6 %multiply_convert_fusion = bf16[16,4,128,128]{3,2,1,0:T(8,128)(2,1)S(1)} fusion(f32[16,4,128,128]{3,2,1,0:T(8,128)S(1)} %fusion.7, f32[16,4,128]{2,1,0:T(4,128)S(1)} %get-tuple-element.50, f32[16,4,128]{2,1,0:T(4,128)S(1)} %get-tuple-element.49, bf16[16,128,128]{2,1,0:T(8,128)(2,1)S(1)} %copy-done.1, bf16[4,128]{1,0:T(4,128)(2,1)S(1)} %copy-done.19, ...), kind=kOutput, calls=%fused_computation.2 | convolution fusion | flops 274726912 | bytes 7406592 | tf_op jit(solution)/shard_map/shqf,skf->shqk/dot_general | solution.py:86
  62.8 0.7 fusion.43
  63.5 1.8 %fusion.37 = f32[16,1,128,128]{3,2,0,1:T(8,128)} fusion(bf16[16,4,128,128]{3,2,1,0:T(8,128)(2,1)S(1)} %multiply_convert_fusion, bf16[4,128]{1,0:T(4,128)(2,1)S(1)} %copy-done.19, bf16[16,128,128]{2,1,0:T(8,128)(2,1)S(1)} %get-tuple-element.34), kind=kOutput, calls=%fused_computation.31 | convolution fusion | flops 269746176 | bytes 3671040 | tf_op jit(solution)/shard_map/shqk,shqf->skf/dot_general | solution.py:96
  65.4 0.8 reduce_sum.97
  66.1 0.6 broadcast_in_dim.22
  66.8 15.2 %all-to-all-start.2 = ((f32[12,5,128]{2,1,0:T(8,128)}), f32[12,5,128]{2,1,0:T(8,128)}, u32[]{:S(2)}, u32[]{:S(2)}) async-start(f32[12,5,128]{2,1,0:T(8,128)} %broadcast_in_dim.22), calls=%async_computation.2 | async-start | bytes 98304 | tf_op jit(solution)/shard_map/all_to_all | solution.py:58
  81.9 1.7 %pad_maximum_fusion = f32[16,2,128,128]{3,2,0,1:T(8,128)S(1)} fusion(f32[16,1,128,128]{3,2,0,1:T(8,128)} %fusion.24, f32[16,1,128,128]{3,2,0,1:T(8,128)} %fusion.37), kind=kLoop, calls=%fused_computation.13 | loop fusion | flops 524288 | bytes 4194304 | tf_op jit(solution)/shard_map/stack | solution.py:248
  83.6 9.2 %all-to-all-done.2 = f32[12,5,128]{2,1,0:T(8,128)} async-done(((f32[12,5,128]{2,1,0:T(8,128)}), f32[12,5,128]{2,1,0:T(8,128)}, u32[]{:S(2)}, u32[]{:S(2)}) %all-to-all-start.2) | async-done | bytes 30752 | tf_op jit(solution)/shard_map/all_to_all | solution.py:58
  92.9 0.8 reduce_sum.98
  93.7 0.9 pad_maximum_fusion.3
  94.6 3.7 %all-to-all-start.3 = ((bf16[8,272,128]{2,1,0:T(8,128)(2,1)}), bf16[8,272,128]{2,1,0:T(8,128)(2,1)S(1)}, u32[]{:S(2)}, u32[]{:S(2)}) async-start(bf16[8,272,128]{2,1,0:T(8,128)(2,1)} %pad_maximum_fusion.3), calls=%async_computation.3 | async-start | bytes 1114112 | tf_op jit(solution)/shard_map/all_to_all | solution.py:243
  98.4 2.6 %fusion.10 = f32[4,2,128,128]{3,0,2,1:T(4,128)S(1)} fusion(f32[16,2,128,128]{3,2,0,1:T(8,128)S(1)} %pad_maximum_fusion, s32[16]{0:T(128)} %copy-done.20), kind=kOutput, calls=%fused_computation.14 | convolution fusion | flops 25165888 | bytes 2621504 | tf_op jit(solution)/shard_map/sr,sxbf->rxbf/dot_general | solution.py:259
  101.2 0.8 fusion.76
  102.1 0.7 fusion.88
  102.8 12.6 %all-to-all-done.3 = bf16[8,272,128]{2,1,0:T(8,128)(2,1)S(1)} async-done(((bf16[8,272,128]{2,1,0:T(8,128)(2,1)}), bf16[8,272,128]{2,1,0:T(8,128)(2,1)S(1)}, u32[]{:S(2)}, u32[]{:S(2)}) %all-to-all-start.3) | async-done | bytes 557088 | tf_op jit(solution)/shard_map/all_to_all | solution.py:243
  115.4 0.6 fusion.66
  116.1 0.6 broadcast_multiply_fusion
  116.7 0.7 fusion.89
  (105 shorter events, 2.0 us)
Async XLA Ops:
  0.6 5.0 %copy-start = (bf16[16,32,128]{2,1,0:T(8,128)(2,1)S(1)}, bf16[16,32,128]{2,1,0:T(8,128)(2,1)}, u32[]{:S(2)}) copy-start(bf16[16,32,128]{2,1,0:T(8,128)(2,1)} %param.12) | copy-start | bytes 393220
  0.6 4.4 %copy-start.17 = (bf16[4,16,32]{2,1,0:T(8,128)(2,1)S(1)}, bf16[4,16,32]{2,1,0:T(8,128)(2,1)}, u32[]{:S(2)}) copy-start(bf16[4,16,32]{2,1,0:T(8,128)(2,1)} %param.13) | copy-start | bytes 12292
  0.7 5.0 %copy-start.5 = (bf16[16,32,128]{2,1,0:T(8,128)(2,1)S(1)}, bf16[16,32,128]{2,1,0:T(8,128)(2,1)}, u32[]{:S(2)}) copy-start(bf16[16,32,128]{2,1,0:T(8,128)(2,1)} %param.8) | copy-start | bytes 393220
  5.4 1.1 copy-start.15
  6.6 1.3 %copy-start.2 = (bf16[16,32,128]{2,1,0:T(8,128)(2,1)S(1)}, bf16[16,32,128]{2,1,0:T(8,128)(2,1)}, u32[]{:S(2)}) copy-start(bf16[16,32,128]{2,1,0:T(8,128)(2,1)} %param.10) | copy-start | bytes 393220
  6.6 1.3 %copy-start.6 = (bf16[16,32,128]{2,1,0:T(8,128)(2,1)S(1)}, bf16[16,32,128]{2,1,0:T(8,128)(2,1)}, u32[]{:S(2)}) copy-start(bf16[16,32,128]{2,1,0:T(8,128)(2,1)} %param.9) | copy-start | bytes 393220
  7.9 38.7 %all-to-all-start = ((bf16[8,576,128]{2,1,0:T(8,128)(2,1)}), bf16[8,576,128]{2,1,0:T(8,128)(2,1)S(1)}, u32[]{:S(2)}, u32[]{:S(2)}) async-start(bf16[8,576,128]{2,1,0:T(8,128)(2,1)} %pad_maximum_fusion.1), calls=%async_computation | async-start | bytes 2359296 | tf_op jit(solution)/shard_map/all_to_all | solution.py:170
  15.6 5.4 %copy-start.26 = (f32[5,128]{1,0:T(8,128)S(1)}, f32[5,128]{1,0:T(8,128)}, u32[]{:S(2)}) copy-start(f32[5,128]{1,0:T(8,128)} %param.15) | copy-start | bytes 7684
  15.6 31.1 %collective-permute-start = (bf16[1,32,128]{2,1,0:T(8,128)(2,1)}, bf16[1,32,128]{2,1,0:T(8,128)(2,1)S(1)}, u32[]{:S(2)}, u32[]{:S(2)}) collective-permute-start(bf16[1,32,128]{2,1,0:T(8,128)(2,1)} %get-tuple-element.42), channel_id=1, source_target_pairs={{8,0},{16,8},{24,16},{32,24},{40,32},{48,40},{56,48},{64,56},{72,6... | collective-permute-start | bytes 24584 | tf_op jit(solution)/shard_map/ppermute | solution.py:186
  17.6 29.1 %collective-permute-start.1 = (bf16[1,32,128]{2,1,0:T(8,128)(2,1)}, bf16[1,32,128]{2,1,0:T(8,128)(2,1)S(1)}, u32[]{:S(2)}, u32[]{:S(2)}) collective-permute-start(bf16[1,32,128]{2,1,0:T(8,128)(2,1)} %get-tuple-element.41), channel_id=1, source_target_pairs={{0,8},{8,16},{16,24},{24,32},{32,40},{40,48},{48,56},{56,64},{64,7... | collective-permute-start | bytes 24584 | tf_op jit(solution)/shard_map/ppermute | solution.py:185
  20.1 3.0 %copy-start.18 = (bf16[4,128]{1,0:T(4,128)(2,1)}, bf16[4,128]{1,0:T(4,128)(2,1)S(1)}, u32[]{:S(2)}) copy-start(bf16[4,128]{1,0:T(4,128)(2,1)S(1)} %fusion.121) | copy-start | bytes 3076
  46.7 8.0 %copy-start.7 = (bf16[16,1,128]{2,1,0:T(2,128)(2,1)}, bf16[16,1,128]{2,1,0:T(2,128)(2,1)S(1)}, u32[]{:S(2)}) copy-start(bf16[16,1,128]{2,1,0:T(2,128)(2,1)S(1)} %copy.184) | copy-start | bytes 12292
  46.7 8.0 %copy-start.9 = (bf16[16,1,128]{2,1,0:T(2,128)(2,1)}, bf16[16,1,128]{2,1,0:T(2,128)(2,1)S(1)}, u32[]{:S(2)}) copy-start(bf16[16,1,128]{2,1,0:T(2,128)(2,1)S(1)} %copy.183) | copy-start | bytes 12292
  46.7 1.3 %copy-start.11 = (bf16[1,32,128]{2,1,0:T(8,128)(2,1)}, bf16[1,32,128]{2,1,0:T(8,128)(2,1)S(1)}, u32[]{:S(2)}) copy-start(bf16[1,32,128]{2,1,0:T(8,128)(2,1)S(1)} %collective-permute-done) | copy-start | bytes 24580
  46.7 1.3 %copy-start.13 = (bf16[1,32,128]{2,1,0:T(8,128)(2,1)}, bf16[1,32,128]{2,1,0:T(8,128)(2,1)S(1)}, u32[]{:S(2)}) copy-start(bf16[1,32,128]{2,1,0:T(8,128)(2,1)S(1)} %collective-permute-done.1) | copy-start | bytes 24580
  49.0 16.4 %all-to-all-start.1 = ((f32[8,5,128]{2,1,0:T(8,128)}), f32[8,5,128]{2,1,0:T(8,128)}, u32[]{:S(2)}, u32[]{:S(2)}) async-start(f32[8,5,128]{2,1,0:T(8,128)} %broadcast_in_dim.21), calls=%async_computation.1 | async-start | bytes 65536 | tf_op jit(solution)/shard_map/all_to_all | solution.py:58
  54.7 0.8 copy-start.20
  54.7 0.8 copy-start.19
  55.5 1.0 copy-start.1
  66.8 26.1 %all-to-all-start.2 = ((f32[12,5,128]{2,1,0:T(8,128)}), f32[12,5,128]{2,1,0:T(8,128)}, u32[]{:S(2)}, u32[]{:S(2)}) async-start(f32[12,5,128]{2,1,0:T(8,128)} %broadcast_in_dim.22), calls=%async_computation.2 | async-start | bytes 98304 | tf_op jit(solution)/shard_map/all_to_all | solution.py:58
  94.6 20.8 %all-to-all-start.3 = ((bf16[8,272,128]{2,1,0:T(8,128)(2,1)}), bf16[8,272,128]{2,1,0:T(8,128)(2,1)S(1)}, u32[]{:S(2)}, u32[]{:S(2)}) async-start(bf16[8,272,128]{2,1,0:T(8,128)(2,1)} %pad_maximum_fusion.3), calls=%async_computation.3 | async-start | bytes 1114112 | tf_op jit(solution)/shard_map/all_to_all | solution.py:243
  98.3 2.9 %copy-start.8 = (bf16[16,1,128]{2,1,0:T(2,128)(2,1)S(1)}, bf16[16,1,128]{2,1,0:T(2,128)(2,1)}, u32[]{:S(2)}) copy-start(bf16[16,1,128]{2,1,0:T(2,128)(2,1)} %copy-done.7) | copy-start | bytes 12292
  98.3 2.9 %copy-start.10 = (bf16[16,1,128]{2,1,0:T(2,128)(2,1)S(1)}, bf16[16,1,128]{2,1,0:T(2,128)(2,1)}, u32[]{:S(2)}) copy-start(bf16[16,1,128]{2,1,0:T(2,128)(2,1)} %copy-done.9) | copy-start | bytes 12292
  98.3 2.9 %copy-start.12 = (bf16[1,32,128]{2,1,0:T(8,128)(2,1)S(1)}, bf16[1,32,128]{2,1,0:T(8,128)(2,1)}, u32[]{:S(2)}) copy-start(bf16[1,32,128]{2,1,0:T(8,128)(2,1)} %copy-done.11) | copy-start | bytes 24580
  98.3 2.9 %copy-start.14 = (bf16[1,32,128]{2,1,0:T(8,128)(2,1)S(1)}, bf16[1,32,128]{2,1,0:T(8,128)(2,1)}, u32[]{:S(2)}) copy-start(bf16[1,32,128]{2,1,0:T(8,128)(2,1)} %copy-done.13) | copy-start | bytes 24580
  98.3 2.9 %copy-start.21 = (f32[128]{0:T(128)S(1)}, f32[128]{0:T(128)}, u32[]{:S(2)}) copy-start(f32[128]{0:T(128)} %get-tuple-element.53) | copy-start | bytes 1540
  98.3 2.9 %copy-start.22 = (f32[128]{0:T(128)S(1)}, f32[128]{0:T(128)}, u32[]{:S(2)}) copy-start(f32[128]{0:T(128)} %get-tuple-element.54) | copy-start | bytes 1540
  98.4 2.9 %copy-start.23 = (f32[128]{0:T(128)S(1)}, f32[128]{0:T(128)}, u32[]{:S(2)}) copy-start(f32[128]{0:T(128)} %get-tuple-element.55) | copy-start | bytes 1540
  98.4 2.9 %copy-start.24 = (f32[128]{0:T(128)S(1)}, f32[128]{0:T(128)}, u32[]{:S(2)}) copy-start(f32[128]{0:T(128)} %get-tuple-element.56) | copy-start | bytes 1540
  98.4 2.9 %copy-start.25 = (f32[128]{0:T(128)S(1)}, f32[128]{0:T(128)}, u32[]{:S(2)}) copy-start(f32[128]{0:T(128)} %get-tuple-element.57) | copy-start | bytes 1540
  101.0 1.1 copy-start.4
  101.0 14.4 %copy-start.16 = (f32[16,4]{0,1:T(4,128)S(1)}, f32[16,4]{0,1:T(4,128)}, u32[]{:S(2)}) copy-start(f32[16,4]{0,1:T(4,128)} %copy-done.15) | copy-start | bytes 772
  101.1 15.5 %copy-start.3 = (f32[4,128,128]{2,1,0:T(8,128)S(1)}, f32[4,128,128]{2,1,0:T(8,128)}, u32[]{:S(2)}) copy-start(f32[4,128,128]{2,1,0:T(8,128)} %fusion.47) | copy-start | bytes 786436

commit v9 on v7

--- a/solution.py
+++ b/solution.py
@@ -167,40 +167,26 @@
         [send_rows.reshape(group_size, capacity, row_count, features), stat_rows, id_rows], 2
     )
     slot_rows = send_pack.shape[2]
-    edges = jnp.concatenate([out_grad[:, 0], out_grad[:, tile_y - 1]], 0)
-    send_pack = jnp.concatenate(
-        [
-            send_pack.reshape(group_size, capacity * slot_rows, features),
-            jnp.broadcast_to(edges[None], (group_size,) + edges.shape),
-        ],
-        1,
-    )
-    send_pack, diag_rows, diag_stats, diag_keys = lax.optimization_barrier(
-        (send_pack, row_pack, stat_blocks, key_pack)
+    send_pack = send_pack.reshape(group_size, capacity * slot_rows, features)
+    send_pack, diag_rows, diag_stats, diag_keys, grad_x, values_x = lax.optimization_barrier(
+        (send_pack, row_pack, stat_blocks, key_pack, out_grad, values)
     )
     pack_in = lax.all_to_all(send_pack, "gy", split_axis=0, concat_axis=0, tiled=True)
-    diag_query, diag_key, diag_value = tile_grads(diag_rows, diag_stats, diag_keys)
-    pack_in, diag_query, diag_key, diag_value = lax.optimization_barrier(
-        (pack_in, diag_query, diag_key, diag_value)
-    )
-    column = lax.axis_index("gy")
-    edge_in = pack_in[:, capacity * slot_rows :]
-    before_col = lax.dynamic_index_in_dim(edge_in, (column + group_size - 1) % group_size, 0, False)
-    after_col = lax.dynamic_index_in_dim(edge_in, (column + 1) % group_size, 0, False)
-    before_col = before_col[tile_x:]
-    after_col = after_col[:tile_x]
-    grad_x, values_x = lax.optimization_barrier((out_grad, values))
     count_x = lax.axis_size("gx")
     ahead = [(i, (i + 1) % count_x) for i in range(count_x)]
     behind = [((i + 1) % count_x, i) for i in range(count_x)]
     from_before = lax.ppermute(grad_x[tile_x - 1 :], "gx", ahead)
     from_after = lax.ppermute(grad_x[:1], "gx", behind)
+    ahead_y = [(i, (i + 1) % group_size) for i in range(group_size)]
+    behind_y = [((i + 1) % group_size, i) for i in range(group_size)]
+    before_col = lax.ppermute(grad_x[:, tile_y - 1 :], "gy", ahead_y)
+    after_col = lax.ppermute(grad_x[:, :1], "gy", behind_y)
     moved = [
         grad_x.astype(jnp.float32),
         jnp.concatenate([grad_x[1:], from_after], 0).astype(jnp.float32),
         jnp.concatenate([from_before, grad_x[:-1]], 0).astype(jnp.float32),
-        jnp.concatenate([grad_x[:, 1:], after_col[:, None]], 1).astype(jnp.float32),
-        jnp.concatenate([before_col[:, None], grad_x[:, :-1]], 1).astype(jnp.float32),
+        jnp.concatenate([grad_x[:, 1:], after_col], 1).astype(jnp.float32),
+        jnp.concatenate([before_col, grad_x[:, :-1]], 1).astype(jnp.float32),
     ]
     value_float = values_x.astype(jnp.float32)
     stencil_term = stencil[0] * moved[0]
@@ -210,9 +196,12 @@
         [jnp.sum(moved[index] * value_float, axis=(0, 1)) for index in range(5)]
     )
     point_count = tile_x * tile_y * count_x * group_size
-    pack_in = pack_in[:, : capacity * slot_rows].reshape(group_size, capacity, slot_rows, features)
-    partial_rows, pack_in = lax.optimization_barrier((partial_rows, pack_in))
-    column_sum = gather_sum(partial_rows, "gx")
+    column_sum = jnp.sum(lax.all_gather(partial_rows, "gx"), 0)
+    diag_query, diag_key, diag_value = tile_grads(diag_rows, diag_stats, diag_keys)
+    pack_in, diag_query, diag_key, diag_value, column_sum = lax.optimization_barrier(
+        (pack_in, diag_query, diag_key, diag_value, column_sum)
+    )
+    pack_in = pack_in.reshape(group_size, capacity, slot_rows, features)
     rows_in = pack_in[:, :, :row_count].reshape(group_size, capacity, 2, BLOCK, features)
     stats_in = pack_in[:, :, row_count : row_count + 2 * HEADS].reshape(
         group_size, capacity, 2, HEADS, BLOCK

time: 116 us -> 154 us (1.33)
  blocking collectives: 0 us -> 73.1 us
  waiting for transfers between devices: 46 us -> 25.3 us
  starting transfers between devices: 34.1 us -> 24.4 us
  local copies, waits for them, and re-layouts: 6.39 us -> 3.78 us
  matrix products: 17.9 us -> 15.5 us
    all_gather x0 -> x1, blocking collectives: none -> 73.1 us  [per_device(): column_sum = jnp.sum(lax.all_gather(partial_rows, 'gx'), 0)]
    all_to_all x1, waiting for transfers between devices: 20.9 us -> 0.01 us  [per_device(): lax.all_to_all(send_pack, 'gy', split_axis=0, concat_axis=0, tiled=True)]
    all_to_all x1 -> x0, starting transfers between devices: 19 us -> none  [gather_sum(): lax.all_to_all(spread, axis, split_axis=0, concat_axis=0, tiled=True)]
    ppermute x0 -> x2, waiting for transfers between devices: none -> 11.5 us  [the longest x1 7.21 us: per_device(): before_col = lax.ppermute(grad_x[:, tile_y - 1:], 'gy', ahead_y)]
    all_to_all x1 -> x0, waiting for transfers between devices: 10.1 us -> none  [gather_sum(): lax.all_to_all(spread, axis, split_axis=0, concat_axis=0, tiled=True)]
    ppermute x0 -> x2, starting transfers between devices: none -> 7.06 us  [the longest x1 3.93 us: per_device(): before_col = lax.ppermute(grad_x[:, tile_y - 1:], 'gy', ahead_y)]
    all_to_all x1, starting transfers between devices: 3.54 us -> 5.81 us  [per_device(): lax.all_to_all(return_pack, 'gy', split_axis=0, concat_axis=0, tiled=True)]
  transfers between devices with their start and end apart: 5 -> 6, of which waited for: 3 -> 3; matrix products, arithmetic and copies ran while one was open for 18% -> 6% of each run, Pallas kernels for 0% -> 0%
where the time goes in v9:
time: 154 us; the launch traced here: 152 us
  blocking collectives  73.1 us (47%)
  waiting for transfers between devices  25.3 us (16%)
  starting transfers between devices  24.4 us (16%)
  matrix products  15.5 us (10%)
  other arithmetic  8.91 us (6%)
  local copies, waits for them, and re-layouts  3.78 us (2%)
    all_gather x1, blocking collectives, per_device(): column_sum = jnp.sum(lax.all_gather(partial_rows, 'gx'), 0)  73.1 us
    all_to_all x1, waiting for transfers between devices, per_device(): lax.all_to_all(return_pack, 'gy', split_axis=0, concat_axis=0, tiled=True)  13.7 us
    all_to_all x1, starting transfers between devices, per_device(): lax.all_to_all(send_pack, 'gy', split_axis=0, concat_axis=0, tiled=True)  7.23 us
    ppermute x1, waiting for transfers between devices, per_device(): before_col = lax.ppermute(grad_x[:, tile_y - 1:], 'gy', ahead_y)  7.21 us
    all_to_all x1, starting transfers between devices, per_device(): lax.all_to_all(return_pack, 'gy', split_axis=0, concat_axis=0, tiled=True)  5.81 us
    ppermute x1, waiting for transfers between devices, per_device(): after_col = lax.ppermute(grad_x[:, :1], 'gy', behind_y)  4.33 us
    ppermute x1, starting transfers between devices, per_device(): before_col = lax.ppermute(grad_x[:, tile_y - 1:], 'gy', ahead_y)  3.93 us
    ppermute x1, starting transfers between devices, per_device(): after_col = lax.ppermute(grad_x[:, :1], 'gy', behind_y)  3.13 us
  transfers between devices with their start and end apart: 6, of which 3 were waited for; matrix products, arithmetic and copies ran while one was open for 6% of the time, Pallas kernels for 0%

profile of v9, /device:TPU:6, one launch (start us, length us, event | category | flops | bytes accessed | tf_op | source)
XLA Modules:
  0.0 152.2 jit_solution(9200542384532898230)
XLA Ops:
  0.7 0.8 copy.123
  1.6 0.2 convert_reduce_fusion
  1.8 0.1 fusion.50
  2.0 1.0 convert_multiply_fusion.10
  3.0 0.4 reshape.268
  3.5 0.7 reduce_sum.82
  4.2 0.1 copy.169
  4.4 0.3 fusion.112
  4.7 0.2 fusion.49
  4.9 0.5 fusion.29
  5.5 0.2 copy.165
  5.8 1.1 pad_maximum_fusion.1
  6.9 7.2 %all-to-all-start = ((bf16[8,544,128]{2,1,0:T(8,128)(2,1)}), bf16[8,544,128]{2,1,0:T(8,128)(2,1)S(1)}, u32[]{:S(2)}, u32[]{:S(2)}) async-start(bf16[8,544,128]{2,1,0:T(8,128)(2,1)} %bitcast.11), calls=%async_computation | async-start | bytes 2228224 | tf_op jit(solution)/shard_map/all_to_all | solution.py:174
  14.1 3.9 %collective-permute-start.3 = (bf16[16,1,128]{2,1,0:T(2,128)(2,1)S(1)}, bf16[16,1,128]{2,1,0:T(2,128)(2,1)S(1)}, u32[]{:S(2)}, u32[]{:S(2)}) collective-permute-start(bf16[16,1,128]{2,1,0:T(2,128)(2,1)S(1)} %get-tuple-element.40), channel_id=1, source_target_pairs={{0,1},{1,2},{2,3},{3,4},{4,5},{5,6},{6,7},{7,0},{8,9},{9,10},{10,1... | collective-permute-start | bytes 12296 | tf_op jit(solution)/shard_map/ppermute | solution.py:182
  18.1 1.9 %collective-permute-start = (bf16[1,32,128]{2,1,0:T(8,128)(2,1)S(1)}, bf16[1,32,128]{2,1,0:T(8,128)(2,1)S(1)}, u32[]{:S(2)}, u32[]{:S(2)}) collective-permute-start(bf16[1,32,128]{2,1,0:T(8,128)(2,1)S(1)} %get-tuple-element.42), channel_id=1, source_target_pairs={{8,0},{16,8},{24,16},{32,24},{40,32},{48,40},{56,48},{64,56},{72,6... | collective-permute-start | bytes 24584 | tf_op jit(solution)/shard_map/ppermute | solution.py:179
  20.0 2.4 %collective-permute-start.1 = (bf16[1,32,128]{2,1,0:T(8,128)(2,1)S(1)}, bf16[1,32,128]{2,1,0:T(8,128)(2,1)S(1)}, u32[]{:S(2)}, u32[]{:S(2)}) collective-permute-start(bf16[1,32,128]{2,1,0:T(8,128)(2,1)S(1)} %get-tuple-element.41), channel_id=1, source_target_pairs={{0,8},{8,16},{16,24},{24,32},{32,40},{40,48},{48,56},{56,64},{64,7... | collective-permute-start | bytes 24584 | tf_op jit(solution)/shard_map/ppermute | solution.py:178
  22.4 3.1 %collective-permute-start.2 = (bf16[16,1,128]{2,1,0:T(2,128)(2,1)S(1)}, bf16[16,1,128]{2,1,0:T(2,128)(2,1)S(1)}, u32[]{:S(2)}, u32[]{:S(2)}) collective-permute-start(bf16[16,1,128]{2,1,0:T(2,128)(2,1)S(1)} %get-tuple-element.39), channel_id=1, source_target_pairs={{1,0},{2,1},{3,2},{4,3},{5,4},{6,5},{7,6},{0,7},{9,8},{10,9},{11,1... | collective-permute-start | bytes 12296 | tf_op jit(solution)/shard_map/ppermute | solution.py:183
  25.8 0.4 fusion.33
  26.2 0.4 fusion.46
  26.6 1.0 fusion.48
  27.6 1.0 fusion.47
  28.6 0.3 convolution_bitcast_fusion
  29.0 7.2 %collective-permute-done.3 = bf16[16,1,128]{2,1,0:T(2,128)(2,1)S(1)} collective-permute-done((bf16[16,1,128]{2,1,0:T(2,128)(2,1)S(1)}, bf16[16,1,128]{2,1,0:T(2,128)(2,1)S(1)}, u32[]{:S(2)}, u32[]{:S(2)}) %collective-permute-start.3) | collective-permute-done | bytes 4128 | tf_op jit(solution)/shard_map/ppermute | solution.py:182
  36.2 4.3 %collective-permute-done.2 = bf16[16,1,128]{2,1,0:T(2,128)(2,1)S(1)} collective-permute-done((bf16[16,1,128]{2,1,0:T(2,128)(2,1)S(1)}, bf16[16,1,128]{2,1,0:T(2,128)(2,1)S(1)}, u32[]{:S(2)}, u32[]{:S(2)}) %collective-permute-start.2) | collective-permute-done | bytes 4128 | tf_op jit(solution)/shard_map/ppermute | solution.py:183
  40.5 0.2 fusion.81
  40.7 73.1 %all-gather.1 = f32[96,5,128]{2,1,0:T(8,128)S(1)} all-gather(f32[1,5,128]{2,1,0:T(8,128)S(1)} %bitcast.205), channel_id=2, replica_groups=mesh['gx'=96,'gy'=8] {'gx'}, dimensions={0}, use_global_device_ids=true | all-gather | bytes 248320 | tf_op jit(solution)/shard_map/all_gather | solution.py:199
  113.9 0.1 reduce_sum.88
  114.0 0.1 slice.140
  114.1 0.4 fusion.113
  114.5 0.9 slice_bitcast_fusion.2
  115.4 0.5 fusion.30
  116.0 0.2 copy.168
  116.2 0.7 fusion.7
  116.9 0.3 copy-done.1
  117.2 2.5 %fusion.24 = f32[16,1,128,128]{3,2,0,1:T(8,128)S(1)} fusion(f32[16,4,128,128]{3,2,1,0:T(8,128)S(1)} %fusion.7, f32[16,4,128]{2,1,0:T(4,128)S(1)} %get-tuple-element.45, bf16[16,128,128]{2,1,0:T(8,128)(2,1)S(1)} %copy-done.1, bf16[4,128]{1,0:T(4,128)(2,1)S(1)} %fusion.124), kind=kOutput, calls=%fused_computation.22 | convolution fusion | flops 272629760 | bytes 5800960 | tf_op jit(solution)/shard_map/shqk,shqf->skf/dot_general | solution.py:103
  119.7 2.6 %multiply_convert_fusion = bf16[16,4,128,128]{3,2,1,0:T(8,128)(2,1)S(1)} fusion(f32[16,4,128,128]{3,2,1,0:T(8,128)S(1)} %fusion.7, f32[16,4,128]{2,1,0:T(4,128)S(1)} %get-tuple-element.46, f32[16,4,128]{2,1,0:T(4,128)S(1)} %get-tuple-element.45, bf16[16,128,128]{2,1,0:T(8,128)(2,1)S(1)} %copy-done.1, bf16[4,128]{1,0:T(4,128)(2,1)S(1)} %fusion.124, ...), kind=kOutput, calls=%fused_computation.2 | convolution fusion | flops 274726912 | bytes 7406592 | tf_op jit(solution)/shard_map/shqf,skf->shqk/dot_general | solution.py:97
  122.3 1.8 %fusion.37 = f32[16,1,128,128]{3,2,0,1:T(8,128)} fusion(bf16[16,4,128,128]{3,2,1,0:T(8,128)(2,1)S(1)} %multiply_convert_fusion, bf16[4,128]{1,0:T(4,128)(2,1)S(1)} %fusion.124, bf16[16,128,128]{2,1,0:T(8,128)(2,1)S(1)} %get-tuple-element.32), kind=kOutput, calls=%fused_computation.31 | convolution fusion | flops 269746176 | bytes 3671040 | tf_op jit(solution)/shard_map/shqk,shqf->skf/dot_general | solution.py:107
  124.1 0.7 fusion.43
  124.8 0.9 pad_maximum_fusion.2
  125.7 5.8 %all-to-all-start.1 = ((bf16[8,272,128]{2,1,0:T(8,128)(2,1)}), bf16[8,272,128]{2,1,0:T(8,128)(2,1)S(1)}, u32[]{:S(2)}, u32[]{:S(2)}) async-start(bf16[8,272,128]{2,1,0:T(8,128)(2,1)} %pad_maximum_fusion.2), calls=%async_computation.1 | async-start | bytes 1114112 | tf_op jit(solution)/shard_map/all_to_all | solution.py:243
  131.5 1.4 pad_maximum_fusion
  132.9 2.0 %fusion.10 = f32[4,2,128,128]{3,0,2,1:T(4,128)S(1)} fusion(f32[16,2,128,128]{3,2,0,1:T(8,128)S(1)} %pad_maximum_fusion, s32[16]{0:T(128)S(1)} %sub.77), kind=kOutput, calls=%fused_computation.14 | convolution fusion | flops 25165888 | bytes 2621504 | tf_op jit(solution)/shard_map/sr,sxbf->rxbf/dot_general | solution.py:259
  135.0 0.8 fusion.76
  135.8 0.7 fusion.88
  136.5 13.7 %all-to-all-done.1 = bf16[8,272,128]{2,1,0:T(8,128)(2,1)S(1)} async-done(((bf16[8,272,128]{2,1,0:T(8,128)(2,1)}), bf16[8,272,128]{2,1,0:T(8,128)(2,1)S(1)}, u32[]{:S(2)}, u32[]{:S(2)}) %all-to-all-start.1) | async-done | bytes 557088 | tf_op jit(solution)/shard_map/all_to_all | solution.py:243
  150.3 0.5 fusion.66
  150.9 0.6 broadcast_multiply_fusion
  151.5 0.7 fusion.89
  (58 shorter events, 1.0 us)
Async XLA Ops:
  0.6 4.2 %copy-start = (bf16[16,32,128]{2,1,0:T(8,128)(2,1)S(1)}, bf16[16,32,128]{2,1,0:T(8,128)(2,1)}, u32[]{:S(2)}) copy-start(bf16[16,32,128]{2,1,0:T(8,128)(2,1)} %param.12) | copy-start | bytes 393220
  0.6 3.6 %copy-start.7 = (bf16[4,16,32]{2,1,0:T(8,128)(2,1)S(1)}, bf16[4,16,32]{2,1,0:T(8,128)(2,1)}, u32[]{:S(2)}) copy-start(bf16[4,16,32]{2,1,0:T(8,128)(2,1)} %param.13) | copy-start | bytes 12292
  0.7 4.2 %copy-start.5 = (bf16[16,32,128]{2,1,0:T(8,128)(2,1)S(1)}, bf16[16,32,128]{2,1,0:T(8,128)(2,1)}, u32[]{:S(2)}) copy-start(bf16[16,32,128]{2,1,0:T(8,128)(2,1)} %param.8) | copy-start | bytes 393220
  4.3 1.4 copy-start.2
  4.3 1.4 copy-start.6
  6.9 18.8 %copy-start.8 = (f32[5,128]{1,0:T(8,128)S(1)}, f32[5,128]{1,0:T(8,128)}, u32[]{:S(2)}) copy-start(f32[5,128]{1,0:T(8,128)} %param.15) | copy-start | bytes 7684
  6.9 107.1 %all-to-all-start = ((bf16[8,544,128]{2,1,0:T(8,128)(2,1)}), bf16[8,544,128]{2,1,0:T(8,128)(2,1)S(1)}, u32[]{:S(2)}, u32[]{:S(2)}) async-start(bf16[8,544,128]{2,1,0:T(8,128)(2,1)} %bitcast.11), calls=%async_computation | async-start | bytes 2228224 | tf_op jit(solution)/shard_map/all_to_all | solution.py:174
  14.1 22.1 %collective-permute-start.3 = (bf16[16,1,128]{2,1,0:T(2,128)(2,1)S(1)}, bf16[16,1,128]{2,1,0:T(2,128)(2,1)S(1)}, u32[]{:S(2)}, u32[]{:S(2)}) collective-permute-start(bf16[16,1,128]{2,1,0:T(2,128)(2,1)S(1)} %get-tuple-element.40), channel_id=1, source_target_pairs={{0,1},{1,2},{2,3},{3,4},{4,5},{5,6},{6,7},{7,0},{8,9},{9,10},{10,1... | collective-permute-start | bytes 12296 | tf_op jit(solution)/shard_map/ppermute | solution.py:182
  18.1 22.4 %collective-permute-start = (bf16[1,32,128]{2,1,0:T(8,128)(2,1)S(1)}, bf16[1,32,128]{2,1,0:T(8,128)(2,1)S(1)}, u32[]{:S(2)}, u32[]{:S(2)}) collective-permute-start(bf16[1,32,128]{2,1,0:T(8,128)(2,1)S(1)} %get-tuple-element.42), channel_id=1, source_target_pairs={{8,0},{16,8},{24,16},{32,24},{40,32},{48,40},{56,48},{64,56},{72,6... | collective-permute-start | bytes 24584 | tf_op jit(solution)/shard_map/ppermute | solution.py:179
  20.0 20.5 %collective-permute-start.1 = (bf16[1,32,128]{2,1,0:T(8,128)(2,1)S(1)}, bf16[1,32,128]{2,1,0:T(8,128)(2,1)S(1)}, u32[]{:S(2)}, u32[]{:S(2)}) collective-permute-start(bf16[1,32,128]{2,1,0:T(8,128)(2,1)S(1)} %get-tuple-element.41), channel_id=1, source_target_pairs={{0,8},{8,16},{16,24},{24,32},{32,40},{40,48},{48,56},{56,64},{64,7... | collective-permute-start | bytes 24584 | tf_op jit(solution)/shard_map/ppermute | solution.py:178
  22.4 18.1 %collective-permute-start.2 = (bf16[16,1,128]{2,1,0:T(2,128)(2,1)S(1)}, bf16[16,1,128]{2,1,0:T(2,128)(2,1)S(1)}, u32[]{:S(2)}, u32[]{:S(2)}) collective-permute-start(bf16[16,1,128]{2,1,0:T(2,128)(2,1)S(1)} %get-tuple-element.39), channel_id=1, source_target_pairs={{1,0},{2,1},{3,2},{4,3},{5,4},{6,5},{7,6},{0,7},{9,8},{10,9},{11,1... | collective-permute-start | bytes 12296 | tf_op jit(solution)/shard_map/ppermute | solution.py:183
  116.2 1.0 copy-start.1
  125.7 24.6 %all-to-all-start.1 = ((bf16[8,272,128]{2,1,0:T(8,128)(2,1)}), bf16[8,272,128]{2,1,0:T(8,128)(2,1)S(1)}, u32[]{:S(2)}, u32[]{:S(2)}) async-start(bf16[8,272,128]{2,1,0:T(8,128)(2,1)} %pad_maximum_fusion.2), calls=%async_computation.1 | async-start | bytes 1114112 | tf_op jit(solution)/shard_map/all_to_all | solution.py:243
  134.9 1.0 copy-start.4
  135.0 16.5 %copy-start.3 = (f32[4,128,128]{2,1,0:T(8,128)S(1)}, f32[4,128,128]{2,1,0:T(8,128)}, u32[]{:S(2)}) copy-start(f32[4,128,128]{2,1,0:T(8,128)} %fusion.47) | copy-start | bytes 786436

commit v10 on v7

--- a/solution.py
+++ b/solution.py
@@ -150,21 +150,22 @@
     ).astype(jnp.float32)
     picker = jnp.dot(placed, source_rows, precision=lax.Precision.HIGHEST)
     picker_low = picker.astype(jnp.bfloat16)
-    send_rows = jnp.dot(
-        picker_low, row_pack.reshape(row_blocks, -1), preferred_element_type=jnp.float32
-    )
-    send_rows = send_rows.astype(jnp.bfloat16).reshape(group_size, capacity, 2, BLOCK, features)
-    send_stats = jnp.dot(
-        picker_low, stat_blocks.reshape(row_blocks, -1), preferred_element_type=jnp.float32
-    )
-    send_stats = send_stats.astype(jnp.bfloat16).reshape(group_size, capacity, 2, HEADS, BLOCK)
+    source_index = jnp.dot(
+        placed, (order // listed + 1).astype(jnp.float32), precision=lax.Precision.HIGHEST
+    ).astype(jnp.int32) - 1
+    source_index = jnp.where(source_index < 0, row_blocks, source_index)
+    source_pack = jnp.concatenate(
+        [row_pack.reshape(row_blocks, 2 * BLOCK, features), stat_blocks.reshape(row_blocks, -1, BLOCK)],
+        1,
+    )
+    source_pack = jnp.pad(source_pack, ((0, 1), (0, 0), (0, 0)))
+    send_pack = jnp.take(source_pack, source_index, axis=0)
     send_ids = jnp.dot(placed, (inner + 1).astype(jnp.float32), precision=lax.Precision.HIGHEST)
     send_ids = send_ids.astype(jnp.bfloat16).reshape(group_size, capacity)
-    stat_rows = send_stats.reshape(group_size, capacity, 2 * HEADS, BLOCK)
     id_rows = jnp.broadcast_to(send_ids[:, :, None, None], (group_size, capacity, 8, features))
     row_count = 2 * BLOCK
     send_pack = jnp.concatenate(
-        [send_rows.reshape(group_size, capacity, row_count, features), stat_rows, id_rows], 2
+        [send_pack.reshape(group_size, capacity, -1, features), id_rows], 2
     )
     slot_rows = send_pack.shape[2]
     edges = jnp.concatenate([out_grad[:, 0], out_grad[:, tile_y - 1]], 0)
@@ -221,12 +222,8 @@
     item_count = rows_in.shape[1]
     total_items = group_size * item_count
     wanted = ids_in.astype(jnp.float32).astype(jnp.int32) - 1
-    chooser = (wanted[..., None] == jnp.arange(row_blocks, dtype=jnp.int32)).astype(jnp.bfloat16)
-    keys_in = jnp.dot(
-        chooser.reshape(-1, row_blocks),
-        key_pack.reshape(row_blocks, -1),
-        preferred_element_type=jnp.float32,
-    )
+    key_index = jnp.where(wanted < 0, row_blocks, wanted).reshape(-1)
+    keys_in = jnp.take(jnp.pad(key_pack, ((0, 1), (0, 0), (0, 0), (0, 0))), key_index, axis=0)
     keys_in = keys_in.astype(jnp.bfloat16).reshape(total_items, 2, BLOCK, features)
     query_part, key_part, value_part = tile_grads(
         rows_in.reshape(total_items, 2, BLOCK, features),

time: 116 us -> 118 us (1.017)
  local copies, waits for them, and re-layouts: 6.39 us -> 9.18 us
  matrix products: 17.9 us -> 15.4 us
  other arithmetic: 8.9 us -> 10.2 us
    dot_general x3 -> x1, matrix products: 2.19 us -> 0.15 us  [per_device(): jnp.dot(placed, (order // listed + 1).astype(jnp.float32), precision=lax....]
    gather x0 -> x2, local copies, waits for them, and re-layouts: none -> 1.51 us  [the longest x1 0.76 us: per_device(): send_pack = jnp.take(source_pack, source_index, axis=0)]
  transfers between devices with their start and end apart: 5 -> 5, of which waited for: 3 -> 3; matrix products, arithmetic and copies ran while one was open for 18% -> 17% of each run, Pallas kernels for 0% -> 0%
where the time goes in v10:
time: 118 us; the launch traced here: 117 us
  waiting for transfers between devices  46.6 us (39%)
  starting transfers between devices  34 us (29%)
  matrix products  15.4 us (13%)
  other arithmetic  10.2 us (9%)
  local copies, waits for them, and re-layouts  9.18 us (8%)
  between operations  1.45 us (1%)
    all_to_all x1, waiting for transfers between devices, per_device(): lax.all_to_all(send_pack, 'gy', split_axis=0, concat_axis=0, tiled=True)  21.8 us
    all_to_all x1, starting transfers between devices, gather_sum(): lax.all_to_all(spread, axis, split_axis=0, concat_axis=0, tiled=True)  19 us
    all_to_all x1, waiting for transfers between devices, per_device(): lax.all_to_all(return_pack, 'gy', split_axis=0, concat_axis=0, tiled=True)  15.1 us
    all_to_all x1, waiting for transfers between devices, gather_sum(): lax.all_to_all(spread, axis, split_axis=0, concat_axis=0, tiled=True)  9.72 us
    all_to_all x1, starting transfers between devices, per_device(): lax.all_to_all(send_pack, 'gy', split_axis=0, concat_axis=0, tiled=True)  7.11 us
    all_to_all x1, starting transfers between devices, per_device(): lax.all_to_all(return_pack, 'gy', split_axis=0, concat_axis=0, tiled=True)  3.54 us
    dot_general x2, matrix products, tile_grads(): jnp.einsum('shqf,skf->shqk', grad_heads, value_rows, preferred_element_ty...  2.94 us
    dot_general x2, matrix products, tile_grads(): jnp.einsum('shqk,shqf->skf', weights_low, grad_heads, preferred_element_t...  2.8 us
  transfers between devices with their start and end apart: 5, of which 3 were waited for; matrix products, arithmetic and copies ran while one was open for 17% of the time, Pallas kernels for 0%

profile of v10, /device:TPU:6, one launch (start us, length us, event | category | flops | bytes accessed | tf_op | source)
XLA Modules:
  0.0 116.9 jit_solution(11441086987478593121)
XLA Ops:
  0.7 0.8 copy.143
  1.6 0.2 convert_reduce_fusion
  1.9 0.1 compare_and_fusion.1
  2.1 0.8 fusion.140
  2.9 1.0 convert_multiply_fusion.10
  3.9 0.4 reshape.319
  4.4 0.7 reduce_sum.82
  5.6 0.8 gather_fusion
  6.3 0.2 broadcast_select_fusion
  6.7 1.1 pad_maximum_fusion.1
  7.9 7.1 %all-to-all-start = ((bf16[8,576,128]{2,1,0:T(8,128)(2,1)}), bf16[8,576,128]{2,1,0:T(8,128)(2,1)S(1)}, u32[]{:S(2)}, u32[]{:S(2)}) async-start(bf16[8,576,128]{2,1,0:T(8,128)(2,1)} %pad_maximum_fusion.1), calls=%async_computation | async-start | bytes 2359296 | tf_op jit(solution)/shard_map/all_to_all | solution.py:182
  15.0 0.6 fusion.138
  15.6 1.9 %collective-permute-start = (bf16[1,32,128]{2,1,0:T(8,128)(2,1)}, bf16[1,32,128]{2,1,0:T(8,128)(2,1)S(1)}, u32[]{:S(2)}, u32[]{:S(2)}) collective-permute-start(bf16[1,32,128]{2,1,0:T(8,128)(2,1)} %get-tuple-element.42), channel_id=1, source_target_pairs={{8,0},{16,8},{24,16},{32,24},{40,32},{48,40},{56,48},{64,56},{72,6... | collective-permute-start | bytes 24584 | tf_op jit(solution)/shard_map/ppermute | solution.py:198
  17.5 2.4 %collective-permute-start.1 = (bf16[1,32,128]{2,1,0:T(8,128)(2,1)}, bf16[1,32,128]{2,1,0:T(8,128)(2,1)S(1)}, u32[]{:S(2)}, u32[]{:S(2)}) collective-permute-start(bf16[1,32,128]{2,1,0:T(8,128)(2,1)} %get-tuple-element.41), channel_id=1, source_target_pairs={{0,8},{8,16},{16,24},{24,32},{32,40},{40,48},{48,56},{56,64},{64,7... | collective-permute-start | bytes 24584 | tf_op jit(solution)/shard_map/ppermute | solution.py:197
  20.1 0.8 convolution_bitcast_fusion.3
  21.0 0.4 fusion.31
  21.4 0.3 convolution_bitcast_fusion
  21.7 0.6 slice_bitcast_fusion.14
  22.4 0.4 fusion.44
  22.8 1.0 fusion.46
  23.9 1.0 fusion.45
  24.8 21.8 %all-to-all-done = bf16[8,576,128]{2,1,0:T(8,128)(2,1)S(1)} async-done(((bf16[8,576,128]{2,1,0:T(8,128)(2,1)}), bf16[8,576,128]{2,1,0:T(8,128)(2,1)S(1)}, u32[]{:S(2)}, u32[]{:S(2)}) %all-to-all-start) | async-done | bytes 1179680 | tf_op jit(solution)/shard_map/all_to_all | solution.py:182
  46.8 1.1 fusion.83
  48.0 0.4 add_reduce_fusion
  48.4 0.6 sub.91
  49.0 0.6 sub.90
  49.7 0.8 broadcast_in_dim.100
  50.4 19.0 %all-to-all-start.1 = ((f32[96,5,128]{2,1,0:T(8,128)}), f32[96,5,128]{2,1,0:T(8,128)S(1)}, u32[]{:S(2)}, u32[]{:S(2)}) async-start(f32[96,5,128]{2,1,0:T(8,128)} %broadcast_in_dim.100), calls=%async_computation.1 | async-start | bytes 786432 | tf_op jit(solution)/shard_map/all_to_all | solution.py:69
  69.4 0.9 slice_bitcast_fusion.2
  70.4 0.7 gather_fusion.1
  71.2 0.2 broadcast_select_fusion.1
  71.4 0.7 fusion.7
  72.1 0.3 copy-done.1
  72.4 2.5 %fusion.24 = f32[16,1,128,128]{3,2,0,1:T(8,128)S(1)} fusion(f32[16,4,128,128]{3,2,1,0:T(8,128)S(1)} %fusion.7, f32[16,4,128]{2,1,0:T(4,128)S(1)} %get-tuple-element.49, bf16[16,128,128]{2,1,0:T(8,128)(2,1)S(1)} %copy-done.1, bf16[4,128]{1,0:T(4,128)(2,1)S(1)} %copy-done.17), kind=kOutput, calls=%fused_computation.22 | convolution fusion | flops 272629760 | bytes 5800960 | tf_op jit(solution)/shard_map/shqk,shqf->skf/dot_general | solution.py:103
  74.9 2.6 %multiply_convert_fusion = bf16[16,4,128,128]{3,2,1,0:T(8,128)(2,1)S(1)} fusion(f32[16,4,128,128]{3,2,1,0:T(8,128)S(1)} %fusion.7, f32[16,4,128]{2,1,0:T(4,128)S(1)} %get-tuple-element.50, f32[16,4,128]{2,1,0:T(4,128)S(1)} %get-tuple-element.49, bf16[16,128,128]{2,1,0:T(8,128)(2,1)S(1)} %copy-done.1, bf16[4,128]{1,0:T(4,128)(2,1)S(1)} %copy-done.17, ...), kind=kOutput, calls=%fused_computation.2 | convolution fusion | flops 274726912 | bytes 7406592 | tf_op jit(solution)/shard_map/shqf,skf->shqk/dot_general | solution.py:97
  77.5 0.8 fusion.35
  78.3 0.2 pad_maximum_fusion
  78.5 1.5 %fusion.41 = bf16[16,128,128]{2,1,0:T(8,128)(2,1)} fusion(bf16[16,4,128,128]{3,2,1,0:T(8,128)(2,1)S(1)} %multiply_convert_fusion, bf16[16,128,128]{2,1,0:T(8,128)(2,1)S(1)} %slice_bitcast_fusion.4, bf16[4,128]{1,0:T(4,128)(2,1)S(1)} %copy-done.17), kind=kOutput, calls=%fused_computation.31 | convolution fusion | flops 270008320 | bytes 3146752 | tf_op jit(solution)/shard_map/shqk,shkf->sqf/dot_general | solution.py:111
  80.0 9.7 %all-to-all-done.1 = f32[96,5,128]{2,1,0:T(8,128)S(1)} async-done(((f32[96,5,128]{2,1,0:T(8,128)}), f32[96,5,128]{2,1,0:T(8,128)S(1)}, u32[]{:S(2)}, u32[]{:S(2)}) %all-to-all-start.1) | async-done | bytes 245792 | tf_op jit(solution)/shard_map/all_to_all | solution.py:69
  89.9 1.9 %pad_maximum_fusion.3 = bf16[8,272,128]{2,1,0:T(8,128)(2,1)} fusion(bf16[8,16,128]{2,1,0:T(8,128)(2,1)S(1)} %broadcast_in_dim.101, bf16[8,256,128]{2,1,0:T(8,128)(2,1)} %bitcast.186), kind=kLoop, calls=%fused_computation.65 | loop fusion | flops 1114112 | bytes 1114112 | tf_op jit(solution)/shard_map/concatenate | solution.py:244
  91.8 3.5 %all-to-all-start.2 = ((bf16[8,272,128]{2,1,0:T(8,128)(2,1)}), bf16[8,272,128]{2,1,0:T(8,128)(2,1)S(1)}, u32[]{:S(2)}, u32[]{:S(2)}) async-start(bf16[8,272,128]{2,1,0:T(8,128)(2,1)} %pad_maximum_fusion.3), calls=%async_computation.2 | async-start | bytes 1114112 | tf_op jit(solution)/shard_map/all_to_all | solution.py:251
  95.5 2.6 %fusion.10 = f32[4,2,128,128]{3,0,2,1:T(4,128)S(1)} fusion(f32[16,2,128,128]{3,2,0,1:T(8,128)S(1)} %pad_maximum_fusion, s32[16]{0:T(128)} %sub.90), kind=kOutput, calls=%fused_computation.14 | convolution fusion | flops 25165888 | bytes 2621504 | tf_op jit(solution)/shard_map/sr,sxbf->rxbf/dot_general | solution.py:267
  98.2 0.8 fusion.78
  99.1 0.7 fusion.86
  99.8 15.1 %all-to-all-done.2 = bf16[8,272,128]{2,1,0:T(8,128)(2,1)S(1)} async-done(((bf16[8,272,128]{2,1,0:T(8,128)(2,1)}), bf16[8,272,128]{2,1,0:T(8,128)(2,1)S(1)}, u32[]{:S(2)}, u32[]{:S(2)}) %all-to-all-start.2) | async-done | bytes 557088 | tf_op jit(solution)/shard_map/all_to_all | solution.py:251
  115.0 0.6 broadcast_multiply_fusion
  115.6 0.5 fusion.67
  116.2 0.7 fusion.87
  (109 shorter events, 1.8 us)
Async XLA Ops:
  0.6 4.8 %copy-start = (bf16[16,32,128]{2,1,0:T(8,128)(2,1)S(1)}, bf16[16,32,128]{2,1,0:T(8,128)(2,1)}, u32[]{:S(2)}) copy-start(bf16[16,32,128]{2,1,0:T(8,128)(2,1)} %param.12) | copy-start | bytes 393220
  0.6 4.6 %copy-start.15 = (bf16[4,16,32]{2,1,0:T(8,128)(2,1)S(1)}, bf16[4,16,32]{2,1,0:T(8,128)(2,1)}, u32[]{:S(2)}) copy-start(bf16[4,16,32]{2,1,0:T(8,128)(2,1)} %param.13) | copy-start | bytes 12292
  0.7 4.8 %copy-start.5 = (bf16[16,32,128]{2,1,0:T(8,128)(2,1)S(1)}, bf16[16,32,128]{2,1,0:T(8,128)(2,1)}, u32[]{:S(2)}) copy-start(bf16[16,32,128]{2,1,0:T(8,128)(2,1)} %param.8) | copy-start | bytes 393220
  6.6 1.3 %copy-start.2 = (bf16[16,32,128]{2,1,0:T(8,128)(2,1)S(1)}, bf16[16,32,128]{2,1,0:T(8,128)(2,1)}, u32[]{:S(2)}) copy-start(bf16[16,32,128]{2,1,0:T(8,128)(2,1)} %param.10) | copy-start | bytes 393220
  6.6 1.3 %copy-start.6 = (bf16[16,32,128]{2,1,0:T(8,128)(2,1)S(1)}, bf16[16,32,128]{2,1,0:T(8,128)(2,1)}, u32[]{:S(2)}) copy-start(bf16[16,32,128]{2,1,0:T(8,128)(2,1)} %param.9) | copy-start | bytes 393220
  7.9 38.7 %all-to-all-start = ((bf16[8,576,128]{2,1,0:T(8,128)(2,1)}), bf16[8,576,128]{2,1,0:T(8,128)(2,1)S(1)}, u32[]{:S(2)}, u32[]{:S(2)}) async-start(bf16[8,576,128]{2,1,0:T(8,128)(2,1)} %pad_maximum_fusion.1), calls=%async_computation | async-start | bytes 2359296 | tf_op jit(solution)/shard_map/all_to_all | solution.py:182
  15.6 31.1 %collective-permute-start = (bf16[1,32,128]{2,1,0:T(8,128)(2,1)}, bf16[1,32,128]{2,1,0:T(8,128)(2,1)S(1)}, u32[]{:S(2)}, u32[]{:S(2)}) collective-permute-start(bf16[1,32,128]{2,1,0:T(8,128)(2,1)} %get-tuple-element.42), channel_id=1, source_target_pairs={{8,0},{16,8},{24,16},{32,24},{40,32},{48,40},{56,48},{64,56},{72,6... | collective-permute-start | bytes 24584 | tf_op jit(solution)/shard_map/ppermute | solution.py:198
  17.5 29.2 %collective-permute-start.1 = (bf16[1,32,128]{2,1,0:T(8,128)(2,1)}, bf16[1,32,128]{2,1,0:T(8,128)(2,1)S(1)}, u32[]{:S(2)}, u32[]{:S(2)}) collective-permute-start(bf16[1,32,128]{2,1,0:T(8,128)(2,1)} %get-tuple-element.41), channel_id=1, source_target_pairs={{0,8},{8,16},{16,24},{24,32},{32,40},{40,48},{48,56},{56,64},{64,7... | collective-permute-start | bytes 24584 | tf_op jit(solution)/shard_map/ppermute | solution.py:197
  20.0 3.8 %copy-start.16 = (bf16[4,128]{1,0:T(4,128)(2,1)}, bf16[4,128]{1,0:T(4,128)(2,1)S(1)}, u32[]{:S(2)}) copy-start(bf16[4,128]{1,0:T(4,128)(2,1)S(1)} %fusion.116) | copy-start | bytes 3076
  20.1 1.7 %copy-start.25 = (f32[5,128]{1,0:T(8,128)S(1)}, f32[5,128]{1,0:T(8,128)}, u32[]{:S(2)}) copy-start(f32[5,128]{1,0:T(8,128)} %param.15) | copy-start | bytes 7684
  46.7 2.3 %copy-start.7 = (bf16[16,1,128]{2,1,0:T(2,128)(2,1)}, bf16[16,1,128]{2,1,0:T(2,128)(2,1)S(1)}, u32[]{:S(2)}) copy-start(bf16[16,1,128]{2,1,0:T(2,128)(2,1)S(1)} %copy.153) | copy-start | bytes 12292
  46.7 2.3 %copy-start.9 = (bf16[16,1,128]{2,1,0:T(2,128)(2,1)}, bf16[16,1,128]{2,1,0:T(2,128)(2,1)S(1)}, u32[]{:S(2)}) copy-start(bf16[16,1,128]{2,1,0:T(2,128)(2,1)S(1)} %copy.152) | copy-start | bytes 12292
  46.8 1.2 copy-start.11
  46.8 2.3 %copy-start.13 = (bf16[1,32,128]{2,1,0:T(8,128)(2,1)}, bf16[1,32,128]{2,1,0:T(8,128)(2,1)S(1)}, u32[]{:S(2)}) copy-start(bf16[1,32,128]{2,1,0:T(8,128)(2,1)S(1)} %collective-permute-done.1) | copy-start | bytes 24580
  49.6 20.7 %copy-start.26 = (s32[16,1]{0,1:T(1,128)S(1)}, s32[16,1]{0,1:T(1,128)}, u32[]{:S(2)}) copy-start(s32[16,1]{0,1:T(1,128)} %sub.91) | copy-start | bytes 196
  49.6 20.7 %copy-start.24 = (s32[16]{0:T(128)S(1)}, s32[16]{0:T(128)}, u32[]{:S(2)}) copy-start(s32[16]{0:T(128)} %sub.90) | copy-start | bytes 196
  50.4 39.3 %all-to-all-start.1 = ((f32[96,5,128]{2,1,0:T(8,128)}), f32[96,5,128]{2,1,0:T(8,128)S(1)}, u32[]{:S(2)}, u32[]{:S(2)}) async-start(f32[96,5,128]{2,1,0:T(8,128)} %broadcast_in_dim.100), calls=%async_computation.1 | async-start | bytes 786432 | tf_op jit(solution)/shard_map/all_to_all | solution.py:69
  70.4 0.9 copy-start.17
  71.4 1.0 copy-start.1
  91.8 23.1 %all-to-all-start.2 = ((bf16[8,272,128]{2,1,0:T(8,128)(2,1)}), bf16[8,272,128]{2,1,0:T(8,128)(2,1)S(1)}, u32[]{:S(2)}, u32[]{:S(2)}) async-start(bf16[8,272,128]{2,1,0:T(8,128)(2,1)} %pad_maximum_fusion.3), calls=%async_computation.2 | async-start | bytes 1114112 | tf_op jit(solution)/shard_map/all_to_all | solution.py:251
  95.4 2.8 %copy-start.8 = (bf16[16,1,128]{2,1,0:T(2,128)(2,1)S(1)}, bf16[16,1,128]{2,1,0:T(2,128)(2,1)}, u32[]{:S(2)}) copy-start(bf16[16,1,128]{2,1,0:T(2,128)(2,1)} %copy-done.7) | copy-start | bytes 12292
  95.4 2.8 %copy-start.10 = (bf16[16,1,128]{2,1,0:T(2,128)(2,1)S(1)}, bf16[16,1,128]{2,1,0:T(2,128)(2,1)}, u32[]{:S(2)}) copy-start(bf16[16,1,128]{2,1,0:T(2,128)(2,1)} %copy-done.9) | copy-start | bytes 12292
  95.4 2.8 %copy-start.12 = (bf16[1,32,128]{2,1,0:T(8,128)(2,1)S(1)}, bf16[1,32,128]{2,1,0:T(8,128)(2,1)}, u32[]{:S(2)}) copy-start(bf16[1,32,128]{2,1,0:T(8,128)(2,1)} %copy-done.11) | copy-start | bytes 24580
  95.4 2.8 %copy-start.14 = (bf16[1,32,128]{2,1,0:T(8,128)(2,1)S(1)}, bf16[1,32,128]{2,1,0:T(8,128)(2,1)}, u32[]{:S(2)}) copy-start(bf16[1,32,128]{2,1,0:T(8,128)(2,1)} %copy-done.13) | copy-start | bytes 24580
  95.4 2.8 %copy-start.19 = (f32[128]{0:T(128)S(1)}, f32[128]{0:T(128)}, u32[]{:S(2)}) copy-start(f32[128]{0:T(128)} %get-tuple-element.53) | copy-start | bytes 1540
  95.4 2.8 %copy-start.20 = (f32[128]{0:T(128)S(1)}, f32[128]{0:T(128)}, u32[]{:S(2)}) copy-start(f32[128]{0:T(128)} %get-tuple-element.54) | copy-start | bytes 1540
  95.4 2.8 %copy-start.21 = (f32[128]{0:T(128)S(1)}, f32[128]{0:T(128)}, u32[]{:S(2)}) copy-start(f32[128]{0:T(128)} %get-tuple-element.55) | copy-start | bytes 1540
  95.4 2.8 %copy-start.22 = (f32[128]{0:T(128)S(1)}, f32[128]{0:T(128)}, u32[]{:S(2)}) copy-start(f32[128]{0:T(128)} %get-tuple-element.56) | copy-start | bytes 1540
  95.5 2.8 %copy-start.23 = (f32[128]{0:T(128)S(1)}, f32[128]{0:T(128)}, u32[]{:S(2)}) copy-start(f32[128]{0:T(128)} %get-tuple-element.57) | copy-start | bytes 1540
  98.0 1.0 copy-start.4
  98.1 17.5 %copy-start.18 = (f32[16,4,1]{0,1,2:T(4,128)S(1)}, f32[16,4,1]{0,1,2:T(4,128)}, u32[]{:S(2)}) copy-start(f32[16,4,1]{0,1,2:T(4,128)} %convolution_bitcast_fusion.3) | copy-start | bytes 772
  98.1 18.0 %copy-start.3 = (f32[4,128,128]{2,1,0:T(8,128)S(1)}, f32[4,128,128]{2,1,0:T(8,128)}, u32[]{:S(2)}) copy-start(f32[4,128,128]{2,1,0:T(8,128)} %fusion.45) | copy-start | bytes 786436

commit v11 on v9

--- a/solution.py
+++ b/solution.py
@@ -196,7 +196,7 @@
         [jnp.sum(moved[index] * value_float, axis=(0, 1)) for index in range(5)]
     )
     point_count = tile_x * tile_y * count_x * group_size
-    column_sum = jnp.sum(lax.all_gather(partial_rows, "gx"), 0)
+    column_sum = exchange_sum(partial_rows, "gx")
     diag_query, diag_key, diag_value = tile_grads(diag_rows, diag_stats, diag_keys)
     pack_in, diag_query, diag_key, diag_value, column_sum = lax.optimization_barrier(
         (pack_in, diag_query, diag_key, diag_value, column_sum)

time: 154 us -> 127 us (0.82)
  blocking collectives: 73.1 us -> 0 us
  starting transfers between devices: 24.4 us -> 57.4 us
  waiting for transfers between devices: 25.3 us -> 36.1 us
  matrix products: 15.5 us -> 18.5 us
    all_gather x1 -> x0, blocking collectives: 73.1 us -> none  [per_device(): column_sum = jnp.sum(lax.all_gather(partial_rows, 'gx'), 0)]
    ppermute x0 -> x7, starting transfers between devices: none -> 33.1 us  [the longest x5 18.3 us: exchange_sum(): value = value + lax.ppermute(value, axis, pairs)]
    ppermute x0 -> x7, waiting for transfers between devices: none -> 14.5 us  [the longest x2 7.36 us: exchange_sum(): received.append(lax.ppermute(value, axis, pairs))]
    all_to_all x1, waiting for transfers between devices: 13.7 us -> 8.62 us  [per_device(): lax.all_to_all(return_pack, 'gy', split_axis=0, concat_axis=0, tiled=True)]
  transfers between devices with their start and end apart: 6 -> 13, of which waited for: 3 -> 8; matrix products, arithmetic and copies ran while one was open for 6% -> 9% of each run, Pallas kernels for 0% -> 0%
where the time goes in v11:
time: 127 us; the launch traced here: 126 us
  starting transfers between devices  57.4 us (45%)
  waiting for transfers between devices  36.1 us (28%)
  matrix products  18.5 us (15%)
  other arithmetic  8.88 us (7%)
  local copies, waits for them, and re-layouts  4.03 us (3%)
  between operations  1.3 us (1%)
    ppermute x5, starting transfers between devices, exchange_sum(): value = value + lax.ppermute(value, axis, pairs)  18.3 us
    ppermute x2, starting transfers between devices, exchange_sum(): received.append(lax.ppermute(value, axis, pairs))  14.8 us
    all_to_all x1, waiting for transfers between devices, per_device(): lax.all_to_all(return_pack, 'gy', split_axis=0, concat_axis=0, tiled=True)  8.62 us
    ppermute x1, waiting for transfers between devices, per_device(): before_col = lax.ppermute(grad_x[:, tile_y - 1:], 'gy', ahead_y)  8.6 us
    ppermute x2, waiting for transfers between devices, exchange_sum(): received.append(lax.ppermute(value, axis, pairs))  7.36 us
    ppermute x5, waiting for transfers between devices, exchange_sum(): value = value + lax.ppermute(value, axis, pairs)  7.15 us
    all_to_all x1, starting transfers between devices, per_device(): lax.all_to_all(send_pack, 'gy', split_axis=0, concat_axis=0, tiled=True)  7.1 us
    all_to_all x1, starting transfers between devices, per_device(): lax.all_to_all(return_pack, 'gy', split_axis=0, concat_axis=0, tiled=True)  5.81 us
  transfers between devices with their start and end apart: 13, of which 8 were waited for; matrix products, arithmetic and copies ran while one was open for 9% of the time, Pallas kernels for 0%

profile of v11, /device:TPU:6, one launch (start us, length us, event | category | flops | bytes accessed | tf_op | source)
XLA Modules:
  0.0 126.2 jit_solution(6695176271361947357)
XLA Ops:
  0.7 0.8 copy.123
  2.0 1.0 convert_multiply_fusion.10
  3.0 0.4 reshape.264
  3.5 0.7 reduce_sum.73
  4.9 0.5 fusion.29
  5.8 1.1 pad_maximum_fusion.1
  6.9 7.1 %all-to-all-start = ((bf16[8,544,128]{2,1,0:T(8,128)(2,1)}), bf16[8,544,128]{2,1,0:T(8,128)(2,1)S(1)}, u32[]{:S(2)}, u32[]{:S(2)}) async-start(bf16[8,544,128]{2,1,0:T(8,128)(2,1)} %bitcast.11), calls=%async_computation | async-start | bytes 2228224 | tf_op jit(solution)/shard_map/all_to_all | solution.py:174
  14.0 3.9 %collective-permute-start.3 = (bf16[16,1,128]{2,1,0:T(2,128)(2,1)S(1)}, bf16[16,1,128]{2,1,0:T(2,128)(2,1)S(1)}, u32[]{:S(2)}, u32[]{:S(2)}) collective-permute-start(bf16[16,1,128]{2,1,0:T(2,128)(2,1)S(1)} %get-tuple-element.40), channel_id=1, source_target_pairs={{0,1},{1,2},{2,3},{3,4},{4,5},{5,6},{6,7},{7,0},{8,9},{9,10},{10,1... | collective-permute-start | bytes 12296 | tf_op jit(solution)/shard_map/ppermute | solution.py:182
  17.9 1.9 %collective-permute-start = (bf16[1,32,128]{2,1,0:T(8,128)(2,1)S(1)}, bf16[1,32,128]{2,1,0:T(8,128)(2,1)S(1)}, u32[]{:S(2)}, u32[]{:S(2)}) collective-permute-start(bf16[1,32,128]{2,1,0:T(8,128)(2,1)S(1)} %get-tuple-element.42), channel_id=1, source_target_pairs={{8,0},{16,8},{24,16},{32,24},{40,32},{48,40},{56,48},{64,56},{72,6... | collective-permute-start | bytes 24584 | tf_op jit(solution)/shard_map/ppermute | solution.py:179
  19.9 2.4 %collective-permute-start.1 = (bf16[1,32,128]{2,1,0:T(8,128)(2,1)S(1)}, bf16[1,32,128]{2,1,0:T(8,128)(2,1)S(1)}, u32[]{:S(2)}, u32[]{:S(2)}) collective-permute-start(bf16[1,32,128]{2,1,0:T(8,128)(2,1)S(1)} %get-tuple-element.41), channel_id=1, source_target_pairs={{0,8},{8,16},{16,24},{24,32},{32,40},{40,48},{48,56},{56,64},{64,7... | collective-permute-start | bytes 24584 | tf_op jit(solution)/shard_map/ppermute | solution.py:178
  22.3 3.1 %collective-permute-start.2 = (bf16[16,1,128]{2,1,0:T(2,128)(2,1)S(1)}, bf16[16,1,128]{2,1,0:T(2,128)(2,1)S(1)}, u32[]{:S(2)}, u32[]{:S(2)}) collective-permute-start(bf16[16,1,128]{2,1,0:T(2,128)(2,1)S(1)} %get-tuple-element.39), channel_id=1, source_target_pairs={{1,0},{2,1},{3,2},{4,3},{5,4},{6,5},{7,6},{0,7},{9,8},{10,9},{11,1... | collective-permute-start | bytes 12296 | tf_op jit(solution)/shard_map/ppermute | solution.py:183
  25.5 0.4 fusion.33
  26.2 1.2 fusion.46
  27.4 8.6 %collective-permute-done.3 = bf16[16,1,128]{2,1,0:T(2,128)(2,1)S(1)} collective-permute-done((bf16[16,1,128]{2,1,0:T(2,128)(2,1)S(1)}, bf16[16,1,128]{2,1,0:T(2,128)(2,1)S(1)}, u32[]{:S(2)}, u32[]{:S(2)}) %collective-permute-start.3) | collective-permute-done | bytes 4128 | tf_op jit(solution)/shard_map/ppermute | solution.py:182
  36.0 4.3 %collective-permute-done.2 = bf16[16,1,128]{2,1,0:T(2,128)(2,1)S(1)} collective-permute-done((bf16[16,1,128]{2,1,0:T(2,128)(2,1)S(1)}, bf16[16,1,128]{2,1,0:T(2,128)(2,1)S(1)}, u32[]{:S(2)}, u32[]{:S(2)}) %collective-permute-start.2) | collective-permute-done | bytes 4128 | tf_op jit(solution)/shard_map/ppermute | solution.py:183
  40.6 1.9 %collective-permute-start.4 = (f32[5,128]{1,0:T(8,128)S(1)}, f32[5,128]{1,0:T(8,128)S(1)}, u32[]{:S(2)}, u32[]{:S(2)}) collective-permute-start(f32[5,128]{1,0:T(8,128)S(1)} %stack.50), channel_id=1, source_target_pairs={{0,8},{8,0},{16,24},{24,16},{32,40},{40,32},{48,56},{56,48},{64,72... | collective-permute-start | bytes 7688 | tf_op jit(solution)/shard_map/ppermute | solution.py:45
  42.5 2.2 %fusion.48 = f32[4,128,128]{2,1,0:T(8,128)} fusion(bf16[4,4,128,128]{3,2,1,0:T(8,128)(2,1)} %fusion.46, bf16[4,128]{1,0:T(4,128)(2,1)S(1)} %fusion.124, bf16[4,128,128]{2,1,0:T(8,128)(2,1)} %copy-done.8), kind=kOutput, calls=%fused_computation.39 | convolution fusion | flops 67436544 | bytes 918528 | tf_op jit(solution)/shard_map/shqk,shqf->skf/dot_general | solution.py:107
  44.7 2.7 %collective-permute-start.5 = (f32[5,128]{1,0:T(8,128)S(1)}, f32[5,128]{1,0:T(8,128)S(1)}, u32[]{:S(2)}, u32[]{:S(2)}) collective-permute-start(f32[5,128]{1,0:T(8,128)S(1)} %add.125), channel_id=1, source_target_pairs={{0,16},{8,24},{16,0},{24,8},{32,48},{40,56},{48,32},{56,40},{64,80... | collective-permute-start | bytes 7688 | tf_op jit(solution)/shard_map/ppermute | solution.py:45
  47.4 2.7 %collective-permute-done.5 = f32[5,128]{1,0:T(8,128)S(1)} collective-permute-done((f32[5,128]{1,0:T(8,128)S(1)}, f32[5,128]{1,0:T(8,128)S(1)}, u32[]{:S(2)}, u32[]{:S(2)}) %collective-permute-start.5) | collective-permute-done | bytes 2592 | tf_op jit(solution)/shard_map/ppermute | solution.py:45
  50.2 3.3 %collective-permute-start.6 = (f32[5,128]{1,0:T(8,128)S(1)}, f32[5,128]{1,0:T(8,128)S(1)}, u32[]{:S(2)}, u32[]{:S(2)}) collective-permute-start(f32[5,128]{1,0:T(8,128)S(1)} %add.126), channel_id=1, source_target_pairs={{0,32},{8,40},{16,48},{24,56},{32,0},{40,8},{48,16},{56,24},{64,96... | collective-permute-start | bytes 7688 | tf_op jit(solution)/shard_map/ppermute | solution.py:45
  53.5 2.0 %fusion.47 = f32[4,128,128]{2,1,0:T(8,128)} fusion(bf16[4,4,128,128]{3,2,1,0:T(8,128)(2,1)} %fusion.46, bf16[4,128,128]{2,1,0:T(8,128)(2,1)S(1)} %slice_bitcast_fusion.7, bf16[4,128]{1,0:T(4,128)(2,1)S(1)} %fusion.124), kind=kOutput, calls=%fused_computation.38 | convolution fusion | flops 67436544 | bytes 918528 | tf_op jit(solution)/shard_map/shqk,shkf->sqf/dot_general | solution.py:111
  55.5 1.6 %collective-permute-done.6 = f32[5,128]{1,0:T(8,128)S(1)} collective-permute-done((f32[5,128]{1,0:T(8,128)S(1)}, f32[5,128]{1,0:T(8,128)S(1)}, u32[]{:S(2)}, u32[]{:S(2)}) %collective-permute-start.6) | collective-permute-done | bytes 2592 | tf_op jit(solution)/shard_map/ppermute | solution.py:45
  57.2 4.3 %collective-permute-start.7 = (f32[5,128]{1,0:T(8,128)S(1)}, f32[5,128]{1,0:T(8,128)S(1)}, u32[]{:S(2)}, u32[]{:S(2)}) collective-permute-start(f32[5,128]{1,0:T(8,128)S(1)} %add.127), channel_id=1, source_target_pairs={{0,64},{8,72},{16,80},{24,88},{32,96},{40,104},{48,112},{56,120},{... | collective-permute-start | bytes 7688 | tf_op jit(solution)/shard_map/ppermute | solution.py:45
  61.5 1.5 %collective-permute-done.7 = f32[5,128]{1,0:T(8,128)S(1)} collective-permute-done((f32[5,128]{1,0:T(8,128)S(1)}, f32[5,128]{1,0:T(8,128)S(1)}, u32[]{:S(2)}, u32[]{:S(2)}) %collective-permute-start.7) | collective-permute-done | bytes 2592 | tf_op jit(solution)/shard_map/ppermute | solution.py:45
  63.0 6.1 %collective-permute-start.8 = (f32[5,128]{1,0:T(8,128)S(1)}, f32[5,128]{1,0:T(8,128)S(1)}, u32[]{:S(2)}, u32[]{:S(2)}) collective-permute-start(f32[5,128]{1,0:T(8,128)S(1)} %add.128), channel_id=1, source_target_pairs={{0,128},{8,136},{16,144},{24,152},{32,160},{40,168},{48,176},{56,1... | collective-permute-start | bytes 7688 | tf_op jit(solution)/shard_map/ppermute | solution.py:45
  69.1 0.3 convolution_bitcast_fusion
  69.5 1.2 collective-permute-done.8
  70.7 12.9 %collective-permute-start.9 = (f32[5,128]{1,0:T(8,128)S(1)}, f32[5,128]{1,0:T(8,128)S(1)}, u32[]{:S(2)}, u32[]{:S(2)}) collective-permute-start(f32[5,128]{1,0:T(8,128)S(1)} %add.129), channel_id=1, source_target_pairs={{0,512},{8,520},{16,528},{24,536},{32,544},{40,552},{48,560},{56,5... | collective-permute-start | bytes 7688 | tf_op jit(solution)/shard_map/ppermute | solution.py:53
  83.6 1.9 %collective-permute-start.10 = (f32[5,128]{1,0:T(8,128)S(1)}, f32[5,128]{1,0:T(8,128)S(1)}, u32[]{:S(2)}, u32[]{:S(2)}) collective-permute-start(f32[5,128]{1,0:T(8,128)S(1)} %add.129), channel_id=1, source_target_pairs={{0,256},{8,264},{16,272},{24,280},{32,288},{40,296},{48,304},{56,3... | collective-permute-start | bytes 7688 | tf_op jit(solution)/shard_map/ppermute | solution.py:53
  85.7 7.4 %collective-permute-done.10 = f32[5,128]{1,0:T(8,128)S(1)} collective-permute-done((f32[5,128]{1,0:T(8,128)S(1)}, f32[5,128]{1,0:T(8,128)S(1)}, u32[]{:S(2)}, u32[]{:S(2)}) %collective-permute-start.10) | collective-permute-done | bytes 2592 | tf_op jit(solution)/shard_map/ppermute | solution.py:53
  93.1 0.4 fusion.113
  93.5 0.9 slice_bitcast_fusion.2
  94.5 0.5 fusion.30
  95.3 0.7 fusion.7
  96.3 2.5 %fusion.24 = f32[16,1,128,128]{3,2,0,1:T(8,128)S(1)} fusion(f32[16,4,128,128]{3,2,1,0:T(8,128)S(1)} %fusion.7, f32[16,4,128]{2,1,0:T(4,128)S(1)} %get-tuple-element.45, bf16[16,128,128]{2,1,0:T(8,128)(2,1)S(1)} %copy-done.1, bf16[4,128]{1,0:T(4,128)(2,1)S(1)} %fusion.124), kind=kOutput, calls=%fused_computation.22 | convolution fusion | flops 272629760 | bytes 5800960 | tf_op jit(solution)/shard_map/shqk,shqf->skf/dot_general | solution.py:103
  98.8 2.6 %multiply_convert_fusion = bf16[16,4,128,128]{3,2,1,0:T(8,128)(2,1)S(1)} fusion(f32[16,4,128,128]{3,2,1,0:T(8,128)S(1)} %fusion.7, f32[16,4,128]{2,1,0:T(4,128)S(1)} %get-tuple-element.46, f32[16,4,128]{2,1,0:T(4,128)S(1)} %get-tuple-element.45, bf16[16,128,128]{2,1,0:T(8,128)(2,1)S(1)} %copy-done.1, bf16[4,128]{1,0:T(4,128)(2,1)S(1)} %fusion.124, ...), kind=kOutput, calls=%fused_computation.2 | convolution fusion | flops 274726912 | bytes 7406592 | tf_op jit(solution)/shard_map/shqf,skf->shqk/dot_general | solution.py:97
  101.4 1.8 %fusion.37 = f32[16,1,128,128]{3,2,0,1:T(8,128)} fusion(bf16[16,4,128,128]{3,2,1,0:T(8,128)(2,1)S(1)} %multiply_convert_fusion, bf16[4,128]{1,0:T(4,128)(2,1)S(1)} %fusion.124, bf16[16,128,128]{2,1,0:T(8,128)(2,1)S(1)} %get-tuple-element.32), kind=kOutput, calls=%fused_computation.31 | convolution fusion | flops 269746176 | bytes 3671040 | tf_op jit(solution)/shard_map/shqk,shqf->skf/dot_general | solution.py:107
  103.2 0.7 fusion.43
  103.9 0.9 pad_maximum_fusion.2
  104.8 5.8 %all-to-all-start.1 = ((bf16[8,272,128]{2,1,0:T(8,128)(2,1)}), bf16[8,272,128]{2,1,0:T(8,128)(2,1)S(1)}, u32[]{:S(2)}, u32[]{:S(2)}) async-start(bf16[8,272,128]{2,1,0:T(8,128)(2,1)} %pad_maximum_fusion.2), calls=%async_computation.1 | async-start | bytes 1114112 | tf_op jit(solution)/shard_map/all_to_all | solution.py:243
  110.6 1.4 %pad_maximum_fusion = f32[16,2,128,128]{3,2,0,1:T(8,128)S(1)} fusion(f32[16,1,128,128]{3,2,0,1:T(8,128)S(1)} %fusion.24, f32[16,1,128,128]{3,2,0,1:T(8,128)} %fusion.37), kind=kLoop, calls=%fused_computation.13 | loop fusion | flops 524288 | bytes 4194304 | tf_op jit(solution)/shard_map/stack | solution.py:248
  112.0 2.0 %fusion.10 = f32[4,2,128,128]{3,0,2,1:T(4,128)S(1)} fusion(f32[16,2,128,128]{3,2,0,1:T(8,128)S(1)} %pad_maximum_fusion, s32[16]{0:T(128)S(1)} %sub.90), kind=kOutput, calls=%fused_computation.14 | convolution fusion | flops 25165888 | bytes 2621504 | tf_op jit(solution)/shard_map/sr,sxbf->rxbf/dot_general | solution.py:259
  114.1 0.9 fusion.76
  114.9 0.7 fusion.88
  115.6 8.6 %all-to-all-done.1 = bf16[8,272,128]{2,1,0:T(8,128)(2,1)S(1)} async-done(((bf16[8,272,128]{2,1,0:T(8,128)(2,1)}), bf16[8,272,128]{2,1,0:T(8,128)(2,1)S(1)}, u32[]{:S(2)}, u32[]{:S(2)}) %all-to-all-start.1) | async-done | bytes 557088 | tf_op jit(solution)/shard_map/all_to_all | solution.py:243
  124.3 0.6 fusion.66
  124.9 0.6 broadcast_multiply_fusion
  125.5 0.7 fusion.89
  (80 shorter events, 3.1 us)
Async XLA Ops:
  0.6 4.2 %copy-start = (bf16[16,32,128]{2,1,0:T(8,128)(2,1)S(1)}, bf16[16,32,128]{2,1,0:T(8,128)(2,1)}, u32[]{:S(2)}) copy-start(bf16[16,32,128]{2,1,0:T(8,128)(2,1)} %param.12) | copy-start | bytes 393220
  0.6 3.6 %copy-start.9 = (bf16[4,16,32]{2,1,0:T(8,128)(2,1)S(1)}, bf16[4,16,32]{2,1,0:T(8,128)(2,1)}, u32[]{:S(2)}) copy-start(bf16[4,16,32]{2,1,0:T(8,128)(2,1)} %param.13) | copy-start | bytes 12292
  0.7 4.2 %copy-start.6 = (bf16[16,32,128]{2,1,0:T(8,128)(2,1)S(1)}, bf16[16,32,128]{2,1,0:T(8,128)(2,1)}, u32[]{:S(2)}) copy-start(bf16[16,32,128]{2,1,0:T(8,128)(2,1)} %param.8) | copy-start | bytes 393220
  4.3 1.4 %copy-start.2 = (bf16[16,32,128]{2,1,0:T(8,128)(2,1)S(1)}, bf16[16,32,128]{2,1,0:T(8,128)(2,1)}, u32[]{:S(2)}) copy-start(bf16[16,32,128]{2,1,0:T(8,128)(2,1)} %param.10) | copy-start | bytes 393220
  4.3 1.4 %copy-start.7 = (bf16[16,32,128]{2,1,0:T(8,128)(2,1)S(1)}, bf16[16,32,128]{2,1,0:T(8,128)(2,1)}, u32[]{:S(2)}) copy-start(bf16[16,32,128]{2,1,0:T(8,128)(2,1)} %param.9) | copy-start | bytes 393220
  6.9 86.2 %all-to-all-start = ((bf16[8,544,128]{2,1,0:T(8,128)(2,1)}), bf16[8,544,128]{2,1,0:T(8,128)(2,1)S(1)}, u32[]{:S(2)}, u32[]{:S(2)}) async-start(bf16[8,544,128]{2,1,0:T(8,128)(2,1)} %bitcast.11), calls=%async_computation | async-start | bytes 2228224 | tf_op jit(solution)/shard_map/all_to_all | solution.py:174
  14.0 22.1 %collective-permute-start.3 = (bf16[16,1,128]{2,1,0:T(2,128)(2,1)S(1)}, bf16[16,1,128]{2,1,0:T(2,128)(2,1)S(1)}, u32[]{:S(2)}, u32[]{:S(2)}) collective-permute-start(bf16[16,1,128]{2,1,0:T(2,128)(2,1)S(1)} %get-tuple-element.40), channel_id=1, source_target_pairs={{0,1},{1,2},{2,3},{3,4},{4,5},{5,6},{6,7},{7,0},{8,9},{9,10},{10,1... | collective-permute-start | bytes 12296 | tf_op jit(solution)/shard_map/ppermute | solution.py:182
  17.9 22.4 %collective-permute-start = (bf16[1,32,128]{2,1,0:T(8,128)(2,1)S(1)}, bf16[1,32,128]{2,1,0:T(8,128)(2,1)S(1)}, u32[]{:S(2)}, u32[]{:S(2)}) collective-permute-start(bf16[1,32,128]{2,1,0:T(8,128)(2,1)S(1)} %get-tuple-element.42), channel_id=1, source_target_pairs={{8,0},{16,8},{24,16},{32,24},{40,32},{48,40},{56,48},{64,56},{72,6... | collective-permute-start | bytes 24584 | tf_op jit(solution)/shard_map/ppermute | solution.py:179
  19.9 20.5 %collective-permute-start.1 = (bf16[1,32,128]{2,1,0:T(8,128)(2,1)S(1)}, bf16[1,32,128]{2,1,0:T(8,128)(2,1)S(1)}, u32[]{:S(2)}, u32[]{:S(2)}) collective-permute-start(bf16[1,32,128]{2,1,0:T(8,128)(2,1)S(1)} %get-tuple-element.41), channel_id=1, source_target_pairs={{0,8},{8,16},{16,24},{24,32},{32,40},{40,48},{48,56},{56,64},{64,7... | collective-permute-start | bytes 24584 | tf_op jit(solution)/shard_map/ppermute | solution.py:178
  22.3 18.1 %collective-permute-start.2 = (bf16[16,1,128]{2,1,0:T(2,128)(2,1)S(1)}, bf16[16,1,128]{2,1,0:T(2,128)(2,1)S(1)}, u32[]{:S(2)}, u32[]{:S(2)}) collective-permute-start(bf16[16,1,128]{2,1,0:T(2,128)(2,1)S(1)} %get-tuple-element.39), channel_id=1, source_target_pairs={{1,0},{2,1},{3,2},{4,3},{5,4},{6,5},{7,6},{0,7},{9,8},{10,9},{11,1... | collective-permute-start | bytes 12296 | tf_op jit(solution)/shard_map/ppermute | solution.py:183
  25.5 0.7 copy-start.8
  25.5 14.9 %copy-start.3 = (bf16[16,32,128]{2,1,0:T(8,128)(2,1)S(1)}, bf16[16,32,128]{2,1,0:T(8,128)(2,1)}, u32[]{:S(2)}) copy-start(bf16[16,32,128]{2,1,0:T(8,128)(2,1)} %param.10) | copy-start | bytes 393220
  27.4 34.1 %copy-start.10 = (f32[5,128]{1,0:T(8,128)S(1)}, f32[5,128]{1,0:T(8,128)}, u32[]{:S(2)}) copy-start(f32[5,128]{1,0:T(8,128)} %param.15) | copy-start | bytes 7684
  40.6 4.1 %collective-permute-start.4 = (f32[5,128]{1,0:T(8,128)S(1)}, f32[5,128]{1,0:T(8,128)S(1)}, u32[]{:S(2)}, u32[]{:S(2)}) collective-permute-start(f32[5,128]{1,0:T(8,128)S(1)} %stack.50), channel_id=1, source_target_pairs={{0,8},{8,0},{16,24},{24,16},{32,40},{40,32},{48,56},{56,48},{64,72... | collective-permute-start | bytes 7688 | tf_op jit(solution)/shard_map/ppermute | solution.py:45
  44.7 5.5 %collective-permute-start.5 = (f32[5,128]{1,0:T(8,128)S(1)}, f32[5,128]{1,0:T(8,128)S(1)}, u32[]{:S(2)}, u32[]{:S(2)}) collective-permute-start(f32[5,128]{1,0:T(8,128)S(1)} %add.125), channel_id=1, source_target_pairs={{0,16},{8,24},{16,0},{24,8},{32,48},{40,56},{48,32},{56,40},{64,80... | collective-permute-start | bytes 7688 | tf_op jit(solution)/shard_map/ppermute | solution.py:45
  50.2 7.0 %collective-permute-start.6 = (f32[5,128]{1,0:T(8,128)S(1)}, f32[5,128]{1,0:T(8,128)S(1)}, u32[]{:S(2)}, u32[]{:S(2)}) collective-permute-start(f32[5,128]{1,0:T(8,128)S(1)} %add.126), channel_id=1, source_target_pairs={{0,32},{8,40},{16,48},{24,56},{32,0},{40,8},{48,16},{56,24},{64,96... | collective-permute-start | bytes 7688 | tf_op jit(solution)/shard_map/ppermute | solution.py:45
  57.2 5.8 %collective-permute-start.7 = (f32[5,128]{1,0:T(8,128)S(1)}, f32[5,128]{1,0:T(8,128)S(1)}, u32[]{:S(2)}, u32[]{:S(2)}) collective-permute-start(f32[5,128]{1,0:T(8,128)S(1)} %add.127), channel_id=1, source_target_pairs={{0,64},{8,72},{16,80},{24,88},{32,96},{40,104},{48,112},{56,120},{... | collective-permute-start | bytes 7688 | tf_op jit(solution)/shard_map/ppermute | solution.py:45
  63.0 7.7 %collective-permute-start.8 = (f32[5,128]{1,0:T(8,128)S(1)}, f32[5,128]{1,0:T(8,128)S(1)}, u32[]{:S(2)}, u32[]{:S(2)}) collective-permute-start(f32[5,128]{1,0:T(8,128)S(1)} %add.128), channel_id=1, source_target_pairs={{0,128},{8,136},{16,144},{24,152},{32,160},{40,168},{48,176},{56,1... | collective-permute-start | bytes 7688 | tf_op jit(solution)/shard_map/ppermute | solution.py:45
  70.7 15.0 %collective-permute-start.9 = (f32[5,128]{1,0:T(8,128)S(1)}, f32[5,128]{1,0:T(8,128)S(1)}, u32[]{:S(2)}, u32[]{:S(2)}) collective-permute-start(f32[5,128]{1,0:T(8,128)S(1)} %add.129), channel_id=1, source_target_pairs={{0,512},{8,520},{16,528},{24,536},{32,544},{40,552},{48,560},{56,5... | collective-permute-start | bytes 7688 | tf_op jit(solution)/shard_map/ppermute | solution.py:53
  83.6 9.4 %collective-permute-start.10 = (f32[5,128]{1,0:T(8,128)S(1)}, f32[5,128]{1,0:T(8,128)S(1)}, u32[]{:S(2)}, u32[]{:S(2)}) collective-permute-start(f32[5,128]{1,0:T(8,128)S(1)} %add.129), channel_id=1, source_target_pairs={{0,256},{8,264},{16,272},{24,280},{32,288},{40,296},{48,304},{56,3... | collective-permute-start | bytes 7688 | tf_op jit(solution)/shard_map/ppermute | solution.py:53
  95.3 1.0 copy-start.1
  104.8 19.5 %all-to-all-start.1 = ((bf16[8,272,128]{2,1,0:T(8,128)(2,1)}), bf16[8,272,128]{2,1,0:T(8,128)(2,1)S(1)}, u32[]{:S(2)}, u32[]{:S(2)}) async-start(bf16[8,272,128]{2,1,0:T(8,128)(2,1)} %pad_maximum_fusion.2), calls=%async_computation.1 | async-start | bytes 1114112 | tf_op jit(solution)/shard_map/all_to_all | solution.py:243
  114.0 1.0 copy-start.4
  114.1 11.4 %copy-start.5 = (f32[4,128,128]{2,1,0:T(8,128)S(1)}, f32[4,128,128]{2,1,0:T(8,128)}, u32[]{:S(2)}) copy-start(f32[4,128,128]{2,1,0:T(8,128)} %fusion.47) | copy-start | bytes 786436

commit v12 on v8

--- a/solution.py
+++ b/solution.py
@@ -200,8 +200,9 @@
     )
     point_count = tile_x * tile_y * count_x * group_size
     pack_in = pack_in[:, : capacity * slot_rows].reshape(group_size, capacity, slot_rows, features)
-    partial_rows, pack_in = lax.optimization_barrier((partial_rows, pack_in))
-    column_sum = gather_sum(gather_sum(partial_rows, INNER), OUTER)
+    plane_sum = gather_sum(partial_rows, INNER)
+    plane_sum, pack_in = lax.optimization_barrier((plane_sum, pack_in))
+    column_sum = gather_sum(plane_sum, OUTER)
     rows_in = pack_in[:, :, :row_count].reshape(group_size, capacity, 2, BLOCK, features)
     stats_in = pack_in[:, :, row_count : row_count + 2 * HEADS].reshape(
         group_size, capacity, 2, HEADS, BLOCK

time: 118 us -> 108 us (0.915)
  waiting for transfers between devices: 44.3 us -> 37.8 us
  other arithmetic: 11.7 us -> 8.57 us
  matrix products: 17.4 us -> 16.1 us
    all_to_all x2, waiting for transfers between devices: 9.24 us -> 4.01 us  [gather_sum(): lax.all_to_all(spread, axis, split_axis=0, concat_axis=0, tiled=True)]
    another operation x1, other arithmetic: 1.68 us -> 0.19 us  [per_device(): jnp.stack([key_part, value_part], 2)]
    dot_general x2, matrix products: 4.01 us -> 2.8 us  [tile_grads(): jnp.einsum('shqk,shqf->skf', weights_low, grad_heads, preferred_element_t...]
  transfers between devices with their start and end apart: 6 -> 6, of which waited for: 3 -> 4; matrix products, arithmetic and copies ran while one was open for 19% -> 18% of each run, Pallas kernels for 0% -> 0%
where the time goes in v12:
time: 108 us; the launch traced here: 106 us
  waiting for transfers between devices  37.8 us (35%)
  starting transfers between devices  35.1 us (32%)
  matrix products  16.1 us (15%)
  other arithmetic  8.57 us (8%)
  local copies, waits for them, and re-layouts  7.23 us (7%)
  between operations  1.47 us (1%)
    all_to_all x1, waiting for transfers between devices, per_device(): lax.all_to_all(send_pack, 'gy', split_axis=0, concat_axis=0, tiled=True)  22.3 us
    all_to_all x2, starting transfers between devices, gather_sum(): lax.all_to_all(spread, axis, split_axis=0, concat_axis=0, tiled=True)  19.9 us
    all_to_all x1, waiting for transfers between devices, per_device(): lax.all_to_all(return_pack, 'gy', split_axis=0, concat_axis=0, tiled=True)  11.5 us
    all_to_all x1, starting transfers between devices, per_device(): lax.all_to_all(send_pack, 'gy', split_axis=0, concat_axis=0, tiled=True)  7.12 us
    all_to_all x2, waiting for transfers between devices, gather_sum(): lax.all_to_all(spread, axis, split_axis=0, concat_axis=0, tiled=True)  4.01 us
    all_to_all x1, starting transfers between devices, per_device(): lax.all_to_all(return_pack, 'gy', split_axis=0, concat_axis=0, tiled=True)  3.72 us
    dot_general x2, matrix products, tile_grads(): jnp.einsum('shqf,skf->shqk', grad_heads, value_rows, preferred_element_ty...  2.94 us
    dot_general x2, matrix products, tile_grads(): jnp.einsum('shqk,shqf->skf', weights_low, grad_heads, preferred_element_t...  2.8 us
  transfers between devices with their start and end apart: 6, of which 4 were waited for; matrix products, arithmetic and copies ran while one was open for 18% of the time, Pallas kernels for 0%

profile of v12, /device:TPU:6, one launch (start us, length us, event | category | flops | bytes accessed | tf_op | source)
XLA Modules:
  0.0 106.3 jit_solution(3113384308987177569)
XLA Ops:
  0.7 0.8 fusion.140
  1.5 0.8 copy.173
  2.8 1.0 convert_multiply_fusion.10
  3.8 0.4 reshape.271
  4.2 0.7 reduce_sum.91
  5.2 0.3 fusion.110
  5.5 0.2 fusion.49
  5.7 0.5 fusion.29
  6.7 1.1 %pad_maximum_fusion.1 = bf16[8,576,128]{2,1,0:T(8,128)(2,1)} fusion(bf16[8,32,128]{2,1,0:T(8,128)(2,1)S(1)} %broadcast_in_dim.18, bf16[8,544,128]{2,1,0:T(8,128)(2,1)S(1)} %bitcast.190), kind=kLoop, calls=%fused_computation.35 | loop fusion | flops 2359296 | bytes 2359296 | tf_op jit(solution)/shard_map/concatenate | solution.py:160
  7.8 7.1 %all-to-all-start = ((bf16[8,576,128]{2,1,0:T(8,128)(2,1)}), bf16[8,576,128]{2,1,0:T(8,128)(2,1)S(1)}, u32[]{:S(2)}, u32[]{:S(2)}) async-start(bf16[8,576,128]{2,1,0:T(8,128)(2,1)} %pad_maximum_fusion.1), calls=%async_computation | async-start | bytes 2359296 | tf_op jit(solution)/shard_map/all_to_all | solution.py:170
  15.0 0.6 fusion.138
  15.6 1.9 %collective-permute-start = (bf16[1,32,128]{2,1,0:T(8,128)(2,1)}, bf16[1,32,128]{2,1,0:T(8,128)(2,1)S(1)}, u32[]{:S(2)}, u32[]{:S(2)}) collective-permute-start(bf16[1,32,128]{2,1,0:T(8,128)(2,1)} %get-tuple-element.42), channel_id=1, source_target_pairs={{8,0},{16,8},{24,16},{32,24},{40,32},{48,40},{56,48},{64,56},{72,6... | collective-permute-start | bytes 24584 | tf_op jit(solution)/shard_map/ppermute | solution.py:186
  17.5 2.4 %collective-permute-start.1 = (bf16[1,32,128]{2,1,0:T(8,128)(2,1)}, bf16[1,32,128]{2,1,0:T(8,128)(2,1)S(1)}, u32[]{:S(2)}, u32[]{:S(2)}) collective-permute-start(bf16[1,32,128]{2,1,0:T(8,128)(2,1)} %get-tuple-element.41), channel_id=1, source_target_pairs={{0,8},{8,16},{16,24},{24,32},{32,40},{40,48},{48,56},{56,64},{64,7... | collective-permute-start | bytes 24584 | tf_op jit(solution)/shard_map/ppermute | solution.py:185
  20.0 0.4 fusion.33
  20.4 0.3 convolution_bitcast_fusion
  20.9 0.4 fusion.46
  21.3 2.0 %fusion.48 = f32[4,128,128]{2,1,0:T(8,128)} fusion(bf16[4,4,128,128]{3,2,1,0:T(8,128)(2,1)S(1)} %fusion.46, bf16[4,128]{1,0:T(4,128)(2,1)S(1)} %fusion.121, bf16[4,128,128]{2,1,0:T(8,128)(2,1)} %copy-done.7), kind=kOutput, calls=%fused_computation.40 | convolution fusion | flops 67436544 | bytes 918528 | tf_op jit(solution)/shard_map/shqk,shqf->skf/dot_general | solution.py:96
  23.3 1.0 fusion.47
  24.3 22.3 %all-to-all-done = bf16[8,576,128]{2,1,0:T(8,128)(2,1)S(1)} async-done(((bf16[8,576,128]{2,1,0:T(8,128)(2,1)}), bf16[8,576,128]{2,1,0:T(8,128)(2,1)S(1)}, u32[]{:S(2)}, u32[]{:S(2)}) %all-to-all-start) | async-done | bytes 1179680 | tf_op jit(solution)/shard_map/all_to_all | solution.py:170
  46.7 0.2 fusion.81
  46.9 0.6 broadcast_in_dim.21
  47.5 4.8 %all-to-all-start.1 = ((f32[8,5,128]{2,1,0:T(8,128)}), f32[8,5,128]{2,1,0:T(8,128)S(1)}, u32[]{:S(2)}, u32[]{:S(2)}) async-start(f32[8,5,128]{2,1,0:T(8,128)} %broadcast_in_dim.21), calls=%async_computation.1 | async-start | bytes 65536 | tf_op jit(solution)/shard_map/all_to_all | solution.py:58
  52.3 0.6 slice_bitcast_fusion.14
  53.0 2.7 %all-to-all-done.1 = f32[8,5,128]{2,1,0:T(8,128)S(1)} async-done(((f32[8,5,128]{2,1,0:T(8,128)}), f32[8,5,128]{2,1,0:T(8,128)S(1)}, u32[]{:S(2)}, u32[]{:S(2)}) %all-to-all-start.1) | async-done | bytes 20512 | tf_op jit(solution)/shard_map/all_to_all | solution.py:58
  55.8 0.4 add_reduce_fusion
  56.2 0.6 broadcast_in_dim.22
  56.8 15.2 %all-to-all-start.2 = ((f32[12,5,128]{2,1,0:T(8,128)}), f32[12,5,128]{2,1,0:T(8,128)}, u32[]{:S(2)}, u32[]{:S(2)}) async-start(f32[12,5,128]{2,1,0:T(8,128)} %broadcast_in_dim.22), calls=%async_computation.2 | async-start | bytes 98304 | tf_op jit(solution)/shard_map/all_to_all | solution.py:58
  72.0 0.9 slice_bitcast_fusion.2
  73.0 0.5 fusion.30
  73.5 0.2 copy.228
  73.8 0.7 fusion.7
  74.5 0.3 copy-done.1
  74.8 2.5 %fusion.24 = f32[16,1,128,128]{3,2,0,1:T(8,128)S(1)} fusion(f32[16,4,128,128]{3,2,1,0:T(8,128)S(1)} %fusion.7, f32[16,4,128]{2,1,0:T(4,128)S(1)} %get-tuple-element.49, bf16[16,128,128]{2,1,0:T(8,128)(2,1)S(1)} %copy-done.1, bf16[4,128]{1,0:T(4,128)(2,1)S(1)} %copy-done.20), kind=kOutput, calls=%fused_computation.22 | convolution fusion | flops 272629760 | bytes 5800960 | tf_op jit(solution)/shard_map/shqk,shqf->skf/dot_general | solution.py:92
  77.3 2.6 %multiply_convert_fusion = bf16[16,4,128,128]{3,2,1,0:T(8,128)(2,1)S(1)} fusion(f32[16,4,128,128]{3,2,1,0:T(8,128)S(1)} %fusion.7, f32[16,4,128]{2,1,0:T(4,128)S(1)} %get-tuple-element.50, f32[16,4,128]{2,1,0:T(4,128)S(1)} %get-tuple-element.49, bf16[16,128,128]{2,1,0:T(8,128)(2,1)S(1)} %copy-done.1, bf16[4,128]{1,0:T(4,128)(2,1)S(1)} %copy-done.20, ...), kind=kOutput, calls=%fused_computation.2 | convolution fusion | flops 274726912 | bytes 7406592 | tf_op jit(solution)/shard_map/shqf,skf->shqk/dot_general | solution.py:86
  79.8 0.8 fusion.37
  80.7 0.7 fusion.43
  81.4 0.2 pad_maximum_fusion
  81.6 1.3 %all-to-all-done.2 = f32[12,5,128]{2,1,0:T(8,128)} async-done(((f32[12,5,128]{2,1,0:T(8,128)}), f32[12,5,128]{2,1,0:T(8,128)}, u32[]{:S(2)}, u32[]{:S(2)}) %all-to-all-start.2) | async-done | bytes 30752 | tf_op jit(solution)/shard_map/all_to_all | solution.py:58
  82.9 0.8 reduce_sum.98
  83.8 0.9 pad_maximum_fusion.3
  84.6 3.7 %all-to-all-start.3 = ((bf16[8,272,128]{2,1,0:T(8,128)(2,1)}), bf16[8,272,128]{2,1,0:T(8,128)(2,1)S(1)}, u32[]{:S(2)}, u32[]{:S(2)}) async-start(bf16[8,272,128]{2,1,0:T(8,128)(2,1)} %pad_maximum_fusion.3), calls=%async_computation.3 | async-start | bytes 1114112 | tf_op jit(solution)/shard_map/all_to_all | solution.py:244
  88.4 2.6 %fusion.10 = f32[4,2,128,128]{3,0,2,1:T(4,128)S(1)} fusion(f32[16,2,128,128]{3,2,0,1:T(8,128)S(1)} %pad_maximum_fusion, s32[16]{0:T(128)} %copy-done.21), kind=kOutput, calls=%fused_computation.14 | convolution fusion | flops 25165888 | bytes 2621504 | tf_op jit(solution)/shard_map/sr,sxbf->rxbf/dot_general | solution.py:260
  91.3 0.8 fusion.76
  92.1 0.7 fusion.88
  92.8 11.5 %all-to-all-done.3 = bf16[8,272,128]{2,1,0:T(8,128)(2,1)S(1)} async-done(((bf16[8,272,128]{2,1,0:T(8,128)(2,1)}), bf16[8,272,128]{2,1,0:T(8,128)(2,1)S(1)}, u32[]{:S(2)}, u32[]{:S(2)}) %all-to-all-start.3) | async-done | bytes 557088 | tf_op jit(solution)/shard_map/all_to_all | solution.py:244
  104.4 0.6 fusion.66
  105.0 0.6 broadcast_multiply_fusion
  105.6 0.7 fusion.89
  (107 shorter events, 2.0 us)
Async XLA Ops:
  0.6 5.0 %copy-start = (bf16[16,32,128]{2,1,0:T(8,128)(2,1)S(1)}, bf16[16,32,128]{2,1,0:T(8,128)(2,1)}, u32[]{:S(2)}) copy-start(bf16[16,32,128]{2,1,0:T(8,128)(2,1)} %param.12) | copy-start | bytes 393220
  0.6 4.4 %copy-start.18 = (bf16[4,16,32]{2,1,0:T(8,128)(2,1)S(1)}, bf16[4,16,32]{2,1,0:T(8,128)(2,1)}, u32[]{:S(2)}) copy-start(bf16[4,16,32]{2,1,0:T(8,128)(2,1)} %param.13) | copy-start | bytes 12292
  0.7 5.0 %copy-start.5 = (bf16[16,32,128]{2,1,0:T(8,128)(2,1)S(1)}, bf16[16,32,128]{2,1,0:T(8,128)(2,1)}, u32[]{:S(2)}) copy-start(bf16[16,32,128]{2,1,0:T(8,128)(2,1)} %param.8) | copy-start | bytes 393220
  5.4 1.1 %copy-start.16 = (f32[16,4]{0,1:T(4,128)}, f32[16,4]{0,1:T(4,128)S(1)}, u32[]{:S(2)}) copy-start(f32[16,4]{0,1:T(4,128)S(1)} %fusion.110) | copy-start | bytes 772
  6.6 1.3 %copy-start.2 = (bf16[16,32,128]{2,1,0:T(8,128)(2,1)S(1)}, bf16[16,32,128]{2,1,0:T(8,128)(2,1)}, u32[]{:S(2)}) copy-start(bf16[16,32,128]{2,1,0:T(8,128)(2,1)} %param.10) | copy-start | bytes 393220
  6.6 1.2 %copy-start.6 = (bf16[16,32,128]{2,1,0:T(8,128)(2,1)S(1)}, bf16[16,32,128]{2,1,0:T(8,128)(2,1)}, u32[]{:S(2)}) copy-start(bf16[16,32,128]{2,1,0:T(8,128)(2,1)} %param.9) | copy-start | bytes 393220
  7.8 38.7 %all-to-all-start = ((bf16[8,576,128]{2,1,0:T(8,128)(2,1)}), bf16[8,576,128]{2,1,0:T(8,128)(2,1)S(1)}, u32[]{:S(2)}, u32[]{:S(2)}) async-start(bf16[8,576,128]{2,1,0:T(8,128)(2,1)} %pad_maximum_fusion.1), calls=%async_computation | async-start | bytes 2359296 | tf_op jit(solution)/shard_map/all_to_all | solution.py:170
  15.6 31.0 %collective-permute-start = (bf16[1,32,128]{2,1,0:T(8,128)(2,1)}, bf16[1,32,128]{2,1,0:T(8,128)(2,1)S(1)}, u32[]{:S(2)}, u32[]{:S(2)}) collective-permute-start(bf16[1,32,128]{2,1,0:T(8,128)(2,1)} %get-tuple-element.42), channel_id=1, source_target_pairs={{8,0},{16,8},{24,16},{32,24},{40,32},{48,40},{56,48},{64,56},{72,6... | collective-permute-start | bytes 24584 | tf_op jit(solution)/shard_map/ppermute | solution.py:186
  17.5 29.2 %collective-permute-start.1 = (bf16[1,32,128]{2,1,0:T(8,128)(2,1)}, bf16[1,32,128]{2,1,0:T(8,128)(2,1)S(1)}, u32[]{:S(2)}, u32[]{:S(2)}) collective-permute-start(bf16[1,32,128]{2,1,0:T(8,128)(2,1)} %get-tuple-element.41), channel_id=1, source_target_pairs={{0,8},{8,16},{16,24},{24,32},{32,40},{40,48},{48,56},{56,64},{64,7... | collective-permute-start | bytes 24584 | tf_op jit(solution)/shard_map/ppermute | solution.py:185
  20.0 0.9 copy-start.7
  20.0 3.2 %copy-start.19 = (bf16[4,128]{1,0:T(4,128)(2,1)}, bf16[4,128]{1,0:T(4,128)(2,1)S(1)}, u32[]{:S(2)}) copy-start(bf16[4,128]{1,0:T(4,128)(2,1)S(1)} %fusion.121) | copy-start | bytes 3076
  20.9 31.4 %copy-start.27 = (f32[5,128]{1,0:T(8,128)S(1)}, f32[5,128]{1,0:T(8,128)}, u32[]{:S(2)}) copy-start(f32[5,128]{1,0:T(8,128)} %param.15) | copy-start | bytes 7684
  46.6 5.7 %copy-start.8 = (bf16[16,1,128]{2,1,0:T(2,128)(2,1)}, bf16[16,1,128]{2,1,0:T(2,128)(2,1)S(1)}, u32[]{:S(2)}) copy-start(bf16[16,1,128]{2,1,0:T(2,128)(2,1)S(1)} %copy.184) | copy-start | bytes 12292
  46.6 5.7 %copy-start.10 = (bf16[16,1,128]{2,1,0:T(2,128)(2,1)}, bf16[16,1,128]{2,1,0:T(2,128)(2,1)S(1)}, u32[]{:S(2)}) copy-start(bf16[16,1,128]{2,1,0:T(2,128)(2,1)S(1)} %copy.183) | copy-start | bytes 12292
  46.6 9.2 %copy-start.12 = (bf16[1,32,128]{2,1,0:T(8,128)(2,1)}, bf16[1,32,128]{2,1,0:T(8,128)(2,1)S(1)}, u32[]{:S(2)}) copy-start(bf16[1,32,128]{2,1,0:T(8,128)(2,1)S(1)} %collective-permute-done) | copy-start | bytes 24580
  46.6 9.1 %copy-start.14 = (bf16[1,32,128]{2,1,0:T(8,128)(2,1)}, bf16[1,32,128]{2,1,0:T(8,128)(2,1)S(1)}, u32[]{:S(2)}) copy-start(bf16[1,32,128]{2,1,0:T(8,128)(2,1)S(1)} %collective-permute-done.1) | copy-start | bytes 24580
  47.5 8.2 %all-to-all-start.1 = ((f32[8,5,128]{2,1,0:T(8,128)}), f32[8,5,128]{2,1,0:T(8,128)S(1)}, u32[]{:S(2)}, u32[]{:S(2)}) async-start(f32[8,5,128]{2,1,0:T(8,128)} %broadcast_in_dim.21), calls=%async_computation.1 | async-start | bytes 65536 | tf_op jit(solution)/shard_map/all_to_all | solution.py:58
  56.8 26.1 %all-to-all-start.2 = ((f32[12,5,128]{2,1,0:T(8,128)}), f32[12,5,128]{2,1,0:T(8,128)}, u32[]{:S(2)}, u32[]{:S(2)}) async-start(f32[12,5,128]{2,1,0:T(8,128)} %broadcast_in_dim.22), calls=%async_computation.2 | async-start | bytes 98304 | tf_op jit(solution)/shard_map/all_to_all | solution.py:58
  73.0 0.8 copy-start.21
  73.0 0.8 copy-start.20
  73.7 1.0 copy-start.1
  84.6 19.7 %all-to-all-start.3 = ((bf16[8,272,128]{2,1,0:T(8,128)(2,1)}), bf16[8,272,128]{2,1,0:T(8,128)(2,1)S(1)}, u32[]{:S(2)}, u32[]{:S(2)}) async-start(bf16[8,272,128]{2,1,0:T(8,128)(2,1)} %pad_maximum_fusion.3), calls=%async_computation.3 | async-start | bytes 1114112 | tf_op jit(solution)/shard_map/all_to_all | solution.py:244
  88.3 2.9 %copy-start.9 = (bf16[16,1,128]{2,1,0:T(2,128)(2,1)S(1)}, bf16[16,1,128]{2,1,0:T(2,128)(2,1)}, u32[]{:S(2)}) copy-start(bf16[16,1,128]{2,1,0:T(2,128)(2,1)} %copy-done.8) | copy-start | bytes 12292
  88.4 2.9 %copy-start.11 = (bf16[16,1,128]{2,1,0:T(2,128)(2,1)S(1)}, bf16[16,1,128]{2,1,0:T(2,128)(2,1)}, u32[]{:S(2)}) copy-start(bf16[16,1,128]{2,1,0:T(2,128)(2,1)} %copy-done.10) | copy-start | bytes 12292
  88.4 2.9 %copy-start.13 = (bf16[1,32,128]{2,1,0:T(8,128)(2,1)S(1)}, bf16[1,32,128]{2,1,0:T(8,128)(2,1)}, u32[]{:S(2)}) copy-start(bf16[1,32,128]{2,1,0:T(8,128)(2,1)} %copy-done.12) | copy-start | bytes 24580
  88.4 2.9 %copy-start.15 = (bf16[1,32,128]{2,1,0:T(8,128)(2,1)S(1)}, bf16[1,32,128]{2,1,0:T(8,128)(2,1)}, u32[]{:S(2)}) copy-start(bf16[1,32,128]{2,1,0:T(8,128)(2,1)} %copy-done.14) | copy-start | bytes 24580
  88.4 2.9 %copy-start.22 = (f32[128]{0:T(128)S(1)}, f32[128]{0:T(128)}, u32[]{:S(2)}) copy-start(f32[128]{0:T(128)} %get-tuple-element.53) | copy-start | bytes 1540
  88.4 2.9 %copy-start.23 = (f32[128]{0:T(128)S(1)}, f32[128]{0:T(128)}, u32[]{:S(2)}) copy-start(f32[128]{0:T(128)} %get-tuple-element.54) | copy-start | bytes 1540
  88.4 2.9 %copy-start.24 = (f32[128]{0:T(128)S(1)}, f32[128]{0:T(128)}, u32[]{:S(2)}) copy-start(f32[128]{0:T(128)} %get-tuple-element.55) | copy-start | bytes 1540
  88.4 2.9 %copy-start.25 = (f32[128]{0:T(128)S(1)}, f32[128]{0:T(128)}, u32[]{:S(2)}) copy-start(f32[128]{0:T(128)} %get-tuple-element.56) | copy-start | bytes 1540
  88.4 2.9 %copy-start.26 = (f32[128]{0:T(128)S(1)}, f32[128]{0:T(128)}, u32[]{:S(2)}) copy-start(f32[128]{0:T(128)} %get-tuple-element.57) | copy-start | bytes 1540
  91.1 1.1 copy-start.4
  91.1 13.3 %copy-start.17 = (f32[16,4]{0,1:T(4,128)S(1)}, f32[16,4]{0,1:T(4,128)}, u32[]{:S(2)}) copy-start(f32[16,4]{0,1:T(4,128)} %copy-done.16) | copy-start | bytes 772
  91.2 14.4 %copy-start.3 = (f32[4,128,128]{2,1,0:T(8,128)S(1)}, f32[4,128,128]{2,1,0:T(8,128)}, u32[]{:S(2)}) copy-start(f32[4,128,128]{2,1,0:T(8,128)} %fusion.47) | copy-start | bytes 786436

commit v13 on v12

--- a/solution.py
+++ b/solution.py
@@ -156,11 +156,13 @@
         [send_rows.reshape(group_size, capacity, row_count, features), stat_rows, id_rows], 2
     )
     slot_rows = send_pack.shape[2]
-    edges = jnp.concatenate([out_grad[:, 0], out_grad[:, tile_y - 1]], 0)
+    target = jnp.arange(group_size, dtype=jnp.int32)[:, None, None]
+    upper = (lax.axis_index("gy") + 1) % group_size
+    edge_out = jnp.where(target == upper, out_grad[None, :, tile_y - 1], out_grad[None, :, 0])
     send_pack = jnp.concatenate(
         [
             send_pack.reshape(group_size, capacity * slot_rows, features),
-            jnp.broadcast_to(edges[None], (group_size,) + edges.shape),
+            edge_out,
         ],
         1,
     )
@@ -176,8 +178,6 @@
     edge_in = pack_in[:, capacity * slot_rows :]
     before_col = lax.dynamic_index_in_dim(edge_in, (column + group_size - 1) % group_size, 0, False)
     after_col = lax.dynamic_index_in_dim(edge_in, (column + 1) % group_size, 0, False)
-    before_col = before_col[tile_x:]
-    after_col = after_col[:tile_x]
     grad_x, values_x = lax.optimization_barrier((out_grad, values))
     count_x = (lax.axis_size(OUTER) * lax.axis_size(INNER))
     ahead = [(i, (i + 1) % count_x) for i in range(count_x)]

time: 108 us -> 108 us (level)
  transfers between devices with their start and end apart: 6 -> 6, of which waited for: 4 -> 4; matrix products, arithmetic and copies ran while one was open for 18% -> 17% of each run, Pallas kernels for 0% -> 0%
where the time goes in v13:
time: 108 us; the launch traced here: 106 us
  waiting for transfers between devices  37.7 us (35%)
  starting transfers between devices  35.1 us (32%)
  matrix products  16.1 us (15%)
  other arithmetic  8.65 us (8%)
  local copies, waits for them, and re-layouts  6.66 us (6%)
  between operations  1.46 us (1%)
    all_to_all x1, waiting for transfers between devices, per_device(): lax.all_to_all(send_pack, 'gy', split_axis=0, concat_axis=0, tiled=True)  22.2 us
    all_to_all x2, starting transfers between devices, gather_sum(): lax.all_to_all(spread, axis, split_axis=0, concat_axis=0, tiled=True)  19.9 us
    all_to_all x1, waiting for transfers between devices, per_device(): lax.all_to_all(return_pack, 'gy', split_axis=0, concat_axis=0, tiled=True)  11.5 us
    all_to_all x1, starting transfers between devices, per_device(): lax.all_to_all(send_pack, 'gy', split_axis=0, concat_axis=0, tiled=True)  7.11 us
    all_to_all x2, waiting for transfers between devices, gather_sum(): lax.all_to_all(spread, axis, split_axis=0, concat_axis=0, tiled=True)  4.01 us
    all_to_all x1, starting transfers between devices, per_device(): lax.all_to_all(return_pack, 'gy', split_axis=0, concat_axis=0, tiled=True)  3.72 us
    dot_general x2, matrix products, tile_grads(): jnp.einsum('shqf,skf->shqk', grad_heads, value_rows, preferred_element_ty...  2.95 us
    dot_general x2, matrix products, tile_grads(): jnp.einsum('shqk,shqf->skf', weights_low, grad_heads, preferred_element_t...  2.79 us
  transfers between devices with their start and end apart: 6, of which 4 were waited for; matrix products, arithmetic and copies ran while one was open for 17% of the time, Pallas kernels for 0%

profile of v13, /device:TPU:6, one launch (start us, length us, event | category | flops | bytes accessed | tf_op | source)
XLA Modules:
  0.0 105.7 jit_solution(12078803651781551749)
XLA Ops:
  0.7 0.9 fusion.140
  1.6 0.8 copy.172
  2.8 1.0 convert_multiply_fusion.10
  3.9 0.4 reshape.275
  4.3 0.7 reduce_sum.91
  5.2 0.3 fusion.110
  5.5 0.2 fusion.49
  5.8 0.5 fusion.29
  6.3 0.2 copy.224
  6.8 1.1 %pad_maximum_fusion.1 = bf16[8,560,128]{2,1,0:T(8,128)(2,1)} fusion(bf16[8,16,128]{2,1,0:T(8,128)(2,1)S(1)} %broadcast_select_fusion, bf16[8,544,128]{2,1,0:T(8,128)(2,1)S(1)} %bitcast.190), kind=kLoop, calls=%fused_computation.40 | loop fusion | flops 2293760 | bytes 2293760 | tf_op jit(solution)/shard_map/concatenate | solution.py:162
  8.0 7.1 %all-to-all-start = ((bf16[8,560,128]{2,1,0:T(8,128)(2,1)}), bf16[8,560,128]{2,1,0:T(8,128)(2,1)S(1)}, u32[]{:S(2)}, u32[]{:S(2)}) async-start(bf16[8,560,128]{2,1,0:T(8,128)(2,1)} %pad_maximum_fusion.1), calls=%async_computation | async-start | bytes 2293760 | tf_op jit(solution)/shard_map/all_to_all | solution.py:172
  15.1 1.9 %collective-permute-start = (bf16[1,32,128]{2,1,0:T(8,128)(2,1)S(1)}, bf16[1,32,128]{2,1,0:T(8,128)(2,1)S(1)}, u32[]{:S(2)}, u32[]{:S(2)}) collective-permute-start(bf16[1,32,128]{2,1,0:T(8,128)(2,1)S(1)} %get-tuple-element.42), channel_id=1, source_target_pairs={{8,0},{16,8},{24,16},{32,24},{40,32},{48,40},{56,48},{64,56},{72,6... | collective-permute-start | bytes 24584 | tf_op jit(solution)/shard_map/ppermute | solution.py:186
  17.0 2.4 %collective-permute-start.1 = (bf16[1,32,128]{2,1,0:T(8,128)(2,1)S(1)}, bf16[1,32,128]{2,1,0:T(8,128)(2,1)S(1)}, u32[]{:S(2)}, u32[]{:S(2)}) collective-permute-start(bf16[1,32,128]{2,1,0:T(8,128)(2,1)S(1)} %get-tuple-element.41), channel_id=1, source_target_pairs={{0,8},{8,16},{16,24},{24,32},{32,40},{40,48},{48,56},{56,64},{64,7... | collective-permute-start | bytes 24584 | tf_op jit(solution)/shard_map/ppermute | solution.py:185
  19.6 0.4 fusion.33
  20.0 0.3 convolution_bitcast_fusion
  20.4 0.4 fusion.46
  20.8 2.0 %fusion.48 = f32[4,128,128]{2,1,0:T(8,128)} fusion(bf16[4,4,128,128]{3,2,1,0:T(8,128)(2,1)S(1)} %fusion.46, bf16[4,128]{1,0:T(4,128)(2,1)S(1)} %fusion.121, bf16[4,128,128]{2,1,0:T(8,128)(2,1)} %copy-done.7), kind=kOutput, calls=%fused_computation.39 | convolution fusion | flops 67436544 | bytes 918528 | tf_op jit(solution)/shard_map/shqk,shqf->skf/dot_general | solution.py:96
  22.8 1.0 fusion.47
  23.8 22.2 %all-to-all-done = bf16[8,560,128]{2,1,0:T(8,128)(2,1)S(1)} async-done(((bf16[8,560,128]{2,1,0:T(8,128)(2,1)}), bf16[8,560,128]{2,1,0:T(8,128)(2,1)S(1)}, u32[]{:S(2)}, u32[]{:S(2)}) %all-to-all-start) | async-done | bytes 1146912 | tf_op jit(solution)/shard_map/all_to_all | solution.py:172
  46.1 0.2 fusion.81
  46.3 0.6 broadcast_in_dim.51
  46.9 4.8 %all-to-all-start.1 = ((f32[8,5,128]{2,1,0:T(8,128)}), f32[8,5,128]{2,1,0:T(8,128)S(1)}, u32[]{:S(2)}, u32[]{:S(2)}) async-start(f32[8,5,128]{2,1,0:T(8,128)} %broadcast_in_dim.51), calls=%async_computation.1 | async-start | bytes 65536 | tf_op jit(solution)/shard_map/all_to_all | solution.py:58
  51.7 0.6 slice_bitcast_fusion.14
  52.4 2.7 %all-to-all-done.1 = f32[8,5,128]{2,1,0:T(8,128)S(1)} async-done(((f32[8,5,128]{2,1,0:T(8,128)}), f32[8,5,128]{2,1,0:T(8,128)S(1)}, u32[]{:S(2)}, u32[]{:S(2)}) %all-to-all-start.1) | async-done | bytes 20512 | tf_op jit(solution)/shard_map/all_to_all | solution.py:58
  55.2 0.4 add_reduce_fusion
  55.6 0.6 broadcast_in_dim.52
  56.2 15.2 %all-to-all-start.2 = ((f32[12,5,128]{2,1,0:T(8,128)}), f32[12,5,128]{2,1,0:T(8,128)}, u32[]{:S(2)}, u32[]{:S(2)}) async-start(f32[12,5,128]{2,1,0:T(8,128)} %broadcast_in_dim.52), calls=%async_computation.2 | async-start | bytes 98304 | tf_op jit(solution)/shard_map/all_to_all | solution.py:58
  71.4 0.9 slice_bitcast_fusion.2
  72.4 0.5 fusion.30
  72.9 0.2 copy.227
  73.2 0.7 fusion.7
  73.9 0.3 copy-done.1
  74.2 2.5 %fusion.24 = f32[16,1,128,128]{3,2,0,1:T(8,128)S(1)} fusion(f32[16,4,128,128]{3,2,1,0:T(8,128)S(1)} %fusion.7, f32[16,4,128]{2,1,0:T(4,128)S(1)} %get-tuple-element.47, bf16[16,128,128]{2,1,0:T(8,128)(2,1)S(1)} %copy-done.1, bf16[4,128]{1,0:T(4,128)(2,1)S(1)} %copy-done.20), kind=kOutput, calls=%fused_computation.22 | convolution fusion | flops 272629760 | bytes 5800960 | tf_op jit(solution)/shard_map/shqk,shqf->skf/dot_general | solution.py:92
  76.7 2.6 %multiply_convert_fusion = bf16[16,4,128,128]{3,2,1,0:T(8,128)(2,1)S(1)} fusion(f32[16,4,128,128]{3,2,1,0:T(8,128)S(1)} %fusion.7, f32[16,4,128]{2,1,0:T(4,128)S(1)} %get-tuple-element.48, f32[16,4,128]{2,1,0:T(4,128)S(1)} %get-tuple-element.47, bf16[16,128,128]{2,1,0:T(8,128)(2,1)S(1)} %copy-done.1, bf16[4,128]{1,0:T(4,128)(2,1)S(1)} %copy-done.20, ...), kind=kOutput, calls=%fused_computation.2 | convolution fusion | flops 274726912 | bytes 7406592 | tf_op jit(solution)/shard_map/shqf,skf->shqk/dot_general | solution.py:86
  79.2 0.8 fusion.37
  80.1 0.7 fusion.43
  80.8 0.2 pad_maximum_fusion
  81.0 1.3 %all-to-all-done.2 = f32[12,5,128]{2,1,0:T(8,128)} async-done(((f32[12,5,128]{2,1,0:T(8,128)}), f32[12,5,128]{2,1,0:T(8,128)}, u32[]{:S(2)}, u32[]{:S(2)}) %all-to-all-start.2) | async-done | bytes 30752 | tf_op jit(solution)/shard_map/all_to_all | solution.py:58
  82.3 0.8 reduce_sum.98
  83.2 0.9 pad_maximum_fusion.3
  84.0 3.7 %all-to-all-start.3 = ((bf16[8,272,128]{2,1,0:T(8,128)(2,1)}), bf16[8,272,128]{2,1,0:T(8,128)(2,1)S(1)}, u32[]{:S(2)}, u32[]{:S(2)}) async-start(bf16[8,272,128]{2,1,0:T(8,128)(2,1)} %pad_maximum_fusion.3), calls=%async_computation.3 | async-start | bytes 1114112 | tf_op jit(solution)/shard_map/all_to_all | solution.py:244
  87.8 2.6 %fusion.10 = f32[4,2,128,128]{3,0,2,1:T(4,128)S(1)} fusion(f32[16,2,128,128]{3,2,0,1:T(8,128)S(1)} %pad_maximum_fusion, s32[16]{0:T(128)} %copy-done.21), kind=kOutput, calls=%fused_computation.14 | convolution fusion | flops 25165888 | bytes 2621504 | tf_op jit(solution)/shard_map/sr,sxbf->rxbf/dot_general | solution.py:260
  90.7 0.8 fusion.76
  91.5 0.7 fusion.88
  92.2 11.5 %all-to-all-done.3 = bf16[8,272,128]{2,1,0:T(8,128)(2,1)S(1)} async-done(((bf16[8,272,128]{2,1,0:T(8,128)(2,1)}), bf16[8,272,128]{2,1,0:T(8,128)(2,1)S(1)}, u32[]{:S(2)}, u32[]{:S(2)}) %all-to-all-start.3) | async-done | bytes 557088 | tf_op jit(solution)/shard_map/all_to_all | solution.py:244
  103.8 0.6 fusion.66
  104.4 0.6 broadcast_multiply_fusion
  105.0 0.7 fusion.89
  (107 shorter events, 1.9 us)
Async XLA Ops:
  0.6 5.1 %copy-start = (bf16[16,32,128]{2,1,0:T(8,128)(2,1)S(1)}, bf16[16,32,128]{2,1,0:T(8,128)(2,1)}, u32[]{:S(2)}) copy-start(bf16[16,32,128]{2,1,0:T(8,128)(2,1)} %param.12) | copy-start | bytes 393220
  0.6 4.5 %copy-start.18 = (bf16[4,16,32]{2,1,0:T(8,128)(2,1)S(1)}, bf16[4,16,32]{2,1,0:T(8,128)(2,1)}, u32[]{:S(2)}) copy-start(bf16[4,16,32]{2,1,0:T(8,128)(2,1)} %param.13) | copy-start | bytes 12292
  0.7 5.1 %copy-start.5 = (bf16[16,32,128]{2,1,0:T(8,128)(2,1)S(1)}, bf16[16,32,128]{2,1,0:T(8,128)(2,1)}, u32[]{:S(2)}) copy-start(bf16[16,32,128]{2,1,0:T(8,128)(2,1)} %param.8) | copy-start | bytes 393220
  5.5 1.2 %copy-start.16 = (f32[16,4]{0,1:T(4,128)}, f32[16,4]{0,1:T(4,128)S(1)}, u32[]{:S(2)}) copy-start(f32[16,4]{0,1:T(4,128)S(1)} %fusion.110) | copy-start | bytes 772
  6.7 1.2 %copy-start.2 = (bf16[16,32,128]{2,1,0:T(8,128)(2,1)S(1)}, bf16[16,32,128]{2,1,0:T(8,128)(2,1)}, u32[]{:S(2)}) copy-start(bf16[16,32,128]{2,1,0:T(8,128)(2,1)} %param.10) | copy-start | bytes 393220
  6.7 1.2 %copy-start.6 = (bf16[16,32,128]{2,1,0:T(8,128)(2,1)S(1)}, bf16[16,32,128]{2,1,0:T(8,128)(2,1)}, u32[]{:S(2)}) copy-start(bf16[16,32,128]{2,1,0:T(8,128)(2,1)} %param.9) | copy-start | bytes 393220
  8.0 38.0 %all-to-all-start = ((bf16[8,560,128]{2,1,0:T(8,128)(2,1)}), bf16[8,560,128]{2,1,0:T(8,128)(2,1)S(1)}, u32[]{:S(2)}, u32[]{:S(2)}) async-start(bf16[8,560,128]{2,1,0:T(8,128)(2,1)} %pad_maximum_fusion.1), calls=%async_computation | async-start | bytes 2293760 | tf_op jit(solution)/shard_map/all_to_all | solution.py:172
  15.1 30.9 %collective-permute-start = (bf16[1,32,128]{2,1,0:T(8,128)(2,1)S(1)}, bf16[1,32,128]{2,1,0:T(8,128)(2,1)S(1)}, u32[]{:S(2)}, u32[]{:S(2)}) collective-permute-start(bf16[1,32,128]{2,1,0:T(8,128)(2,1)S(1)} %get-tuple-element.42), channel_id=1, source_target_pairs={{8,0},{16,8},{24,16},{32,24},{40,32},{48,40},{56,48},{64,56},{72,6... | collective-permute-start | bytes 24584 | tf_op jit(solution)/shard_map/ppermute | solution.py:186
  17.0 29.0 %collective-permute-start.1 = (bf16[1,32,128]{2,1,0:T(8,128)(2,1)S(1)}, bf16[1,32,128]{2,1,0:T(8,128)(2,1)S(1)}, u32[]{:S(2)}, u32[]{:S(2)}) collective-permute-start(bf16[1,32,128]{2,1,0:T(8,128)(2,1)S(1)} %get-tuple-element.41), channel_id=1, source_target_pairs={{0,8},{8,16},{16,24},{24,32},{32,40},{40,48},{48,56},{56,64},{64,7... | collective-permute-start | bytes 24584 | tf_op jit(solution)/shard_map/ppermute | solution.py:185
  19.5 0.9 copy-start.7
  19.6 3.2 %copy-start.19 = (bf16[4,128]{1,0:T(4,128)(2,1)}, bf16[4,128]{1,0:T(4,128)(2,1)S(1)}, u32[]{:S(2)}) copy-start(bf16[4,128]{1,0:T(4,128)(2,1)S(1)} %fusion.121) | copy-start | bytes 3076
  20.4 31.3 %copy-start.27 = (f32[5,128]{1,0:T(8,128)S(1)}, f32[5,128]{1,0:T(8,128)}, u32[]{:S(2)}) copy-start(f32[5,128]{1,0:T(8,128)} %param.15) | copy-start | bytes 7684
  46.0 5.7 %copy-start.8 = (bf16[16,1,128]{2,1,0:T(2,128)(2,1)}, bf16[16,1,128]{2,1,0:T(2,128)(2,1)S(1)}, u32[]{:S(2)}) copy-start(bf16[16,1,128]{2,1,0:T(2,128)(2,1)S(1)} %copy.183) | copy-start | bytes 12292
  46.0 5.7 %copy-start.10 = (bf16[16,1,128]{2,1,0:T(2,128)(2,1)}, bf16[16,1,128]{2,1,0:T(2,128)(2,1)S(1)}, u32[]{:S(2)}) copy-start(bf16[16,1,128]{2,1,0:T(2,128)(2,1)S(1)} %copy.182) | copy-start | bytes 12292
  46.0 9.2 %copy-start.12 = (bf16[1,32,128]{2,1,0:T(8,128)(2,1)}, bf16[1,32,128]{2,1,0:T(8,128)(2,1)S(1)}, u32[]{:S(2)}) copy-start(bf16[1,32,128]{2,1,0:T(8,128)(2,1)S(1)} %collective-permute-done) | copy-start | bytes 24580
  46.0 9.1 %copy-start.14 = (bf16[1,32,128]{2,1,0:T(8,128)(2,1)}, bf16[1,32,128]{2,1,0:T(8,128)(2,1)S(1)}, u32[]{:S(2)}) copy-start(bf16[1,32,128]{2,1,0:T(8,128)(2,1)S(1)} %collective-permute-done.1) | copy-start | bytes 24580
  46.9 8.2 %all-to-all-start.1 = ((f32[8,5,128]{2,1,0:T(8,128)}), f32[8,5,128]{2,1,0:T(8,128)S(1)}, u32[]{:S(2)}, u32[]{:S(2)}) async-start(f32[8,5,128]{2,1,0:T(8,128)} %broadcast_in_dim.51), calls=%async_computation.1 | async-start | bytes 65536 | tf_op jit(solution)/shard_map/all_to_all | solution.py:58
  56.2 26.1 %all-to-all-start.2 = ((f32[12,5,128]{2,1,0:T(8,128)}), f32[12,5,128]{2,1,0:T(8,128)}, u32[]{:S(2)}, u32[]{:S(2)}) async-start(f32[12,5,128]{2,1,0:T(8,128)} %broadcast_in_dim.52), calls=%async_computation.2 | async-start | bytes 98304 | tf_op jit(solution)/shard_map/all_to_all | solution.py:58
  72.4 0.8 copy-start.21
  72.4 0.8 copy-start.20
  73.2 1.0 copy-start.1
  84.0 19.7 %all-to-all-start.3 = ((bf16[8,272,128]{2,1,0:T(8,128)(2,1)}), bf16[8,272,128]{2,1,0:T(8,128)(2,1)S(1)}, u32[]{:S(2)}, u32[]{:S(2)}) async-start(bf16[8,272,128]{2,1,0:T(8,128)(2,1)} %pad_maximum_fusion.3), calls=%async_computation.3 | async-start | bytes 1114112 | tf_op jit(solution)/shard_map/all_to_all | solution.py:244
  87.7 2.9 %copy-start.9 = (bf16[16,1,128]{2,1,0:T(2,128)(2,1)S(1)}, bf16[16,1,128]{2,1,0:T(2,128)(2,1)}, u32[]{:S(2)}) copy-start(bf16[16,1,128]{2,1,0:T(2,128)(2,1)} %copy-done.8) | copy-start | bytes 12292
  87.8 2.9 %copy-start.11 = (bf16[16,1,128]{2,1,0:T(2,128)(2,1)S(1)}, bf16[16,1,128]{2,1,0:T(2,128)(2,1)}, u32[]{:S(2)}) copy-start(bf16[16,1,128]{2,1,0:T(2,128)(2,1)} %copy-done.10) | copy-start | bytes 12292
  87.8 2.9 %copy-start.13 = (bf16[1,32,128]{2,1,0:T(8,128)(2,1)S(1)}, bf16[1,32,128]{2,1,0:T(8,128)(2,1)}, u32[]{:S(2)}) copy-start(bf16[1,32,128]{2,1,0:T(8,128)(2,1)} %copy-done.12) | copy-start | bytes 24580
  87.8 2.9 %copy-start.15 = (bf16[1,32,128]{2,1,0:T(8,128)(2,1)S(1)}, bf16[1,32,128]{2,1,0:T(8,128)(2,1)}, u32[]{:S(2)}) copy-start(bf16[1,32,128]{2,1,0:T(8,128)(2,1)} %copy-done.14) | copy-start | bytes 24580
  87.8 2.9 %copy-start.22 = (f32[128]{0:T(128)S(1)}, f32[128]{0:T(128)}, u32[]{:S(2)}) copy-start(f32[128]{0:T(128)} %get-tuple-element.53) | copy-start | bytes 1540
  87.8 2.9 %copy-start.23 = (f32[128]{0:T(128)S(1)}, f32[128]{0:T(128)}, u32[]{:S(2)}) copy-start(f32[128]{0:T(128)} %get-tuple-element.54) | copy-start | bytes 1540
  87.8 2.9 %copy-start.24 = (f32[128]{0:T(128)S(1)}, f32[128]{0:T(128)}, u32[]{:S(2)}) copy-start(f32[128]{0:T(128)} %get-tuple-element.55) | copy-start | bytes 1540
  87.8 2.9 %copy-start.25 = (f32[128]{0:T(128)S(1)}, f32[128]{0:T(128)}, u32[]{:S(2)}) copy-start(f32[128]{0:T(128)} %get-tuple-element.56) | copy-start | bytes 1540
  87.8 2.9 %copy-start.26 = (f32[128]{0:T(128)S(1)}, f32[128]{0:T(128)}, u32[]{:S(2)}) copy-start(f32[128]{0:T(128)} %get-tuple-element.57) | copy-start | bytes 1540
  90.5 1.1 copy-start.4
  90.5 13.3 %copy-start.17 = (f32[16,4]{0,1:T(4,128)S(1)}, f32[16,4]{0,1:T(4,128)}, u32[]{:S(2)}) copy-start(f32[16,4]{0,1:T(4,128)} %copy-done.16) | copy-start | bytes 772
  90.6 14.4 %copy-start.3 = (f32[4,128,128]{2,1,0:T(8,128)S(1)}, f32[4,128,128]{2,1,0:T(8,128)}, u32[]{:S(2)}) copy-start(f32[4,128,128]{2,1,0:T(8,128)} %fusion.47) | copy-start | bytes 786436
